TPU v7x, 32 devices: a whole 2x2x4 slice. The times are simulated.
32 devices in a mesh: groups: 2 (over y), seq: 4 (over z), head: 2 (over x), rep: 2 (over core).
Axes of the slice: x: 2, y: 2, z: 4, core: 2. Of those that a mesh axis runs over, the one named last changes fastest.
Arguments:
- segment_ids: int32 [2048], P(('groups', 'seq')), parts along dimension 0, may hold values from 0 to 3, never falling along the last dimension, each value on 1 to 640 neighbouring positions
- window_query: bfloat16 [2048, 8, 512], P(('groups', 'seq'), 'head', 'rep'), parts along dimension 0, may hold values from -120 to 120
- window_keys: bfloat16 [2048, 512], P(('groups', 'seq'), 'head'), parts along dimension 0, may hold values from -4 to 4
- window_values: bfloat16 [2048, 512], P(('groups', 'seq'), 'head'), parts along dimension 0, may hold values from -6 to 6
- window_grad_out: bfloat16 [2048, 8, 512], P(('groups', 'seq'), 'head', 'rep'), parts along dimension 0, may hold values from -6 to 6
- window_sinks: float32 [8, 8], P('head', 'rep'), may hold values from 1 to 6
- full_query: bfloat16 [2048, 8, 512], P(('groups', 'seq'), 'head', 'rep'), parts along dimension 0, may hold values from -120 to 120
- full_keys: bfloat16 [2048, 512], P(('groups', 'seq'), 'head'), parts along dimension 0, may hold values from -4 to 4
- full_values: bfloat16 [2048, 512], P(('groups', 'seq'), 'head'), parts along dimension 0, may hold values from -6 to 6
- full_grad_out: bfloat16 [2048, 8, 512], P(('groups', 'seq'), 'head', 'rep'), parts along dimension 0, may hold values from -6 to 6
- full_sinks: float32 [8, 8], P('head', 'rep'), may hold values from 1 to 6
Outputs:
- window_dq: bfloat16 [2048, 8, 512], P(('groups', 'seq'), 'head', 'rep'), parts along dimension 0
- window_dk: bfloat16 [2048, 512], P(('groups', 'seq'), 'head'), parts along dimension 0
- window_dv: bfloat16 [2048, 512], P(('groups', 'seq'), 'head'), parts along dimension 0
- full_dq: bfloat16 [2048, 8, 512], P(('groups', 'seq'), 'head', 'rep'), parts along dimension 0
- full_dk: bfloat16 [2048, 512], P(('groups', 'seq'), 'head'), parts along dimension 0
- full_dv: bfloat16 [2048, 512], P(('groups', 'seq'), 'head'), parts along dimension 0
There are 2 independent parts, one for each index of `groups`. A program takes and returns all parts, laid end to end along the dimension named above; an argument that names none is the same for every part. Nothing has to cross between parts.
Inputs may be any that keep to these rules, and one draw needn't show every extreme that they name: `segment_ids`: ids never fall along the sequence; there are 4 documents, the longest exactly 640 positions.
All inputs are finite; a program needn't handle non-finite values.
Results may differ from a plain program's by a relative error of at most 0.02.
Values may be sent and summed in bfloat16 or wider, within the bound.
No kernel may reach another device: no remote copies, remote signals or barrier semaphores. Data moves between devices by JAX's collectives and lax.ppermute only.
A program may use at most 64 MiB of HBM per device.

v0:
```python
import math

import jax
import jax.numpy as jnp
from jax import lax
from jax.sharding import PartitionSpec as P

HD = 64
WINDOW = 128


neg_big = -1e30


def passed_along(value, axis, steps):
    count = lax.axis_size(axis)
    first, last = (max(0, -steps), min(count, count - steps))
    return lax.ppermute(value, axis, [(source, source + steps) for source in range(first, last)])


def shifted(block, axis, distance):
    devices = range(lax.axis_size(axis))
    route = [((i - distance) % len(devices), i) for i in devices]
    return lax.ppermute(block, axis, route)


def score_block(queries, key_block, score_scale):
    return (
        jnp.einsum("qgjd,kgd->gjqk", queries, key_block, preferred_element_type=jnp.float32)
        * score_scale
    )


def fold_block(running, queries, key_block, value_block, visible, score_scale):
    run_max, run_sum, weighted = running
    scores = jnp.where(visible[None, None], score_block(queries, key_block, score_scale), neg_big)
    new_max = jnp.maximum(run_max, jnp.max(scores, axis=-1))
    factor = jnp.exp(run_max - new_max)
    weights = jnp.exp(scores - new_max[..., None])
    run_sum = run_sum * factor + jnp.sum(weights, axis=-1)
    weighted = weighted * factor[..., None] + jnp.einsum(
        "gjqk,kgd->gjqd",
        weights.astype(jnp.bfloat16),
        value_block,
        preferred_element_type=jnp.float32,
    )
    return (new_max, run_sum, weighted)


def grad_core(weights, queries, grad_heads, key_block, value_block, row_delta, score_scale):
    grad_weights = jnp.einsum(
        "qgjd,kgd->gjqk", grad_heads, value_block, preferred_element_type=jnp.float32
    )
    grad_scores = weights * (grad_weights - row_delta[..., None])
    weights_low = weights.astype(jnp.bfloat16)
    scores_low = grad_scores.astype(jnp.bfloat16)
    value_grad = jnp.einsum(
        "gjqk,qgjd->kgd", weights_low, grad_heads, preferred_element_type=jnp.float32
    )
    key_grad = (
        jnp.einsum("gjqk,qgjd->kgd", scores_low, queries, preferred_element_type=jnp.float32)
        * score_scale
    )
    query_grad = (
        jnp.einsum("gjqk,kgd->qgjd", scores_low, key_block, preferred_element_type=jnp.float32)
        * score_scale
    )
    return (query_grad, key_grad, value_grad)


def output_delta(grad_heads, attended):
    return jnp.sum(jnp.transpose(grad_heads.astype(jnp.float32), (1, 2, 0, 3)) * attended, axis=-1)


def window_layer(
    segment_ids, query_rows, key_rows, value_rows, grad_rows, sink_logits, score_scale
):
    local_rows = query_rows.shape[0]
    key_cols = key_rows.shape[1]
    groups = key_cols // HD
    window_rows = WINDOW
    tail_keys = key_rows[local_rows - window_rows :]
    tail_values = value_rows[local_rows - window_rows :]
    tail_segs = segment_ids[local_rows - window_rows :]
    halo_keys, halo_values, halo_segs = passed_along((tail_keys, tail_values, tail_segs), "seq", 1)
    first_row = lax.axis_index("seq") * local_rows
    seen_keys = jnp.concatenate([halo_keys, key_rows], axis=0).reshape(
        local_rows + window_rows, groups, HD
    )
    seen_values = jnp.concatenate([halo_values, value_rows], axis=0).reshape(
        local_rows + window_rows, groups, HD
    )
    seen_segs = jnp.concatenate([halo_segs, segment_ids], axis=0)
    key_pos = first_row - window_rows + jnp.arange(local_rows + window_rows)
    query_pos = first_row + jnp.arange(local_rows)
    distance = query_pos[:, None] - key_pos[None, :]
    visible = (
        (distance >= 0)
        & (distance < window_rows)
        & (key_pos[None, :] >= 0)
        & (segment_ids[:, None] == seen_segs[None, :])
    )
    queries = query_rows.reshape(local_rows, groups, -1, HD)
    grad_heads = grad_rows.reshape(local_rows, groups, -1, HD)
    scores = jnp.where(visible[None, None], score_block(queries, seen_keys, score_scale), neg_big)
    sink_rows = sink_logits[:, :, None]
    row_max = jnp.maximum(jnp.max(scores, axis=-1), sink_rows)
    denominator = jnp.sum(jnp.exp(scores - row_max[..., None]), axis=-1) + jnp.exp(
        sink_rows - row_max
    )
    log_total = row_max + jnp.log(denominator)
    weights = jnp.where(visible[None, None], jnp.exp(scores - log_total[..., None]), 0.0)
    attended = jnp.einsum(
        "gjqk,kgd->gjqd",
        weights.astype(jnp.bfloat16),
        seen_values,
        preferred_element_type=jnp.float32,
    )
    row_delta = output_delta(grad_heads, attended)
    query_grad, key_grad, value_grad = grad_core(
        weights, queries, grad_heads, seen_keys, seen_values, row_delta, score_scale
    )
    key_grad = key_grad.reshape(local_rows + window_rows, key_cols)
    value_grad = value_grad.reshape(local_rows + window_rows, key_cols)
    back_keys, back_values = (
        passed_along(key_grad[:window_rows].astype(jnp.bfloat16), "seq", -1).astype(jnp.float32),
        passed_along(value_grad[:window_rows].astype(jnp.bfloat16), "seq", -1).astype(jnp.float32),
    )
    own_keys = key_grad[window_rows:]
    own_values = value_grad[window_rows:]
    split_at = local_rows - window_rows
    own_keys = jnp.concatenate([own_keys[:split_at], own_keys[split_at:] + back_keys], axis=0)
    own_values = jnp.concatenate(
        [own_values[:split_at], own_values[split_at:] + back_values], axis=0
    )
    return (query_grad.reshape(local_rows, groups, -1).astype(jnp.bfloat16), own_keys, own_values)


def body(
    segment_ids,
    window_query,
    window_keys,
    window_values,
    window_grad_out,
    window_sinks,
    full_query,
    full_keys,
    full_values,
    full_grad_out,
    full_sinks,
):
    score_scale = 1.0 / math.sqrt(HD)
    window_dq, window_kpart, window_vpart = window_layer(
        segment_ids,
        window_query,
        window_keys,
        window_values,
        window_grad_out,
        window_sinks,
        score_scale,
    )
    local_rows = full_query.shape[0]
    key_cols = full_keys.shape[1]
    groups = key_cols // HD
    seq_index = lax.axis_index("seq")
    seq_count = lax.axis_size("seq")
    query_pos = seq_index * local_rows + jnp.arange(local_rows)
    queries = full_query.reshape(local_rows, groups, -1, HD)
    grad_heads = full_grad_out.reshape(local_rows, groups, -1, HD)
    heads_per = queries.shape[2]
    sink_rows = jnp.broadcast_to(full_sinks[:, :, None], (groups, heads_per, local_rows))
    start_state = (
        sink_rows,
        jnp.ones_like(sink_rows),
        jnp.zeros((groups, heads_per, local_rows, HD), jnp.float32),
    )
    running = start_state
    first_row = jnp.int32(0)
    key_piece = lax.all_gather(full_keys, "seq", axis=0, tiled=True)
    value_piece = lax.all_gather(full_values, "seq", axis=0, tiled=True)
    seg_piece = lax.all_gather(segment_ids, "seq", axis=0, tiled=True)
    key_count = key_piece.shape[0]
    sub_rows = math.gcd(key_count, 512)
    for offset in range(0, key_count, sub_rows):
        key_block = key_piece[offset : offset + sub_rows].reshape(sub_rows, groups, HD)
        value_block = value_piece[offset : offset + sub_rows].reshape(sub_rows, groups, HD)
        seg_block = seg_piece[offset : offset + sub_rows]
        key_pos = first_row + offset + jnp.arange(sub_rows)
        visible = (query_pos[:, None] >= key_pos[None, :]) & (
            segment_ids[:, None] == seg_block[None, :]
        )
        previous = running
        running = fold_block(previous, queries, key_block, value_block, visible, score_scale)
    run_max, run_sum, weighted = running
    log_total = run_max + jnp.log(run_sum)
    row_delta = output_delta(grad_heads, weighted / run_sum[..., None])

    def contribution(source, keys_now, values_now, segs_now):
        key_pos = source * local_rows + jnp.arange(local_rows)
        visible = (query_pos[:, None] >= key_pos[None, :]) & (
            segment_ids[:, None] == segs_now[None, :]
        )
        key_block = keys_now.reshape(local_rows, groups, HD)
        value_block = values_now.reshape(local_rows, groups, HD)
        scores = score_block(queries, key_block, score_scale)
        weights = jnp.where(visible[None, None], jnp.exp(scores - log_total[..., None]), 0.0)
        query_grad, key_grad, value_grad = grad_core(
            weights, queries, grad_heads, key_block, value_block, row_delta, score_scale
        )
        return (
            query_grad,
            key_grad.reshape(local_rows, key_cols),
            value_grad.reshape(local_rows, key_cols),
        )

    query_start = jnp.zeros(queries.shape, jnp.float32)

    def circle_turn(turn_index, circle_state):
        query_acc, keys_now, values_now, segs_now, acc_keys, acc_values = circle_state
        source = (seq_index - turn_index) % seq_count
        query_part, key_part, value_part = contribution(source, keys_now, values_now, segs_now)
        keys_now, values_now, segs_now = passed_along((keys_now, values_now, segs_now), "seq", 1)
        acc_keys, acc_values = (
            shifted((acc_keys + key_part).astype(jnp.bfloat16), "seq", 1).astype(jnp.float32),
            shifted((acc_values + value_part).astype(jnp.bfloat16), "seq", 1).astype(jnp.float32),
        )
        return (query_acc + query_part, keys_now, values_now, segs_now, acc_keys, acc_values)

    zero_acc = jnp.zeros((local_rows, key_cols), jnp.float32)
    circle_state = (query_start, full_keys, full_values, segment_ids, zero_acc, zero_acc)
    query_acc, keys_now, values_now, segs_now, acc_keys, acc_values = lax.fori_loop(
        0, seq_count, circle_turn, circle_state
    )
    window_ksum, window_vsum, full_ksum, full_vsum = (
        lax.psum(window_kpart.astype(jnp.bfloat16), "rep").astype(jnp.float32),
        lax.psum(window_vpart.astype(jnp.bfloat16), "rep").astype(jnp.float32),
        lax.psum(acc_keys.astype(jnp.bfloat16), "rep").astype(jnp.float32),
        lax.psum(acc_values.astype(jnp.bfloat16), "rep").astype(jnp.float32),
    )
    full_dq = query_acc.reshape(local_rows, groups, -1).astype(jnp.bfloat16)
    return (
        window_dq,
        window_ksum.astype(jnp.bfloat16),
        window_vsum.astype(jnp.bfloat16),
        full_dq,
        full_ksum.astype(jnp.bfloat16),
        full_vsum.astype(jnp.bfloat16),
    )


def solution(mesh):
    placed = (
        P(("groups", "seq")),
        P(("groups", "seq"), "head", "rep"),
        P(("groups", "seq"), "head"),
        P(("groups", "seq"), "head"),
        P(("groups", "seq"), "head", "rep"),
        P("head", "rep"),
        P(("groups", "seq"), "head", "rep"),
        P(("groups", "seq"), "head"),
        P(("groups", "seq"), "head"),
        P(("groups", "seq"), "head", "rep"),
        P("head", "rep"),
    )
    return jax.shard_map(
        body,
        mesh=mesh,
        in_specs=placed,
        out_specs=(
            P(("groups", "seq"), "head", "rep"),
            P(("groups", "seq"), "head"),
            P(("groups", "seq"), "head"),
            P(("groups", "seq"), "head", "rep"),
            P(("groups", "seq"), "head"),
            P(("groups", "seq"), "head"),
        ),
        check_vma=False,
    )
```

profile of v0, /device:TPU:0, one launch (start us, length us, event | category | flops | bytes accessed | tf_op | source)
XLA Modules:
  0.0 240.3 jit_solution(12734191691278870327)
XLA Ops:
  7.3 17.6 %all_gather.10 = bf16[1024,256]{1,0:T(8,128)(2,1)S(1)} all-gather(bf16[256,256]{1,0:T(8,128)(2,1)} %param.20), channel_id=1, replica_groups=mesh['groups'=2,'seq'=4,'head'=2,'rep'=2] {'seq'}, dimensions={0}, use_global_device_ids=true | all-gather | bytes 655360 | tf_op jit(solution)/shard_map/all_gather | solution.py:179
  25.8 16.6 %all_gather.11 = bf16[1024,256]{1,0:T(8,128)(2,1)S(1)} all-gather(bf16[256,256]{1,0:T(8,128)(2,1)} %param.21), channel_id=1, replica_groups=mesh['groups'=2,'seq'=4,'head'=2,'rep'=2] {'seq'}, dimensions={0}, use_global_device_ids=true | all-gather | bytes 655360 | tf_op jit(solution)/shard_map/all_gather | solution.py:180
  45.9 10.6 %all-gather = s32[4,1,256]{2,1,0:T(1,128)S(1)} all-gather(s32[1,1,256]{2,1,0:T(1,128)} %bitcast.254), channel_id=1, replica_groups=mesh['groups'=2,'seq'=4,'head'=2,'rep'=2] {'seq'}, dimensions={0}, use_global_device_ids=true | all-gather | bytes 5120 | tf_op jit(solution)/shard_map/all_gather | solution.py:181
  64.4 2.1 copy.100
  70.4 3.8 %fusion.18 = (f32[4,4,256]{2,1,0:T(4,128)S(1)}, f32[4,4,256]{2,1,0:T(4,128)S(1)}) fusion(f32[4,512,256,4]{2,1,3,0:T(8,128)S(1)} %get-tuple-element.506, f32[4,4,256]{2,1,0:T(4,128)S(1)} %get-tuple-element.483, pred[256,512]{0,1:T(8,128)(4,1)S(1)} %get-tuple-element.498, f32[4,4,256]{2,1,0:T(4,128)S(1)} %max.50, ...), kind=kLoop, calls=%fused_computation.29 | loop fusion | flops 16769024 | bytes 17104896 | tf_op jit(solution)/shard_map/reduce_sum | solution.py:40
  74.4 2.1 fusion.39
  76.5 3.2 %fusion.46 = f32[4,4,256]{2,1,0:T(4,128)S(1)} fusion(bf16[256,4,4,64]{0,3,2,1:T(8,128)(2,1)} %bitcast.42, f32[4,4,256,64]{2,3,1,0:T(8,128)S(1)} %fusion.39, bf16[512,4,64,1]{0,2,3,1:T(8,128)(2,1)S(1)} %bitcast.246, f32[4,512,256,4]{2,1,3,0:T(8,128)S(1)} %get-tuple-element.508, f32[4,4,256]{2,1,0:T(4,128)S(1)} %max.50, ...), kind=kOutput, calls=%fused_computation.58 | convolution fusion | flops 278130688 | bytes 10403840 | tf_op jit(solution)/shard_map/gjqk,kgd->gjqd/dot_general | solution.py:41
  79.8 86.5 %while.26 = (s32[]{:T(128)}, f32[256,4,4,64]{0,3,2,1:T(8,128)S(1)}, bf16[256,256]{0,1:T(8,128)(2,1)S(1)}, bf16[256,256]{0,1:T(8,128)(2,1)S(1)}, s32[256]{0:T(256...) while((s32[]{:T(128)}, f32[256,4,4,64]{0,3,2,1:T(8,128)S(1)}, ...), condition=%wide.region_11.12_spmd.clone, body=%wide.region_10.11_spmd.clone.sunk | while | flops 683147776 | bytes 28963340 | solution.py:231
  79.8 1.4 collective-permute-start
  81.3 2.7 %collective-permute-start.1 = (bf16[256,256]{0,1:T(8,128)(2,1)S(1)}, bf16[256,256]{0,1:T(8,128)(2,1)S(1)}, u32[]{:S(2)}, u32[]{:S(2)}) collective-permute-start(bf16[256,256]{0,1:T(8,128)(2,1)S(1)} %copy.142), channel_id=1, source_target_pairs={{0,4},{4,8},{8,12},{1,5},{5,9},{9,13},{2,6},{6,10},{10,14},{3,7},{... | collective-permute-start | bytes 393224 | tf_op jit(solution)/shard_map/while/body/eval_jaxpr/ppermute | solution.py:18
  84.0 2.6 %collective-permute-start.2 = (s32[256]{0:T(256)S(1)}, s32[256]{0:T(256)S(1)}, u32[]{:S(2)}, u32[]{:S(2)}) collective-permute-start(s32[256]{0:T(256)S(1)} %copy.143), channel_id=1, source_target_pairs={{0,4},{4,8},{8,12},{1,5},{5,9},{9,13},{2,6},{6,10},{10,14},{3,7},{... | collective-permute-start | bytes 3080 | tf_op jit(solution)/shard_map/while/body/eval_jaxpr/ppermute | solution.py:18
  87.5 2.4 %fusion.121 = bf16[4,4,256,256]{2,3,1,0:T(8,128)(2,1)S(1)} fusion(f32[4,256,256,4]{2,1,3,0:T(8,128)S(1)} %fusion.120, bf16[256,4,64,1]{0,2,3,1:T(8,128)(2,1)S(1)} %bitcast.234, bf16[256,4,4,64]{0,3,2,1:T(8,128)(2,1)} %get-tuple-element.645, f32[4,4,256]{2,1,0:T(4,128)S(1)} %get-tuple-element.646, f32[4,4,256]{2,1,0:T(4,128)S(1)} %get-tuple-element.644, ...), kind=kOutput, calls=%fused_computation.3.clone.1 | convolution fusion | flops 140509184 | bytes 7045120 | tf_op jit(solution)/shard_map/while/body/eval_jaxpr/qgjd,kgd->gjqk/dot_general | solution.py:51
  90.8 1.9 fusion.125
  93.4 4.2 %collective-permute-done.3 = bf16[256,256]{0,1:T(8,128)(2,1)S(1)} collective-permute-done((bf16[256,256]{0,1:T(8,128)(2,1)S(1)}, bf16[256,256]{0,1:T(8,128)(2,1)S(1)}, u32[]{:S(2)}, u32[]{:S(2)}) %collective-permute-start.3) | collective-permute-done | bytes 131104 | tf_op jit(solution)/shard_map/while/body/eval_jaxpr/ppermute | solution.py:24
  97.6 2.0 collective-permute-done.4
  101.1 3.6 %collective-permute-start.1 = (bf16[256,256]{0,1:T(8,128)(2,1)S(1)}, bf16[256,256]{0,1:T(8,128)(2,1)S(1)}, u32[]{:S(2)}, u32[]{:S(2)}) collective-permute-start(bf16[256,256]{0,1:T(8,128)(2,1)S(1)} %copy.142), channel_id=1, source_target_pairs={{0,4},{4,8},{8,12},{1,5},{5,9},{9,13},{2,6},{6,10},{10,14},{3,7},{... | collective-permute-start | bytes 393224 | tf_op jit(solution)/shard_map/while/body/eval_jaxpr/ppermute | solution.py:18
  104.8 4.4 %collective-permute-start.2 = (s32[256]{0:T(256)S(1)}, s32[256]{0:T(256)S(1)}, u32[]{:S(2)}, u32[]{:S(2)}) collective-permute-start(s32[256]{0:T(256)S(1)} %copy.143), channel_id=1, source_target_pairs={{0,4},{4,8},{8,12},{1,5},{5,9},{9,13},{2,6},{6,10},{10,14},{3,7},{... | collective-permute-start | bytes 3080 | tf_op jit(solution)/shard_map/while/body/eval_jaxpr/ppermute | solution.py:18
  110.1 2.4 %fusion.121 = bf16[4,4,256,256]{2,3,1,0:T(8,128)(2,1)S(1)} fusion(f32[4,256,256,4]{2,1,3,0:T(8,128)S(1)} %fusion.120, bf16[256,4,64,1]{0,2,3,1:T(8,128)(2,1)S(1)} %bitcast.234, bf16[256,4,4,64]{0,3,2,1:T(8,128)(2,1)} %get-tuple-element.645, f32[4,4,256]{2,1,0:T(4,128)S(1)} %get-tuple-element.646, f32[4,4,256]{2,1,0:T(4,128)S(1)} %get-tuple-element.644, ...), kind=kOutput, calls=%fused_computation.3.clone.1 | convolution fusion | flops 140509184 | bytes 7045120 | tf_op jit(solution)/shard_map/while/body/eval_jaxpr/qgjd,kgd->gjqk/dot_general | solution.py:51
  113.4 1.9 fusion.125
  116.0 4.2 %collective-permute-done.3 = bf16[256,256]{0,1:T(8,128)(2,1)S(1)} collective-permute-done((bf16[256,256]{0,1:T(8,128)(2,1)S(1)}, bf16[256,256]{0,1:T(8,128)(2,1)S(1)}, u32[]{:S(2)}, u32[]{:S(2)}) %collective-permute-start.3) | collective-permute-done | bytes 131104 | tf_op jit(solution)/shard_map/while/body/eval_jaxpr/ppermute | solution.py:24
  120.2 2.0 collective-permute-done.4
  123.6 3.2 %collective-permute-start.1 = (bf16[256,256]{0,1:T(8,128)(2,1)S(1)}, bf16[256,256]{0,1:T(8,128)(2,1)S(1)}, u32[]{:S(2)}, u32[]{:S(2)}) collective-permute-start(bf16[256,256]{0,1:T(8,128)(2,1)S(1)} %copy.142), channel_id=1, source_target_pairs={{0,4},{4,8},{8,12},{1,5},{5,9},{9,13},{2,6},{6,10},{10,14},{3,7},{... | collective-permute-start | bytes 393224 | tf_op jit(solution)/shard_map/while/body/eval_jaxpr/ppermute | solution.py:18
  126.8 4.3 %collective-permute-start.2 = (s32[256]{0:T(256)S(1)}, s32[256]{0:T(256)S(1)}, u32[]{:S(2)}, u32[]{:S(2)}) collective-permute-start(s32[256]{0:T(256)S(1)} %copy.143), channel_id=1, source_target_pairs={{0,4},{4,8},{8,12},{1,5},{5,9},{9,13},{2,6},{6,10},{10,14},{3,7},{... | collective-permute-start | bytes 3080 | tf_op jit(solution)/shard_map/while/body/eval_jaxpr/ppermute | solution.py:18
  132.1 2.4 %fusion.121 = bf16[4,4,256,256]{2,3,1,0:T(8,128)(2,1)S(1)} fusion(f32[4,256,256,4]{2,1,3,0:T(8,128)S(1)} %fusion.120, bf16[256,4,64,1]{0,2,3,1:T(8,128)(2,1)S(1)} %bitcast.234, bf16[256,4,4,64]{0,3,2,1:T(8,128)(2,1)} %get-tuple-element.645, f32[4,4,256]{2,1,0:T(4,128)S(1)} %get-tuple-element.646, f32[4,4,256]{2,1,0:T(4,128)S(1)} %get-tuple-element.644, ...), kind=kOutput, calls=%fused_computation.3.clone.1 | convolution fusion | flops 140509184 | bytes 7045120 | tf_op jit(solution)/shard_map/while/body/eval_jaxpr/qgjd,kgd->gjqk/dot_general | solution.py:51
  135.4 1.9 fusion.125
  138.0 4.2 %collective-permute-done.3 = bf16[256,256]{0,1:T(8,128)(2,1)S(1)} collective-permute-done((bf16[256,256]{0,1:T(8,128)(2,1)S(1)}, bf16[256,256]{0,1:T(8,128)(2,1)S(1)}, u32[]{:S(2)}, u32[]{:S(2)}) %collective-permute-start.3) | collective-permute-done | bytes 131104 | tf_op jit(solution)/shard_map/while/body/eval_jaxpr/ppermute | solution.py:24
  142.2 2.0 collective-permute-done.4
  145.6 3.2 %collective-permute-start.1 = (bf16[256,256]{0,1:T(8,128)(2,1)S(1)}, bf16[256,256]{0,1:T(8,128)(2,1)S(1)}, u32[]{:S(2)}, u32[]{:S(2)}) collective-permute-start(bf16[256,256]{0,1:T(8,128)(2,1)S(1)} %copy.142), channel_id=1, source_target_pairs={{0,4},{4,8},{8,12},{1,5},{5,9},{9,13},{2,6},{6,10},{10,14},{3,7},{... | collective-permute-start | bytes 393224 | tf_op jit(solution)/shard_map/while/body/eval_jaxpr/ppermute | solution.py:18
  148.8 4.3 %collective-permute-start.2 = (s32[256]{0:T(256)S(1)}, s32[256]{0:T(256)S(1)}, u32[]{:S(2)}, u32[]{:S(2)}) collective-permute-start(s32[256]{0:T(256)S(1)} %copy.143), channel_id=1, source_target_pairs={{0,4},{4,8},{8,12},{1,5},{5,9},{9,13},{2,6},{6,10},{10,14},{3,7},{... | collective-permute-start | bytes 3080 | tf_op jit(solution)/shard_map/while/body/eval_jaxpr/ppermute | solution.py:18
  154.1 2.4 %fusion.121 = bf16[4,4,256,256]{2,3,1,0:T(8,128)(2,1)S(1)} fusion(f32[4,256,256,4]{2,1,3,0:T(8,128)S(1)} %fusion.120, bf16[256,4,64,1]{0,2,3,1:T(8,128)(2,1)S(1)} %bitcast.234, bf16[256,4,4,64]{0,3,2,1:T(8,128)(2,1)} %get-tuple-element.645, f32[4,4,256]{2,1,0:T(4,128)S(1)} %get-tuple-element.646, f32[4,4,256]{2,1,0:T(4,128)S(1)} %get-tuple-element.644, ...), kind=kOutput, calls=%fused_computation.3.clone.1 | convolution fusion | flops 140509184 | bytes 7045120 | tf_op jit(solution)/shard_map/while/body/eval_jaxpr/qgjd,kgd->gjqk/dot_general | solution.py:51
  157.4 1.9 fusion.125
  160.0 4.2 %collective-permute-done.3 = bf16[256,256]{0,1:T(8,128)(2,1)S(1)} collective-permute-done((bf16[256,256]{0,1:T(8,128)(2,1)S(1)}, bf16[256,256]{0,1:T(8,128)(2,1)S(1)}, u32[]{:S(2)}, u32[]{:S(2)}) %collective-permute-start.3) | collective-permute-done | bytes 131104 | tf_op jit(solution)/shard_map/while/body/eval_jaxpr/ppermute | solution.py:24
  164.2 2.0 collective-permute-done.4
  167.6 3.2 %collective-permute-start.5 = (bf16[128,256]{1,0:T(8,128)(2,1)S(1)}, bf16[128,256]{1,0:T(8,128)(2,1)S(1)}, u32[]{:S(2)}, u32[]{:S(2)}) collective-permute-start(bf16[128,256]{1,0:T(8,128)(2,1)S(1)} %slice.71), channel_id=1, source_target_pairs={{0,4},{4,8},{8,12},{1,5},{5,9},{9,13},{2,6},{6,10},{10,14},{3,7},{... | collective-permute-start | bytes 196616 | tf_op jit(solution)/shard_map/ppermute | solution.py:18
  170.8 4.6 %collective-permute-start.7 = (bf16[128,256]{1,0:T(8,128)(2,1)S(1)}, bf16[128,256]{1,0:T(8,128)(2,1)S(1)}, u32[]{:S(2)}, u32[]{:S(2)}) collective-permute-start(bf16[128,256]{1,0:T(8,128)(2,1)S(1)} %slice.73), channel_id=1, source_target_pairs={{0,4},{4,8},{8,12},{1,5},{5,9},{9,13},{2,6},{6,10},{10,14},{3,7},{... | collective-permute-start | bytes 196616 | tf_op jit(solution)/shard_map/ppermute | solution.py:18
  178.3 1.5 copy.86
  182.9 2.5 %fusion.66 = (bf16[384,4,64]{0,2,1:T(8,128)(2,1)S(1)}, f32[384,4,64]{0,2,1:T(8,128)}) fusion(bf16[256,4,4,64]{0,3,2,1:T(8,128)(2,1)S(1)} %bitcast.241, f32[4,384,256,4]{2,1,3,0:T(8,128)S(1)} %get-tuple-element.500, f32[4,4,256]{2,1,0:T(4,128)S(1)} %log_add_fusion.1, pred[256,384]{0,1:T(8,128)(4,1)S(1)} %fusion.52), kind=kOutput, calls=%fused_computation.96 | convolution fusion | flops 209289216 | bytes 7520256 | tf_op jit(solution)/shard_map/gjqk,qgjd->kgd/dot_general | solution.py:57
  188.2 1.9 copy.85
  190.1 4.8 %fusion.43 = f32[4,4,256]{2,1,0:T(4,128)S(1)} fusion(bf16[384,4,64,1]{0,2,3,1:T(8,128)(2,1)} %bitcast.252, bf16[256,4,4,64]{0,3,2,1:T(8,128)(2,1)} %bitcast.242, f32[4,384,256,4]{2,1,3,0:T(8,128)} %copy-done, f32[4,4,256]{2,1,0:T(4,128)S(1)} %log_add_fusion.1, pred[256,384]{0,1:T(8,128)(4,1)S(1)} %fusion.52), kind=kOutput, calls=%fused_computation.52 | convolution fusion | flops 209973248 | bytes 7143424 | tf_op jit(solution)/shard_map/gjqk,kgd->gjqd/dot_general | solution.py:113
  195.0 2.0 fusion.24
  197.0 1.6 copy-done.1
  204.1 3.7 %collective-permute-done.8 = bf16[128,256]{1,0:T(8,128)(2,1)S(1)} collective-permute-done((bf16[128,256]{1,0:T(8,128)(2,1)S(1)}, bf16[128,256]{1,0:T(8,128)(2,1)S(1)}, u32[]{:S(2)}, u32[]{:S(2)}) %collective-permute-start.8) | collective-permute-done | bytes 65568 | tf_op jit(solution)/shard_map/ppermute | solution.py:18
  209.6 2.6 %fusion.42 = bf16[4,64,4,256]{3,1,2,0:T(8,128)(2,1)S(1)} fusion(bf16[384,4,64,1]{0,2,3,1:T(8,128)(2,1)S(1)} %bitcast.237, bf16[4,4,256,384]{2,3,1,0:T(8,128)(2,1)} %copy-done.1), kind=kOutput, calls=%fused_computation.51 | convolution fusion | flops 201850880 | bytes 3866624 | tf_op jit(solution)/shard_map/gjqk,kgd->qgjd/dot_general | solution.py:65
  213.3 13.9 %all-reduce.3.cloned.1.call-done = (bf16[256,256]{1,0:T(8,128)(2,1)}, bf16[256,256]{1,0:T(8,128)(2,1)}, bf16[256,256]{1,0:T(8,128)(2,1)}, bf16[256,256]{1,0:T(8,128)(2,1)}) async-done(((bf16[256,256]{1,0:T(8,128)(2,1)}, bf16[256,256]{1,0:T(8,128)(2,1)}, bf16[256,256]{1,0:T(8,128)(2,1)}, bf16[256,256]{1,0:T(8,128)(2,1)}), (bf16[256,256]{1,0:T(8,128)(2,1)}, bf16[256,256]{1,0:T(8,128)(2,1)}, ...) | async-done | bytes 524304 | tf_op jit(solution)/shard_map/psum | solution.py:235
  227.1 1.6 copy.157
  228.7 1.6 copy.158
  230.3 1.6 copy.159
  231.8 1.6 copy.160
  (175 shorter events, 48.3 us)
Async XLA Ops:
  7.2 59.4 %copy-start.10 = (s32[256]{0:T(256)S(1)}, s32[256]{0:T(256)}, u32[]{:S(2)}) copy-start(s32[256]{0:T(256)} %param.13) | copy-start | bytes 3076
  7.2 220.0 %all-reduce.3.cloned.1.call-start = ((), (), s32[]{:S(2)}) async-start(), calls=%async_computation | async-start | bytes 1048576 | tf_op jit(solution)/shard_map/psum | solution.py:235
  67.5 1.4 copy-start.11
  79.7 86.5 %copy-start.14 = (s32[128]{0:T(128)S(1)}, s32[128]{0:T(128)}, u32[]{:S(2)}) copy-start(s32[128]{0:T(128)} %slice.72) | copy-start | bytes 1540
  79.7 87.8 %copy-start.6 = (bf16[256,256]{1,0:T(8,128)(2,1)S(1)}, bf16[256,256]{1,0:T(8,128)(2,1)}, u32[]{:S(2)}) copy-start(bf16[256,256]{1,0:T(8,128)(2,1)} %param.15) | copy-start | bytes 393220
  79.8 91.1 %copy-start.7 = (bf16[256,256]{1,0:T(8,128)(2,1)S(1)}, bf16[256,256]{1,0:T(8,128)(2,1)}, u32[]{:S(2)}) copy-start(bf16[256,256]{1,0:T(8,128)(2,1)} %param.16) | copy-start | bytes 393220
  79.8 100.1 %copy-start.13 = (s32[256]{0:T(256)S(1)}, s32[256]{0:T(256)}, u32[]{:S(2)}) copy-start(s32[256]{0:T(256)} %iota_add_fusion.4) | copy-start | bytes 3076
  79.8 19.8 %collective-permute-start = (bf16[256,256]{0,1:T(8,128)(2,1)S(1)}, bf16[256,256]{0,1:T(8,128)(2,1)S(1)}, u32[]{:S(2)}, u32[]{:S(2)}) collective-permute-start(bf16[256,256]{0,1:T(8,128)(2,1)S(1)} %copy.141), channel_id=1, source_target_pairs={{0,4},{4,8},{8,12},{1,5},{5,9},{9,13},{2,6},{6,10},{10,14},{3,7},{... | collective-permute-start | bytes 393224 | tf_op jit(solution)/shard_map/while/body/eval_jaxpr/ppermute | solution.py:18
  81.3 18.4 %collective-permute-start.1 = (bf16[256,256]{0,1:T(8,128)(2,1)S(1)}, bf16[256,256]{0,1:T(8,128)(2,1)S(1)}, u32[]{:S(2)}, u32[]{:S(2)}) collective-permute-start(bf16[256,256]{0,1:T(8,128)(2,1)S(1)} %copy.142), channel_id=1, source_target_pairs={{0,4},{4,8},{8,12},{1,5},{5,9},{9,13},{2,6},{6,10},{10,14},{3,7},{... | collective-permute-start | bytes 393224 | tf_op jit(solution)/shard_map/while/body/eval_jaxpr/ppermute | solution.py:18
  84.0 15.6 %collective-permute-start.2 = (s32[256]{0:T(256)S(1)}, s32[256]{0:T(256)S(1)}, u32[]{:S(2)}, u32[]{:S(2)}) collective-permute-start(s32[256]{0:T(256)S(1)} %copy.143), channel_id=1, source_target_pairs={{0,4},{4,8},{8,12},{1,5},{5,9},{9,13},{2,6},{6,10},{10,14},{3,7},{... | collective-permute-start | bytes 3080 | tf_op jit(solution)/shard_map/while/body/eval_jaxpr/ppermute | solution.py:18
  90.8 6.8 %collective-permute-start.3 = (bf16[256,256]{0,1:T(8,128)(2,1)S(1)}, bf16[256,256]{0,1:T(8,128)(2,1)S(1)}, u32[]{:S(2)}, u32[]{:S(2)}) collective-permute-start(bf16[256,256]{0,1:T(8,128)(2,1)S(1)} %fusion.124), channel_id=1, source_target_pairs={{12,0},{0,4},{4,8},{8,12},{13,1},{1,5},{5,9},{9,13},{14,2},{2,6},{... | collective-permute-start | bytes 393224 | tf_op jit(solution)/shard_map/while/body/eval_jaxpr/ppermute | solution.py:24
  92.8 6.8 %collective-permute-start.4 = (bf16[256,256]{0,1:T(8,128)(2,1)S(1)}, bf16[256,256]{0,1:T(8,128)(2,1)S(1)}, u32[]{:S(2)}, u32[]{:S(2)}) collective-permute-start(bf16[256,256]{0,1:T(8,128)(2,1)S(1)} %fusion.126), channel_id=1, source_target_pairs={{12,0},{0,4},{4,8},{8,12},{13,1},{1,5},{5,9},{9,13},{14,2},{2,6},{... | collective-permute-start | bytes 393224 | tf_op jit(solution)/shard_map/while/body/eval_jaxpr/ppermute | solution.py:24
  99.7 22.5 %collective-permute-start = (bf16[256,256]{0,1:T(8,128)(2,1)S(1)}, bf16[256,256]{0,1:T(8,128)(2,1)S(1)}, u32[]{:S(2)}, u32[]{:S(2)}) collective-permute-start(bf16[256,256]{0,1:T(8,128)(2,1)S(1)} %copy.141), channel_id=1, source_target_pairs={{0,4},{4,8},{8,12},{1,5},{5,9},{9,13},{2,6},{6,10},{10,14},{3,7},{... | collective-permute-start | bytes 393224 | tf_op jit(solution)/shard_map/while/body/eval_jaxpr/ppermute | solution.py:18
  101.1 21.1 %collective-permute-start.1 = (bf16[256,256]{0,1:T(8,128)(2,1)S(1)}, bf16[256,256]{0,1:T(8,128)(2,1)S(1)}, u32[]{:S(2)}, u32[]{:S(2)}) collective-permute-start(bf16[256,256]{0,1:T(8,128)(2,1)S(1)} %copy.142), channel_id=1, source_target_pairs={{0,4},{4,8},{8,12},{1,5},{5,9},{9,13},{2,6},{6,10},{10,14},{3,7},{... | collective-permute-start | bytes 393224 | tf_op jit(solution)/shard_map/while/body/eval_jaxpr/ppermute | solution.py:18
  104.8 17.4 %collective-permute-start.2 = (s32[256]{0:T(256)S(1)}, s32[256]{0:T(256)S(1)}, u32[]{:S(2)}, u32[]{:S(2)}) collective-permute-start(s32[256]{0:T(256)S(1)} %copy.143), channel_id=1, source_target_pairs={{0,4},{4,8},{8,12},{1,5},{5,9},{9,13},{2,6},{6,10},{10,14},{3,7},{... | collective-permute-start | bytes 3080 | tf_op jit(solution)/shard_map/while/body/eval_jaxpr/ppermute | solution.py:18
  113.3 6.8 %collective-permute-start.3 = (bf16[256,256]{0,1:T(8,128)(2,1)S(1)}, bf16[256,256]{0,1:T(8,128)(2,1)S(1)}, u32[]{:S(2)}, u32[]{:S(2)}) collective-permute-start(bf16[256,256]{0,1:T(8,128)(2,1)S(1)} %fusion.124), channel_id=1, source_target_pairs={{12,0},{0,4},{4,8},{8,12},{13,1},{1,5},{5,9},{9,13},{14,2},{2,6},{... | collective-permute-start | bytes 393224 | tf_op jit(solution)/shard_map/while/body/eval_jaxpr/ppermute | solution.py:24
  115.4 6.8 %collective-permute-start.4 = (bf16[256,256]{0,1:T(8,128)(2,1)S(1)}, bf16[256,256]{0,1:T(8,128)(2,1)S(1)}, u32[]{:S(2)}, u32[]{:S(2)}) collective-permute-start(bf16[256,256]{0,1:T(8,128)(2,1)S(1)} %fusion.126), channel_id=1, source_target_pairs={{12,0},{0,4},{4,8},{8,12},{13,1},{1,5},{5,9},{9,13},{14,2},{2,6},{... | collective-permute-start | bytes 393224 | tf_op jit(solution)/shard_map/while/body/eval_jaxpr/ppermute | solution.py:24
  122.3 22.0 %collective-permute-start = (bf16[256,256]{0,1:T(8,128)(2,1)S(1)}, bf16[256,256]{0,1:T(8,128)(2,1)S(1)}, u32[]{:S(2)}, u32[]{:S(2)}) collective-permute-start(bf16[256,256]{0,1:T(8,128)(2,1)S(1)} %copy.141), channel_id=1, source_target_pairs={{0,4},{4,8},{8,12},{1,5},{5,9},{9,13},{2,6},{6,10},{10,14},{3,7},{... | collective-permute-start | bytes 393224 | tf_op jit(solution)/shard_map/while/body/eval_jaxpr/ppermute | solution.py:18
  123.6 20.6 %collective-permute-start.1 = (bf16[256,256]{0,1:T(8,128)(2,1)S(1)}, bf16[256,256]{0,1:T(8,128)(2,1)S(1)}, u32[]{:S(2)}, u32[]{:S(2)}) collective-permute-start(bf16[256,256]{0,1:T(8,128)(2,1)S(1)} %copy.142), channel_id=1, source_target_pairs={{0,4},{4,8},{8,12},{1,5},{5,9},{9,13},{2,6},{6,10},{10,14},{3,7},{... | collective-permute-start | bytes 393224 | tf_op jit(solution)/shard_map/while/body/eval_jaxpr/ppermute | solution.py:18
  126.8 17.4 %collective-permute-start.2 = (s32[256]{0:T(256)S(1)}, s32[256]{0:T(256)S(1)}, u32[]{:S(2)}, u32[]{:S(2)}) collective-permute-start(s32[256]{0:T(256)S(1)} %copy.143), channel_id=1, source_target_pairs={{0,4},{4,8},{8,12},{1,5},{5,9},{9,13},{2,6},{6,10},{10,14},{3,7},{... | collective-permute-start | bytes 3080 | tf_op jit(solution)/shard_map/while/body/eval_jaxpr/ppermute | solution.py:18
  135.3 6.8 %collective-permute-start.3 = (bf16[256,256]{0,1:T(8,128)(2,1)S(1)}, bf16[256,256]{0,1:T(8,128)(2,1)S(1)}, u32[]{:S(2)}, u32[]{:S(2)}) collective-permute-start(bf16[256,256]{0,1:T(8,128)(2,1)S(1)} %fusion.124), channel_id=1, source_target_pairs={{12,0},{0,4},{4,8},{8,12},{13,1},{1,5},{5,9},{9,13},{14,2},{2,6},{... | collective-permute-start | bytes 393224 | tf_op jit(solution)/shard_map/while/body/eval_jaxpr/ppermute | solution.py:24
  137.4 6.8 %collective-permute-start.4 = (bf16[256,256]{0,1:T(8,128)(2,1)S(1)}, bf16[256,256]{0,1:T(8,128)(2,1)S(1)}, u32[]{:S(2)}, u32[]{:S(2)}) collective-permute-start(bf16[256,256]{0,1:T(8,128)(2,1)S(1)} %fusion.126), channel_id=1, source_target_pairs={{12,0},{0,4},{4,8},{8,12},{13,1},{1,5},{5,9},{9,13},{14,2},{2,6},{... | collective-permute-start | bytes 393224 | tf_op jit(solution)/shard_map/while/body/eval_jaxpr/ppermute | solution.py:24
  144.3 22.0 %collective-permute-start = (bf16[256,256]{0,1:T(8,128)(2,1)S(1)}, bf16[256,256]{0,1:T(8,128)(2,1)S(1)}, u32[]{:S(2)}, u32[]{:S(2)}) collective-permute-start(bf16[256,256]{0,1:T(8,128)(2,1)S(1)} %copy.141), channel_id=1, source_target_pairs={{0,4},{4,8},{8,12},{1,5},{5,9},{9,13},{2,6},{6,10},{10,14},{3,7},{... | collective-permute-start | bytes 393224 | tf_op jit(solution)/shard_map/while/body/eval_jaxpr/ppermute | solution.py:18
  145.6 20.6 %collective-permute-start.1 = (bf16[256,256]{0,1:T(8,128)(2,1)S(1)}, bf16[256,256]{0,1:T(8,128)(2,1)S(1)}, u32[]{:S(2)}, u32[]{:S(2)}) collective-permute-start(bf16[256,256]{0,1:T(8,128)(2,1)S(1)} %copy.142), channel_id=1, source_target_pairs={{0,4},{4,8},{8,12},{1,5},{5,9},{9,13},{2,6},{6,10},{10,14},{3,7},{... | collective-permute-start | bytes 393224 | tf_op jit(solution)/shard_map/while/body/eval_jaxpr/ppermute | solution.py:18
  148.8 17.4 %collective-permute-start.2 = (s32[256]{0:T(256)S(1)}, s32[256]{0:T(256)S(1)}, u32[]{:S(2)}, u32[]{:S(2)}) collective-permute-start(s32[256]{0:T(256)S(1)} %copy.143), channel_id=1, source_target_pairs={{0,4},{4,8},{8,12},{1,5},{5,9},{9,13},{2,6},{6,10},{10,14},{3,7},{... | collective-permute-start | bytes 3080 | tf_op jit(solution)/shard_map/while/body/eval_jaxpr/ppermute | solution.py:18
  157.3 6.8 %collective-permute-start.3 = (bf16[256,256]{0,1:T(8,128)(2,1)S(1)}, bf16[256,256]{0,1:T(8,128)(2,1)S(1)}, u32[]{:S(2)}, u32[]{:S(2)}) collective-permute-start(bf16[256,256]{0,1:T(8,128)(2,1)S(1)} %fusion.124), channel_id=1, source_target_pairs={{12,0},{0,4},{4,8},{8,12},{13,1},{1,5},{5,9},{9,13},{14,2},{2,6},{... | collective-permute-start | bytes 393224 | tf_op jit(solution)/shard_map/while/body/eval_jaxpr/ppermute | solution.py:24
  159.4 6.8 %collective-permute-start.4 = (bf16[256,256]{0,1:T(8,128)(2,1)S(1)}, bf16[256,256]{0,1:T(8,128)(2,1)S(1)}, u32[]{:S(2)}, u32[]{:S(2)}) collective-permute-start(bf16[256,256]{0,1:T(8,128)(2,1)S(1)} %fusion.126), channel_id=1, source_target_pairs={{12,0},{0,4},{4,8},{8,12},{13,1},{1,5},{5,9},{9,13},{14,2},{2,6},{... | collective-permute-start | bytes 393224 | tf_op jit(solution)/shard_map/while/body/eval_jaxpr/ppermute | solution.py:24
  166.3 15.1 %copy-start.12 = (f32[4,4]{1,0:T(4,128)S(1)}, f32[4,4]{1,0:T(4,128)}, u32[]{:S(2)}) copy-start(f32[4,4]{1,0:T(4,128)} %param.18) | copy-start | bytes 196
  166.3 13.6 %collective-permute-start.6 = (s32[128]{0:T(128)S(1)}, s32[128]{0:T(128)S(1)}, u32[]{:S(2)}, u32[]{:S(2)}) collective-permute-start(s32[128]{0:T(128)S(1)} %copy-done.14), channel_id=1, source_target_pairs={{0,4},{4,8},{8,12},{1,5},{5,9},{9,13},{2,6},{6,10},{10,14},{3,7},{... | collective-permute-start | bytes 1544 | tf_op jit(solution)/shard_map/ppermute | solution.py:18
  167.6 12.5 %collective-permute-start.5 = (bf16[128,256]{1,0:T(8,128)(2,1)S(1)}, bf16[128,256]{1,0:T(8,128)(2,1)S(1)}, u32[]{:S(2)}, u32[]{:S(2)}) collective-permute-start(bf16[128,256]{1,0:T(8,128)(2,1)S(1)} %slice.71), channel_id=1, source_target_pairs={{0,4},{4,8},{8,12},{1,5},{5,9},{9,13},{2,6},{6,10},{10,14},{3,7},{... | collective-permute-start | bytes 196616 | tf_op jit(solution)/shard_map/ppermute | solution.py:18
  170.8 16.7 %collective-permute-start.7 = (bf16[128,256]{1,0:T(8,128)(2,1)S(1)}, bf16[128,256]{1,0:T(8,128)(2,1)S(1)}, u32[]{:S(2)}, u32[]{:S(2)}) collective-permute-start(bf16[128,256]{1,0:T(8,128)(2,1)S(1)} %slice.73), channel_id=1, source_target_pairs={{0,4},{4,8},{8,12},{1,5},{5,9},{9,13},{2,6},{6,10},{10,14},{3,7},{... | collective-permute-start | bytes 196616 | tf_op jit(solution)/shard_map/ppermute | solution.py:18
  178.3 4.5 %copy-start.2 = (bf16[256,4,256]{0,2,1:T(8,128)(2,1)}, bf16[256,4,256]{0,2,1:T(8,128)(2,1)S(1)}, u32[]{:S(2)}) copy-start(bf16[256,4,256]{0,2,1:T(8,128)(2,1)S(1)} %copy.84) | copy-start | bytes 1572868
  179.8 3.1 %copy-start.4 = (bf16[256,4,256]{0,2,1:T(8,128)(2,1)}, bf16[256,4,256]{0,2,1:T(8,128)(2,1)S(1)}, u32[]{:S(2)}) copy-start(bf16[256,4,256]{0,2,1:T(8,128)(2,1)S(1)} %copy.86) | copy-start | bytes 1572868
  181.4 4.0 %copy-start = (f32[4,384,256,4]{2,1,3,0:T(8,128)}, f32[4,384,256,4]{2,1,3,0:T(8,128)S(1)}, u32[]{:S(2)}) copy-start(f32[4,384,256,4]{2,1,3,0:T(8,128)S(1)} %get-tuple-element.500) | copy-start | bytes 18874372
  182.9 4.6 %copy-start.8 = (bf16[256,256]{1,0:T(8,128)(2,1)S(1)}, bf16[256,256]{1,0:T(8,128)(2,1)}, u32[]{:S(2)}) copy-start(bf16[256,256]{1,0:T(8,128)(2,1)} %param.16) | copy-start | bytes 393220
  186.2 16.3 %collective-permute-start.9 = (bf16[128,256]{1,0:T(8,128)(2,1)}, bf16[128,256]{1,0:T(8,128)(2,1)}, u32[]{:S(2)}, u32[]{:S(2)}) collective-permute-start(bf16[128,256]{1,0:T(8,128)(2,1)} %copy.94), channel_id=1, source_target_pairs={{4,0},{8,4},{12,8},{5,1},{9,5},{13,9},{6,2},{10,6},{14,10},{7,3},{... | collective-permute-start | bytes 196616 | tf_op jit(solution)/shard_map/ppermute | solution.py:18
  188.2 6.7 %slice-start = ((s8[6291456]{0:T(1024)(128)(4,1)}), s8[2097152]{0:T(1024)(128)(4,1)S(1)}, s32[]{:S(2)}) async-start(s8[6291456]{0:T(1024)(128)(4,1)} %bitcast.230), calls=%async_computation.1 | async-start | bytes 4194304
  190.1 4.8 %copy-start.5 = (bf16[256,4,256]{0,2,1:T(8,128)(2,1)S(1)}, bf16[256,4,256]{0,2,1:T(8,128)(2,1)}, u32[]{:S(2)}) copy-start(bf16[256,4,256]{0,2,1:T(8,128)(2,1)} %copy-done.4) | copy-start | bytes 1572868
  190.1 4.8 %copy-start.9 = (bf16[384,256]{0,1:T(8,128)(2,1)S(1)}, bf16[384,256]{0,1:T(8,128)(2,1)}, u32[]{:S(2)}) copy-start(bf16[384,256]{0,1:T(8,128)(2,1)} %copy.85) | copy-start | bytes 589828
  190.1 4.8 %slice-start.1 = ((s8[6291456]{0:T(1024)(128)(4,1)}), s8[4194304]{0:T(1024)(128)(4,1)S(1)}, s32[]{:S(2)}) async-start(s8[6291456]{0:T(1024)(128)(4,1)} %bitcast.230), calls=%async_computation.2 | async-start | bytes 8388608
  195.0 3.7 %copy-start.3 = (bf16[256,4,256]{0,2,1:T(8,128)(2,1)S(1)}, bf16[256,4,256]{0,2,1:T(8,128)(2,1)}, u32[]{:S(2)}) copy-start(bf16[256,4,256]{0,2,1:T(8,128)(2,1)} %copy-done.2) | copy-start | bytes 1572868
  197.0 1.6 copy-start.1
  201.0 6.8 %collective-permute-start.8 = (bf16[128,256]{1,0:T(8,128)(2,1)S(1)}, bf16[128,256]{1,0:T(8,128)(2,1)S(1)}, u32[]{:S(2)}, u32[]{:S(2)}) collective-permute-start(bf16[128,256]{1,0:T(8,128)(2,1)S(1)} %copy.90), channel_id=1, source_target_pairs={{4,0},{8,4},{12,8},{5,1},{9,5},{13,9},{6,2},{10,6},{14,10},{7,3},{... | collective-permute-start | bytes 196616 | tf_op jit(solution)/shard_map/ppermute | solution.py:18
Sparse Core Ops, SparseCore 0:
  208.6 18.4 all-reduce.2
where the time goes:
time: 242 us; the launch traced here: 240 us
  matrix products  47.6 us (20%)
  starting transfers between devices  46.1 us (19%)
  blocking collectives  44.7 us (18%)
  waiting for transfers between devices  42.4 us (18%)
  local copies, waits for them, and re-layouts  32.8 us (14%)
  between operations  14.6 us (6%)
  other arithmetic  11.3 us (5%)
    ppermute x17, starting transfers between devices, passed_along(): lax.ppermute(value, axis, [(source, source + steps) for source in range(f...  45.5 us
    ppermute x8, waiting for transfers between devices, shifted(): return lax.ppermute(block, axis, route)  24.7 us
    unnamed x47, local copies, waits for them, and re-layouts  19 us
    all_gather x1, blocking collectives, body(): key_piece = lax.all_gather(full_keys, 'seq', axis=0, tiled=True)  17.6 us
    all_gather x1, blocking collectives, body(): value_piece = lax.all_gather(full_values, 'seq', axis=0, tiled=True)  16.6 us
    psum x1, waiting for transfers between devices, body(): lax.psum(window_kpart.astype(jnp.bfloat16), 'rep').astype(jnp.float32)  13.9 us
    dot_general x5, matrix products, grad_core(): jnp.einsum('qgjd,kgd->gjqk', grad_heads, value_block, preferred_element_t...  11.7 us
    all_gather x1, blocking collectives, body(): seg_piece = lax.all_gather(segment_ids, 'seq', axis=0, tiled=True)  10.6 us
  transfers between devices with their start and end apart: 26, of which 10 were waited for; matrix products, arithmetic and copies ran while one was open for 23% of the time, Pallas kernels for 0%

commit v1 on v0

v1 whole, which is shorter than its diff:
```python
import functools
import math

import jax
import jax.numpy as jnp
from jax import lax
from jax.experimental import pallas as pl
from jax.experimental.pallas import tpu as pltpu
from jax.sharding import PartitionSpec as P

HD = 64
WINDOW = 128
NEG = -1e30
NT_DIMS = (((1,), (1,)), ((), ()))


def passed_along(value, axis, steps):
    count = lax.axis_size(axis)
    first, last = (max(0, -steps), min(count, count - steps))
    return lax.ppermute(value, axis, [(source, source + steps) for source in range(first, last)])


def pick_half(block, half):
    return jnp.where(half == 0, block[:, :HD], block[:, HD:])


def attn_bwd_kernel(sink_ref, q_ref, do_ref, k_ref, v_ref, bias_ref, dq_ref, dk_ref, dv_ref):
    g = pl.program_id(0)
    i = pl.program_id(1)
    j = pl.program_id(2)
    groups = dk_ref.shape[1] // HD

    @pl.when((g == 0) & (i == 0) & (j == 0))
    def _():
        dk_ref[...] = jnp.zeros_like(dk_ref)
        dv_ref[...] = jnp.zeros_like(dv_ref)

    k = pick_half(k_ref[...], g % 2)
    v = pick_half(v_ref[...], g % 2)
    q = pick_half(q_ref[...], j % 2)
    do = pick_half(do_ref[...], j % 2)
    sink = sink_ref[g, j]

    s = lax.dot_general(q, k, NT_DIMS, preferred_element_type=jnp.float32) + bias_ref[...]
    row_max = jnp.maximum(jnp.max(s, axis=1, keepdims=True), sink)
    e = jnp.exp(s - row_max)
    total = jnp.sum(e, axis=1, keepdims=True) + jnp.exp(sink - row_max)
    p = e * (1.0 / total)
    p_low = p.astype(jnp.bfloat16)
    o = jnp.dot(p_low, v, preferred_element_type=jnp.float32)
    delta = jnp.sum(do.astype(jnp.float32) * o, axis=1, keepdims=True)
    dp = lax.dot_general(do, v, NT_DIMS, preferred_element_type=jnp.float32)
    ds_low = (p * (dp - delta)).astype(jnp.bfloat16)
    dq = (jnp.dot(ds_low, k, preferred_element_type=jnp.float32) * 0.125).astype(dq_ref.dtype)
    dk = jnp.dot(ds_low.T, q, preferred_element_type=jnp.float32)
    dv = jnp.dot(p_low.T, do, preferred_element_type=jnp.float32)

    @pl.when(j % 2 == 0)
    def _():
        dq_ref[:, :HD] = dq

    @pl.when(j % 2 == 1)
    def _():
        dq_ref[:, HD:] = dq

    for gg in range(groups):
        @pl.when(g == gg)
        def _():
            dk_ref[:, gg * HD:(gg + 1) * HD] += dk
            dv_ref[:, gg * HD:(gg + 1) * HD] += dv


def attn_bwd(sinks, queries, grads, keys, values, bias):
    n = queries.shape[0]
    m = keys.shape[0]
    groups, heads = sinks.shape
    rows = n
    while rows > 8 and rows * m > (1 << 18):
        rows //= 2
    grid = (groups, n // rows, heads)

    def q_map(g, i, j):
        return (i, (g * heads + j) // 2)

    return pl.pallas_call(
        attn_bwd_kernel,
        grid=grid,
        in_specs=[
            pl.BlockSpec(memory_space=pltpu.SMEM),
            pl.BlockSpec((rows, 2 * HD), q_map),
            pl.BlockSpec((rows, 2 * HD), q_map),
            pl.BlockSpec((m, 2 * HD), lambda g, i, j: (0, g // 2)),
            pl.BlockSpec((m, 2 * HD), lambda g, i, j: (0, g // 2)),
            pl.BlockSpec((rows, m), lambda g, i, j: (i, 0)),
        ],
        out_specs=[
            pl.BlockSpec((rows, 2 * HD), q_map),
            pl.BlockSpec((m, groups * HD), lambda g, i, j: (0, 0)),
            pl.BlockSpec((m, groups * HD), lambda g, i, j: (0, 0)),
        ],
        out_shape=[
            jax.ShapeDtypeStruct(queries.shape, jnp.bfloat16),
            jax.ShapeDtypeStruct((m, groups * HD), jnp.float32),
            jax.ShapeDtypeStruct((m, groups * HD), jnp.float32),
        ],
        compiler_params=pltpu.CompilerParams(
            dimension_semantics=("arbitrary", "arbitrary", "arbitrary"),
            vmem_limit_bytes=60 * 1024 * 1024,
        ),
    )(sinks, queries, grads, keys, values, bias)


def make_bias(query_pos, query_seg, key_pos, key_seg, window):
    distance = query_pos[:, None] - key_pos[None, :]
    visible = (distance >= 0) & (key_pos[None, :] >= 0) & (query_seg[:, None] == key_seg[None, :])
    if window is not None:
        visible = visible & (distance < window)
    return jnp.where(visible, 0.0, NEG).astype(jnp.float32)


def body(
    segment_ids,
    window_query,
    window_keys,
    window_values,
    window_grad_out,
    window_sinks,
    full_query,
    full_keys,
    full_values,
    full_grad_out,
    full_sinks,
):
    n = window_query.shape[0]
    key_cols = window_keys.shape[1]
    seq_count = lax.axis_size("seq")
    seq_index = lax.axis_index("seq")
    query_pos = seq_index * n + jnp.arange(n)

    full_kv = jnp.concatenate([full_keys, full_values], axis=1)
    received = {}
    for d in range(1, seq_count):
        received[d] = passed_along((full_kv, segment_ids), "seq", d)

    halo_kv, halo_seg = passed_along(
        (
            jnp.concatenate([window_keys[n - WINDOW:], window_values[n - WINDOW:]], axis=1),
            segment_ids[n - WINDOW:],
        ),
        "seq",
        1,
    )
    w_keys = jnp.concatenate([halo_kv[:, :key_cols], window_keys], axis=0)
    w_values = jnp.concatenate([halo_kv[:, key_cols:], window_values], axis=0)
    w_seg = jnp.concatenate([halo_seg, segment_ids], axis=0)
    w_pos = seq_index * n - WINDOW + jnp.arange(n + WINDOW)
    w_bias = make_bias(query_pos, segment_ids, w_pos, w_seg, WINDOW)
    w_q = (window_query.reshape(n, -1) * 0.125).astype(jnp.bfloat16)
    w_do = window_grad_out.reshape(n, -1)
    w_dq, w_dk, w_dv = attn_bwd(window_sinks, w_q, w_do, w_keys, w_values, w_bias)
    back_w = passed_along(
        jnp.concatenate([w_dk[:WINDOW], w_dv[:WINDOW]], axis=1).astype(jnp.bfloat16), "seq", -1
    ).astype(jnp.float32)
    w_kv = jnp.concatenate([w_dk[WINDOW:], w_dv[WINDOW:]], axis=1)
    w_kv = jnp.concatenate([w_kv[: n - WINDOW], w_kv[n - WINDOW:] + back_w], axis=0)

    order = list(range(seq_count - 1, 0, -1))
    f_kv = jnp.concatenate([received[d][0] for d in order] + [full_kv], axis=0)
    f_seg = jnp.concatenate([received[d][1] for d in order] + [segment_ids], axis=0)
    f_pos = (seq_index - (seq_count - 1)) * n + jnp.arange(seq_count * n)
    f_bias = make_bias(query_pos, segment_ids, f_pos, f_seg, None)
    f_q = (full_query.reshape(n, -1) * 0.125).astype(jnp.bfloat16)
    f_do = full_grad_out.reshape(n, -1)
    f_dq, f_dk, f_dv = attn_bwd(
        full_sinks, f_q, f_do, f_kv[:, :key_cols], f_kv[:, key_cols:], f_bias
    )
    f_part = jnp.concatenate([f_dk, f_dv], axis=1)
    f_own = f_part[(seq_count - 1) * n:]
    for jj, d in enumerate(order):
        piece = f_part[jj * n:(jj + 1) * n].astype(jnp.bfloat16)
        f_own = f_own + passed_along(piece, "seq", -d).astype(jnp.float32)

    both = jnp.concatenate([w_kv, f_own], axis=1)
    if lax.axis_size("rep") == 2:
        both = both + lax.ppermute(both, "rep", [(0, 1), (1, 0)])
    else:
        both = lax.psum(both, "rep")
    both = both.astype(jnp.bfloat16)
    return (
        w_dq.reshape(window_query.shape),
        both[:, :key_cols],
        both[:, key_cols:2 * key_cols],
        f_dq.reshape(full_query.shape),
        both[:, 2 * key_cols:3 * key_cols],
        both[:, 3 * key_cols:],
    )


def solution(mesh):
    placed = (
        P(("groups", "seq")),
        P(("groups", "seq"), "head", "rep"),
        P(("groups", "seq"), "head"),
        P(("groups", "seq"), "head"),
        P(("groups", "seq"), "head", "rep"),
        P("head", "rep"),
        P(("groups", "seq"), "head", "rep"),
        P(("groups", "seq"), "head"),
        P(("groups", "seq"), "head"),
        P(("groups", "seq"), "head", "rep"),
        P("head", "rep"),
    )
    return jax.shard_map(
        body,
        mesh=mesh,
        in_specs=placed,
        out_specs=(
            P(("groups", "seq"), "head", "rep"),
            P(("groups", "seq"), "head"),
            P(("groups", "seq"), "head"),
            P(("groups", "seq"), "head", "rep"),
            P(("groups", "seq"), "head"),
            P(("groups", "seq"), "head"),
        ),
        check_vma=False,
    )
```

time: 242 us -> 141 us (0.58)
  Pallas kernels: 0 us -> 58.3 us
  matrix products: 47.6 us -> 0 us
  blocking collectives: 44.7 us -> 0 us
  waiting for transfers between devices: 42.4 us -> 24.1 us
  local copies, waits for them, and re-layouts: 32.8 us -> 16.1 us
  between operations: 14.6 us -> 1.09 us
  starting transfers between devices: 46.1 us -> 32.8 us
  other arithmetic: 11.3 us -> 5.33 us
    pallas_call x0 -> x2, Pallas kernels: none -> 58.3 us  [attn_bwd(): pl.pallas_call(attn_bwd_kernel, grid=grid, in_specs=[pl.BlockSpec(memory_...]
    dot_general x30 -> x0, matrix products: 47.6 us -> none  [the longest x5 11.7 us: grad_core(): jnp.einsum('qgjd,kgd->gjqk', grad_heads, value_block, preferred_element_t...]
    all_gather x3 -> x0, blocking collectives: 44.7 us -> none  [the longest x1 17.6 us: body(): key_piece = lax.all_gather(full_keys, 'seq', axis=0, tiled=True)]
    ppermute x8 -> x1, waiting for transfers between devices: 24.7 us -> 0.01 us  [body(): both = both + lax.ppermute(both, 'rep', [(0, 1), (1, 0)])]
    ppermute x17 -> x12, waiting for transfers between devices: 3.76 us -> 24.1 us  [passed_along(): lax.ppermute(value, axis, [(source, source + steps) for source in range(f...]
    psum x1 -> x0, waiting for transfers between devices: 13.9 us -> none  [body(): lax.psum(window_kpart.astype(jnp.bfloat16), 'rep').astype(jnp.float32)]
    unnamed x47 -> x24, local copies, waits for them, and re-layouts: 19 us -> 6.15 us
    ppermute x17 -> x12, starting transfers between devices: 45.5 us -> 32.8 us  [passed_along(): lax.ppermute(value, axis, [(source, source + steps) for source in range(f...]
  transfers between devices with their start and end apart: 26 -> 13, of which waited for: 10 -> 2; matrix products, arithmetic and copies ran while one was open for 23% -> 13% of each run, Pallas kernels for 0% -> 42%
where the time goes in v1:
time: 141 us; the launch traced here: 138 us
  Pallas kernels  58.3 us (41%)
  starting transfers between devices  32.8 us (23%)
  waiting for transfers between devices  24.1 us (17%)
  local copies, waits for them, and re-layouts  16.1 us (11%)
  other arithmetic  5.33 us (4%)
    pallas_call x2, Pallas kernels, attn_bwd(): pl.pallas_call(attn_bwd_kernel, grid=grid, in_specs=[pl.BlockSpec(memory_...  58.3 us
    ppermute x12, starting transfers between devices, passed_along(): lax.ppermute(value, axis, [(source, source + steps) for source in range(f...  32.8 us
    ppermute x12, waiting for transfers between devices, passed_along(): lax.ppermute(value, axis, [(source, source + steps) for source in range(f...  24.1 us
    unnamed x24, local copies, waits for them, and re-layouts  6.15 us
  transfers between devices with their start and end apart: 13, of which 2 were waited for; matrix products, arithmetic and copies ran while one was open for 13% of the time, Pallas kernels for 42%

profile of v1, /device:TPU:0, one launch (start us, length us, event | category | flops | bytes accessed | tf_op | source)
XLA Modules:
  0.0 137.8 jit_solution(10738139548070329092)
XLA Ops:
  0.6 0.0 slice-start
  0.6 0.0 slice-start.1
  0.7 1.0 constant_dynamic-update-slice_fusion.1
  1.7 0.9 constant_dynamic-update-slice_fusion
  2.6 7.0 %collective-permute-start.3 = (bf16[256,512]{1,0:T(8,128)(2,1)S(1)}, bf16[256,512]{1,0:T(8,128)(2,1)S(1)}, u32[]{:S(2)}, u32[]{:S(2)}) collective-permute-start(bf16[256,512]{1,0:T(8,128)(2,1)S(1)} %constant_dynamic-update-slice_fusion), channel_id=1, source_target_pairs={{0,12},{1,13},{2,14},{3,15},{16,28},{17,29},{18,30},{19,31}} | collective-permute-start | bytes 786440 | tf_op jit(solution)/shard_map/ppermute | solution.py:20
  9.6 1.3 collective-permute-start.4
  10.9 1.3 collective-permute-start.6
  12.2 1.3 collective-permute-start.7
  13.5 0.7 slice.72
  14.2 2.4 %collective-permute-start.1 = (s32[128]{0:T(128)S(1)}, s32[128]{0:T(128)S(1)}, u32[]{:S(2)}, u32[]{:S(2)}) collective-permute-start(s32[128]{0:T(128)S(1)} %slice.72), channel_id=1, source_target_pairs={{0,4},{4,8},{8,12},{1,5},{5,9},{9,13},{2,6},{6,10},{10,14},{3,7},{... | collective-permute-start | bytes 1544 | tf_op jit(solution)/shard_map/ppermute | solution.py:20
  16.7 1.3 broadcast_multiply_fusion
  18.0 0.0 copy-start.3
  18.0 0.2 broadcast_multiply_fusion.1
  18.3 0.9 copy.19
  19.2 0.9 copy.20
  20.1 0.9 copy.17
  21.0 0.9 copy.18
  21.9 7.9 %collective-permute-start.8 = (s32[256]{0:T(256)S(1)}, s32[256]{0:T(256)S(1)}, u32[]{:S(2)}, u32[]{:S(2)}) collective-permute-start(s32[256]{0:T(256)S(1)} %copy-done.8), channel_id=1, source_target_pairs={{0,4},{4,8},{8,12},{1,5},{5,9},{9,13},{2,6},{6,10},{10,14},{3,7},{... | collective-permute-start | bytes 3080 | tf_op jit(solution)/shard_map/ppermute | solution.py:20
  29.8 1.0 fusion.8.bias_ref
  30.8 4.3 %collective-permute-start.5 = (bf16[256,512]{1,0:T(8,128)(2,1)S(1)}, bf16[256,512]{1,0:T(8,128)(2,1)S(1)}, u32[]{:S(2)}, u32[]{:S(2)}) collective-permute-start(bf16[256,512]{1,0:T(8,128)(2,1)S(1)} %constant_dynamic-update-slice_fusion), channel_id=1, source_target_pairs={{0,4},{4,8},{8,12},{1,5},{5,9},{9,13},{2,6},{6,10},{10,14},{3,7},{... | collective-permute-start | bytes 786440 | tf_op jit(solution)/shard_map/ppermute | solution.py:20
  35.2 1.9 %collective-permute-start = (bf16[128,512]{1,0:T(8,128)(2,1)S(1)}, bf16[128,512]{1,0:T(8,128)(2,1)S(1)}, u32[]{:S(2)}, u32[]{:S(2)}) collective-permute-start(bf16[128,512]{1,0:T(8,128)(2,1)S(1)} %pad_maximum_fusion.5), channel_id=1, source_target_pairs={{0,4},{4,8},{8,12},{1,5},{5,9},{9,13},{2,6},{6,10},{10,14},{3,7},{... | collective-permute-start | bytes 393224 | tf_op jit(solution)/shard_map/ppermute | solution.py:20
  37.1 1.4 fusion.2.bias_ref
  38.5 4.6 %collective-permute-done = bf16[128,512]{1,0:T(8,128)(2,1)S(1)} collective-permute-done((bf16[128,512]{1,0:T(8,128)(2,1)S(1)}, bf16[128,512]{1,0:T(8,128)(2,1)S(1)}, u32[]{:S(2)}, u32[]{:S(2)}) %collective-permute-start) | collective-permute-done | bytes 131104 | tf_op jit(solution)/shard_map/ppermute | solution.py:20
  43.2 0.8 pad_maximum_fusion.3
  43.9 23.9 %shard_map.154 = (bf16[256,1024]{1,0:T(8,128)(2,1)}, f32[384,256]{1,0:T(8,128)}, f32[384,256]{1,0:T(8,128)}) custom-call(f32[4,4]{1,0:T(4,128)} %sink_ref.2, bf16[256,1024]{1,0:T(8,128)(2,1)} %bitcast.12, bf16[256,1024]{1,0:T(8,128)(2,1)} %bitcast.13, bf16[384,256]{1,0:T(8,128)(2,1)} %get-tuple-element.31.k_ref, bf16[384,256]{1,0:T(8,128)(2,1)} %get-tuple-element.32.v_ref, ...), custom_call_target="tpu_custom_call" | custom-call | tf_op jit(solution)/shard_map/pallas_call | solution.py:85
  67.8 0.9 slice.118
  68.7 0.9 slice.119
  69.7 1.3 collective-permute-start.2
  71.0 0.1 pad_maximum_fusion
  71.1 1.0 fusion.12
  72.1 34.5 %shard_map.155 = (bf16[256,1024]{1,0:T(8,128)(2,1)}, f32[1024,256]{1,0:T(8,128)}, f32[1024,256]{1,0:T(8,128)}) custom-call(f32[4,4]{1,0:T(4,128)} %sink_ref.3, bf16[256,1024]{1,0:T(8,128)(2,1)} %bitcast.10, bf16[256,1024]{1,0:T(8,128)(2,1)} %bitcast.11, bf16[1024,256]{1,0:T(8,128)(2,1)} %get-tuple-element.22.k_ref, ...), custom_call_target="tpu_custom_call" | custom-call | tf_op jit(solution)/shard_map/pallas_call | solution.py:85
  106.6 1.4 %constant_dynamic-update-slice_fusion.3 = f32[1024,512]{1,0:T(8,128)S(1)} fusion(f32[1024,256]{1,0:T(8,128)} %get-tuple-element.15), kind=kLoop, calls=%fused_computation.32 | loop fusion | bytes 2097152
  108.0 0.1 copy-done
  108.1 0.1 constant_dynamic-update-slice_fusion.2
  108.2 0.1 convert.15
  108.4 0.1 fusion.11
  108.5 1.4 %collective-permute-start.10 = (bf16[256,512]{1,0:T(8,128)(2,1)S(1)}, bf16[256,512]{1,0:T(8,128)(2,1)S(1)}, u32[]{:S(2)}, u32[]{:S(2)}) collective-permute-start(bf16[256,512]{1,0:T(8,128)(2,1)S(1)} %get-tuple-element.20), channel_id=1, source_target_pairs={{8,0},{12,4},{9,1},{13,5},{10,2},{14,6},{11,3},{15,7},{24,16},{28,... | collective-permute-start | bytes 786440 | tf_op jit(solution)/shard_map/ppermute | solution.py:20
  109.9 1.3 collective-permute-start.11
  111.2 1.3 collective-permute-start.9
  112.6 0.1 fusion.9
  112.6 19.4 %collective-permute-done.10 = bf16[256,512]{1,0:T(8,128)(2,1)S(1)} collective-permute-done((bf16[256,512]{1,0:T(8,128)(2,1)S(1)}, bf16[256,512]{1,0:T(8,128)(2,1)S(1)}, u32[]{:S(2)}, u32[]{:S(2)}) %collective-permute-start.10) | collective-permute-done | bytes 262176 | tf_op jit(solution)/shard_map/ppermute | solution.py:20
  132.1 0.1 fusion.4
  132.2 0.1 pad_maximum_fusion.1
  132.3 0.1 collective-permute-start.12
  132.4 2.2 %reshape.54 = bf16[256,4,256]{2,1,0:T(4,128)(2,1)} reshape(bf16[256,1024]{1,0:T(8,128)(2,1)} %get-tuple-element.12) | data formatting | bytes 1048576 | tf_op jit(solution)/shard_map/reshape | solution.py:190
  134.6 2.2 %reshape.56 = bf16[256,4,256]{2,1,0:T(4,128)(2,1)} reshape(bf16[256,1024]{1,0:T(8,128)(2,1)} %get-tuple-element.17) | data formatting | bytes 1048576 | tf_op jit(solution)/shard_map/reshape | solution.py:193
  136.8 0.2 add_convert_fusion
  137.0 0.8 fusion.13
  (41 shorter events, 0.2 us)
Async XLA Ops:
  0.6 17.6 %slice-start = ((bf16[256,256]{1,0:T(8,128)(2,1)}), bf16[128,256]{1,0:T(8,128)(2,1)S(1)}, s32[]{:S(2)}) async-start(bf16[256,256]{1,0:T(8,128)(2,1)} %param.13), calls=%async_computation | async-start | bytes 131072 | tf_op jit(solution)/shard_map/slice | solution.py:147
  0.6 17.6 %slice-start.1 = ((bf16[256,256]{1,0:T(8,128)(2,1)}), bf16[128,256]{1,0:T(8,128)(2,1)S(1)}, s32[]{:S(2)}) async-start(bf16[256,256]{1,0:T(8,128)(2,1)} %param.14), calls=%async_computation.1 | async-start | bytes 131072 | tf_op jit(solution)/shard_map/slice | solution.py:147
  0.7 17.3 %copy-start.1 = (bf16[256,4,256]{2,1,0:T(4,128)(2,1)S(1)}, bf16[256,4,256]{2,1,0:T(4,128)(2,1)}, u32[]{:S(2)}) copy-start(bf16[256,4,256]{2,1,0:T(4,128)(2,1)} %param.12) | copy-start | bytes 1572868
  0.7 18.5 %copy-start.2 = (bf16[256,4,256]{2,1,0:T(4,128)(2,1)S(1)}, bf16[256,4,256]{2,1,0:T(4,128)(2,1)}, u32[]{:S(2)}) copy-start(bf16[256,4,256]{2,1,0:T(4,128)(2,1)} %param.20) | copy-start | bytes 1572868
  2.6 68.3 %collective-permute-start.3 = (bf16[256,512]{1,0:T(8,128)(2,1)S(1)}, bf16[256,512]{1,0:T(8,128)(2,1)S(1)}, u32[]{:S(2)}, u32[]{:S(2)}) collective-permute-start(bf16[256,512]{1,0:T(8,128)(2,1)S(1)} %constant_dynamic-update-slice_fusion), channel_id=1, source_target_pairs={{0,12},{1,13},{2,14},{3,15},{16,28},{17,29},{18,30},{19,31}} | collective-permute-start | bytes 786440 | tf_op jit(solution)/shard_map/ppermute | solution.py:20
  9.6 61.4 %collective-permute-start.4 = (bf16[256,512]{1,0:T(8,128)(2,1)S(1)}, bf16[256,512]{1,0:T(8,128)(2,1)S(1)}, u32[]{:S(2)}, u32[]{:S(2)}) collective-permute-start(bf16[256,512]{1,0:T(8,128)(2,1)S(1)} %constant_dynamic-update-slice_fusion), channel_id=1, source_target_pairs={{0,8},{4,12},{1,9},{5,13},{2,10},{6,14},{3,11},{7,15},{16,24},{20,... | collective-permute-start | bytes 786440 | tf_op jit(solution)/shard_map/ppermute | solution.py:20
  10.9 19.9 %collective-permute-start.6 = (s32[256]{0:T(256)}, s32[256]{0:T(256)S(1)}, u32[]{:S(2)}, u32[]{:S(2)}) collective-permute-start(s32[256]{0:T(256)} %param.11), channel_id=1, source_target_pairs={{0,12},{1,13},{2,14},{3,15},{16,28},{17,29},{18,30},{19,31}} | collective-permute-start | bytes 3080 | tf_op jit(solution)/shard_map/ppermute | solution.py:20
  12.2 23.0 %collective-permute-start.7 = (s32[256]{0:T(256)}, s32[256]{0:T(256)S(1)}, u32[]{:S(2)}, u32[]{:S(2)}) collective-permute-start(s32[256]{0:T(256)} %param.11), channel_id=1, source_target_pairs={{0,8},{4,12},{1,9},{5,13},{2,10},{6,14},{3,11},{7,15},{16,24},{20,... | collective-permute-start | bytes 3080 | tf_op jit(solution)/shard_map/ppermute | solution.py:20
  14.2 7.7 %collective-permute-start.1 = (s32[128]{0:T(128)S(1)}, s32[128]{0:T(128)S(1)}, u32[]{:S(2)}, u32[]{:S(2)}) collective-permute-start(s32[128]{0:T(128)S(1)} %slice.72), channel_id=1, source_target_pairs={{0,4},{4,8},{8,12},{1,5},{5,9},{9,13},{2,6},{6,10},{10,14},{3,7},{... | collective-permute-start | bytes 1544 | tf_op jit(solution)/shard_map/ppermute | solution.py:20
  18.0 3.0 %copy-start.3 = (bf16[256,4,256]{2,1,0:T(4,128)(2,1)S(1)}, bf16[256,4,256]{2,1,0:T(4,128)(2,1)}, u32[]{:S(2)}) copy-start(bf16[256,4,256]{2,1,0:T(4,128)(2,1)} %param.15) | copy-start | bytes 1572868
  18.3 3.6 %copy-start.8 = (s32[256]{0:T(256)S(1)}, s32[256]{0:T(256)}, u32[]{:S(2)}) copy-start(s32[256]{0:T(256)} %param.11) | copy-start | bytes 3076
  20.1 23.0 %copy-start.4 = (bf16[256,256]{1,0:T(8,128)(2,1)S(1)}, bf16[256,256]{1,0:T(8,128)(2,1)}, u32[]{:S(2)}) copy-start(bf16[256,256]{1,0:T(8,128)(2,1)} %param.13) | copy-start | bytes 393220
  20.1 23.1 %copy-start.5 = (bf16[256,256]{1,0:T(8,128)(2,1)S(1)}, bf16[256,256]{1,0:T(8,128)(2,1)}, u32[]{:S(2)}) copy-start(bf16[256,256]{1,0:T(8,128)(2,1)} %param.14) | copy-start | bytes 393220
  21.9 15.2 %collective-permute-start.8 = (s32[256]{0:T(256)S(1)}, s32[256]{0:T(256)S(1)}, u32[]{:S(2)}, u32[]{:S(2)}) collective-permute-start(s32[256]{0:T(256)S(1)} %copy-done.8), channel_id=1, source_target_pairs={{0,4},{4,8},{8,12},{1,5},{5,9},{9,13},{2,6},{6,10},{10,14},{3,7},{... | collective-permute-start | bytes 3080 | tf_op jit(solution)/shard_map/ppermute | solution.py:20
  30.8 40.1 %collective-permute-start.5 = (bf16[256,512]{1,0:T(8,128)(2,1)S(1)}, bf16[256,512]{1,0:T(8,128)(2,1)S(1)}, u32[]{:S(2)}, u32[]{:S(2)}) collective-permute-start(bf16[256,512]{1,0:T(8,128)(2,1)S(1)} %constant_dynamic-update-slice_fusion), channel_id=1, source_target_pairs={{0,4},{4,8},{8,12},{1,5},{5,9},{9,13},{2,6},{6,10},{10,14},{3,7},{... | collective-permute-start | bytes 786440 | tf_op jit(solution)/shard_map/ppermute | solution.py:20
  35.2 7.9 %collective-permute-start = (bf16[128,512]{1,0:T(8,128)(2,1)S(1)}, bf16[128,512]{1,0:T(8,128)(2,1)S(1)}, u32[]{:S(2)}, u32[]{:S(2)}) collective-permute-start(bf16[128,512]{1,0:T(8,128)(2,1)S(1)} %pad_maximum_fusion.5), channel_id=1, source_target_pairs={{0,4},{4,8},{8,12},{1,5},{5,9},{9,13},{2,6},{6,10},{10,14},{3,7},{... | collective-permute-start | bytes 393224 | tf_op jit(solution)/shard_map/ppermute | solution.py:20
  69.7 42.9 %collective-permute-start.2 = (bf16[128,512]{1,0:T(8,128)(2,1)S(1)}, bf16[128,512]{1,0:T(8,128)(2,1)S(1)}, u32[]{:S(2)}, u32[]{:S(2)}) collective-permute-start(bf16[128,512]{1,0:T(8,128)(2,1)S(1)} %pad_maximum_fusion.6), channel_id=1, source_target_pairs={{4,0},{8,4},{12,8},{5,1},{9,5},{13,9},{6,2},{10,6},{14,10},{7,3},{... | collective-permute-start | bytes 393224 | tf_op jit(solution)/shard_map/ppermute | solution.py:20
  106.6 1.5 %copy-start = (f32[1024,256]{1,0:T(8,128)S(1)}, f32[1024,256]{1,0:T(8,128)}, u32[]{:S(2)}) copy-start(f32[1024,256]{1,0:T(8,128)} %get-tuple-element.16) | copy-start | bytes 3145732
  108.2 4.3 %copy-start.7 = (f32[384,256]{1,0:T(8,128)S(1)}, f32[384,256]{1,0:T(8,128)}, u32[]{:S(2)}) copy-start(f32[384,256]{1,0:T(8,128)} %get-tuple-element.13) | copy-start | bytes 1179652
  108.2 4.3 %copy-start.6 = (f32[384,256]{1,0:T(8,128)S(1)}, f32[384,256]{1,0:T(8,128)}, u32[]{:S(2)}) copy-start(f32[384,256]{1,0:T(8,128)} %get-tuple-element.14) | copy-start | bytes 1179652
  108.5 23.6 %collective-permute-start.10 = (bf16[256,512]{1,0:T(8,128)(2,1)S(1)}, bf16[256,512]{1,0:T(8,128)(2,1)S(1)}, u32[]{:S(2)}, u32[]{:S(2)}) collective-permute-start(bf16[256,512]{1,0:T(8,128)(2,1)S(1)} %get-tuple-element.20), channel_id=1, source_target_pairs={{8,0},{12,4},{9,1},{13,5},{10,2},{14,6},{11,3},{15,7},{24,16},{28,... | collective-permute-start | bytes 786440 | tf_op jit(solution)/shard_map/ppermute | solution.py:20
  109.9 22.2 %collective-permute-start.11 = (bf16[256,512]{1,0:T(8,128)(2,1)S(1)}, bf16[256,512]{1,0:T(8,128)(2,1)S(1)}, u32[]{:S(2)}, u32[]{:S(2)}) collective-permute-start(bf16[256,512]{1,0:T(8,128)(2,1)S(1)} %get-tuple-element.19), channel_id=1, source_target_pairs={{4,0},{8,4},{12,8},{5,1},{9,5},{13,9},{6,2},{10,6},{14,10},{7,3},{... | collective-permute-start | bytes 786440 | tf_op jit(solution)/shard_map/ppermute | solution.py:20
  111.2 20.9 %collective-permute-start.9 = (bf16[256,512]{1,0:T(8,128)(2,1)S(1)}, bf16[256,512]{1,0:T(8,128)(2,1)S(1)}, u32[]{:S(2)}, u32[]{:S(2)}) collective-permute-start(bf16[256,512]{1,0:T(8,128)(2,1)S(1)} %get-tuple-element.18), channel_id=1, source_target_pairs={{12,0},{13,1},{14,2},{15,3},{28,16},{29,17},{30,18},{31,19}} | collective-permute-start | bytes 786440 | tf_op jit(solution)/shard_map/ppermute | solution.py:20
  132.3 4.5 %collective-permute-start.12 = (f32[256,1024]{1,0:T(8,128)S(1)}, f32[256,1024]{1,0:T(8,128)S(1)}, u32[]{:S(2)}, u32[]{:S(2)}) collective-permute-start(f32[256,1024]{1,0:T(8,128)S(1)} %pad_maximum_fusion.1), channel_id=1, source_target_pairs={{0,1},{1,0},{2,3},{3,2},{4,5},{5,4},{6,7},{7,6},{8,9},{9,8},{10,11... | collective-permute-start | bytes 3145736 | tf_op jit(solution)/shard_map/ppermute | solution.py:185

commit v2 on v1

v2 whole, which is shorter than its diff:
```python
import functools
import math

import jax
import jax.numpy as jnp
from jax import lax
from jax.experimental import pallas as pl
from jax.experimental.pallas import tpu as pltpu
from jax.sharding import PartitionSpec as P

HD = 64
WINDOW = 128
NEG = -1e30
NT_DIMS = (((1,), (1,)), ((), ()))


def passed_along(value, axis, steps):
    count = lax.axis_size(axis)
    first, last = (max(0, -steps), min(count, count - steps))
    return lax.ppermute(value, axis, [(source, source + steps) for source in range(first, last)])


def pick_half(block, half):
    return jnp.where(half == 0, block[:, :HD], block[:, HD:])


def attn_bwd_kernel(g0, gn, sink_ref, q_ref, do_ref, k_ref, v_ref, bias_ref, dq_ref, dk_ref, dv_ref):
    g_rel = pl.program_id(0)
    g = g_rel + g0
    i = pl.program_id(1)
    j = pl.program_id(2)

    @pl.when((g_rel == 0) & (i == 0) & (j == 0))
    def _():
        dk_ref[...] = jnp.zeros_like(dk_ref)
        dv_ref[...] = jnp.zeros_like(dv_ref)

    k = pick_half(k_ref[...], g % 2)
    v = pick_half(v_ref[...], g % 2)
    q = pick_half(q_ref[...], j % 2)
    do = pick_half(do_ref[...], j % 2)
    sink = sink_ref[g, j]

    s = lax.dot_general(q, k, NT_DIMS, preferred_element_type=jnp.float32) + bias_ref[...]
    row_max = jnp.maximum(jnp.max(s, axis=1, keepdims=True), sink)
    e = jnp.exp(s - row_max)
    total = jnp.sum(e, axis=1, keepdims=True) + jnp.exp(sink - row_max)
    p = e * (1.0 / total)
    p_low = p.astype(jnp.bfloat16)
    o = jnp.dot(p_low, v, preferred_element_type=jnp.float32)
    delta = jnp.sum(do.astype(jnp.float32) * o, axis=1, keepdims=True)
    dp = lax.dot_general(do, v, NT_DIMS, preferred_element_type=jnp.float32)
    ds_low = (p * (dp - delta)).astype(jnp.bfloat16)
    dq = (jnp.dot(ds_low, k, preferred_element_type=jnp.float32) * 0.125).astype(dq_ref.dtype)
    dk = jnp.dot(ds_low.T, q, preferred_element_type=jnp.float32)
    dv = jnp.dot(p_low.T, do, preferred_element_type=jnp.float32)

    @pl.when(j % 2 == 0)
    def _():
        dq_ref[:, :HD] = dq

    @pl.when(j % 2 == 1)
    def _():
        dq_ref[:, HD:] = dq

    for gg in range(gn):
        @pl.when(g_rel == gg)
        def _():
            dk_ref[:, gg * HD:(gg + 1) * HD] += dk
            dv_ref[:, gg * HD:(gg + 1) * HD] += dv


def attn_bwd(sinks, queries, grads, keys, values, bias, g0, gn):
    n = queries.shape[0]
    m = keys.shape[0]
    heads = sinks.shape[1]
    rows = n
    while rows > 8 and rows * m > (1 << 18):
        rows //= 2
    grid = (gn, n // rows, heads)

    def q_map(g, i, j):
        return (i, ((g + g0) * heads + j) // 2)

    def out_q_map(g, i, j):
        return (i, (g * heads + j) // 2)

    return pl.pallas_call(
        functools.partial(attn_bwd_kernel, g0, gn),
        grid=grid,
        in_specs=[
            pl.BlockSpec(memory_space=pltpu.SMEM),
            pl.BlockSpec((rows, 2 * HD), q_map),
            pl.BlockSpec((rows, 2 * HD), q_map),
            pl.BlockSpec((m, 2 * HD), lambda g, i, j: (0, (g + g0) // 2)),
            pl.BlockSpec((m, 2 * HD), lambda g, i, j: (0, (g + g0) // 2)),
            pl.BlockSpec((rows, m), lambda g, i, j: (i, 0)),
        ],
        out_specs=[
            pl.BlockSpec((rows, 2 * HD), out_q_map),
            pl.BlockSpec((m, gn * HD), lambda g, i, j: (0, 0)),
            pl.BlockSpec((m, gn * HD), lambda g, i, j: (0, 0)),
        ],
        out_shape=[
            jax.ShapeDtypeStruct((n, gn * heads * HD), jnp.bfloat16),
            jax.ShapeDtypeStruct((m, gn * HD), jnp.float32),
            jax.ShapeDtypeStruct((m, gn * HD), jnp.float32),
        ],
        compiler_params=pltpu.CompilerParams(
            dimension_semantics=("arbitrary", "arbitrary", "arbitrary"),
            vmem_limit_bytes=60 * 1024 * 1024,
        ),
        cost_estimate=pl.CostEstimate(
            flops=12 * gn * heads * n * m * HD,
            transcendentals=gn * heads * n * m,
            bytes_accessed=4 * n * m + 4 * n * gn * heads * HD * 3 + 12 * m * gn * HD,
        ),
    )(sinks, queries, grads, keys, values, bias)


def make_bias(query_pos, query_seg, key_pos, key_seg, window):
    distance = query_pos[:, None] - key_pos[None, :]
    visible = (distance >= 0) & (key_pos[None, :] >= 0) & (query_seg[:, None] == key_seg[None, :])
    if window is not None:
        visible = visible & (distance < window)
    return jnp.where(visible, 0.0, NEG).astype(jnp.float32)


def seg_rows(ids, width):
    count = ids.shape[0]
    lines = -(-count // width)
    flat = jnp.zeros((16 * (-(-lines // 16)) * width,), jnp.bfloat16)
    flat = flat.at[:count].set(ids.astype(jnp.bfloat16))
    return flat.reshape(-1, width)


def read_seg(block, count):
    return block.reshape(-1)[:count].astype(jnp.float32).astype(jnp.int32)


def body(
    segment_ids,
    window_query,
    window_keys,
    window_values,
    window_grad_out,
    window_sinks,
    full_query,
    full_keys,
    full_values,
    full_grad_out,
    full_sinks,
):
    n = window_query.shape[0]
    cols = window_keys.shape[1]
    groups = cols // HD
    seq_count = lax.axis_size("seq")
    seq_index = lax.axis_index("seq")
    rep_index = lax.axis_index("rep")
    first = rep_index == 0
    query_pos = seq_index * n + jnp.arange(n)
    order = list(range(seq_count - 1, 0, -1))
    swap = [(0, 1), (1, 0)]

    halo_in = jnp.concatenate(
        [
            jnp.concatenate([window_keys[n - WINDOW:], window_values[n - WINDOW:]], axis=1),
            seg_rows(segment_ids[n - WINDOW:], 2 * cols),
        ],
        axis=0,
    )
    halo = passed_along(halo_in, "seq", 1)

    own_half = jnp.where(first, full_keys, full_values)
    seg_block = seg_rows(segment_ids, cols)
    payload = jnp.concatenate([own_half, seg_block], axis=0)
    halo, payload = lax.optimization_barrier((halo, payload))
    arrived = [passed_along(payload, "seq", d) for d in order]

    w_keys = jnp.concatenate([halo[:WINDOW, :cols], window_keys], axis=0)
    w_values = jnp.concatenate([halo[:WINDOW, cols:], window_values], axis=0)
    w_seg = jnp.concatenate([read_seg(halo[WINDOW:], WINDOW), segment_ids], axis=0)
    w_pos = seq_index * n - WINDOW + jnp.arange(n + WINDOW)
    w_bias = make_bias(query_pos, segment_ids, w_pos, w_seg, WINDOW)
    w_q = (window_query.reshape(n, -1) * 0.125).astype(jnp.bfloat16)
    w_do = window_grad_out.reshape(n, -1)
    g_split = groups // 2 if groups > 1 else groups
    w_out1 = attn_bwd(window_sinks, w_q, w_do, w_keys, w_values, w_bias, 0, g_split)

    w_out1, arrived = lax.optimization_barrier((w_out1, arrived))
    mine = jnp.concatenate(arrived, axis=0)
    other = lax.ppermute(mine, "rep", swap)
    step = n + seg_block.shape[0]
    key_parts, value_parts, seg_parts = [], [], []
    for idx in range(len(order)):
        a = mine[idx * step:(idx + 1) * step]
        b = other[idx * step:(idx + 1) * step]
        key_parts.append(jnp.where(first, a[:n], b[:n]))
        value_parts.append(jnp.where(first, b[:n], a[:n]))
        seg_parts.append(read_seg(a[n:], n))
    f_keys = jnp.concatenate(key_parts + [full_keys], axis=0)
    f_values = jnp.concatenate(value_parts + [full_values], axis=0)
    f_seg = jnp.concatenate(seg_parts + [segment_ids], axis=0)
    f_pos = (seq_index - (seq_count - 1)) * n + jnp.arange(seq_count * n)
    f_bias = make_bias(query_pos, segment_ids, f_pos, f_seg, None)
    f_q = (full_query.reshape(n, -1) * 0.125).astype(jnp.bfloat16)
    f_do = full_grad_out.reshape(n, -1)
    f_dq, f_dk, f_dv = attn_bwd(full_sinks, f_q, f_do, f_keys, f_values, f_bias, 0, groups)

    give = jnp.where(first, f_dv, f_dk)
    keep = jnp.where(first, f_dk, f_dv)
    summed = keep + lax.ppermute(give, "rep", swap)
    f_final = summed[(seq_count - 1) * n:]
    for jj, d in enumerate(order):
        piece = summed[jj * n:(jj + 1) * n].astype(jnp.bfloat16)
        f_final = f_final + passed_along(piece, "seq", -d).astype(jnp.float32)

    if g_split < groups:
        w_out2 = attn_bwd(window_sinks, w_q, w_do, w_keys, w_values, w_bias, g_split, groups - g_split)
        w_dq = jnp.concatenate([w_out1[0], w_out2[0]], axis=1)
        w_dk = jnp.concatenate([w_out1[1], w_out2[1]], axis=1)
        w_dv = jnp.concatenate([w_out1[2], w_out2[2]], axis=1)
    else:
        w_dq, w_dk, w_dv = w_out1
    back_w = passed_along(
        jnp.concatenate([w_dk[:WINDOW], w_dv[:WINDOW]], axis=1).astype(jnp.bfloat16), "seq", -1
    ).astype(jnp.float32)
    w_kv = jnp.concatenate([w_dk[WINDOW:], w_dv[WINDOW:]], axis=1)
    w_kv = jnp.concatenate([w_kv[: n - WINDOW], w_kv[n - WINDOW:] + back_w], axis=0)

    both = jnp.concatenate([w_kv, f_final], axis=1)
    peer = lax.ppermute(both, "rep", swap)
    w_sum = (w_kv + peer[:, :2 * cols]).astype(jnp.bfloat16)
    f_other = peer[:, 2 * cols:]
    f_dk_out = jnp.where(first, f_final, f_other).astype(jnp.bfloat16)
    f_dv_out = jnp.where(first, f_other, f_final).astype(jnp.bfloat16)
    return (
        w_dq.reshape(window_query.shape),
        w_sum[:, :cols],
        w_sum[:, cols:],
        f_dq.reshape(full_query.shape),
        f_dk_out,
        f_dv_out,
    )


def solution(mesh):
    placed = (
        P(("groups", "seq")),
        P(("groups", "seq"), "head", "rep"),
        P(("groups", "seq"), "head"),
        P(("groups", "seq"), "head"),
        P(("groups", "seq"), "head", "rep"),
        P("head", "rep"),
        P(("groups", "seq"), "head", "rep"),
        P(("groups", "seq"), "head"),
        P(("groups", "seq"), "head"),
        P(("groups", "seq"), "head", "rep"),
        P("head", "rep"),
    )
    return jax.shard_map(
        body,
        mesh=mesh,
        in_specs=placed,
        out_specs=(
            P(("groups", "seq"), "head", "rep"),
            P(("groups", "seq"), "head"),
            P(("groups", "seq"), "head"),
            P(("groups", "seq"), "head", "rep"),
            P(("groups", "seq"), "head"),
            P(("groups", "seq"), "head"),
        ),
        check_vma=False,
    )
```

time: 141 us -> 117 us (0.83); the launches traced: 138 us -> 116 us
  starting transfers between devices: 32.8 us -> 18.2 us
  waiting for transfers between devices: 24.1 us -> 14.3 us
  other arithmetic: 5.33 us -> 8.79 us
  local copies, waits for them, and re-layouts: 16.1 us -> 13.9 us
  Pallas kernels: 58.3 us -> 60.1 us
    ppermute x12 -> x8, starting transfers between devices: 32.8 us -> 17.8 us  [passed_along(): lax.ppermute(value, axis, [(source, source + steps) for source in range(f...]
    ppermute x12 -> x8, waiting for transfers between devices: 24.1 us -> 13.9 us  [passed_along(): lax.ppermute(value, axis, [(source, source + steps) for source in range(f...]
    unnamed x24 -> x44, local copies, waits for them, and re-layouts: 6.15 us -> 8.98 us
    pallas_call x2 -> x3, Pallas kernels: 58.3 us -> 60.1 us  [attn_bwd(): pl.pallas_call(functools.partial(attn_bwd_kernel, g0, gn), grid=grid, in_...]
    concatenate x6 -> x10, other arithmetic: 0.96 us -> 2.65 us  [the longest x1 0.86 us: body(): f_keys = jnp.concatenate(key_parts + [full_keys], axis=0)]
    select_n x0 -> x3, other arithmetic: none -> 1.44 us  [the longest x1 1.37 us: body(): give = jnp.where(first, f_dv, f_dk)]
  transfers between devices with their start and end apart: 13 -> 11, of which waited for: 2 -> 5; matrix products, arithmetic and copies ran while one was open for 13% -> 9% of each run, Pallas kernels for 42% -> 22%
where the time goes in v2:
time: 117 us; the launch traced here: 116 us
  Pallas kernels  60.1 us (51%)
  starting transfers between devices  18.2 us (16%)
  waiting for transfers between devices  14.3 us (12%)
  local copies, waits for them, and re-layouts  13.9 us (12%)
  other arithmetic  8.79 us (8%)
    pallas_call x3, Pallas kernels, attn_bwd(): pl.pallas_call(functools.partial(attn_bwd_kernel, g0, gn), grid=grid, in_...  60.1 us
    ppermute x8, starting transfers between devices, passed_along(): lax.ppermute(value, axis, [(source, source + steps) for source in range(f...  17.8 us
    ppermute x8, waiting for transfers between devices, passed_along(): lax.ppermute(value, axis, [(source, source + steps) for source in range(f...  13.9 us
    unnamed x44, local copies, waits for them, and re-layouts  8.98 us
  transfers between devices with their start and end apart: 11, of which 5 were waited for; matrix products, arithmetic and copies ran while one was open for 9% of the time, Pallas kernels for 22%

profile of v2, /device:TPU:0, one launch (start us, length us, event | category | flops | bytes accessed | tf_op | source)
XLA Modules:
  0.0 116.4 jit_solution(8835867489300753206)
XLA Ops:
  0.6 0.7 convert.16
  1.4 0.8 slice.139
  2.3 0.8 slice.140
  3.1 4.9 %collective-permute-start = (bf16[144,512]{1,0:T(8,128)(2,1)S(1)}, bf16[144,512]{1,0:T(8,128)(2,1)S(1)}, u32[]{:S(2)}, u32[]{:S(2)}) collective-permute-start(bf16[144,512]{1,0:T(8,128)(2,1)S(1)} %pad_maximum_fusion.8), channel_id=1, source_target_pairs={{0,4},{4,8},{8,12},{1,5},{5,9},{9,13},{2,6},{6,10},{10,14},{3,7},{... | collective-permute-start | bytes 442376 | tf_op jit(solution)/shard_map/ppermute | solution.py:20
  8.2 0.2 broadcast_multiply_fusion.1
  8.4 0.8 copy-done.3
  9.2 0.2 broadcast_multiply_fusion
  9.4 0.7 copy-done.7
  10.2 0.9 copy.17
  11.1 0.2 copy-done.4
  11.3 0.9 copy.18
  12.2 0.9 copy.20
  13.1 0.2 copy-done.5
  13.4 0.9 copy.21
  14.3 3.5 %collective-permute-start.3 = (bf16[272,256]{1,0:T(8,128)(2,1)S(1)}, bf16[272,256]{1,0:T(8,128)(2,1)S(1)}, u32[]{:S(2)}, u32[]{:S(2)}) collective-permute-start(bf16[272,256]{1,0:T(8,128)(2,1)S(1)} %pad_maximum_fusion.9), channel_id=1, source_target_pairs={{0,4},{4,8},{8,12},{1,5},{5,9},{9,13},{2,6},{6,10},{10,14},{3,7},{... | collective-permute-start | bytes 417800 | tf_op jit(solution)/shard_map/ppermute | solution.py:20
  17.8 2.9 %collective-permute-start.2 = (bf16[272,256]{1,0:T(8,128)(2,1)S(1)}, bf16[272,256]{1,0:T(8,128)(2,1)S(1)}, u32[]{:S(2)}, u32[]{:S(2)}) collective-permute-start(bf16[272,256]{1,0:T(8,128)(2,1)S(1)} %pad_maximum_fusion.9), channel_id=1, source_target_pairs={{0,8},{4,12},{1,9},{5,13},{2,10},{6,14},{3,11},{7,15},{16,24},{20,... | collective-permute-start | bytes 417800 | tf_op jit(solution)/shard_map/ppermute | solution.py:20
  20.7 1.3 %collective-permute-start.1 = (bf16[272,256]{1,0:T(8,128)(2,1)S(1)}, bf16[272,256]{1,0:T(8,128)(2,1)S(1)}, u32[]{:S(2)}, u32[]{:S(2)}) collective-permute-start(bf16[272,256]{1,0:T(8,128)(2,1)S(1)} %pad_maximum_fusion.9), channel_id=1, source_target_pairs={{0,12},{1,13},{2,14},{3,15},{16,28},{17,29},{18,30},{19,31}} | collective-permute-start | bytes 417800 | tf_op jit(solution)/shard_map/ppermute | solution.py:20
  22.1 0.7 copy-done.17
  22.8 1.0 fusion.7.bias_ref
  23.7 0.8 pad_maximum_fusion.6
  24.5 12.7 %shard_map.154 = (bf16[256,512]{1,0:T(8,128)(2,1)}, f32[384,128]{1,0:T(8,128)}, f32[384,128]{1,0:T(8,128)}) custom-call(f32[4,4]{1,0:T(4,128)} %sink_ref.4, bf16[256,1024]{1,0:T(8,128)(2,1)} %bitcast.18, bf16[256,1024]{1,0:T(8,128)(2,1)} %bitcast.20, bf16[384,256]{1,0:T(8,128)(2,1)} %get-tuple-element.87.k_ref, bf16[384,256]{1,0:T(8,128)(2,1)} %get-tuple-element.88.v_ref, ...), custom_call_target="tpu_custom_call" | custom-call | flops 603979776 | bytes 2555904 | tf_op jit(solution)/shard_map/pallas_call | solution.py:88
  37.5 1.4 %fusion.2.bias_ref = f32[256,1024]{1,0:T(8,128)} fusion(s32[1024]{0:T(1024)S(1)} %pad_add_fusion, s32[1024]{0:T(1024)S(1)} %iota_add_fusion, s32[256]{0:T(256)S(1)} %iota_add_fusion.2, s32[256]{0:T(256)S(1)} %copy-done.17, pred[1024]{0:T(1024)(128)(4,1)S(1)} %broadcast_compare_fusion), kind=kLoop, calls=%fused_computation.4 | loop fusion | flops 1572864 | bytes 1059840 | tf_op jit(solution)/shard_map/jit(_where)/select_n | solution.py:126
  38.8 0.4 collective-permute-done.5
  39.2 0.8 pad_maximum_fusion.3.v_ref
  40.1 0.9 pad_maximum_fusion.2.k_ref
  40.9 34.5 %shard_map.156 = (bf16[256,1024]{1,0:T(8,128)(2,1)}, f32[1024,256]{1,0:T(8,128)}, f32[1024,256]{1,0:T(8,128)}) custom-call(f32[4,4]{1,0:T(4,128)} %sink_ref.5, bf16[256,1024]{1,0:T(8,128)(2,1)} %bitcast.22, bf16[256,1024]{1,0:T(8,128)(2,1)} %bitcast.23, bf16[1024,256]{1,0:T(8,128)(2,1)} %pad_maximum_fusion.2.k_ref, ...), custom_call_target="tpu_custom_call" | custom-call | flops 3221225472 | bytes 7340032 | tf_op jit(solution)/shard_map/pallas_call | solution.py:88
  75.4 1.4 %broadcast_select_fusion = f32[1024,256]{1,0:T(8,128)S(1)} fusion(f32[1024,256]{1,0:T(8,128)} %get-tuple-element.62, f32[1024,256]{1,0:T(8,128)} %get-tuple-element.61, pred[]{:T(512)S(6)} %eq.14), kind=kLoop, calls=%fused_computation.15 | loop fusion | flops 262144 | bytes 3145729 | tf_op jit(solution)/shard_map/jit(_where)/select_n | solution.py:210
  76.8 0.2 collective-permute-start.6
  77.0 12.8 %shard_map.155 = (bf16[256,512]{1,0:T(8,128)(2,1)}, f32[384,128]{1,0:T(8,128)}, f32[384,128]{1,0:T(8,128)}) custom-call(f32[4,4]{1,0:T(4,128)} %sink_ref.4, bf16[256,1024]{1,0:T(8,128)(2,1)} %bitcast.19, bf16[256,1024]{1,0:T(8,128)(2,1)} %bitcast.21, bf16[384,256]{1,0:T(8,128)(2,1)} %get-tuple-element.87.k_ref, bf16[384,256]{1,0:T(8,128)(2,1)} %get-tuple-element.88.v_ref, ...), custom_call_target="tpu_custom_call" | custom-call | flops 603979776 | bytes 2555904 | tf_op jit(solution)/shard_map/pallas_call | solution.py:88
  89.9 0.9 copy-done.16
  90.9 0.8 copy-done.13
  91.7 0.1 copy-done.15
  91.9 1.3 %collective-permute-start.4 = (bf16[128,512]{1,0:T(8,128)(2,1)S(1)}, bf16[128,512]{1,0:T(8,128)(2,1)S(1)}, u32[]{:S(2)}, u32[]{:S(2)}) collective-permute-start(bf16[128,512]{1,0:T(8,128)(2,1)S(1)} %pad_maximum_fusion.10), channel_id=1, source_target_pairs={{4,0},{8,4},{12,8},{5,1},{9,5},{13,9},{6,2},{10,6},{14,10},{7,3},{... | collective-permute-start | bytes 393224 | tf_op jit(solution)/shard_map/ppermute | solution.py:20
  93.2 0.2 fusion.13
  93.5 1.3 %collective-permute-start.7 = (bf16[256,256]{1,0:T(8,128)(2,1)S(1)}, bf16[256,256]{1,0:T(8,128)(2,1)S(1)}, u32[]{:S(2)}, u32[]{:S(2)}) collective-permute-start(bf16[256,256]{1,0:T(8,128)(2,1)S(1)} %get-tuple-element.76), channel_id=1, source_target_pairs={{12,0},{13,1},{14,2},{15,3},{28,16},{29,17},{30,18},{31,19}} | collective-permute-start | bytes 393224 | tf_op jit(solution)/shard_map/ppermute | solution.py:20
  94.8 1.3 %collective-permute-start.9 = (bf16[256,256]{1,0:T(8,128)(2,1)S(1)}, bf16[256,256]{1,0:T(8,128)(2,1)S(1)}, u32[]{:S(2)}, u32[]{:S(2)}) collective-permute-start(bf16[256,256]{1,0:T(8,128)(2,1)S(1)} %get-tuple-element.77), channel_id=1, source_target_pairs={{4,0},{8,4},{12,8},{5,1},{9,5},{13,9},{6,2},{10,6},{14,10},{7,3},{... | collective-permute-start | bytes 393224 | tf_op jit(solution)/shard_map/ppermute | solution.py:20
  96.1 1.3 %collective-permute-start.8 = (bf16[256,256]{1,0:T(8,128)(2,1)S(1)}, bf16[256,256]{1,0:T(8,128)(2,1)S(1)}, u32[]{:S(2)}, u32[]{:S(2)}) collective-permute-start(bf16[256,256]{1,0:T(8,128)(2,1)S(1)} %get-tuple-element.78), channel_id=1, source_target_pairs={{8,0},{12,4},{9,1},{13,5},{10,2},{14,6},{11,3},{15,7},{24,16},{28,... | collective-permute-start | bytes 393224 | tf_op jit(solution)/shard_map/ppermute | solution.py:20
  97.4 2.2 %collective-permute-done.4 = bf16[128,512]{1,0:T(8,128)(2,1)S(1)} collective-permute-done((bf16[128,512]{1,0:T(8,128)(2,1)S(1)}, bf16[128,512]{1,0:T(8,128)(2,1)S(1)}, u32[]{:S(2)}, u32[]{:S(2)}) %collective-permute-start.4) | collective-permute-done | bytes 131104 | tf_op jit(solution)/shard_map/ppermute | solution.py:20
  99.6 3.9 %collective-permute-done.7 = bf16[256,256]{1,0:T(8,128)(2,1)S(1)} collective-permute-done((bf16[256,256]{1,0:T(8,128)(2,1)S(1)}, bf16[256,256]{1,0:T(8,128)(2,1)S(1)}, u32[]{:S(2)}, u32[]{:S(2)}) %collective-permute-start.7) | collective-permute-done | bytes 131104 | tf_op jit(solution)/shard_map/ppermute | solution.py:20
  103.5 1.7 %collective-permute-done.9 = bf16[256,256]{1,0:T(8,128)(2,1)S(1)} collective-permute-done((bf16[256,256]{1,0:T(8,128)(2,1)S(1)}, bf16[256,256]{1,0:T(8,128)(2,1)S(1)}, u32[]{:S(2)}, u32[]{:S(2)}) %collective-permute-start.9) | collective-permute-done | bytes 131104 | tf_op jit(solution)/shard_map/ppermute | solution.py:20
  105.2 6.1 %collective-permute-done.8 = bf16[256,256]{1,0:T(8,128)(2,1)S(1)} collective-permute-done((bf16[256,256]{1,0:T(8,128)(2,1)S(1)}, bf16[256,256]{1,0:T(8,128)(2,1)S(1)}, u32[]{:S(2)}, u32[]{:S(2)}) %collective-permute-start.8) | collective-permute-done | bytes 131104 | tf_op jit(solution)/shard_map/ppermute | solution.py:20
  111.5 0.1 collective-permute-start.10
  111.6 0.8 copy-done.11
  112.3 0.1 copy-done.12
  112.5 1.2 %reshape.119 = bf16[256,4,256]{2,1,0:T(4,128)(2,1)} reshape(bf16[256,1024]{1,0:T(8,128)(2,1)S(1)} %pad_maximum_fusion.1) | data formatting | bytes 1048576 | tf_op jit(solution)/shard_map/reshape | solution.py:238
  113.7 1.2 %reshape.121 = bf16[256,4,256]{2,1,0:T(4,128)(2,1)} reshape(bf16[256,1024]{1,0:T(8,128)(2,1)S(1)} %copy-done.6) | data formatting | bytes 1048576 | tf_op jit(solution)/shard_map/reshape | solution.py:241
  114.9 0.7 fusion.15
  115.6 0.7 select_convert_fusion
  (71 shorter events, 0.9 us)
Async XLA Ops:
  0.6 7.5 %copy-start.2 = (bf16[256,4,256]{2,1,0:T(4,128)(2,1)S(1)}, bf16[256,4,256]{2,1,0:T(4,128)(2,1)}, u32[]{:S(2)}) copy-start(bf16[256,4,256]{2,1,0:T(4,128)(2,1)} %param.16) | copy-start | bytes 1572868
  3.1 11.1 %collective-permute-start = (bf16[144,512]{1,0:T(8,128)(2,1)S(1)}, bf16[144,512]{1,0:T(8,128)(2,1)S(1)}, u32[]{:S(2)}, u32[]{:S(2)}) collective-permute-start(bf16[144,512]{1,0:T(8,128)(2,1)S(1)} %pad_maximum_fusion.8), channel_id=1, source_target_pairs={{0,4},{4,8},{8,12},{1,5},{5,9},{9,13},{2,6},{6,10},{10,14},{3,7},{... | collective-permute-start | bytes 442376 | tf_op jit(solution)/shard_map/ppermute | solution.py:20
  8.1 1.0 copy-start.3
  9.2 0.9 copy-start.7
  9.2 1.0 copy-start.8
  10.2 1.1 copy-start.4
  12.2 1.1 copy-start.5
  14.3 23.0 %collective-permute-start.3 = (bf16[272,256]{1,0:T(8,128)(2,1)S(1)}, bf16[272,256]{1,0:T(8,128)(2,1)S(1)}, u32[]{:S(2)}, u32[]{:S(2)}) collective-permute-start(bf16[272,256]{1,0:T(8,128)(2,1)S(1)} %pad_maximum_fusion.9), channel_id=1, source_target_pairs={{0,4},{4,8},{8,12},{1,5},{5,9},{9,13},{2,6},{6,10},{10,14},{3,7},{... | collective-permute-start | bytes 417800 | tf_op jit(solution)/shard_map/ppermute | solution.py:20
  17.8 19.5 %collective-permute-start.2 = (bf16[272,256]{1,0:T(8,128)(2,1)S(1)}, bf16[272,256]{1,0:T(8,128)(2,1)S(1)}, u32[]{:S(2)}, u32[]{:S(2)}) collective-permute-start(bf16[272,256]{1,0:T(8,128)(2,1)S(1)} %pad_maximum_fusion.9), channel_id=1, source_target_pairs={{0,8},{4,12},{1,9},{5,13},{2,10},{6,14},{3,11},{7,15},{16,24},{20,... | collective-permute-start | bytes 417800 | tf_op jit(solution)/shard_map/ppermute | solution.py:20
  20.7 16.5 %collective-permute-start.1 = (bf16[272,256]{1,0:T(8,128)(2,1)S(1)}, bf16[272,256]{1,0:T(8,128)(2,1)S(1)}, u32[]{:S(2)}, u32[]{:S(2)}) collective-permute-start(bf16[272,256]{1,0:T(8,128)(2,1)S(1)} %pad_maximum_fusion.9), channel_id=1, source_target_pairs={{0,12},{1,13},{2,14},{3,15},{16,28},{17,29},{18,30},{19,31}} | collective-permute-start | bytes 417800 | tf_op jit(solution)/shard_map/ppermute | solution.py:20
  22.1 0.7 copy-start.17
  22.8 1.0 copy-start.9
  22.8 1.0 copy-start.10
  37.3 1.8 %collective-permute-start.5 = (bf16[816,256]{1,0:T(8,128)(2,1)S(1)}, bf16[816,256]{1,0:T(8,128)(2,1)S(1)}, u32[]{:S(2)}, u32[]{:S(2)}) collective-permute-start(bf16[816,256]{1,0:T(8,128)(2,1)S(1)} %pad_maximum_fusion.4), channel_id=1, source_target_pairs={{0,1},{1,0},{2,3},{3,2},{4,5},{5,4},{6,7},{7,6},{8,9},{9,8},{10,11... | collective-permute-start | bytes 1253384 | tf_op jit(solution)/shard_map/ppermute | solution.py:192
  76.8 13.0 %copy-start.14 = (f32[384,128]{1,0:T(8,128)S(1)}, f32[384,128]{1,0:T(8,128)}, u32[]{:S(2)}) copy-start(f32[384,128]{1,0:T(8,128)} %get-tuple-element.54) | copy-start | bytes 589828
  76.8 16.4 %collective-permute-start.6 = (f32[1024,256]{1,0:T(8,128)S(1)}, f32[1024,256]{1,0:T(8,128)S(1)}, u32[]{:S(2)}, u32[]{:S(2)}) collective-permute-start(f32[1024,256]{1,0:T(8,128)S(1)} %broadcast_select_fusion), channel_id=1, source_target_pairs={{0,1},{1,0},{2,3},{3,2},{4,5},{5,4},{6,7},{7,6},{8,9},{9,8},{10,11... | collective-permute-start | bytes 3145736 | tf_op jit(solution)/shard_map/ppermute | solution.py:212
  89.8 0.9 copy-start.16
  90.8 0.9 copy-start.13
  90.8 1.0 copy-start.15
  90.8 2.4 %copy-start = (f32[1024,256]{1,0:T(8,128)S(1)}, f32[1024,256]{1,0:T(8,128)}, u32[]{:S(2)}) copy-start(f32[1024,256]{1,0:T(8,128)} %get-tuple-element.61) | copy-start | bytes 3145732
  90.8 2.4 %copy-start.1 = (f32[1024,256]{1,0:T(8,128)S(1)}, f32[1024,256]{1,0:T(8,128)}, u32[]{:S(2)}) copy-start(f32[1024,256]{1,0:T(8,128)} %get-tuple-element.62) | copy-start | bytes 3145732
  91.9 7.7 %collective-permute-start.4 = (bf16[128,512]{1,0:T(8,128)(2,1)S(1)}, bf16[128,512]{1,0:T(8,128)(2,1)S(1)}, u32[]{:S(2)}, u32[]{:S(2)}) collective-permute-start(bf16[128,512]{1,0:T(8,128)(2,1)S(1)} %pad_maximum_fusion.10), channel_id=1, source_target_pairs={{4,0},{8,4},{12,8},{5,1},{9,5},{13,9},{6,2},{10,6},{14,10},{7,3},{... | collective-permute-start | bytes 393224 | tf_op jit(solution)/shard_map/ppermute | solution.py:20
  93.5 10.0 %collective-permute-start.7 = (bf16[256,256]{1,0:T(8,128)(2,1)S(1)}, bf16[256,256]{1,0:T(8,128)(2,1)S(1)}, u32[]{:S(2)}, u32[]{:S(2)}) collective-permute-start(bf16[256,256]{1,0:T(8,128)(2,1)S(1)} %get-tuple-element.76), channel_id=1, source_target_pairs={{12,0},{13,1},{14,2},{15,3},{28,16},{29,17},{30,18},{31,19}} | collective-permute-start | bytes 393224 | tf_op jit(solution)/shard_map/ppermute | solution.py:20
  94.8 10.5 %collective-permute-start.9 = (bf16[256,256]{1,0:T(8,128)(2,1)S(1)}, bf16[256,256]{1,0:T(8,128)(2,1)S(1)}, u32[]{:S(2)}, u32[]{:S(2)}) collective-permute-start(bf16[256,256]{1,0:T(8,128)(2,1)S(1)} %get-tuple-element.77), channel_id=1, source_target_pairs={{4,0},{8,4},{12,8},{5,1},{9,5},{13,9},{6,2},{10,6},{14,10},{7,3},{... | collective-permute-start | bytes 393224 | tf_op jit(solution)/shard_map/ppermute | solution.py:20
  96.1 15.3 %collective-permute-start.8 = (bf16[256,256]{1,0:T(8,128)(2,1)S(1)}, bf16[256,256]{1,0:T(8,128)(2,1)S(1)}, u32[]{:S(2)}, u32[]{:S(2)}) collective-permute-start(bf16[256,256]{1,0:T(8,128)(2,1)S(1)} %get-tuple-element.78), channel_id=1, source_target_pairs={{8,0},{12,4},{9,1},{13,5},{10,2},{14,6},{11,3},{15,7},{24,16},{28,... | collective-permute-start | bytes 393224 | tf_op jit(solution)/shard_map/ppermute | solution.py:20
  111.4 1.0 copy-start.11
  111.4 1.0 copy-start.12
  111.5 3.4 %collective-permute-start.10 = (f32[256,768]{1,0:T(8,128)S(1)}, f32[256,768]{1,0:T(8,128)S(1)}, u32[]{:S(2)}, u32[]{:S(2)}) collective-permute-start(f32[256,768]{1,0:T(8,128)S(1)} %pad_maximum_fusion), channel_id=1, source_target_pairs={{0,1},{1,0},{2,3},{3,2},{4,5},{5,4},{6,7},{7,6},{8,9},{9,8},{10,11... | collective-permute-start | bytes 2359304 | tf_op jit(solution)/shard_map/ppermute | solution.py:232
  112.5 1.2 %copy-start.6 = (bf16[256,1024]{1,0:T(8,128)(2,1)S(1)}, bf16[256,1024]{1,0:T(8,128)(2,1)}, u32[]{:S(2)}) copy-start(bf16[256,1024]{1,0:T(8,128)(2,1)} %get-tuple-element.63) | copy-start | bytes 1572868

commit v3 on v2

--- a/solution.py
+++ b/solution.py
@@ -28,46 +28,47 @@
     g_rel = pl.program_id(0)
     g = g_rel + g0
     i = pl.program_id(1)
-    j = pl.program_id(2)
-
-    @pl.when((g_rel == 0) & (i == 0) & (j == 0))
+    heads = q_ref.shape[1] // HD
+
+    @pl.when((g_rel == 0) & (i == 0))
     def _():
         dk_ref[...] = jnp.zeros_like(dk_ref)
         dv_ref[...] = jnp.zeros_like(dv_ref)
 
     k = pick_half(k_ref[...], g % 2)
     v = pick_half(v_ref[...], g % 2)
-    q = pick_half(q_ref[...], j % 2)
-    do = pick_half(do_ref[...], j % 2)
-    sink = sink_ref[g, j]
-
-    s = lax.dot_general(q, k, NT_DIMS, preferred_element_type=jnp.float32) + bias_ref[...]
-    row_max = jnp.maximum(jnp.max(s, axis=1, keepdims=True), sink)
-    e = jnp.exp(s - row_max)
-    total = jnp.sum(e, axis=1, keepdims=True) + jnp.exp(sink - row_max)
-    p = e * (1.0 / total)
-    p_low = p.astype(jnp.bfloat16)
-    o = jnp.dot(p_low, v, preferred_element_type=jnp.float32)
-    delta = jnp.sum(do.astype(jnp.float32) * o, axis=1, keepdims=True)
-    dp = lax.dot_general(do, v, NT_DIMS, preferred_element_type=jnp.float32)
-    ds_low = (p * (dp - delta)).astype(jnp.bfloat16)
-    dq = (jnp.dot(ds_low, k, preferred_element_type=jnp.float32) * 0.125).astype(dq_ref.dtype)
-    dk = jnp.dot(ds_low.T, q, preferred_element_type=jnp.float32)
-    dv = jnp.dot(p_low.T, do, preferred_element_type=jnp.float32)
-
-    @pl.when(j % 2 == 0)
-    def _():
-        dq_ref[:, :HD] = dq
-
-    @pl.when(j % 2 == 1)
-    def _():
-        dq_ref[:, HD:] = dq
+    bias = bias_ref[...]
+    dk_acc = None
+    dv_acc = None
+    dq_parts = []
+    for j in range(heads):
+        q = q_ref[:, j * HD:(j + 1) * HD]
+        do = do_ref[:, j * HD:(j + 1) * HD]
+        sink = sink_ref[g, j]
+        s = lax.dot_general(q, k, NT_DIMS, preferred_element_type=jnp.float32) + bias
+        row_max = jnp.maximum(jnp.max(s, axis=1, keepdims=True), sink)
+        e = jnp.exp(s - row_max)
+        total = jnp.sum(e, axis=1, keepdims=True) + jnp.exp(sink - row_max)
+        p = e * (1.0 / total)
+        p_low = p.astype(jnp.bfloat16)
+        o = jnp.dot(p_low, v, preferred_element_type=jnp.float32)
+        delta = jnp.sum(do.astype(jnp.float32) * o, axis=1, keepdims=True)
+        dp = lax.dot_general(do, v, NT_DIMS, preferred_element_type=jnp.float32)
+        ds_low = (p * (dp - delta)).astype(jnp.bfloat16)
+        dq_parts.append(
+            (jnp.dot(ds_low, k, preferred_element_type=jnp.float32) * 0.125).astype(dq_ref.dtype)
+        )
+        dk = jnp.dot(ds_low.T, q, preferred_element_type=jnp.float32)
+        dv = jnp.dot(p_low.T, do, preferred_element_type=jnp.float32)
+        dk_acc = dk if dk_acc is None else dk_acc + dk
+        dv_acc = dv if dv_acc is None else dv_acc + dv
+    dq_ref[...] = jnp.concatenate(dq_parts, axis=1)
 
     for gg in range(gn):
         @pl.when(g_rel == gg)
         def _():
-            dk_ref[:, gg * HD:(gg + 1) * HD] += dk
-            dv_ref[:, gg * HD:(gg + 1) * HD] += dv
+            dk_ref[:, gg * HD:(gg + 1) * HD] += dk_acc
+            dv_ref[:, gg * HD:(gg + 1) * HD] += dv_acc
 
 
 def attn_bwd(sinks, queries, grads, keys, values, bias, g0, gn):
@@ -77,37 +78,32 @@
     rows = n
     while rows > 8 and rows * m > (1 << 18):
         rows //= 2
-    grid = (gn, n // rows, heads)
-
-    def q_map(g, i, j):
-        return (i, ((g + g0) * heads + j) // 2)
-
-    def out_q_map(g, i, j):
-        return (i, (g * heads + j) // 2)
+    grid = (gn, n // rows)
+    width = heads * HD
 
     return pl.pallas_call(
         functools.partial(attn_bwd_kernel, g0, gn),
         grid=grid,
         in_specs=[
             pl.BlockSpec(memory_space=pltpu.SMEM),
-            pl.BlockSpec((rows, 2 * HD), q_map),
-            pl.BlockSpec((rows, 2 * HD), q_map),
-            pl.BlockSpec((m, 2 * HD), lambda g, i, j: (0, (g + g0) // 2)),
-            pl.BlockSpec((m, 2 * HD), lambda g, i, j: (0, (g + g0) // 2)),
-            pl.BlockSpec((rows, m), lambda g, i, j: (i, 0)),
+            pl.BlockSpec((rows, width), lambda g, i: (i, g + g0)),
+            pl.BlockSpec((rows, width), lambda g, i: (i, g + g0)),
+            pl.BlockSpec((m, 2 * HD), lambda g, i: (0, (g + g0) // 2)),
+            pl.BlockSpec((m, 2 * HD), lambda g, i: (0, (g + g0) // 2)),
+            pl.BlockSpec((rows, m), lambda g, i: (i, 0)),
         ],
         out_specs=[
-            pl.BlockSpec((rows, 2 * HD), out_q_map),
-            pl.BlockSpec((m, gn * HD), lambda g, i, j: (0, 0)),
-            pl.BlockSpec((m, gn * HD), lambda g, i, j: (0, 0)),
+            pl.BlockSpec((rows, width), lambda g, i: (i, g)),
+            pl.BlockSpec((m, gn * HD), lambda g, i: (0, 0)),
+            pl.BlockSpec((m, gn * HD), lambda g, i: (0, 0)),
         ],
         out_shape=[
-            jax.ShapeDtypeStruct((n, gn * heads * HD), jnp.bfloat16),
+            jax.ShapeDtypeStruct((n, gn * width), jnp.bfloat16),
             jax.ShapeDtypeStruct((m, gn * HD), jnp.float32),
             jax.ShapeDtypeStruct((m, gn * HD), jnp.float32),
         ],
         compiler_params=pltpu.CompilerParams(
-            dimension_semantics=("arbitrary", "arbitrary", "arbitrary"),
+            dimension_semantics=("arbitrary", "arbitrary"),
             vmem_limit_bytes=60 * 1024 * 1024,
         ),
         cost_estimate=pl.CostEstimate(

time: 117 us -> 103 us (0.88)
  Pallas kernels: 60.1 us -> 46.2 us
    pallas_call x3, Pallas kernels: 60.1 us -> 46.2 us  [attn_bwd(): pl.pallas_call(functools.partial(attn_bwd_kernel, g0, gn), grid=grid, in_...]
  transfers between devices with their start and end apart: 11 -> 11, of which waited for: 5 -> 5; matrix products, arithmetic and copies ran while one was open for 9% -> 10% of each run, Pallas kernels for 22% -> 19%
where the time goes in v3:
time: 103 us; the launch traced here: 102 us
  Pallas kernels  46.2 us (45%)
  starting transfers between devices  18.2 us (18%)
  waiting for transfers between devices  14.2 us (14%)
  local copies, waits for them, and re-layouts  13.9 us (13%)
  other arithmetic  8.79 us (9%)
  between operations  1.15 us (1%)
    pallas_call x3, Pallas kernels, attn_bwd(): pl.pallas_call(functools.partial(attn_bwd_kernel, g0, gn), grid=grid, in_...  46.2 us
    ppermute x8, starting transfers between devices, passed_along(): lax.ppermute(value, axis, [(source, source + steps) for source in range(f...  17.8 us
    ppermute x8, waiting for transfers between devices, passed_along(): lax.ppermute(value, axis, [(source, source + steps) for source in range(f...  13.8 us
    unnamed x44, local copies, waits for them, and re-layouts  8.98 us
    select_n x2, other arithmetic, make_bias(): return jnp.where(visible, 0.0, NEG).astype(jnp.float32)  2.33 us
  transfers between devices with their start and end apart: 11, of which 5 were waited for; matrix products, arithmetic and copies ran while one was open for 10% of the time, Pallas kernels for 19%

profile of v3, /device:TPU:0, one launch (start us, length us, event | category | flops | bytes accessed | tf_op | source)
XLA Modules:
  0.0 102.4 jit_solution(3702900590502642394)
XLA Ops:
  0.6 0.7 convert.16
  1.4 0.8 slice.139
  2.3 0.8 slice.140
  3.1 4.9 %collective-permute-start = (bf16[144,512]{1,0:T(8,128)(2,1)S(1)}, bf16[144,512]{1,0:T(8,128)(2,1)S(1)}, u32[]{:S(2)}, u32[]{:S(2)}) collective-permute-start(bf16[144,512]{1,0:T(8,128)(2,1)S(1)} %pad_maximum_fusion.8), channel_id=1, source_target_pairs={{0,4},{4,8},{8,12},{1,5},{5,9},{9,13},{2,6},{6,10},{10,14},{3,7},{... | collective-permute-start | bytes 442376 | tf_op jit(solution)/shard_map/ppermute | solution.py:20
  8.2 0.2 broadcast_multiply_fusion.1
  8.4 0.8 copy-done.3
  9.2 0.2 broadcast_multiply_fusion
  9.4 0.7 copy-done.7
  10.2 0.9 copy.17
  11.1 0.2 copy-done.4
  11.3 0.9 copy.18
  12.2 0.9 copy.20
  13.1 0.2 copy-done.5
  13.4 0.9 copy.21
  14.3 3.5 %collective-permute-start.3 = (bf16[272,256]{1,0:T(8,128)(2,1)S(1)}, bf16[272,256]{1,0:T(8,128)(2,1)S(1)}, u32[]{:S(2)}, u32[]{:S(2)}) collective-permute-start(bf16[272,256]{1,0:T(8,128)(2,1)S(1)} %pad_maximum_fusion.9), channel_id=1, source_target_pairs={{0,4},{4,8},{8,12},{1,5},{5,9},{9,13},{2,6},{6,10},{10,14},{3,7},{... | collective-permute-start | bytes 417800 | tf_op jit(solution)/shard_map/ppermute | solution.py:20
  17.8 2.9 %collective-permute-start.2 = (bf16[272,256]{1,0:T(8,128)(2,1)S(1)}, bf16[272,256]{1,0:T(8,128)(2,1)S(1)}, u32[]{:S(2)}, u32[]{:S(2)}) collective-permute-start(bf16[272,256]{1,0:T(8,128)(2,1)S(1)} %pad_maximum_fusion.9), channel_id=1, source_target_pairs={{0,8},{4,12},{1,9},{5,13},{2,10},{6,14},{3,11},{7,15},{16,24},{20,... | collective-permute-start | bytes 417800 | tf_op jit(solution)/shard_map/ppermute | solution.py:20
  20.7 1.3 %collective-permute-start.1 = (bf16[272,256]{1,0:T(8,128)(2,1)S(1)}, bf16[272,256]{1,0:T(8,128)(2,1)S(1)}, u32[]{:S(2)}, u32[]{:S(2)}) collective-permute-start(bf16[272,256]{1,0:T(8,128)(2,1)S(1)} %pad_maximum_fusion.9), channel_id=1, source_target_pairs={{0,12},{1,13},{2,14},{3,15},{16,28},{17,29},{18,30},{19,31}} | collective-permute-start | bytes 417800 | tf_op jit(solution)/shard_map/ppermute | solution.py:20
  22.1 0.7 copy-done.17
  22.8 1.0 fusion.7.bias_ref
  23.7 0.8 pad_maximum_fusion.6
  24.5 9.8 %shard_map.154 = (bf16[256,512]{1,0:T(8,128)(2,1)}, f32[384,128]{1,0:T(8,128)}, f32[384,128]{1,0:T(8,128)}) custom-call(f32[4,4]{1,0:T(4,128)} %sink_ref.4, bf16[256,1024]{1,0:T(8,128)(2,1)} %bitcast.18, bf16[256,1024]{1,0:T(8,128)(2,1)} %bitcast.20, bf16[384,256]{1,0:T(8,128)(2,1)} %get-tuple-element.87.k_ref, bf16[384,256]{1,0:T(8,128)(2,1)} %get-tuple-element.88.v_ref, ...), custom_call_target="tpu_custom_call" | custom-call | flops 603979776 | bytes 2555904 | tf_op jit(solution)/shard_map/pallas_call | solution.py:84
  34.5 1.4 %fusion.2.bias_ref = f32[256,1024]{1,0:T(8,128)} fusion(s32[1024]{0:T(1024)S(1)} %pad_add_fusion, s32[1024]{0:T(1024)S(1)} %iota_add_fusion, s32[256]{0:T(256)S(1)} %iota_add_fusion.2, s32[256]{0:T(256)S(1)} %copy-done.17, pred[1024]{0:T(1024)(128)(4,1)S(1)} %broadcast_compare_fusion), kind=kLoop, calls=%fused_computation.4 | loop fusion | flops 1572864 | bytes 1059840 | tf_op jit(solution)/shard_map/jit(_where)/select_n | solution.py:122
  35.9 0.4 collective-permute-done.5
  36.3 0.8 pad_maximum_fusion.3.v_ref
  37.1 0.9 pad_maximum_fusion.2.k_ref
  38.0 26.5 %shard_map.156 = (bf16[256,1024]{1,0:T(8,128)(2,1)}, f32[1024,256]{1,0:T(8,128)}, f32[1024,256]{1,0:T(8,128)}) custom-call(f32[4,4]{1,0:T(4,128)} %sink_ref.5, bf16[256,1024]{1,0:T(8,128)(2,1)} %bitcast.22, bf16[256,1024]{1,0:T(8,128)(2,1)} %bitcast.23, bf16[1024,256]{1,0:T(8,128)(2,1)} %pad_maximum_fusion.2.k_ref, ...), custom_call_target="tpu_custom_call" | custom-call | flops 3221225472 | bytes 7340032 | tf_op jit(solution)/shard_map/pallas_call | solution.py:84
  64.5 1.4 %broadcast_select_fusion = f32[1024,256]{1,0:T(8,128)S(1)} fusion(f32[1024,256]{1,0:T(8,128)} %get-tuple-element.62, f32[1024,256]{1,0:T(8,128)} %get-tuple-element.61, pred[]{:T(512)S(6)} %eq.14), kind=kLoop, calls=%fused_computation.15 | loop fusion | flops 262144 | bytes 3145729 | tf_op jit(solution)/shard_map/jit(_where)/select_n | solution.py:206
  65.9 0.2 collective-permute-start.6
  66.1 9.9 %shard_map.155 = (bf16[256,512]{1,0:T(8,128)(2,1)}, f32[384,128]{1,0:T(8,128)}, f32[384,128]{1,0:T(8,128)}) custom-call(f32[4,4]{1,0:T(4,128)} %sink_ref.4, bf16[256,1024]{1,0:T(8,128)(2,1)} %bitcast.19, bf16[256,1024]{1,0:T(8,128)(2,1)} %bitcast.21, bf16[384,256]{1,0:T(8,128)(2,1)} %get-tuple-element.87.k_ref, bf16[384,256]{1,0:T(8,128)(2,1)} %get-tuple-element.88.v_ref, ...), custom_call_target="tpu_custom_call" | custom-call | flops 603979776 | bytes 2555904 | tf_op jit(solution)/shard_map/pallas_call | solution.py:84
  76.0 0.9 copy-done.16
  77.0 0.8 copy-done.13
  77.8 0.1 copy-done.15
  78.0 1.3 %collective-permute-start.4 = (bf16[128,512]{1,0:T(8,128)(2,1)S(1)}, bf16[128,512]{1,0:T(8,128)(2,1)S(1)}, u32[]{:S(2)}, u32[]{:S(2)}) collective-permute-start(bf16[128,512]{1,0:T(8,128)(2,1)S(1)} %pad_maximum_fusion.10), channel_id=1, source_target_pairs={{4,0},{8,4},{12,8},{5,1},{9,5},{13,9},{6,2},{10,6},{14,10},{7,3},{... | collective-permute-start | bytes 393224 | tf_op jit(solution)/shard_map/ppermute | solution.py:20
  79.3 0.2 fusion.13
  79.5 1.3 %collective-permute-start.7 = (bf16[256,256]{1,0:T(8,128)(2,1)S(1)}, bf16[256,256]{1,0:T(8,128)(2,1)S(1)}, u32[]{:S(2)}, u32[]{:S(2)}) collective-permute-start(bf16[256,256]{1,0:T(8,128)(2,1)S(1)} %get-tuple-element.76), channel_id=1, source_target_pairs={{12,0},{13,1},{14,2},{15,3},{28,16},{29,17},{30,18},{31,19}} | collective-permute-start | bytes 393224 | tf_op jit(solution)/shard_map/ppermute | solution.py:20
  80.8 1.3 %collective-permute-start.9 = (bf16[256,256]{1,0:T(8,128)(2,1)S(1)}, bf16[256,256]{1,0:T(8,128)(2,1)S(1)}, u32[]{:S(2)}, u32[]{:S(2)}) collective-permute-start(bf16[256,256]{1,0:T(8,128)(2,1)S(1)} %get-tuple-element.77), channel_id=1, source_target_pairs={{4,0},{8,4},{12,8},{5,1},{9,5},{13,9},{6,2},{10,6},{14,10},{7,3},{... | collective-permute-start | bytes 393224 | tf_op jit(solution)/shard_map/ppermute | solution.py:20
  82.1 1.3 %collective-permute-start.8 = (bf16[256,256]{1,0:T(8,128)(2,1)S(1)}, bf16[256,256]{1,0:T(8,128)(2,1)S(1)}, u32[]{:S(2)}, u32[]{:S(2)}) collective-permute-start(bf16[256,256]{1,0:T(8,128)(2,1)S(1)} %get-tuple-element.78), channel_id=1, source_target_pairs={{8,0},{12,4},{9,1},{13,5},{10,2},{14,6},{11,3},{15,7},{24,16},{28,... | collective-permute-start | bytes 393224 | tf_op jit(solution)/shard_map/ppermute | solution.py:20
  83.4 2.1 %collective-permute-done.4 = bf16[128,512]{1,0:T(8,128)(2,1)S(1)} collective-permute-done((bf16[128,512]{1,0:T(8,128)(2,1)S(1)}, bf16[128,512]{1,0:T(8,128)(2,1)S(1)}, u32[]{:S(2)}, u32[]{:S(2)}) %collective-permute-start.4) | collective-permute-done | bytes 131104 | tf_op jit(solution)/shard_map/ppermute | solution.py:20
  85.6 4.0 %collective-permute-done.7 = bf16[256,256]{1,0:T(8,128)(2,1)S(1)} collective-permute-done((bf16[256,256]{1,0:T(8,128)(2,1)S(1)}, bf16[256,256]{1,0:T(8,128)(2,1)S(1)}, u32[]{:S(2)}, u32[]{:S(2)}) %collective-permute-start.7) | collective-permute-done | bytes 131104 | tf_op jit(solution)/shard_map/ppermute | solution.py:20
  89.6 1.6 %collective-permute-done.9 = bf16[256,256]{1,0:T(8,128)(2,1)S(1)} collective-permute-done((bf16[256,256]{1,0:T(8,128)(2,1)S(1)}, bf16[256,256]{1,0:T(8,128)(2,1)S(1)}, u32[]{:S(2)}, u32[]{:S(2)}) %collective-permute-start.9) | collective-permute-done | bytes 131104 | tf_op jit(solution)/shard_map/ppermute | solution.py:20
  91.2 6.1 %collective-permute-done.8 = bf16[256,256]{1,0:T(8,128)(2,1)S(1)} collective-permute-done((bf16[256,256]{1,0:T(8,128)(2,1)S(1)}, bf16[256,256]{1,0:T(8,128)(2,1)S(1)}, u32[]{:S(2)}, u32[]{:S(2)}) %collective-permute-start.8) | collective-permute-done | bytes 131104 | tf_op jit(solution)/shard_map/ppermute | solution.py:20
  97.5 0.1 collective-permute-start.10
  97.6 0.8 copy-done.11
  98.3 0.1 copy-done.12
  98.5 1.2 %reshape.119 = bf16[256,4,256]{2,1,0:T(4,128)(2,1)} reshape(bf16[256,1024]{1,0:T(8,128)(2,1)S(1)} %pad_maximum_fusion.1) | data formatting | bytes 1048576 | tf_op jit(solution)/shard_map/reshape | solution.py:234
  99.7 1.2 %reshape.121 = bf16[256,4,256]{2,1,0:T(4,128)(2,1)} reshape(bf16[256,1024]{1,0:T(8,128)(2,1)S(1)} %copy-done.6) | data formatting | bytes 1048576 | tf_op jit(solution)/shard_map/reshape | solution.py:237
  100.9 0.7 fusion.15
  101.6 0.7 select_convert_fusion
  (71 shorter events, 0.9 us)
Async XLA Ops:
  0.6 7.5 %copy-start.2 = (bf16[256,4,256]{2,1,0:T(4,128)(2,1)S(1)}, bf16[256,4,256]{2,1,0:T(4,128)(2,1)}, u32[]{:S(2)}) copy-start(bf16[256,4,256]{2,1,0:T(4,128)(2,1)} %param.16) | copy-start | bytes 1572868
  3.1 11.1 %collective-permute-start = (bf16[144,512]{1,0:T(8,128)(2,1)S(1)}, bf16[144,512]{1,0:T(8,128)(2,1)S(1)}, u32[]{:S(2)}, u32[]{:S(2)}) collective-permute-start(bf16[144,512]{1,0:T(8,128)(2,1)S(1)} %pad_maximum_fusion.8), channel_id=1, source_target_pairs={{0,4},{4,8},{8,12},{1,5},{5,9},{9,13},{2,6},{6,10},{10,14},{3,7},{... | collective-permute-start | bytes 442376 | tf_op jit(solution)/shard_map/ppermute | solution.py:20
  8.1 1.0 %copy-start.3 = (bf16[256,4,256]{2,1,0:T(4,128)(2,1)S(1)}, bf16[256,4,256]{2,1,0:T(4,128)(2,1)}, u32[]{:S(2)}) copy-start(bf16[256,4,256]{2,1,0:T(4,128)(2,1)} %param.21) | copy-start | bytes 1572868
  9.2 0.9 copy-start.7
  9.2 1.0 copy-start.8
  10.2 1.1 %copy-start.4 = (bf16[256,4,256]{2,1,0:T(4,128)(2,1)S(1)}, bf16[256,4,256]{2,1,0:T(4,128)(2,1)}, u32[]{:S(2)}) copy-start(bf16[256,4,256]{2,1,0:T(4,128)(2,1)} %param.19) | copy-start | bytes 1572868
  12.2 1.1 %copy-start.5 = (bf16[256,4,256]{2,1,0:T(4,128)(2,1)S(1)}, bf16[256,4,256]{2,1,0:T(4,128)(2,1)}, u32[]{:S(2)}) copy-start(bf16[256,4,256]{2,1,0:T(4,128)(2,1)} %param.24) | copy-start | bytes 1572868
  14.3 20.0 %collective-permute-start.3 = (bf16[272,256]{1,0:T(8,128)(2,1)S(1)}, bf16[272,256]{1,0:T(8,128)(2,1)S(1)}, u32[]{:S(2)}, u32[]{:S(2)}) collective-permute-start(bf16[272,256]{1,0:T(8,128)(2,1)S(1)} %pad_maximum_fusion.9), channel_id=1, source_target_pairs={{0,4},{4,8},{8,12},{1,5},{5,9},{9,13},{2,6},{6,10},{10,14},{3,7},{... | collective-permute-start | bytes 417800 | tf_op jit(solution)/shard_map/ppermute | solution.py:20
  17.8 16.5 %collective-permute-start.2 = (bf16[272,256]{1,0:T(8,128)(2,1)S(1)}, bf16[272,256]{1,0:T(8,128)(2,1)S(1)}, u32[]{:S(2)}, u32[]{:S(2)}) collective-permute-start(bf16[272,256]{1,0:T(8,128)(2,1)S(1)} %pad_maximum_fusion.9), channel_id=1, source_target_pairs={{0,8},{4,12},{1,9},{5,13},{2,10},{6,14},{3,11},{7,15},{16,24},{20,... | collective-permute-start | bytes 417800 | tf_op jit(solution)/shard_map/ppermute | solution.py:20
  20.7 13.6 %collective-permute-start.1 = (bf16[272,256]{1,0:T(8,128)(2,1)S(1)}, bf16[272,256]{1,0:T(8,128)(2,1)S(1)}, u32[]{:S(2)}, u32[]{:S(2)}) collective-permute-start(bf16[272,256]{1,0:T(8,128)(2,1)S(1)} %pad_maximum_fusion.9), channel_id=1, source_target_pairs={{0,12},{1,13},{2,14},{3,15},{16,28},{17,29},{18,30},{19,31}} | collective-permute-start | bytes 417800 | tf_op jit(solution)/shard_map/ppermute | solution.py:20
  22.1 0.7 copy-start.17
  22.8 1.0 copy-start.9
  22.8 1.0 copy-start.10
  34.4 1.8 %collective-permute-start.5 = (bf16[816,256]{1,0:T(8,128)(2,1)S(1)}, bf16[816,256]{1,0:T(8,128)(2,1)S(1)}, u32[]{:S(2)}, u32[]{:S(2)}) collective-permute-start(bf16[816,256]{1,0:T(8,128)(2,1)S(1)} %pad_maximum_fusion.4), channel_id=1, source_target_pairs={{0,1},{1,0},{2,3},{3,2},{4,5},{5,4},{6,7},{7,6},{8,9},{9,8},{10,11... | collective-permute-start | bytes 1253384 | tf_op jit(solution)/shard_map/ppermute | solution.py:188
  65.9 10.1 %copy-start.14 = (f32[384,128]{1,0:T(8,128)S(1)}, f32[384,128]{1,0:T(8,128)}, u32[]{:S(2)}) copy-start(f32[384,128]{1,0:T(8,128)} %get-tuple-element.54) | copy-start | bytes 589828
  65.9 13.4 %collective-permute-start.6 = (f32[1024,256]{1,0:T(8,128)S(1)}, f32[1024,256]{1,0:T(8,128)S(1)}, u32[]{:S(2)}, u32[]{:S(2)}) collective-permute-start(f32[1024,256]{1,0:T(8,128)S(1)} %broadcast_select_fusion), channel_id=1, source_target_pairs={{0,1},{1,0},{2,3},{3,2},{4,5},{5,4},{6,7},{7,6},{8,9},{9,8},{10,11... | collective-permute-start | bytes 3145736 | tf_op jit(solution)/shard_map/ppermute | solution.py:208
  75.9 0.9 copy-start.16
  76.9 0.9 copy-start.13
  76.9 1.0 copy-start.15
  76.9 2.4 %copy-start = (f32[1024,256]{1,0:T(8,128)S(1)}, f32[1024,256]{1,0:T(8,128)}, u32[]{:S(2)}) copy-start(f32[1024,256]{1,0:T(8,128)} %get-tuple-element.61) | copy-start | bytes 3145732
  76.9 2.4 %copy-start.1 = (f32[1024,256]{1,0:T(8,128)S(1)}, f32[1024,256]{1,0:T(8,128)}, u32[]{:S(2)}) copy-start(f32[1024,256]{1,0:T(8,128)} %get-tuple-element.62) | copy-start | bytes 3145732
  78.0 7.6 %collective-permute-start.4 = (bf16[128,512]{1,0:T(8,128)(2,1)S(1)}, bf16[128,512]{1,0:T(8,128)(2,1)S(1)}, u32[]{:S(2)}, u32[]{:S(2)}) collective-permute-start(bf16[128,512]{1,0:T(8,128)(2,1)S(1)} %pad_maximum_fusion.10), channel_id=1, source_target_pairs={{4,0},{8,4},{12,8},{5,1},{9,5},{13,9},{6,2},{10,6},{14,10},{7,3},{... | collective-permute-start | bytes 393224 | tf_op jit(solution)/shard_map/ppermute | solution.py:20
  79.5 10.0 %collective-permute-start.7 = (bf16[256,256]{1,0:T(8,128)(2,1)S(1)}, bf16[256,256]{1,0:T(8,128)(2,1)S(1)}, u32[]{:S(2)}, u32[]{:S(2)}) collective-permute-start(bf16[256,256]{1,0:T(8,128)(2,1)S(1)} %get-tuple-element.76), channel_id=1, source_target_pairs={{12,0},{13,1},{14,2},{15,3},{28,16},{29,17},{30,18},{31,19}} | collective-permute-start | bytes 393224 | tf_op jit(solution)/shard_map/ppermute | solution.py:20
  80.8 10.4 %collective-permute-start.9 = (bf16[256,256]{1,0:T(8,128)(2,1)S(1)}, bf16[256,256]{1,0:T(8,128)(2,1)S(1)}, u32[]{:S(2)}, u32[]{:S(2)}) collective-permute-start(bf16[256,256]{1,0:T(8,128)(2,1)S(1)} %get-tuple-element.77), channel_id=1, source_target_pairs={{4,0},{8,4},{12,8},{5,1},{9,5},{13,9},{6,2},{10,6},{14,10},{7,3},{... | collective-permute-start | bytes 393224 | tf_op jit(solution)/shard_map/ppermute | solution.py:20
  82.1 15.2 %collective-permute-start.8 = (bf16[256,256]{1,0:T(8,128)(2,1)S(1)}, bf16[256,256]{1,0:T(8,128)(2,1)S(1)}, u32[]{:S(2)}, u32[]{:S(2)}) collective-permute-start(bf16[256,256]{1,0:T(8,128)(2,1)S(1)} %get-tuple-element.78), channel_id=1, source_target_pairs={{8,0},{12,4},{9,1},{13,5},{10,2},{14,6},{11,3},{15,7},{24,16},{28,... | collective-permute-start | bytes 393224 | tf_op jit(solution)/shard_map/ppermute | solution.py:20
  97.4 1.0 copy-start.11
  97.4 1.0 copy-start.12
  97.5 3.4 %collective-permute-start.10 = (f32[256,768]{1,0:T(8,128)S(1)}, f32[256,768]{1,0:T(8,128)S(1)}, u32[]{:S(2)}, u32[]{:S(2)}) collective-permute-start(f32[256,768]{1,0:T(8,128)S(1)} %pad_maximum_fusion), channel_id=1, source_target_pairs={{0,1},{1,0},{2,3},{3,2},{4,5},{5,4},{6,7},{7,6},{8,9},{9,8},{10,11... | collective-permute-start | bytes 2359304 | tf_op jit(solution)/shard_map/ppermute | solution.py:228
  98.5 1.2 %copy-start.6 = (bf16[256,1024]{1,0:T(8,128)(2,1)S(1)}, bf16[256,1024]{1,0:T(8,128)(2,1)}, u32[]{:S(2)}) copy-start(bf16[256,1024]{1,0:T(8,128)(2,1)} %get-tuple-element.63) | copy-start | bytes 1572868

commit v4 on v3

--- a/solution.py
+++ b/solution.py
@@ -203,21 +203,23 @@
     f_do = full_grad_out.reshape(n, -1)
     f_dq, f_dk, f_dv = attn_bwd(full_sinks, f_q, f_do, f_keys, f_values, f_bias, 0, groups)
 
-    give = jnp.where(first, f_dv, f_dk)
-    keep = jnp.where(first, f_dk, f_dv)
-    summed = keep + lax.ppermute(give, "rep", swap)
-    f_final = summed[(seq_count - 1) * n:]
-    for jj, d in enumerate(order):
-        piece = summed[jj * n:(jj + 1) * n].astype(jnp.bfloat16)
-        f_final = f_final + passed_along(piece, "seq", -d).astype(jnp.float32)
-
+    summed = jnp.concatenate([f_dk, f_dv], axis=1)
+    returned = [
+        passed_along(summed[jj * n:(jj + 1) * n].astype(jnp.bfloat16), "seq", -d)
+        for jj, d in enumerate(order)
+    ]
     if g_split < groups:
+        summed, w_q = lax.optimization_barrier((summed, w_q))
         w_out2 = attn_bwd(window_sinks, w_q, w_do, w_keys, w_values, w_bias, g_split, groups - g_split)
         w_dq = jnp.concatenate([w_out1[0], w_out2[0]], axis=1)
         w_dk = jnp.concatenate([w_out1[1], w_out2[1]], axis=1)
         w_dv = jnp.concatenate([w_out1[2], w_out2[2]], axis=1)
     else:
         w_dq, w_dk, w_dv = w_out1
+    w_dk, returned = lax.optimization_barrier((w_dk, returned))
+    f_final = summed[(seq_count - 1) * n:]
+    for piece in returned:
+        f_final = f_final + piece.astype(jnp.float32)
     back_w = passed_along(
         jnp.concatenate([w_dk[:WINDOW], w_dv[:WINDOW]], axis=1).astype(jnp.bfloat16), "seq", -1
     ).astype(jnp.float32)
@@ -225,11 +227,10 @@
     w_kv = jnp.concatenate([w_kv[: n - WINDOW], w_kv[n - WINDOW:] + back_w], axis=0)
 
     both = jnp.concatenate([w_kv, f_final], axis=1)
-    peer = lax.ppermute(both, "rep", swap)
-    w_sum = (w_kv + peer[:, :2 * cols]).astype(jnp.bfloat16)
-    f_other = peer[:, 2 * cols:]
-    f_dk_out = jnp.where(first, f_final, f_other).astype(jnp.bfloat16)
-    f_dv_out = jnp.where(first, f_other, f_final).astype(jnp.bfloat16)
+    both = (both + lax.ppermute(both, "rep", swap)).astype(jnp.bfloat16)
+    w_sum = both[:, :2 * cols]
+    f_dk_out = both[:, 2 * cols:3 * cols]
+    f_dv_out = both[:, 3 * cols:]
     return (
         w_dq.reshape(window_query.shape),
         w_sum[:, :cols],

time: 103 us -> 108 us (1.049)
  waiting for transfers between devices: 14.2 us -> 18.8 us
  other arithmetic: 8.79 us -> 11 us
    ppermute x8, waiting for transfers between devices: 13.8 us -> 18.3 us  [passed_along(): lax.ppermute(value, axis, [(source, source + steps) for source in range(f...]
    unnamed x44 -> x30, local copies, waits for them, and re-layouts: 8.98 us -> 6.14 us
    select_n x1 -> x0, other arithmetic: 1.37 us -> none  [body(): give = jnp.where(first, f_dv, f_dk)]
    mul x1, other arithmetic: 0.23 us -> 1.33 us  [body(): f_q = (full_query.reshape(n, -1) * 0.125).astype(jnp.bfloat16)]
  transfers between devices with their start and end apart: 11 -> 10, of which waited for: 5 -> 3; matrix products, arithmetic and copies ran while one was open for 10% -> 14% of each run, Pallas kernels for 19% -> 18%
where the time goes in v4:
time: 108 us; the launch traced here: 107 us
  Pallas kernels  46 us (43%)
  waiting for transfers between devices  18.8 us (17%)
  starting transfers between devices  17.4 us (16%)
  local copies, waits for them, and re-layouts  13 us (12%)
  other arithmetic  11 us (10%)
  between operations  1.1 us (1%)
    pallas_call x3, Pallas kernels, attn_bwd(): pl.pallas_call(functools.partial(attn_bwd_kernel, g0, gn), grid=grid, in_...  46 us
    ppermute x8, waiting for transfers between devices, passed_along(): lax.ppermute(value, axis, [(source, source + steps) for source in range(f...  18.3 us
    ppermute x8, starting transfers between devices, passed_along(): lax.ppermute(value, axis, [(source, source + steps) for source in range(f...  17.4 us
    unnamed x30, local copies, waits for them, and re-layouts  6.14 us
    select_n x2, other arithmetic, make_bias(): return jnp.where(visible, 0.0, NEG).astype(jnp.float32)  2.35 us
  transfers between devices with their start and end apart: 10, of which 3 were waited for; matrix products, arithmetic and copies ran while one was open for 14% of the time, Pallas kernels for 18%

profile of v4, /device:TPU:0, one launch (start us, length us, event | category | flops | bytes accessed | tf_op | source)
XLA Modules:
  0.0 107.3 jit_solution(14217310233211327869)
XLA Ops:
  0.7 0.7 convert.16
  1.4 0.9 slice.142
  2.3 0.8 slice.143
  3.2 4.9 %collective-permute-start = (bf16[144,512]{1,0:T(8,128)(2,1)S(1)}, bf16[144,512]{1,0:T(8,128)(2,1)S(1)}, u32[]{:S(2)}, u32[]{:S(2)}) collective-permute-start(bf16[144,512]{1,0:T(8,128)(2,1)S(1)} %pad_maximum_fusion.9), channel_id=1, source_target_pairs={{0,4},{4,8},{8,12},{1,5},{5,9},{9,13},{2,6},{6,10},{10,14},{3,7},{... | collective-permute-start | bytes 442376 | tf_op jit(solution)/shard_map/ppermute | solution.py:20
  8.2 1.3 %broadcast_multiply_fusion.1 = bf16[256,4,256]{2,1,0:T(4,128)(2,1)S(1)} fusion(bf16[256,4,256]{2,1,0:T(4,128)(2,1)} %param.16), kind=kLoop, calls=%fused_computation.24 | loop fusion | flops 262144 | bytes 1048576 | tf_op jit(solution)/shard_map/mul | solution.py:181
  9.5 0.0 copy-start.2
  9.5 1.3 %broadcast_multiply_fusion = bf16[256,4,256]{2,1,0:T(4,128)(2,1)S(1)} fusion(bf16[256,4,256]{2,1,0:T(4,128)(2,1)} %param.21), kind=kLoop, calls=%fused_computation.23 | loop fusion | flops 262144 | bytes 1048576 | tf_op jit(solution)/shard_map/mul | solution.py:202
  10.9 0.9 copy.17
  11.8 0.9 copy.18
  12.7 0.9 copy.20
  13.6 0.9 copy.21
  14.5 0.0 collective-permute-done
  14.6 3.3 %collective-permute-start.1 = (bf16[272,256]{1,0:T(8,128)(2,1)S(1)}, bf16[272,256]{1,0:T(8,128)(2,1)S(1)}, u32[]{:S(2)}, u32[]{:S(2)}) collective-permute-start(bf16[272,256]{1,0:T(8,128)(2,1)S(1)} %pad_maximum_fusion.10), channel_id=1, source_target_pairs={{0,12},{1,13},{2,14},{3,15},{16,28},{17,29},{18,30},{19,31}} | collective-permute-start | bytes 417800 | tf_op jit(solution)/shard_map/ppermute | solution.py:20
  17.9 1.8 %collective-permute-start.2 = (bf16[272,256]{1,0:T(8,128)(2,1)S(1)}, bf16[272,256]{1,0:T(8,128)(2,1)S(1)}, u32[]{:S(2)}, u32[]{:S(2)}) collective-permute-start(bf16[272,256]{1,0:T(8,128)(2,1)S(1)} %pad_maximum_fusion.10), channel_id=1, source_target_pairs={{0,8},{4,12},{1,9},{5,13},{2,10},{6,14},{3,11},{7,15},{16,24},{20,... | collective-permute-start | bytes 417800 | tf_op jit(solution)/shard_map/ppermute | solution.py:20
  19.8 1.9 %collective-permute-start.3 = (bf16[272,256]{1,0:T(8,128)(2,1)S(1)}, bf16[272,256]{1,0:T(8,128)(2,1)S(1)}, u32[]{:S(2)}, u32[]{:S(2)}) collective-permute-start(bf16[272,256]{1,0:T(8,128)(2,1)S(1)} %pad_maximum_fusion.10), channel_id=1, source_target_pairs={{0,4},{4,8},{8,12},{1,5},{5,9},{9,13},{2,6},{6,10},{10,14},{3,7},{... | collective-permute-start | bytes 417800 | tf_op jit(solution)/shard_map/ppermute | solution.py:20
  21.7 1.0 fusion.6.bias_ref
  22.7 0.8 pad_maximum_fusion.7
  23.5 9.7 %shard_map.154 = (bf16[256,512]{1,0:T(8,128)(2,1)}, f32[384,128]{1,0:T(8,128)}, f32[384,128]{1,0:T(8,128)}) custom-call(f32[4,4]{1,0:T(4,128)} %sink_ref.5, bf16[256,1024]{1,0:T(8,128)(2,1)} %bitcast.18, bf16[256,1024]{1,0:T(8,128)(2,1)} %bitcast.20, bf16[384,256]{1,0:T(8,128)(2,1)} %get-tuple-element.97.k_ref, bf16[384,256]{1,0:T(8,128)(2,1)} %get-tuple-element.98.v_ref, ...), custom_call_target="tpu_custom_call" | custom-call | flops 603979776 | bytes 2555904 | tf_op jit(solution)/shard_map/pallas_call | solution.py:84
  33.3 0.1 collective-permute-start.4
  33.4 0.9 constant_dynamic-update-slice_fusion.3
  34.4 1.4 %fusion.2.bias_ref = f32[256,1024]{1,0:T(8,128)} fusion(s32[1024]{0:T(1024)S(1)} %pad_add_fusion, s32[1024]{0:T(1024)S(1)} %iota_add_fusion, s32[256]{0:T(256)S(1)} %iota_add_fusion.2, s32[256]{0:T(256)S(1)} %copy-done.10, pred[1024]{0:T(1024)(128)(4,1)S(1)} %broadcast_compare_fusion), kind=kLoop, calls=%fused_computation.5 | loop fusion | flops 1572864 | bytes 1059840 | tf_op jit(solution)/shard_map/jit(_where)/select_n | solution.py:122
  35.8 0.1 broadcast_select_fusion.2
  35.8 0.8 pad_maximum_fusion.2.v_ref
  36.7 0.9 pad_maximum_fusion.1.k_ref
  37.5 26.5 %shard_map.155 = (bf16[256,1024]{1,0:T(8,128)(2,1)}, f32[1024,256]{1,0:T(8,128)}, f32[1024,256]{1,0:T(8,128)}) custom-call(f32[4,4]{1,0:T(4,128)} %sink_ref.4, bf16[256,1024]{1,0:T(8,128)(2,1)} %bitcast.22, bf16[256,1024]{1,0:T(8,128)(2,1)} %bitcast.23, bf16[1024,256]{1,0:T(8,128)(2,1)} %pad_maximum_fusion.1.k_ref, ...), custom_call_target="tpu_custom_call" | custom-call | flops 3221225472 | bytes 7340032 | tf_op jit(solution)/shard_map/pallas_call | solution.py:84
  64.0 1.5 %constant_dynamic-update-slice_fusion.1 = f32[1024,512]{1,0:T(8,128)S(1)} fusion(f32[1024,256]{1,0:T(8,128)} %get-tuple-element.62), kind=kLoop, calls=%fused_computation.41 | loop fusion | bytes 2097152
  65.5 0.1 copy-done
  65.5 0.1 constant_dynamic-update-slice_fusion
  65.7 0.1 convert.17
  65.8 0.8 fusion.10
  66.6 1.5 %collective-permute-start.5 = (bf16[256,512]{1,0:T(8,128)(2,1)}, bf16[256,512]{1,0:T(8,128)(2,1)S(1)}, u32[]{:S(2)}, u32[]{:S(2)}) collective-permute-start(bf16[256,512]{1,0:T(8,128)(2,1)} %get-tuple-element.78), channel_id=1, source_target_pairs={{12,0},{13,1},{14,2},{15,3},{28,16},{29,17},{30,18},{31,19}} | collective-permute-start | bytes 786440 | tf_op jit(solution)/shard_map/ppermute | solution.py:20
  68.1 1.3 %collective-permute-start.6 = (bf16[256,512]{1,0:T(8,128)(2,1)S(1)}, bf16[256,512]{1,0:T(8,128)(2,1)S(1)}, u32[]{:S(2)}, u32[]{:S(2)}) collective-permute-start(bf16[256,512]{1,0:T(8,128)(2,1)S(1)} %get-tuple-element.77), channel_id=1, source_target_pairs={{8,0},{12,4},{9,1},{13,5},{10,2},{14,6},{11,3},{15,7},{24,16},{28,... | collective-permute-start | bytes 786440 | tf_op jit(solution)/shard_map/ppermute | solution.py:20
  69.4 1.3 %collective-permute-start.7 = (bf16[256,512]{1,0:T(8,128)(2,1)S(1)}, bf16[256,512]{1,0:T(8,128)(2,1)S(1)}, u32[]{:S(2)}, u32[]{:S(2)}) collective-permute-start(bf16[256,512]{1,0:T(8,128)(2,1)S(1)} %get-tuple-element.76), channel_id=1, source_target_pairs={{4,0},{8,4},{12,8},{5,1},{9,5},{13,9},{6,2},{10,6},{14,10},{7,3},{... | collective-permute-start | bytes 786440 | tf_op jit(solution)/shard_map/ppermute | solution.py:20
  70.7 9.8 %shard_map.156 = (bf16[256,512]{1,0:T(8,128)(2,1)}, f32[384,128]{1,0:T(8,128)}, f32[384,128]{1,0:T(8,128)}) custom-call(f32[4,4]{1,0:T(4,128)} %sink_ref.5, bf16[256,1024]{1,0:T(8,128)(2,1)} %bitcast.19, bf16[256,1024]{1,0:T(8,128)(2,1)} %bitcast.21, bf16[384,256]{1,0:T(8,128)(2,1)} %get-tuple-element.97.k_ref, bf16[384,256]{1,0:T(8,128)(2,1)} %get-tuple-element.98.v_ref, ...), custom_call_target="tpu_custom_call" | custom-call | flops 603979776 | bytes 2555904 | tf_op jit(solution)/shard_map/pallas_call | solution.py:84
  80.4 0.9 constant_dynamic-update-slice_fusion.2
  81.4 1.0 pad_maximum_fusion.5
  82.5 8.0 %collective-permute-done.6 = bf16[256,512]{1,0:T(8,128)(2,1)S(1)} collective-permute-done((bf16[256,512]{1,0:T(8,128)(2,1)S(1)}, bf16[256,512]{1,0:T(8,128)(2,1)S(1)}, u32[]{:S(2)}, u32[]{:S(2)}) %collective-permute-start.6) | collective-permute-done | bytes 262176 | tf_op jit(solution)/shard_map/ppermute | solution.py:20
  90.5 1.3 %collective-permute-start.8 = (bf16[128,512]{1,0:T(8,128)(2,1)S(1)}, bf16[128,512]{1,0:T(8,128)(2,1)S(1)}, u32[]{:S(2)}, u32[]{:S(2)}) collective-permute-start(bf16[128,512]{1,0:T(8,128)(2,1)S(1)} %pad_maximum_fusion.11), channel_id=1, source_target_pairs={{4,0},{8,4},{12,8},{5,1},{9,5},{13,9},{6,2},{10,6},{14,10},{7,3},{... | collective-permute-start | bytes 393224 | tf_op jit(solution)/shard_map/ppermute | solution.py:20
  91.8 0.1 convert_add_fusion
  92.0 10.3 %collective-permute-done.8 = bf16[128,512]{1,0:T(8,128)(2,1)S(1)} collective-permute-done((bf16[128,512]{1,0:T(8,128)(2,1)S(1)}, bf16[128,512]{1,0:T(8,128)(2,1)S(1)}, u32[]{:S(2)}, u32[]{:S(2)}) %collective-permute-start.8) | collective-permute-done | bytes 131104 | tf_op jit(solution)/shard_map/ppermute | solution.py:20
  102.3 0.1 fusion.7
  102.4 1.1 pad_maximum_fusion
  103.5 0.1 pad_maximum_fusion.3
  103.5 1.2 %reshape.120 = bf16[256,4,256]{2,1,0:T(4,128)(2,1)} reshape(bf16[256,1024]{1,0:T(8,128)(2,1)S(1)} %pad_maximum_fusion.3) | data formatting | bytes 1048576 | tf_op jit(solution)/shard_map/reshape | solution.py:235
  104.7 1.2 %reshape.121 = bf16[256,4,256]{2,1,0:T(4,128)(2,1)} reshape(bf16[256,1024]{1,0:T(8,128)(2,1)S(1)} %copy-done.3) | data formatting | bytes 1048576 | tf_op jit(solution)/shard_map/reshape | solution.py:238
  105.9 0.4 collective-permute-done.9
  106.3 0.2 add_convert_fusion
  106.5 0.8 fusion.11
  (54 shorter events, 0.3 us)
Async XLA Ops:
  0.6 10.2 %copy-start.5 = (bf16[256,256]{1,0:T(8,128)(2,1)S(1)}, bf16[256,256]{1,0:T(8,128)(2,1)}, u32[]{:S(2)}) copy-start(bf16[256,256]{1,0:T(8,128)(2,1)} %param.22) | copy-start | bytes 393220
  0.6 10.2 %copy-start.4 = (bf16[256,256]{1,0:T(8,128)(2,1)S(1)}, bf16[256,256]{1,0:T(8,128)(2,1)}, u32[]{:S(2)}) copy-start(bf16[256,256]{1,0:T(8,128)(2,1)} %param.23) | copy-start | bytes 393220
  1.4 10.4 %copy-start.1 = (bf16[256,4,256]{2,1,0:T(4,128)(2,1)S(1)}, bf16[256,4,256]{2,1,0:T(4,128)(2,1)}, u32[]{:S(2)}) copy-start(bf16[256,4,256]{2,1,0:T(4,128)(2,1)} %param.19) | copy-start | bytes 1572868
  3.2 11.3 %collective-permute-start = (bf16[144,512]{1,0:T(8,128)(2,1)S(1)}, bf16[144,512]{1,0:T(8,128)(2,1)S(1)}, u32[]{:S(2)}, u32[]{:S(2)}) collective-permute-start(bf16[144,512]{1,0:T(8,128)(2,1)S(1)} %pad_maximum_fusion.9), channel_id=1, source_target_pairs={{0,4},{4,8},{8,12},{1,5},{5,9},{9,13},{2,6},{6,10},{10,14},{3,7},{... | collective-permute-start | bytes 442376 | tf_op jit(solution)/shard_map/ppermute | solution.py:20
  9.5 4.1 %copy-start.2 = (bf16[256,4,256]{2,1,0:T(4,128)(2,1)S(1)}, bf16[256,4,256]{2,1,0:T(4,128)(2,1)}, u32[]{:S(2)}) copy-start(bf16[256,4,256]{2,1,0:T(4,128)(2,1)} %param.24) | copy-start | bytes 1572868
  11.8 9.9 %copy-start.10 = (s32[256]{0:T(256)S(1)}, s32[256]{0:T(256)}, u32[]{:S(2)}) copy-start(s32[256]{0:T(256)} %param.15) | copy-start | bytes 3076
  11.8 10.9 %copy-start.6 = (bf16[256,256]{1,0:T(8,128)(2,1)S(1)}, bf16[256,256]{1,0:T(8,128)(2,1)}, u32[]{:S(2)}) copy-start(bf16[256,256]{1,0:T(8,128)(2,1)} %param.17) | copy-start | bytes 393220
  11.8 10.9 %copy-start.7 = (bf16[256,256]{1,0:T(8,128)(2,1)S(1)}, bf16[256,256]{1,0:T(8,128)(2,1)}, u32[]{:S(2)}) copy-start(bf16[256,256]{1,0:T(8,128)(2,1)} %param.18) | copy-start | bytes 393220
  14.6 18.7 %collective-permute-start.1 = (bf16[272,256]{1,0:T(8,128)(2,1)S(1)}, bf16[272,256]{1,0:T(8,128)(2,1)S(1)}, u32[]{:S(2)}, u32[]{:S(2)}) collective-permute-start(bf16[272,256]{1,0:T(8,128)(2,1)S(1)} %pad_maximum_fusion.10), channel_id=1, source_target_pairs={{0,12},{1,13},{2,14},{3,15},{16,28},{17,29},{18,30},{19,31}} | collective-permute-start | bytes 417800 | tf_op jit(solution)/shard_map/ppermute | solution.py:20
  17.9 15.3 %collective-permute-start.2 = (bf16[272,256]{1,0:T(8,128)(2,1)S(1)}, bf16[272,256]{1,0:T(8,128)(2,1)S(1)}, u32[]{:S(2)}, u32[]{:S(2)}) collective-permute-start(bf16[272,256]{1,0:T(8,128)(2,1)S(1)} %pad_maximum_fusion.10), channel_id=1, source_target_pairs={{0,8},{4,12},{1,9},{5,13},{2,10},{6,14},{3,11},{7,15},{16,24},{20,... | collective-permute-start | bytes 417800 | tf_op jit(solution)/shard_map/ppermute | solution.py:20
  19.8 13.5 %collective-permute-start.3 = (bf16[272,256]{1,0:T(8,128)(2,1)S(1)}, bf16[272,256]{1,0:T(8,128)(2,1)S(1)}, u32[]{:S(2)}, u32[]{:S(2)}) collective-permute-start(bf16[272,256]{1,0:T(8,128)(2,1)S(1)} %pad_maximum_fusion.10), channel_id=1, source_target_pairs={{0,4},{4,8},{8,12},{1,5},{5,9},{9,13},{2,6},{6,10},{10,14},{3,7},{... | collective-permute-start | bytes 417800 | tf_op jit(solution)/shard_map/ppermute | solution.py:20
  33.3 2.4 %collective-permute-start.4 = (bf16[816,256]{1,0:T(8,128)(2,1)S(1)}, bf16[816,256]{1,0:T(8,128)(2,1)S(1)}, u32[]{:S(2)}, u32[]{:S(2)}) collective-permute-start(bf16[816,256]{1,0:T(8,128)(2,1)S(1)} %pad_maximum_fusion.4), channel_id=1, source_target_pairs={{0,1},{1,0},{2,3},{3,2},{4,5},{5,4},{6,7},{7,6},{8,9},{9,8},{10,11... | collective-permute-start | bytes 1253384 | tf_op jit(solution)/shard_map/ppermute | solution.py:188
  64.0 1.5 %copy-start = (f32[1024,256]{1,0:T(8,128)S(1)}, f32[1024,256]{1,0:T(8,128)}, u32[]{:S(2)}) copy-start(f32[1024,256]{1,0:T(8,128)} %get-tuple-element.63) | copy-start | bytes 3145732
  66.6 15.9 %collective-permute-start.5 = (bf16[256,512]{1,0:T(8,128)(2,1)}, bf16[256,512]{1,0:T(8,128)(2,1)S(1)}, u32[]{:S(2)}, u32[]{:S(2)}) collective-permute-start(bf16[256,512]{1,0:T(8,128)(2,1)} %get-tuple-element.78), channel_id=1, source_target_pairs={{12,0},{13,1},{14,2},{15,3},{28,16},{29,17},{30,18},{31,19}} | collective-permute-start | bytes 786440 | tf_op jit(solution)/shard_map/ppermute | solution.py:20
  68.1 22.4 %collective-permute-start.6 = (bf16[256,512]{1,0:T(8,128)(2,1)S(1)}, bf16[256,512]{1,0:T(8,128)(2,1)S(1)}, u32[]{:S(2)}, u32[]{:S(2)}) collective-permute-start(bf16[256,512]{1,0:T(8,128)(2,1)S(1)} %get-tuple-element.77), channel_id=1, source_target_pairs={{8,0},{12,4},{9,1},{13,5},{10,2},{14,6},{11,3},{15,7},{24,16},{28,... | collective-permute-start | bytes 786440 | tf_op jit(solution)/shard_map/ppermute | solution.py:20
  69.4 21.1 %collective-permute-start.7 = (bf16[256,512]{1,0:T(8,128)(2,1)S(1)}, bf16[256,512]{1,0:T(8,128)(2,1)S(1)}, u32[]{:S(2)}, u32[]{:S(2)}) collective-permute-start(bf16[256,512]{1,0:T(8,128)(2,1)S(1)} %get-tuple-element.76), channel_id=1, source_target_pairs={{4,0},{8,4},{12,8},{5,1},{9,5},{13,9},{6,2},{10,6},{14,10},{7,3},{... | collective-permute-start | bytes 786440 | tf_op jit(solution)/shard_map/ppermute | solution.py:20
  90.5 11.8 %collective-permute-start.8 = (bf16[128,512]{1,0:T(8,128)(2,1)S(1)}, bf16[128,512]{1,0:T(8,128)(2,1)S(1)}, u32[]{:S(2)}, u32[]{:S(2)}) collective-permute-start(bf16[128,512]{1,0:T(8,128)(2,1)S(1)} %pad_maximum_fusion.11), channel_id=1, source_target_pairs={{4,0},{8,4},{12,8},{5,1},{9,5},{13,9},{6,2},{10,6},{14,10},{7,3},{... | collective-permute-start | bytes 393224 | tf_op jit(solution)/shard_map/ppermute | solution.py:20
  92.0 11.5 %copy-start.8 = (bf16[256,512]{1,0:T(8,128)(2,1)S(1)}, bf16[256,512]{1,0:T(8,128)(2,1)}, u32[]{:S(2)}) copy-start(bf16[256,512]{1,0:T(8,128)(2,1)} %get-tuple-element.58) | copy-start | bytes 786436
  92.0 11.5 %copy-start.9 = (bf16[256,512]{1,0:T(8,128)(2,1)S(1)}, bf16[256,512]{1,0:T(8,128)(2,1)}, u32[]{:S(2)}) copy-start(bf16[256,512]{1,0:T(8,128)(2,1)} %get-tuple-element.65) | copy-start | bytes 786436
  102.4 2.3 %copy-start.3 = (bf16[256,1024]{1,0:T(8,128)(2,1)S(1)}, bf16[256,1024]{1,0:T(8,128)(2,1)}, u32[]{:S(2)}) copy-start(bf16[256,1024]{1,0:T(8,128)(2,1)} %get-tuple-element.75) | copy-start | bytes 1572868
  103.4 2.9 %collective-permute-start.9 = (f32[256,1024]{1,0:T(8,128)}, f32[256,1024]{1,0:T(8,128)S(1)}, u32[]{:S(2)}, u32[]{:S(2)}) collective-permute-start(f32[256,1024]{1,0:T(8,128)} %pad_maximum_fusion), channel_id=1, source_target_pairs={{0,1},{1,0},{2,3},{3,2},{4,5},{5,4},{6,7},{7,6},{8,9},{9,8},{10,11... | collective-permute-start | bytes 3145736 | tf_op jit(solution)/shard_map/ppermute | solution.py:230

commit v5 on v3

--- a/solution.py
+++ b/solution.py
@@ -51,9 +51,8 @@
         total = jnp.sum(e, axis=1, keepdims=True) + jnp.exp(sink - row_max)
         p = e * (1.0 / total)
         p_low = p.astype(jnp.bfloat16)
-        o = jnp.dot(p_low, v, preferred_element_type=jnp.float32)
-        delta = jnp.sum(do.astype(jnp.float32) * o, axis=1, keepdims=True)
         dp = lax.dot_general(do, v, NT_DIMS, preferred_element_type=jnp.float32)
+        delta = jnp.sum(p_low.astype(jnp.float32) * dp, axis=1, keepdims=True)
         ds_low = (p * (dp - delta)).astype(jnp.bfloat16)
         dq_parts.append(
             (jnp.dot(ds_low, k, preferred_element_type=jnp.float32) * 0.125).astype(dq_ref.dtype)
@@ -107,7 +106,7 @@
             vmem_limit_bytes=60 * 1024 * 1024,
         ),
         cost_estimate=pl.CostEstimate(
-            flops=12 * gn * heads * n * m * HD,
+            flops=10 * gn * heads * n * m * HD,
             transcendentals=gn * heads * n * m,
             bytes_accessed=4 * n * m + 4 * n * gn * heads * HD * 3 + 12 * m * gn * HD,
         ),

time: 103 us -> 95.9 us (0.931)
  Pallas kernels: 46.2 us -> 38.8 us
    pallas_call x3, Pallas kernels: 46.2 us -> 38.8 us  [attn_bwd(): pl.pallas_call(functools.partial(attn_bwd_kernel, g0, gn), grid=grid, in_...]
  transfers between devices with their start and end apart: 11 -> 11, of which waited for: 5 -> 5; matrix products, arithmetic and copies ran while one was open for 10% -> 11% of each run, Pallas kernels for 19% -> 16%
where the time goes in v5:
time: 95.9 us; the launch traced here: 95.1 us
  Pallas kernels  38.8 us (40%)
  starting transfers between devices  18.2 us (19%)
  waiting for transfers between devices  14.3 us (15%)
  local copies, waits for them, and re-layouts  13.9 us (14%)
  other arithmetic  8.79 us (9%)
  between operations  1.15 us (1%)
    pallas_call x3, Pallas kernels, attn_bwd(): pl.pallas_call(functools.partial(attn_bwd_kernel, g0, gn), grid=grid, in_...  38.8 us
    ppermute x8, starting transfers between devices, passed_along(): lax.ppermute(value, axis, [(source, source + steps) for source in range(f...  17.8 us
    ppermute x8, waiting for transfers between devices, passed_along(): lax.ppermute(value, axis, [(source, source + steps) for source in range(f...  13.9 us
    unnamed x44, local copies, waits for them, and re-layouts  8.98 us
    select_n x2, other arithmetic, make_bias(): return jnp.where(visible, 0.0, NEG).astype(jnp.float32)  2.33 us
  transfers between devices with their start and end apart: 11, of which 5 were waited for; matrix products, arithmetic and copies ran while one was open for 11% of the time, Pallas kernels for 16%

profile of v5, /device:TPU:0, one launch (start us, length us, event | category | flops | bytes accessed | tf_op | source)
XLA Modules:
  0.0 95.1 jit_solution(17257172534466884558)
XLA Ops:
  0.6 0.7 convert.16
  1.4 0.8 slice.139
  2.3 0.8 slice.140
  3.1 4.9 %collective-permute-start = (bf16[144,512]{1,0:T(8,128)(2,1)S(1)}, bf16[144,512]{1,0:T(8,128)(2,1)S(1)}, u32[]{:S(2)}, u32[]{:S(2)}) collective-permute-start(bf16[144,512]{1,0:T(8,128)(2,1)S(1)} %pad_maximum_fusion.8), channel_id=1, source_target_pairs={{0,4},{4,8},{8,12},{1,5},{5,9},{9,13},{2,6},{6,10},{10,14},{3,7},{... | collective-permute-start | bytes 442376 | tf_op jit(solution)/shard_map/ppermute | solution.py:20
  8.2 0.2 broadcast_multiply_fusion.1
  8.4 0.8 copy-done.3
  9.2 0.2 broadcast_multiply_fusion
  9.4 0.7 copy-done.7
  10.2 0.9 copy.17
  11.1 0.2 copy-done.4
  11.3 0.9 copy.18
  12.2 0.9 copy.20
  13.1 0.2 copy-done.5
  13.4 0.9 copy.21
  14.3 3.5 %collective-permute-start.3 = (bf16[272,256]{1,0:T(8,128)(2,1)S(1)}, bf16[272,256]{1,0:T(8,128)(2,1)S(1)}, u32[]{:S(2)}, u32[]{:S(2)}) collective-permute-start(bf16[272,256]{1,0:T(8,128)(2,1)S(1)} %pad_maximum_fusion.9), channel_id=1, source_target_pairs={{0,4},{4,8},{8,12},{1,5},{5,9},{9,13},{2,6},{6,10},{10,14},{3,7},{... | collective-permute-start | bytes 417800 | tf_op jit(solution)/shard_map/ppermute | solution.py:20
  17.8 2.9 %collective-permute-start.2 = (bf16[272,256]{1,0:T(8,128)(2,1)S(1)}, bf16[272,256]{1,0:T(8,128)(2,1)S(1)}, u32[]{:S(2)}, u32[]{:S(2)}) collective-permute-start(bf16[272,256]{1,0:T(8,128)(2,1)S(1)} %pad_maximum_fusion.9), channel_id=1, source_target_pairs={{0,8},{4,12},{1,9},{5,13},{2,10},{6,14},{3,11},{7,15},{16,24},{20,... | collective-permute-start | bytes 417800 | tf_op jit(solution)/shard_map/ppermute | solution.py:20
  20.7 1.3 %collective-permute-start.1 = (bf16[272,256]{1,0:T(8,128)(2,1)S(1)}, bf16[272,256]{1,0:T(8,128)(2,1)S(1)}, u32[]{:S(2)}, u32[]{:S(2)}) collective-permute-start(bf16[272,256]{1,0:T(8,128)(2,1)S(1)} %pad_maximum_fusion.9), channel_id=1, source_target_pairs={{0,12},{1,13},{2,14},{3,15},{16,28},{17,29},{18,30},{19,31}} | collective-permute-start | bytes 417800 | tf_op jit(solution)/shard_map/ppermute | solution.py:20
  22.1 0.7 copy-done.17
  22.8 1.0 %fusion.7.bias_ref = f32[256,384]{1,0:T(8,128)} fusion(s32[384]{0:T(512)S(1)} %get-tuple-element.89, s32[384]{0:T(512)S(1)} %get-tuple-element.90, s32[256]{0:T(256)S(1)} %iota_add_fusion.2, s32[256]{0:T(256)S(1)} %copy-done.17, pred[384]{0:T(512)(128)(4,1)S(1)} %broadcast_compare_fusion.1), kind=kLoop, calls=%fused_computation.20 | loop fusion | flops 786432 | bytes 398720 | tf_op jit(solution)/shard_map/jit(_where)/select_n | solution.py:121
  23.7 0.8 pad_maximum_fusion.6
  24.5 7.8 %shard_map.154 = (bf16[256,512]{1,0:T(8,128)(2,1)}, f32[384,128]{1,0:T(8,128)}, f32[384,128]{1,0:T(8,128)}) custom-call(f32[4,4]{1,0:T(4,128)} %sink_ref.4, bf16[256,1024]{1,0:T(8,128)(2,1)} %bitcast.18, bf16[256,1024]{1,0:T(8,128)(2,1)} %bitcast.20, bf16[384,256]{1,0:T(8,128)(2,1)} %get-tuple-element.87.k_ref, bf16[384,256]{1,0:T(8,128)(2,1)} %get-tuple-element.88.v_ref, ...), custom_call_target="tpu_custom_call" | custom-call | flops 503316480 | bytes 2555904 | tf_op jit(solution)/shard_map/pallas_call | solution.py:83
  32.5 1.4 %fusion.2.bias_ref = f32[256,1024]{1,0:T(8,128)} fusion(s32[1024]{0:T(1024)S(1)} %pad_add_fusion, s32[1024]{0:T(1024)S(1)} %iota_add_fusion, s32[256]{0:T(256)S(1)} %iota_add_fusion.2, s32[256]{0:T(256)S(1)} %copy-done.17, pred[1024]{0:T(1024)(128)(4,1)S(1)} %broadcast_compare_fusion), kind=kLoop, calls=%fused_computation.4 | loop fusion | flops 1572864 | bytes 1059840 | tf_op jit(solution)/shard_map/jit(_where)/select_n | solution.py:121
  33.9 0.4 collective-permute-done.5
  34.3 0.8 pad_maximum_fusion.3.v_ref
  35.1 0.9 pad_maximum_fusion.2.k_ref
  36.0 23.3 %shard_map.156 = (bf16[256,1024]{1,0:T(8,128)(2,1)}, f32[1024,256]{1,0:T(8,128)}, f32[1024,256]{1,0:T(8,128)}) custom-call(f32[4,4]{1,0:T(4,128)} %sink_ref.5, bf16[256,1024]{1,0:T(8,128)(2,1)} %bitcast.22, bf16[256,1024]{1,0:T(8,128)(2,1)} %bitcast.23, bf16[1024,256]{1,0:T(8,128)(2,1)} %pad_maximum_fusion.2.k_ref, ...), custom_call_target="tpu_custom_call" | custom-call | flops 2684354560 | bytes 7340032 | tf_op jit(solution)/shard_map/pallas_call | solution.py:83
  59.2 1.4 %broadcast_select_fusion = f32[1024,256]{1,0:T(8,128)S(1)} fusion(f32[1024,256]{1,0:T(8,128)} %get-tuple-element.62, f32[1024,256]{1,0:T(8,128)} %get-tuple-element.61, pred[]{:T(512)S(6)} %eq.14), kind=kLoop, calls=%fused_computation.15 | loop fusion | flops 262144 | bytes 3145729 | tf_op jit(solution)/shard_map/jit(_where)/select_n | solution.py:205
  60.6 0.2 collective-permute-start.6
  60.8 7.8 %shard_map.155 = (bf16[256,512]{1,0:T(8,128)(2,1)}, f32[384,128]{1,0:T(8,128)}, f32[384,128]{1,0:T(8,128)}) custom-call(f32[4,4]{1,0:T(4,128)} %sink_ref.4, bf16[256,1024]{1,0:T(8,128)(2,1)} %bitcast.19, bf16[256,1024]{1,0:T(8,128)(2,1)} %bitcast.21, bf16[384,256]{1,0:T(8,128)(2,1)} %get-tuple-element.87.k_ref, bf16[384,256]{1,0:T(8,128)(2,1)} %get-tuple-element.88.v_ref, ...), custom_call_target="tpu_custom_call" | custom-call | flops 503316480 | bytes 2555904 | tf_op jit(solution)/shard_map/pallas_call | solution.py:83
  68.6 0.9 copy-done.16
  69.6 0.8 copy-done.13
  70.4 0.1 copy-done.15
  70.6 1.3 %collective-permute-start.4 = (bf16[128,512]{1,0:T(8,128)(2,1)S(1)}, bf16[128,512]{1,0:T(8,128)(2,1)S(1)}, u32[]{:S(2)}, u32[]{:S(2)}) collective-permute-start(bf16[128,512]{1,0:T(8,128)(2,1)S(1)} %pad_maximum_fusion.10), channel_id=1, source_target_pairs={{4,0},{8,4},{12,8},{5,1},{9,5},{13,9},{6,2},{10,6},{14,10},{7,3},{... | collective-permute-start | bytes 393224 | tf_op jit(solution)/shard_map/ppermute | solution.py:20
  71.9 0.2 fusion.13
  72.2 1.3 %collective-permute-start.7 = (bf16[256,256]{1,0:T(8,128)(2,1)S(1)}, bf16[256,256]{1,0:T(8,128)(2,1)S(1)}, u32[]{:S(2)}, u32[]{:S(2)}) collective-permute-start(bf16[256,256]{1,0:T(8,128)(2,1)S(1)} %get-tuple-element.76), channel_id=1, source_target_pairs={{12,0},{13,1},{14,2},{15,3},{28,16},{29,17},{30,18},{31,19}} | collective-permute-start | bytes 393224 | tf_op jit(solution)/shard_map/ppermute | solution.py:20
  73.5 1.3 %collective-permute-start.9 = (bf16[256,256]{1,0:T(8,128)(2,1)S(1)}, bf16[256,256]{1,0:T(8,128)(2,1)S(1)}, u32[]{:S(2)}, u32[]{:S(2)}) collective-permute-start(bf16[256,256]{1,0:T(8,128)(2,1)S(1)} %get-tuple-element.77), channel_id=1, source_target_pairs={{4,0},{8,4},{12,8},{5,1},{9,5},{13,9},{6,2},{10,6},{14,10},{7,3},{... | collective-permute-start | bytes 393224 | tf_op jit(solution)/shard_map/ppermute | solution.py:20
  74.8 1.3 %collective-permute-start.8 = (bf16[256,256]{1,0:T(8,128)(2,1)S(1)}, bf16[256,256]{1,0:T(8,128)(2,1)S(1)}, u32[]{:S(2)}, u32[]{:S(2)}) collective-permute-start(bf16[256,256]{1,0:T(8,128)(2,1)S(1)} %get-tuple-element.78), channel_id=1, source_target_pairs={{8,0},{12,4},{9,1},{13,5},{10,2},{14,6},{11,3},{15,7},{24,16},{28,... | collective-permute-start | bytes 393224 | tf_op jit(solution)/shard_map/ppermute | solution.py:20
  76.1 2.2 %collective-permute-done.4 = bf16[128,512]{1,0:T(8,128)(2,1)S(1)} collective-permute-done((bf16[128,512]{1,0:T(8,128)(2,1)S(1)}, bf16[128,512]{1,0:T(8,128)(2,1)S(1)}, u32[]{:S(2)}, u32[]{:S(2)}) %collective-permute-start.4) | collective-permute-done | bytes 131104 | tf_op jit(solution)/shard_map/ppermute | solution.py:20
  78.3 3.9 %collective-permute-done.7 = bf16[256,256]{1,0:T(8,128)(2,1)S(1)} collective-permute-done((bf16[256,256]{1,0:T(8,128)(2,1)S(1)}, bf16[256,256]{1,0:T(8,128)(2,1)S(1)}, u32[]{:S(2)}, u32[]{:S(2)}) %collective-permute-start.7) | collective-permute-done | bytes 131104 | tf_op jit(solution)/shard_map/ppermute | solution.py:20
  82.2 1.7 %collective-permute-done.9 = bf16[256,256]{1,0:T(8,128)(2,1)S(1)} collective-permute-done((bf16[256,256]{1,0:T(8,128)(2,1)S(1)}, bf16[256,256]{1,0:T(8,128)(2,1)S(1)}, u32[]{:S(2)}, u32[]{:S(2)}) %collective-permute-start.9) | collective-permute-done | bytes 131104 | tf_op jit(solution)/shard_map/ppermute | solution.py:20
  84.0 6.1 %collective-permute-done.8 = bf16[256,256]{1,0:T(8,128)(2,1)S(1)} collective-permute-done((bf16[256,256]{1,0:T(8,128)(2,1)S(1)}, bf16[256,256]{1,0:T(8,128)(2,1)S(1)}, u32[]{:S(2)}, u32[]{:S(2)}) %collective-permute-start.8) | collective-permute-done | bytes 131104 | tf_op jit(solution)/shard_map/ppermute | solution.py:20
  90.2 0.1 collective-permute-start.10
  90.3 0.8 copy-done.11
  91.1 0.1 copy-done.12
  91.2 1.2 %reshape.119 = bf16[256,4,256]{2,1,0:T(4,128)(2,1)} reshape(bf16[256,1024]{1,0:T(8,128)(2,1)S(1)} %pad_maximum_fusion.1) | data formatting | bytes 1048576 | tf_op jit(solution)/shard_map/reshape | solution.py:233
  92.4 1.2 %reshape.121 = bf16[256,4,256]{2,1,0:T(4,128)(2,1)} reshape(bf16[256,1024]{1,0:T(8,128)(2,1)S(1)} %copy-done.6) | data formatting | bytes 1048576 | tf_op jit(solution)/shard_map/reshape | solution.py:236
  93.7 0.7 fusion.15
  94.4 0.7 select_convert_fusion
  (71 shorter events, 0.9 us)
Async XLA Ops:
  0.6 7.5 %copy-start.2 = (bf16[256,4,256]{2,1,0:T(4,128)(2,1)S(1)}, bf16[256,4,256]{2,1,0:T(4,128)(2,1)}, u32[]{:S(2)}) copy-start(bf16[256,4,256]{2,1,0:T(4,128)(2,1)} %param.16) | copy-start | bytes 1572868
  3.1 11.1 %collective-permute-start = (bf16[144,512]{1,0:T(8,128)(2,1)S(1)}, bf16[144,512]{1,0:T(8,128)(2,1)S(1)}, u32[]{:S(2)}, u32[]{:S(2)}) collective-permute-start(bf16[144,512]{1,0:T(8,128)(2,1)S(1)} %pad_maximum_fusion.8), channel_id=1, source_target_pairs={{0,4},{4,8},{8,12},{1,5},{5,9},{9,13},{2,6},{6,10},{10,14},{3,7},{... | collective-permute-start | bytes 442376 | tf_op jit(solution)/shard_map/ppermute | solution.py:20
  8.1 1.0 %copy-start.3 = (bf16[256,4,256]{2,1,0:T(4,128)(2,1)S(1)}, bf16[256,4,256]{2,1,0:T(4,128)(2,1)}, u32[]{:S(2)}) copy-start(bf16[256,4,256]{2,1,0:T(4,128)(2,1)} %param.21) | copy-start | bytes 1572868
  9.2 0.9 copy-start.7
  9.2 1.0 %copy-start.8 = (bf16[256,256]{1,0:T(8,128)(2,1)S(1)}, bf16[256,256]{1,0:T(8,128)(2,1)}, u32[]{:S(2)}) copy-start(bf16[256,256]{1,0:T(8,128)(2,1)} %param.22) | copy-start | bytes 393220
  10.2 1.1 %copy-start.4 = (bf16[256,4,256]{2,1,0:T(4,128)(2,1)S(1)}, bf16[256,4,256]{2,1,0:T(4,128)(2,1)}, u32[]{:S(2)}) copy-start(bf16[256,4,256]{2,1,0:T(4,128)(2,1)} %param.19) | copy-start | bytes 1572868
  12.2 1.1 %copy-start.5 = (bf16[256,4,256]{2,1,0:T(4,128)(2,1)S(1)}, bf16[256,4,256]{2,1,0:T(4,128)(2,1)}, u32[]{:S(2)}) copy-start(bf16[256,4,256]{2,1,0:T(4,128)(2,1)} %param.24) | copy-start | bytes 1572868
  14.3 18.0 %collective-permute-start.3 = (bf16[272,256]{1,0:T(8,128)(2,1)S(1)}, bf16[272,256]{1,0:T(8,128)(2,1)S(1)}, u32[]{:S(2)}, u32[]{:S(2)}) collective-permute-start(bf16[272,256]{1,0:T(8,128)(2,1)S(1)} %pad_maximum_fusion.9), channel_id=1, source_target_pairs={{0,4},{4,8},{8,12},{1,5},{5,9},{9,13},{2,6},{6,10},{10,14},{3,7},{... | collective-permute-start | bytes 417800 | tf_op jit(solution)/shard_map/ppermute | solution.py:20
  17.8 14.5 %collective-permute-start.2 = (bf16[272,256]{1,0:T(8,128)(2,1)S(1)}, bf16[272,256]{1,0:T(8,128)(2,1)S(1)}, u32[]{:S(2)}, u32[]{:S(2)}) collective-permute-start(bf16[272,256]{1,0:T(8,128)(2,1)S(1)} %pad_maximum_fusion.9), channel_id=1, source_target_pairs={{0,8},{4,12},{1,9},{5,13},{2,10},{6,14},{3,11},{7,15},{16,24},{20,... | collective-permute-start | bytes 417800 | tf_op jit(solution)/shard_map/ppermute | solution.py:20
  20.7 11.6 %collective-permute-start.1 = (bf16[272,256]{1,0:T(8,128)(2,1)S(1)}, bf16[272,256]{1,0:T(8,128)(2,1)S(1)}, u32[]{:S(2)}, u32[]{:S(2)}) collective-permute-start(bf16[272,256]{1,0:T(8,128)(2,1)S(1)} %pad_maximum_fusion.9), channel_id=1, source_target_pairs={{0,12},{1,13},{2,14},{3,15},{16,28},{17,29},{18,30},{19,31}} | collective-permute-start | bytes 417800 | tf_op jit(solution)/shard_map/ppermute | solution.py:20
  22.1 0.7 copy-start.17
  22.8 1.0 %copy-start.9 = (bf16[256,256]{1,0:T(8,128)(2,1)S(1)}, bf16[256,256]{1,0:T(8,128)(2,1)}, u32[]{:S(2)}) copy-start(bf16[256,256]{1,0:T(8,128)(2,1)} %param.17) | copy-start | bytes 393220
  22.8 1.0 %copy-start.10 = (bf16[256,256]{1,0:T(8,128)(2,1)S(1)}, bf16[256,256]{1,0:T(8,128)(2,1)}, u32[]{:S(2)}) copy-start(bf16[256,256]{1,0:T(8,128)(2,1)} %param.18) | copy-start | bytes 393220
  32.4 1.8 %collective-permute-start.5 = (bf16[816,256]{1,0:T(8,128)(2,1)S(1)}, bf16[816,256]{1,0:T(8,128)(2,1)S(1)}, u32[]{:S(2)}, u32[]{:S(2)}) collective-permute-start(bf16[816,256]{1,0:T(8,128)(2,1)S(1)} %pad_maximum_fusion.4), channel_id=1, source_target_pairs={{0,1},{1,0},{2,3},{3,2},{4,5},{5,4},{6,7},{7,6},{8,9},{9,8},{10,11... | collective-permute-start | bytes 1253384 | tf_op jit(solution)/shard_map/ppermute | solution.py:187
  60.6 8.0 %copy-start.14 = (f32[384,128]{1,0:T(8,128)S(1)}, f32[384,128]{1,0:T(8,128)}, u32[]{:S(2)}) copy-start(f32[384,128]{1,0:T(8,128)} %get-tuple-element.54) | copy-start | bytes 589828
  60.6 11.3 %collective-permute-start.6 = (f32[1024,256]{1,0:T(8,128)S(1)}, f32[1024,256]{1,0:T(8,128)S(1)}, u32[]{:S(2)}, u32[]{:S(2)}) collective-permute-start(f32[1024,256]{1,0:T(8,128)S(1)} %broadcast_select_fusion), channel_id=1, source_target_pairs={{0,1},{1,0},{2,3},{3,2},{4,5},{5,4},{6,7},{7,6},{8,9},{9,8},{10,11... | collective-permute-start | bytes 3145736 | tf_op jit(solution)/shard_map/ppermute | solution.py:207
  68.6 0.9 copy-start.16
  69.5 0.9 copy-start.13
  69.5 1.0 %copy-start.15 = (f32[384,128]{1,0:T(8,128)S(1)}, f32[384,128]{1,0:T(8,128)}, u32[]{:S(2)}) copy-start(f32[384,128]{1,0:T(8,128)} %get-tuple-element.57) | copy-start | bytes 589828
  69.5 2.4 %copy-start = (f32[1024,256]{1,0:T(8,128)S(1)}, f32[1024,256]{1,0:T(8,128)}, u32[]{:S(2)}) copy-start(f32[1024,256]{1,0:T(8,128)} %get-tuple-element.61) | copy-start | bytes 3145732
  69.6 2.4 %copy-start.1 = (f32[1024,256]{1,0:T(8,128)S(1)}, f32[1024,256]{1,0:T(8,128)}, u32[]{:S(2)}) copy-start(f32[1024,256]{1,0:T(8,128)} %get-tuple-element.62) | copy-start | bytes 3145732
  70.6 7.7 %collective-permute-start.4 = (bf16[128,512]{1,0:T(8,128)(2,1)S(1)}, bf16[128,512]{1,0:T(8,128)(2,1)S(1)}, u32[]{:S(2)}, u32[]{:S(2)}) collective-permute-start(bf16[128,512]{1,0:T(8,128)(2,1)S(1)} %pad_maximum_fusion.10), channel_id=1, source_target_pairs={{4,0},{8,4},{12,8},{5,1},{9,5},{13,9},{6,2},{10,6},{14,10},{7,3},{... | collective-permute-start | bytes 393224 | tf_op jit(solution)/shard_map/ppermute | solution.py:20
  72.2 10.0 %collective-permute-start.7 = (bf16[256,256]{1,0:T(8,128)(2,1)S(1)}, bf16[256,256]{1,0:T(8,128)(2,1)S(1)}, u32[]{:S(2)}, u32[]{:S(2)}) collective-permute-start(bf16[256,256]{1,0:T(8,128)(2,1)S(1)} %get-tuple-element.76), channel_id=1, source_target_pairs={{12,0},{13,1},{14,2},{15,3},{28,16},{29,17},{30,18},{31,19}} | collective-permute-start | bytes 393224 | tf_op jit(solution)/shard_map/ppermute | solution.py:20
  73.5 10.5 %collective-permute-start.9 = (bf16[256,256]{1,0:T(8,128)(2,1)S(1)}, bf16[256,256]{1,0:T(8,128)(2,1)S(1)}, u32[]{:S(2)}, u32[]{:S(2)}) collective-permute-start(bf16[256,256]{1,0:T(8,128)(2,1)S(1)} %get-tuple-element.77), channel_id=1, source_target_pairs={{4,0},{8,4},{12,8},{5,1},{9,5},{13,9},{6,2},{10,6},{14,10},{7,3},{... | collective-permute-start | bytes 393224 | tf_op jit(solution)/shard_map/ppermute | solution.py:20
  74.8 15.3 %collective-permute-start.8 = (bf16[256,256]{1,0:T(8,128)(2,1)S(1)}, bf16[256,256]{1,0:T(8,128)(2,1)S(1)}, u32[]{:S(2)}, u32[]{:S(2)}) collective-permute-start(bf16[256,256]{1,0:T(8,128)(2,1)S(1)} %get-tuple-element.78), channel_id=1, source_target_pairs={{8,0},{12,4},{9,1},{13,5},{10,2},{14,6},{11,3},{15,7},{24,16},{28,... | collective-permute-start | bytes 393224 | tf_op jit(solution)/shard_map/ppermute | solution.py:20
  90.1 1.0 copy-start.11
  90.1 1.0 %copy-start.12 = (bf16[256,512]{1,0:T(8,128)(2,1)S(1)}, bf16[256,512]{1,0:T(8,128)(2,1)}, u32[]{:S(2)}) copy-start(bf16[256,512]{1,0:T(8,128)(2,1)} %get-tuple-element.53) | copy-start | bytes 786436
  90.2 3.4 %collective-permute-start.10 = (f32[256,768]{1,0:T(8,128)S(1)}, f32[256,768]{1,0:T(8,128)S(1)}, u32[]{:S(2)}, u32[]{:S(2)}) collective-permute-start(f32[256,768]{1,0:T(8,128)S(1)} %pad_maximum_fusion), channel_id=1, source_target_pairs={{0,1},{1,0},{2,3},{3,2},{4,5},{5,4},{6,7},{7,6},{8,9},{9,8},{10,11... | collective-permute-start | bytes 2359304 | tf_op jit(solution)/shard_map/ppermute | solution.py:227
  91.2 1.2 %copy-start.6 = (bf16[256,1024]{1,0:T(8,128)(2,1)S(1)}, bf16[256,1024]{1,0:T(8,128)(2,1)}, u32[]{:S(2)}) copy-start(bf16[256,1024]{1,0:T(8,128)(2,1)} %get-tuple-element.63) | copy-start | bytes 1572868

commit v6 on v5

--- a/solution.py
+++ b/solution.py
@@ -38,30 +38,26 @@
     k = pick_half(k_ref[...], g % 2)
     v = pick_half(v_ref[...], g % 2)
     bias = bias_ref[...]
-    dk_acc = None
-    dv_acc = None
-    dq_parts = []
-    for j in range(heads):
-        q = q_ref[:, j * HD:(j + 1) * HD]
-        do = do_ref[:, j * HD:(j + 1) * HD]
-        sink = sink_ref[g, j]
-        s = lax.dot_general(q, k, NT_DIMS, preferred_element_type=jnp.float32) + bias
-        row_max = jnp.maximum(jnp.max(s, axis=1, keepdims=True), sink)
-        e = jnp.exp(s - row_max)
-        total = jnp.sum(e, axis=1, keepdims=True) + jnp.exp(sink - row_max)
-        p = e * (1.0 / total)
-        p_low = p.astype(jnp.bfloat16)
-        dp = lax.dot_general(do, v, NT_DIMS, preferred_element_type=jnp.float32)
-        delta = jnp.sum(p_low.astype(jnp.float32) * dp, axis=1, keepdims=True)
-        ds_low = (p * (dp - delta)).astype(jnp.bfloat16)
-        dq_parts.append(
-            (jnp.dot(ds_low, k, preferred_element_type=jnp.float32) * 0.125).astype(dq_ref.dtype)
-        )
-        dk = jnp.dot(ds_low.T, q, preferred_element_type=jnp.float32)
-        dv = jnp.dot(p_low.T, do, preferred_element_type=jnp.float32)
-        dk_acc = dk if dk_acc is None else dk_acc + dk
-        dv_acc = dv if dv_acc is None else dv_acc + dv
-    dq_ref[...] = jnp.concatenate(dq_parts, axis=1)
+    rows, m = bias.shape
+    q = jnp.concatenate([q_ref[:, j * HD:(j + 1) * HD] for j in range(heads)], axis=0)
+    do = jnp.concatenate([do_ref[:, j * HD:(j + 1) * HD] for j in range(heads)], axis=0)
+    sink = jnp.concatenate(
+        [jnp.full((rows, 1), sink_ref[g, j], jnp.float32) for j in range(heads)], axis=0
+    )
+    s = lax.dot_general(q, k, NT_DIMS, preferred_element_type=jnp.float32)
+    s = (s.reshape(heads, rows, m) + bias[None]).reshape(heads * rows, m)
+    row_max = jnp.maximum(jnp.max(s, axis=1, keepdims=True), sink)
+    e = jnp.exp(s - row_max)
+    total = jnp.sum(e, axis=1, keepdims=True) + jnp.exp(sink - row_max)
+    p = e * (1.0 / total)
+    p_low = p.astype(jnp.bfloat16)
+    dp = lax.dot_general(do, v, NT_DIMS, preferred_element_type=jnp.float32)
+    delta = jnp.sum(p_low.astype(jnp.float32) * dp, axis=1, keepdims=True)
+    ds_low = (p * (dp - delta)).astype(jnp.bfloat16)
+    dq = (jnp.dot(ds_low, k, preferred_element_type=jnp.float32) * 0.125).astype(dq_ref.dtype)
+    dq_ref[...] = jnp.concatenate([dq[j * rows:(j + 1) * rows] for j in range(heads)], axis=1)
+    dk_acc = jnp.dot(ds_low.T, q, preferred_element_type=jnp.float32)
+    dv_acc = jnp.dot(p_low.T, do, preferred_element_type=jnp.float32)
 
     for gg in range(gn):
         @pl.when(g_rel == gg)
@@ -75,7 +71,7 @@
     m = keys.shape[0]
     heads = sinks.shape[1]
     rows = n
-    while rows > 8 and rows * m > (1 << 18):
+    while rows > 8 and heads * rows * m > (1 << 20):
         rows //= 2
     grid = (gn, n // rows)
     width = heads * HD

time: 95.9 us -> 102 us (1.064)
  Pallas kernels: 38.8 us -> 44.6 us
    pallas_call x3, Pallas kernels: 38.8 us -> 44.6 us  [attn_bwd(): pl.pallas_call(functools.partial(attn_bwd_kernel, g0, gn), grid=grid, in_...]
  transfers between devices with their start and end apart: 11 -> 11, of which waited for: 5 -> 5; matrix products, arithmetic and copies ran while one was open for 11% -> 10% of each run, Pallas kernels for 16% -> 18%
where the time goes in v6:
time: 102 us; the launch traced here: 101 us
  Pallas kernels  44.6 us (44%)
  starting transfers between devices  18.2 us (18%)
  waiting for transfers between devices  14.2 us (14%)
  local copies, waits for them, and re-layouts  13.9 us (14%)
  other arithmetic  8.79 us (9%)
  between operations  1.15 us (1%)
    pallas_call x3, Pallas kernels, attn_bwd(): pl.pallas_call(functools.partial(attn_bwd_kernel, g0, gn), grid=grid, in_...  44.6 us
    ppermute x8, starting transfers between devices, passed_along(): lax.ppermute(value, axis, [(source, source + steps) for source in range(f...  17.8 us
    ppermute x8, waiting for transfers between devices, passed_along(): lax.ppermute(value, axis, [(source, source + steps) for source in range(f...  13.8 us
    unnamed x44, local copies, waits for them, and re-layouts  8.98 us
    select_n x2, other arithmetic, make_bias(): return jnp.where(visible, 0.0, NEG).astype(jnp.float32)  2.33 us
  transfers between devices with their start and end apart: 11, of which 5 were waited for; matrix products, arithmetic and copies ran while one was open for 10% of the time, Pallas kernels for 18%

profile of v6, /device:TPU:0, one launch (start us, length us, event | category | flops | bytes accessed | tf_op | source)
XLA Modules:
  0.0 100.8 jit_solution(3327849693431765740)
XLA Ops:
  0.6 0.7 convert.16
  1.4 0.8 slice.139
  2.3 0.8 slice.140
  3.1 4.9 %collective-permute-start = (bf16[144,512]{1,0:T(8,128)(2,1)S(1)}, bf16[144,512]{1,0:T(8,128)(2,1)S(1)}, u32[]{:S(2)}, u32[]{:S(2)}) collective-permute-start(bf16[144,512]{1,0:T(8,128)(2,1)S(1)} %pad_maximum_fusion.8), channel_id=1, source_target_pairs={{0,4},{4,8},{8,12},{1,5},{5,9},{9,13},{2,6},{6,10},{10,14},{3,7},{... | collective-permute-start | bytes 442376 | tf_op jit(solution)/shard_map/ppermute | solution.py:20
  8.2 0.2 broadcast_multiply_fusion.1
  8.4 0.8 copy-done.3
  9.2 0.2 broadcast_multiply_fusion
  9.4 0.7 copy-done.7
  10.2 0.9 copy.17
  11.1 0.2 copy-done.4
  11.3 0.9 copy.18
  12.2 0.9 copy.20
  13.1 0.2 copy-done.5
  13.4 0.9 copy.21
  14.3 3.5 %collective-permute-start.3 = (bf16[272,256]{1,0:T(8,128)(2,1)S(1)}, bf16[272,256]{1,0:T(8,128)(2,1)S(1)}, u32[]{:S(2)}, u32[]{:S(2)}) collective-permute-start(bf16[272,256]{1,0:T(8,128)(2,1)S(1)} %pad_maximum_fusion.9), channel_id=1, source_target_pairs={{0,4},{4,8},{8,12},{1,5},{5,9},{9,13},{2,6},{6,10},{10,14},{3,7},{... | collective-permute-start | bytes 417800 | tf_op jit(solution)/shard_map/ppermute | solution.py:20
  17.8 2.9 %collective-permute-start.2 = (bf16[272,256]{1,0:T(8,128)(2,1)S(1)}, bf16[272,256]{1,0:T(8,128)(2,1)S(1)}, u32[]{:S(2)}, u32[]{:S(2)}) collective-permute-start(bf16[272,256]{1,0:T(8,128)(2,1)S(1)} %pad_maximum_fusion.9), channel_id=1, source_target_pairs={{0,8},{4,12},{1,9},{5,13},{2,10},{6,14},{3,11},{7,15},{16,24},{20,... | collective-permute-start | bytes 417800 | tf_op jit(solution)/shard_map/ppermute | solution.py:20
  20.7 1.3 %collective-permute-start.1 = (bf16[272,256]{1,0:T(8,128)(2,1)S(1)}, bf16[272,256]{1,0:T(8,128)(2,1)S(1)}, u32[]{:S(2)}, u32[]{:S(2)}) collective-permute-start(bf16[272,256]{1,0:T(8,128)(2,1)S(1)} %pad_maximum_fusion.9), channel_id=1, source_target_pairs={{0,12},{1,13},{2,14},{3,15},{16,28},{17,29},{18,30},{19,31}} | collective-permute-start | bytes 417800 | tf_op jit(solution)/shard_map/ppermute | solution.py:20
  22.1 0.7 copy-done.17
  22.8 1.0 fusion.7.bias_ref
  23.7 0.8 pad_maximum_fusion.6
  24.5 8.8 %shard_map.154 = (bf16[256,512]{1,0:T(8,128)(2,1)}, f32[384,128]{1,0:T(8,128)}, f32[384,128]{1,0:T(8,128)}) custom-call(f32[4,4]{1,0:T(4,128)} %sink_ref.4, bf16[256,1024]{1,0:T(8,128)(2,1)} %bitcast.18, bf16[256,1024]{1,0:T(8,128)(2,1)} %bitcast.20, bf16[384,256]{1,0:T(8,128)(2,1)} %get-tuple-element.87.k_ref, bf16[384,256]{1,0:T(8,128)(2,1)} %get-tuple-element.88.v_ref, ...), custom_call_target="tpu_custom_call" | custom-call | flops 503316480 | bytes 2555904 | tf_op jit(solution)/shard_map/pallas_call | solution.py:79
  33.5 1.4 %fusion.2.bias_ref = f32[256,1024]{1,0:T(8,128)} fusion(s32[1024]{0:T(1024)S(1)} %pad_add_fusion, s32[1024]{0:T(1024)S(1)} %iota_add_fusion, s32[256]{0:T(256)S(1)} %iota_add_fusion.2, s32[256]{0:T(256)S(1)} %copy-done.17, pred[1024]{0:T(1024)(128)(4,1)S(1)} %broadcast_compare_fusion), kind=kLoop, calls=%fused_computation.4 | loop fusion | flops 1572864 | bytes 1059840 | tf_op jit(solution)/shard_map/jit(_where)/select_n | solution.py:117
  34.9 0.4 collective-permute-done.5
  35.3 0.8 pad_maximum_fusion.3.v_ref
  36.1 0.9 pad_maximum_fusion.2.k_ref
  37.0 26.9 %shard_map.156 = (bf16[256,1024]{1,0:T(8,128)(2,1)}, f32[1024,256]{1,0:T(8,128)}, f32[1024,256]{1,0:T(8,128)}) custom-call(f32[4,4]{1,0:T(4,128)} %sink_ref.5, bf16[256,1024]{1,0:T(8,128)(2,1)} %bitcast.22, bf16[256,1024]{1,0:T(8,128)(2,1)} %bitcast.23, bf16[1024,256]{1,0:T(8,128)(2,1)} %pad_maximum_fusion.2.k_ref, ...), custom_call_target="tpu_custom_call" | custom-call | flops 2684354560 | bytes 7340032 | tf_op jit(solution)/shard_map/pallas_call | solution.py:79
  63.9 1.4 %broadcast_select_fusion = f32[1024,256]{1,0:T(8,128)S(1)} fusion(f32[1024,256]{1,0:T(8,128)} %get-tuple-element.62, f32[1024,256]{1,0:T(8,128)} %get-tuple-element.61, pred[]{:T(512)S(6)} %eq.14), kind=kLoop, calls=%fused_computation.15 | loop fusion | flops 262144 | bytes 3145729 | tf_op jit(solution)/shard_map/jit(_where)/select_n | solution.py:201
  65.2 0.2 collective-permute-start.6
  65.5 8.9 %shard_map.155 = (bf16[256,512]{1,0:T(8,128)(2,1)}, f32[384,128]{1,0:T(8,128)}, f32[384,128]{1,0:T(8,128)}) custom-call(f32[4,4]{1,0:T(4,128)} %sink_ref.4, bf16[256,1024]{1,0:T(8,128)(2,1)} %bitcast.19, bf16[256,1024]{1,0:T(8,128)(2,1)} %bitcast.21, bf16[384,256]{1,0:T(8,128)(2,1)} %get-tuple-element.87.k_ref, bf16[384,256]{1,0:T(8,128)(2,1)} %get-tuple-element.88.v_ref, ...), custom_call_target="tpu_custom_call" | custom-call | flops 503316480 | bytes 2555904 | tf_op jit(solution)/shard_map/pallas_call | solution.py:79
  74.4 0.9 copy-done.16
  75.4 0.8 copy-done.13
  76.2 0.1 copy-done.15
  76.4 1.3 %collective-permute-start.4 = (bf16[128,512]{1,0:T(8,128)(2,1)S(1)}, bf16[128,512]{1,0:T(8,128)(2,1)S(1)}, u32[]{:S(2)}, u32[]{:S(2)}) collective-permute-start(bf16[128,512]{1,0:T(8,128)(2,1)S(1)} %pad_maximum_fusion.10), channel_id=1, source_target_pairs={{4,0},{8,4},{12,8},{5,1},{9,5},{13,9},{6,2},{10,6},{14,10},{7,3},{... | collective-permute-start | bytes 393224 | tf_op jit(solution)/shard_map/ppermute | solution.py:20
  77.7 0.2 fusion.13
  78.0 1.3 %collective-permute-start.7 = (bf16[256,256]{1,0:T(8,128)(2,1)S(1)}, bf16[256,256]{1,0:T(8,128)(2,1)S(1)}, u32[]{:S(2)}, u32[]{:S(2)}) collective-permute-start(bf16[256,256]{1,0:T(8,128)(2,1)S(1)} %get-tuple-element.76), channel_id=1, source_target_pairs={{12,0},{13,1},{14,2},{15,3},{28,16},{29,17},{30,18},{31,19}} | collective-permute-start | bytes 393224 | tf_op jit(solution)/shard_map/ppermute | solution.py:20
  79.3 1.3 %collective-permute-start.9 = (bf16[256,256]{1,0:T(8,128)(2,1)S(1)}, bf16[256,256]{1,0:T(8,128)(2,1)S(1)}, u32[]{:S(2)}, u32[]{:S(2)}) collective-permute-start(bf16[256,256]{1,0:T(8,128)(2,1)S(1)} %get-tuple-element.77), channel_id=1, source_target_pairs={{4,0},{8,4},{12,8},{5,1},{9,5},{13,9},{6,2},{10,6},{14,10},{7,3},{... | collective-permute-start | bytes 393224 | tf_op jit(solution)/shard_map/ppermute | solution.py:20
  80.6 1.3 %collective-permute-start.8 = (bf16[256,256]{1,0:T(8,128)(2,1)S(1)}, bf16[256,256]{1,0:T(8,128)(2,1)S(1)}, u32[]{:S(2)}, u32[]{:S(2)}) collective-permute-start(bf16[256,256]{1,0:T(8,128)(2,1)S(1)} %get-tuple-element.78), channel_id=1, source_target_pairs={{8,0},{12,4},{9,1},{13,5},{10,2},{14,6},{11,3},{15,7},{24,16},{28,... | collective-permute-start | bytes 393224 | tf_op jit(solution)/shard_map/ppermute | solution.py:20
  81.9 2.1 %collective-permute-done.4 = bf16[128,512]{1,0:T(8,128)(2,1)S(1)} collective-permute-done((bf16[128,512]{1,0:T(8,128)(2,1)S(1)}, bf16[128,512]{1,0:T(8,128)(2,1)S(1)}, u32[]{:S(2)}, u32[]{:S(2)}) %collective-permute-start.4) | collective-permute-done | bytes 131104 | tf_op jit(solution)/shard_map/ppermute | solution.py:20
  84.0 4.0 %collective-permute-done.7 = bf16[256,256]{1,0:T(8,128)(2,1)S(1)} collective-permute-done((bf16[256,256]{1,0:T(8,128)(2,1)S(1)}, bf16[256,256]{1,0:T(8,128)(2,1)S(1)}, u32[]{:S(2)}, u32[]{:S(2)}) %collective-permute-start.7) | collective-permute-done | bytes 131104 | tf_op jit(solution)/shard_map/ppermute | solution.py:20
  88.0 1.6 %collective-permute-done.9 = bf16[256,256]{1,0:T(8,128)(2,1)S(1)} collective-permute-done((bf16[256,256]{1,0:T(8,128)(2,1)S(1)}, bf16[256,256]{1,0:T(8,128)(2,1)S(1)}, u32[]{:S(2)}, u32[]{:S(2)}) %collective-permute-start.9) | collective-permute-done | bytes 131104 | tf_op jit(solution)/shard_map/ppermute | solution.py:20
  89.6 6.1 %collective-permute-done.8 = bf16[256,256]{1,0:T(8,128)(2,1)S(1)} collective-permute-done((bf16[256,256]{1,0:T(8,128)(2,1)S(1)}, bf16[256,256]{1,0:T(8,128)(2,1)S(1)}, u32[]{:S(2)}, u32[]{:S(2)}) %collective-permute-start.8) | collective-permute-done | bytes 131104 | tf_op jit(solution)/shard_map/ppermute | solution.py:20
  95.9 0.1 collective-permute-start.10
  96.0 0.8 copy-done.11
  96.7 0.1 copy-done.12
  96.9 1.2 %reshape.119 = bf16[256,4,256]{2,1,0:T(4,128)(2,1)} reshape(bf16[256,1024]{1,0:T(8,128)(2,1)S(1)} %pad_maximum_fusion.1) | data formatting | bytes 1048576 | tf_op jit(solution)/shard_map/reshape | solution.py:229
  98.1 1.2 %reshape.121 = bf16[256,4,256]{2,1,0:T(4,128)(2,1)} reshape(bf16[256,1024]{1,0:T(8,128)(2,1)S(1)} %copy-done.6) | data formatting | bytes 1048576 | tf_op jit(solution)/shard_map/reshape | solution.py:232
  99.3 0.7 fusion.15
  100.0 0.7 select_convert_fusion
  (71 shorter events, 0.9 us)
Async XLA Ops:
  0.6 7.5 %copy-start.2 = (bf16[256,4,256]{2,1,0:T(4,128)(2,1)S(1)}, bf16[256,4,256]{2,1,0:T(4,128)(2,1)}, u32[]{:S(2)}) copy-start(bf16[256,4,256]{2,1,0:T(4,128)(2,1)} %param.16) | copy-start | bytes 1572868
  3.1 11.1 %collective-permute-start = (bf16[144,512]{1,0:T(8,128)(2,1)S(1)}, bf16[144,512]{1,0:T(8,128)(2,1)S(1)}, u32[]{:S(2)}, u32[]{:S(2)}) collective-permute-start(bf16[144,512]{1,0:T(8,128)(2,1)S(1)} %pad_maximum_fusion.8), channel_id=1, source_target_pairs={{0,4},{4,8},{8,12},{1,5},{5,9},{9,13},{2,6},{6,10},{10,14},{3,7},{... | collective-permute-start | bytes 442376 | tf_op jit(solution)/shard_map/ppermute | solution.py:20
  8.1 1.0 %copy-start.3 = (bf16[256,4,256]{2,1,0:T(4,128)(2,1)S(1)}, bf16[256,4,256]{2,1,0:T(4,128)(2,1)}, u32[]{:S(2)}) copy-start(bf16[256,4,256]{2,1,0:T(4,128)(2,1)} %param.21) | copy-start | bytes 1572868
  9.2 0.9 copy-start.7
  9.2 1.0 copy-start.8
  10.2 1.1 %copy-start.4 = (bf16[256,4,256]{2,1,0:T(4,128)(2,1)S(1)}, bf16[256,4,256]{2,1,0:T(4,128)(2,1)}, u32[]{:S(2)}) copy-start(bf16[256,4,256]{2,1,0:T(4,128)(2,1)} %param.19) | copy-start | bytes 1572868
  12.2 1.1 %copy-start.5 = (bf16[256,4,256]{2,1,0:T(4,128)(2,1)S(1)}, bf16[256,4,256]{2,1,0:T(4,128)(2,1)}, u32[]{:S(2)}) copy-start(bf16[256,4,256]{2,1,0:T(4,128)(2,1)} %param.24) | copy-start | bytes 1572868
  14.3 19.0 %collective-permute-start.3 = (bf16[272,256]{1,0:T(8,128)(2,1)S(1)}, bf16[272,256]{1,0:T(8,128)(2,1)S(1)}, u32[]{:S(2)}, u32[]{:S(2)}) collective-permute-start(bf16[272,256]{1,0:T(8,128)(2,1)S(1)} %pad_maximum_fusion.9), channel_id=1, source_target_pairs={{0,4},{4,8},{8,12},{1,5},{5,9},{9,13},{2,6},{6,10},{10,14},{3,7},{... | collective-permute-start | bytes 417800 | tf_op jit(solution)/shard_map/ppermute | solution.py:20
  17.8 15.5 %collective-permute-start.2 = (bf16[272,256]{1,0:T(8,128)(2,1)S(1)}, bf16[272,256]{1,0:T(8,128)(2,1)S(1)}, u32[]{:S(2)}, u32[]{:S(2)}) collective-permute-start(bf16[272,256]{1,0:T(8,128)(2,1)S(1)} %pad_maximum_fusion.9), channel_id=1, source_target_pairs={{0,8},{4,12},{1,9},{5,13},{2,10},{6,14},{3,11},{7,15},{16,24},{20,... | collective-permute-start | bytes 417800 | tf_op jit(solution)/shard_map/ppermute | solution.py:20
  20.7 12.6 %collective-permute-start.1 = (bf16[272,256]{1,0:T(8,128)(2,1)S(1)}, bf16[272,256]{1,0:T(8,128)(2,1)S(1)}, u32[]{:S(2)}, u32[]{:S(2)}) collective-permute-start(bf16[272,256]{1,0:T(8,128)(2,1)S(1)} %pad_maximum_fusion.9), channel_id=1, source_target_pairs={{0,12},{1,13},{2,14},{3,15},{16,28},{17,29},{18,30},{19,31}} | collective-permute-start | bytes 417800 | tf_op jit(solution)/shard_map/ppermute | solution.py:20
  22.1 0.7 copy-start.17
  22.8 1.0 copy-start.9
  22.8 1.0 copy-start.10
  33.4 1.8 %collective-permute-start.5 = (bf16[816,256]{1,0:T(8,128)(2,1)S(1)}, bf16[816,256]{1,0:T(8,128)(2,1)S(1)}, u32[]{:S(2)}, u32[]{:S(2)}) collective-permute-start(bf16[816,256]{1,0:T(8,128)(2,1)S(1)} %pad_maximum_fusion.4), channel_id=1, source_target_pairs={{0,1},{1,0},{2,3},{3,2},{4,5},{5,4},{6,7},{7,6},{8,9},{9,8},{10,11... | collective-permute-start | bytes 1253384 | tf_op jit(solution)/shard_map/ppermute | solution.py:183
  65.2 9.1 %copy-start.14 = (f32[384,128]{1,0:T(8,128)S(1)}, f32[384,128]{1,0:T(8,128)}, u32[]{:S(2)}) copy-start(f32[384,128]{1,0:T(8,128)} %get-tuple-element.54) | copy-start | bytes 589828
  65.2 12.4 %collective-permute-start.6 = (f32[1024,256]{1,0:T(8,128)S(1)}, f32[1024,256]{1,0:T(8,128)S(1)}, u32[]{:S(2)}, u32[]{:S(2)}) collective-permute-start(f32[1024,256]{1,0:T(8,128)S(1)} %broadcast_select_fusion), channel_id=1, source_target_pairs={{0,1},{1,0},{2,3},{3,2},{4,5},{5,4},{6,7},{7,6},{8,9},{9,8},{10,11... | collective-permute-start | bytes 3145736 | tf_op jit(solution)/shard_map/ppermute | solution.py:203
  74.3 0.9 copy-start.16
  75.3 0.9 copy-start.13
  75.3 1.0 copy-start.15
  75.3 2.4 %copy-start = (f32[1024,256]{1,0:T(8,128)S(1)}, f32[1024,256]{1,0:T(8,128)}, u32[]{:S(2)}) copy-start(f32[1024,256]{1,0:T(8,128)} %get-tuple-element.61) | copy-start | bytes 3145732
  75.3 2.4 %copy-start.1 = (f32[1024,256]{1,0:T(8,128)S(1)}, f32[1024,256]{1,0:T(8,128)}, u32[]{:S(2)}) copy-start(f32[1024,256]{1,0:T(8,128)} %get-tuple-element.62) | copy-start | bytes 3145732
  76.4 7.6 %collective-permute-start.4 = (bf16[128,512]{1,0:T(8,128)(2,1)S(1)}, bf16[128,512]{1,0:T(8,128)(2,1)S(1)}, u32[]{:S(2)}, u32[]{:S(2)}) collective-permute-start(bf16[128,512]{1,0:T(8,128)(2,1)S(1)} %pad_maximum_fusion.10), channel_id=1, source_target_pairs={{4,0},{8,4},{12,8},{5,1},{9,5},{13,9},{6,2},{10,6},{14,10},{7,3},{... | collective-permute-start | bytes 393224 | tf_op jit(solution)/shard_map/ppermute | solution.py:20
  78.0 10.0 %collective-permute-start.7 = (bf16[256,256]{1,0:T(8,128)(2,1)S(1)}, bf16[256,256]{1,0:T(8,128)(2,1)S(1)}, u32[]{:S(2)}, u32[]{:S(2)}) collective-permute-start(bf16[256,256]{1,0:T(8,128)(2,1)S(1)} %get-tuple-element.76), channel_id=1, source_target_pairs={{12,0},{13,1},{14,2},{15,3},{28,16},{29,17},{30,18},{31,19}} | collective-permute-start | bytes 393224 | tf_op jit(solution)/shard_map/ppermute | solution.py:20
  79.3 10.4 %collective-permute-start.9 = (bf16[256,256]{1,0:T(8,128)(2,1)S(1)}, bf16[256,256]{1,0:T(8,128)(2,1)S(1)}, u32[]{:S(2)}, u32[]{:S(2)}) collective-permute-start(bf16[256,256]{1,0:T(8,128)(2,1)S(1)} %get-tuple-element.77), channel_id=1, source_target_pairs={{4,0},{8,4},{12,8},{5,1},{9,5},{13,9},{6,2},{10,6},{14,10},{7,3},{... | collective-permute-start | bytes 393224 | tf_op jit(solution)/shard_map/ppermute | solution.py:20
  80.6 15.2 %collective-permute-start.8 = (bf16[256,256]{1,0:T(8,128)(2,1)S(1)}, bf16[256,256]{1,0:T(8,128)(2,1)S(1)}, u32[]{:S(2)}, u32[]{:S(2)}) collective-permute-start(bf16[256,256]{1,0:T(8,128)(2,1)S(1)} %get-tuple-element.78), channel_id=1, source_target_pairs={{8,0},{12,4},{9,1},{13,5},{10,2},{14,6},{11,3},{15,7},{24,16},{28,... | collective-permute-start | bytes 393224 | tf_op jit(solution)/shard_map/ppermute | solution.py:20
  95.8 1.0 copy-start.11
  95.8 1.0 %copy-start.12 = (bf16[256,512]{1,0:T(8,128)(2,1)S(1)}, bf16[256,512]{1,0:T(8,128)(2,1)}, u32[]{:S(2)}) copy-start(bf16[256,512]{1,0:T(8,128)(2,1)} %get-tuple-element.53) | copy-start | bytes 786436
  95.9 3.4 %collective-permute-start.10 = (f32[256,768]{1,0:T(8,128)S(1)}, f32[256,768]{1,0:T(8,128)S(1)}, u32[]{:S(2)}, u32[]{:S(2)}) collective-permute-start(f32[256,768]{1,0:T(8,128)S(1)} %pad_maximum_fusion), channel_id=1, source_target_pairs={{0,1},{1,0},{2,3},{3,2},{4,5},{5,4},{6,7},{7,6},{8,9},{9,8},{10,11... | collective-permute-start | bytes 2359304 | tf_op jit(solution)/shard_map/ppermute | solution.py:223
  96.9 1.2 %copy-start.6 = (bf16[256,1024]{1,0:T(8,128)(2,1)S(1)}, bf16[256,1024]{1,0:T(8,128)(2,1)}, u32[]{:S(2)}) copy-start(bf16[256,1024]{1,0:T(8,128)(2,1)} %get-tuple-element.63) | copy-start | bytes 1572868

commit v7 on v5

--- a/solution.py
+++ b/solution.py
@@ -24,7 +24,7 @@
     return jnp.where(half == 0, block[:, :HD], block[:, HD:])
 
 
-def attn_bwd_kernel(g0, gn, sink_ref, q_ref, do_ref, k_ref, v_ref, bias_ref, dq_ref, dk_ref, dv_ref):
+def attn_bwd_kernel(g0, gn, band, sink_ref, q_ref, do_ref, k_ref, v_ref, bias_ref, dq_ref, dk_ref, dv_ref):
     g_rel = pl.program_id(0)
     g = g_rel + g0
     i = pl.program_id(1)
@@ -63,33 +63,52 @@
         dv_acc = dv if dv_acc is None else dv_acc + dv
     dq_ref[...] = jnp.concatenate(dq_parts, axis=1)
 
+    key_rows = k.shape[0]
+    if band:
+        key_span = pl.ds(pl.multiple_of(i * band, band), key_rows)
+    else:
+        key_span = slice(None)
     for gg in range(gn):
         @pl.when(g_rel == gg)
         def _():
-            dk_ref[:, gg * HD:(gg + 1) * HD] += dk_acc
-            dv_ref[:, gg * HD:(gg + 1) * HD] += dv_acc
-
-
-def attn_bwd(sinks, queries, grads, keys, values, bias, g0, gn):
+            dk_ref[key_span, gg * HD:(gg + 1) * HD] += dk_acc
+            dv_ref[key_span, gg * HD:(gg + 1) * HD] += dv_acc
+
+
+def attn_bwd(sinks, queries, grads, keys, values, bias, g0, gn, band=None):
     n = queries.shape[0]
     m = keys.shape[0]
     heads = sinks.shape[1]
     rows = n
     while rows > 8 and rows * m > (1 << 18):
         rows //= 2
+    width = heads * HD
+    if band:
+        rows = band
+        span = 2 * band
+        key_spec = pl.BlockSpec(
+            (pl.Element(span), pl.Element(2 * HD)),
+            lambda g, i: (i * band, ((g + g0) // 2) * 2 * HD),
+        )
+        bias_spec = pl.BlockSpec(
+            (pl.Element(band), pl.Element(span)), lambda g, i: (i * band, i * band)
+        )
+    else:
+        span = m
+        key_spec = pl.BlockSpec((m, 2 * HD), lambda g, i: (0, (g + g0) // 2))
+        bias_spec = pl.BlockSpec((rows, m), lambda g, i: (i, 0))
     grid = (gn, n // rows)
-    width = heads * HD
 
     return pl.pallas_call(
-        functools.partial(attn_bwd_kernel, g0, gn),
+        functools.partial(attn_bwd_kernel, g0, gn, band),
         grid=grid,
         in_specs=[
             pl.BlockSpec(memory_space=pltpu.SMEM),
             pl.BlockSpec((rows, width), lambda g, i: (i, g + g0)),
             pl.BlockSpec((rows, width), lambda g, i: (i, g + g0)),
-            pl.BlockSpec((m, 2 * HD), lambda g, i: (0, (g + g0) // 2)),
-            pl.BlockSpec((m, 2 * HD), lambda g, i: (0, (g + g0) // 2)),
-            pl.BlockSpec((rows, m), lambda g, i: (i, 0)),
+            key_spec,
+            key_spec,
+            bias_spec,
         ],
         out_specs=[
             pl.BlockSpec((rows, width), lambda g, i: (i, g)),
@@ -106,9 +125,9 @@
             vmem_limit_bytes=60 * 1024 * 1024,
         ),
         cost_estimate=pl.CostEstimate(
-            flops=10 * gn * heads * n * m * HD,
-            transcendentals=gn * heads * n * m,
-            bytes_accessed=4 * n * m + 4 * n * gn * heads * HD * 3 + 12 * m * gn * HD,
+            flops=10 * gn * heads * n * span * HD,
+            transcendentals=gn * heads * n * span,
+            bytes_accessed=4 * n * span + 4 * n * gn * heads * HD * 3 + 12 * m * gn * HD,
         ),
     )(sinks, queries, grads, keys, values, bias)
 
@@ -180,7 +199,8 @@
     w_q = (window_query.reshape(n, -1) * 0.125).astype(jnp.bfloat16)
     w_do = window_grad_out.reshape(n, -1)
     g_split = groups // 2 if groups > 1 else groups
-    w_out1 = attn_bwd(window_sinks, w_q, w_do, w_keys, w_values, w_bias, 0, g_split)
+    w_band = WINDOW if n % WINDOW == 0 else None
+    w_out1 = attn_bwd(window_sinks, w_q, w_do, w_keys, w_values, w_bias, 0, g_split, w_band)
 
     w_out1, arrived = lax.optimization_barrier((w_out1, arrived))
     mine = jnp.concatenate(arrived, axis=0)
@@ -211,7 +231,9 @@
         f_final = f_final + passed_along(piece, "seq", -d).astype(jnp.float32)
 
     if g_split < groups:
-        w_out2 = attn_bwd(window_sinks, w_q, w_do, w_keys, w_values, w_bias, g_split, groups - g_split)
+        w_out2 = attn_bwd(
+            window_sinks, w_q, w_do, w_keys, w_values, w_bias, g_split, groups - g_split, w_band
+        )
         w_dq = jnp.concatenate([w_out1[0], w_out2[0]], axis=1)
         w_dk = jnp.concatenate([w_out1[1], w_out2[1]], axis=1)
         w_dv = jnp.concatenate([w_out1[2], w_out2[2]], axis=1)

time: 95.9 us -> 101 us (1.053)
  Pallas kernels: 38.8 us -> 43.7 us
    pallas_call x3, Pallas kernels: 38.8 us -> 43.7 us  [attn_bwd(): pl.pallas_call(functools.partial(attn_bwd_kernel, g0, gn, band), grid=gri...]
  transfers between devices with their start and end apart: 11 -> 11, of which waited for: 5 -> 5; matrix products, arithmetic and copies ran while one was open for 11% -> 10% of each run, Pallas kernels for 16% -> 20%
where the time goes in v7:
time: 101 us; the launch traced here: 100 us
  Pallas kernels  43.7 us (43%)
  starting transfers between devices  18.2 us (18%)
  waiting for transfers between devices  14.3 us (14%)
  local copies, waits for them, and re-layouts  13.9 us (14%)
  other arithmetic  8.79 us (9%)
  between operations  1.15 us (1%)
    pallas_call x3, Pallas kernels, attn_bwd(): pl.pallas_call(functools.partial(attn_bwd_kernel, g0, gn, band), grid=gri...  43.7 us
    ppermute x8, starting transfers between devices, passed_along(): lax.ppermute(value, axis, [(source, source + steps) for source in range(f...  17.8 us
    ppermute x8, waiting for transfers between devices, passed_along(): lax.ppermute(value, axis, [(source, source + steps) for source in range(f...  13.9 us
    unnamed x44, local copies, waits for them, and re-layouts  8.98 us
    select_n x2, other arithmetic, make_bias(): return jnp.where(visible, 0.0, NEG).astype(jnp.float32)  2.33 us
  transfers between devices with their start and end apart: 11, of which 5 were waited for; matrix products, arithmetic and copies ran while one was open for 10% of the time, Pallas kernels for 20%

profile of v7, /device:TPU:0, one launch (start us, length us, event | category | flops | bytes accessed | tf_op | source)
XLA Modules:
  0.0 100.0 jit_solution(12383053872882113718)
XLA Ops:
  0.6 0.7 convert.16
  1.4 0.8 slice.139
  2.3 0.8 slice.140
  3.1 4.9 %collective-permute-start = (bf16[144,512]{1,0:T(8,128)(2,1)S(1)}, bf16[144,512]{1,0:T(8,128)(2,1)S(1)}, u32[]{:S(2)}, u32[]{:S(2)}) collective-permute-start(bf16[144,512]{1,0:T(8,128)(2,1)S(1)} %pad_maximum_fusion.8), channel_id=1, source_target_pairs={{0,4},{4,8},{8,12},{1,5},{5,9},{9,13},{2,6},{6,10},{10,14},{3,7},{... | collective-permute-start | bytes 442376 | tf_op jit(solution)/shard_map/ppermute | solution.py:20
  8.2 0.2 broadcast_multiply_fusion.1
  8.4 0.8 copy-done.3
  9.2 0.2 broadcast_multiply_fusion
  9.4 0.7 copy-done.7
  10.2 0.9 copy.17
  11.1 0.2 copy-done.4
  11.3 0.9 copy.18
  12.2 0.9 copy.20
  13.1 0.2 copy-done.5
  13.4 0.9 copy.21
  14.3 3.5 %collective-permute-start.3 = (bf16[272,256]{1,0:T(8,128)(2,1)S(1)}, bf16[272,256]{1,0:T(8,128)(2,1)S(1)}, u32[]{:S(2)}, u32[]{:S(2)}) collective-permute-start(bf16[272,256]{1,0:T(8,128)(2,1)S(1)} %pad_maximum_fusion.9), channel_id=1, source_target_pairs={{0,4},{4,8},{8,12},{1,5},{5,9},{9,13},{2,6},{6,10},{10,14},{3,7},{... | collective-permute-start | bytes 417800 | tf_op jit(solution)/shard_map/ppermute | solution.py:20
  17.8 2.9 %collective-permute-start.2 = (bf16[272,256]{1,0:T(8,128)(2,1)S(1)}, bf16[272,256]{1,0:T(8,128)(2,1)S(1)}, u32[]{:S(2)}, u32[]{:S(2)}) collective-permute-start(bf16[272,256]{1,0:T(8,128)(2,1)S(1)} %pad_maximum_fusion.9), channel_id=1, source_target_pairs={{0,8},{4,12},{1,9},{5,13},{2,10},{6,14},{3,11},{7,15},{16,24},{20,... | collective-permute-start | bytes 417800 | tf_op jit(solution)/shard_map/ppermute | solution.py:20
  20.7 1.3 %collective-permute-start.1 = (bf16[272,256]{1,0:T(8,128)(2,1)S(1)}, bf16[272,256]{1,0:T(8,128)(2,1)S(1)}, u32[]{:S(2)}, u32[]{:S(2)}) collective-permute-start(bf16[272,256]{1,0:T(8,128)(2,1)S(1)} %pad_maximum_fusion.9), channel_id=1, source_target_pairs={{0,12},{1,13},{2,14},{3,15},{16,28},{17,29},{18,30},{19,31}} | collective-permute-start | bytes 417800 | tf_op jit(solution)/shard_map/ppermute | solution.py:20
  22.1 0.7 copy-done.17
  22.8 1.0 fusion.7.bias_ref
  23.7 0.8 pad_maximum_fusion.6
  24.5 10.2 %shard_map.154 = (bf16[256,512]{1,0:T(8,128)(2,1)}, f32[384,128]{1,0:T(8,128)}, f32[384,128]{1,0:T(8,128)}) custom-call(f32[4,4]{1,0:T(4,128)} %sink_ref.4, bf16[256,1024]{1,0:T(8,128)(2,1)} %bitcast.14, bf16[256,1024]{1,0:T(8,128)(2,1)} %bitcast.16, bf16[384,256]{1,0:T(8,128)(2,1)} %get-tuple-element.87.k_ref, bf16[384,256]{1,0:T(8,128)(2,1)} %get-tuple-element.88.v_ref, ...), custom_call_target="tpu_custom_call" | custom-call | flops 335544320 | bytes 2424832 | tf_op jit(solution)/shard_map/pallas_call | solution.py:102
  34.9 1.4 %fusion.2.bias_ref = f32[256,1024]{1,0:T(8,128)} fusion(s32[1024]{0:T(1024)S(1)} %pad_add_fusion, s32[1024]{0:T(1024)S(1)} %iota_add_fusion, s32[256]{0:T(256)S(1)} %iota_add_fusion.2, s32[256]{0:T(256)S(1)} %copy-done.17, pred[1024]{0:T(1024)(128)(4,1)S(1)} %broadcast_compare_fusion), kind=kLoop, calls=%fused_computation.4 | loop fusion | flops 1572864 | bytes 1059840 | tf_op jit(solution)/shard_map/jit(_where)/select_n | solution.py:140
  36.3 0.4 collective-permute-done.5
  36.7 0.8 pad_maximum_fusion.3.v_ref
  37.5 0.9 pad_maximum_fusion.2.k_ref
  38.4 23.3 %shard_map.156 = (bf16[256,1024]{1,0:T(8,128)(2,1)}, f32[1024,256]{1,0:T(8,128)}, f32[1024,256]{1,0:T(8,128)}) custom-call(f32[4,4]{1,0:T(4,128)} %sink_ref.5, bf16[256,1024]{1,0:T(8,128)(2,1)} %bitcast.22, bf16[256,1024]{1,0:T(8,128)(2,1)} %bitcast.23, bf16[1024,256]{1,0:T(8,128)(2,1)} %pad_maximum_fusion.2.k_ref, ...), custom_call_target="tpu_custom_call" | custom-call | flops 2684354560 | bytes 7340032 | tf_op jit(solution)/shard_map/pallas_call | solution.py:102
  61.6 1.4 %broadcast_select_fusion = f32[1024,256]{1,0:T(8,128)S(1)} fusion(f32[1024,256]{1,0:T(8,128)} %get-tuple-element.62, f32[1024,256]{1,0:T(8,128)} %get-tuple-element.61, pred[]{:T(512)S(6)} %eq.14), kind=kLoop, calls=%fused_computation.15 | loop fusion | flops 262144 | bytes 3145729 | tf_op jit(solution)/shard_map/jit(_where)/select_n | solution.py:225
  63.0 0.2 collective-permute-start.6
  63.2 10.2 %shard_map.155 = (bf16[256,512]{1,0:T(8,128)(2,1)}, f32[384,128]{1,0:T(8,128)}, f32[384,128]{1,0:T(8,128)}) custom-call(f32[4,4]{1,0:T(4,128)} %sink_ref.4, bf16[256,1024]{1,0:T(8,128)(2,1)} %bitcast.15, bf16[256,1024]{1,0:T(8,128)(2,1)} %bitcast.17, bf16[384,256]{1,0:T(8,128)(2,1)} %get-tuple-element.87.k_ref, bf16[384,256]{1,0:T(8,128)(2,1)} %get-tuple-element.88.v_ref, ...), custom_call_target="tpu_custom_call" | custom-call | flops 335544320 | bytes 2424832 | tf_op jit(solution)/shard_map/pallas_call | solution.py:102
  73.5 0.9 copy-done.16
  74.5 0.8 copy-done.13
  75.3 0.1 copy-done.15
  75.5 1.3 %collective-permute-start.4 = (bf16[128,512]{1,0:T(8,128)(2,1)S(1)}, bf16[128,512]{1,0:T(8,128)(2,1)S(1)}, u32[]{:S(2)}, u32[]{:S(2)}) collective-permute-start(bf16[128,512]{1,0:T(8,128)(2,1)S(1)} %pad_maximum_fusion.10), channel_id=1, source_target_pairs={{4,0},{8,4},{12,8},{5,1},{9,5},{13,9},{6,2},{10,6},{14,10},{7,3},{... | collective-permute-start | bytes 393224 | tf_op jit(solution)/shard_map/ppermute | solution.py:20
  76.8 0.2 fusion.13
  77.1 1.3 %collective-permute-start.7 = (bf16[256,256]{1,0:T(8,128)(2,1)S(1)}, bf16[256,256]{1,0:T(8,128)(2,1)S(1)}, u32[]{:S(2)}, u32[]{:S(2)}) collective-permute-start(bf16[256,256]{1,0:T(8,128)(2,1)S(1)} %get-tuple-element.76), channel_id=1, source_target_pairs={{12,0},{13,1},{14,2},{15,3},{28,16},{29,17},{30,18},{31,19}} | collective-permute-start | bytes 393224 | tf_op jit(solution)/shard_map/ppermute | solution.py:20
  78.4 1.3 %collective-permute-start.9 = (bf16[256,256]{1,0:T(8,128)(2,1)S(1)}, bf16[256,256]{1,0:T(8,128)(2,1)S(1)}, u32[]{:S(2)}, u32[]{:S(2)}) collective-permute-start(bf16[256,256]{1,0:T(8,128)(2,1)S(1)} %get-tuple-element.77), channel_id=1, source_target_pairs={{4,0},{8,4},{12,8},{5,1},{9,5},{13,9},{6,2},{10,6},{14,10},{7,3},{... | collective-permute-start | bytes 393224 | tf_op jit(solution)/shard_map/ppermute | solution.py:20
  79.7 1.3 %collective-permute-start.8 = (bf16[256,256]{1,0:T(8,128)(2,1)S(1)}, bf16[256,256]{1,0:T(8,128)(2,1)S(1)}, u32[]{:S(2)}, u32[]{:S(2)}) collective-permute-start(bf16[256,256]{1,0:T(8,128)(2,1)S(1)} %get-tuple-element.78), channel_id=1, source_target_pairs={{8,0},{12,4},{9,1},{13,5},{10,2},{14,6},{11,3},{15,7},{24,16},{28,... | collective-permute-start | bytes 393224 | tf_op jit(solution)/shard_map/ppermute | solution.py:20
  81.0 2.2 %collective-permute-done.4 = bf16[128,512]{1,0:T(8,128)(2,1)S(1)} collective-permute-done((bf16[128,512]{1,0:T(8,128)(2,1)S(1)}, bf16[128,512]{1,0:T(8,128)(2,1)S(1)}, u32[]{:S(2)}, u32[]{:S(2)}) %collective-permute-start.4) | collective-permute-done | bytes 131104 | tf_op jit(solution)/shard_map/ppermute | solution.py:20
  83.2 3.9 %collective-permute-done.7 = bf16[256,256]{1,0:T(8,128)(2,1)S(1)} collective-permute-done((bf16[256,256]{1,0:T(8,128)(2,1)S(1)}, bf16[256,256]{1,0:T(8,128)(2,1)S(1)}, u32[]{:S(2)}, u32[]{:S(2)}) %collective-permute-start.7) | collective-permute-done | bytes 131104 | tf_op jit(solution)/shard_map/ppermute | solution.py:20
  87.1 1.7 %collective-permute-done.9 = bf16[256,256]{1,0:T(8,128)(2,1)S(1)} collective-permute-done((bf16[256,256]{1,0:T(8,128)(2,1)S(1)}, bf16[256,256]{1,0:T(8,128)(2,1)S(1)}, u32[]{:S(2)}, u32[]{:S(2)}) %collective-permute-start.9) | collective-permute-done | bytes 131104 | tf_op jit(solution)/shard_map/ppermute | solution.py:20
  88.9 6.1 %collective-permute-done.8 = bf16[256,256]{1,0:T(8,128)(2,1)S(1)} collective-permute-done((bf16[256,256]{1,0:T(8,128)(2,1)S(1)}, bf16[256,256]{1,0:T(8,128)(2,1)S(1)}, u32[]{:S(2)}, u32[]{:S(2)}) %collective-permute-start.8) | collective-permute-done | bytes 131104 | tf_op jit(solution)/shard_map/ppermute | solution.py:20
  95.1 0.1 collective-permute-start.10
  95.2 0.8 copy-done.11
  96.0 0.1 copy-done.12
  96.1 1.2 %reshape.119 = bf16[256,4,256]{2,1,0:T(4,128)(2,1)} reshape(bf16[256,1024]{1,0:T(8,128)(2,1)S(1)} %pad_maximum_fusion.1) | data formatting | bytes 1048576 | tf_op jit(solution)/shard_map/reshape | solution.py:255
  97.3 1.2 %reshape.121 = bf16[256,4,256]{2,1,0:T(4,128)(2,1)} reshape(bf16[256,1024]{1,0:T(8,128)(2,1)S(1)} %copy-done.6) | data formatting | bytes 1048576 | tf_op jit(solution)/shard_map/reshape | solution.py:258
  98.6 0.7 fusion.15
  99.3 0.7 select_convert_fusion
  (71 shorter events, 0.9 us)
Async XLA Ops:
  0.6 7.5 %copy-start.2 = (bf16[256,4,256]{2,1,0:T(4,128)(2,1)S(1)}, bf16[256,4,256]{2,1,0:T(4,128)(2,1)}, u32[]{:S(2)}) copy-start(bf16[256,4,256]{2,1,0:T(4,128)(2,1)} %param.16) | copy-start | bytes 1572868
  3.1 11.1 %collective-permute-start = (bf16[144,512]{1,0:T(8,128)(2,1)S(1)}, bf16[144,512]{1,0:T(8,128)(2,1)S(1)}, u32[]{:S(2)}, u32[]{:S(2)}) collective-permute-start(bf16[144,512]{1,0:T(8,128)(2,1)S(1)} %pad_maximum_fusion.8), channel_id=1, source_target_pairs={{0,4},{4,8},{8,12},{1,5},{5,9},{9,13},{2,6},{6,10},{10,14},{3,7},{... | collective-permute-start | bytes 442376 | tf_op jit(solution)/shard_map/ppermute | solution.py:20
  8.1 1.0 %copy-start.3 = (bf16[256,4,256]{2,1,0:T(4,128)(2,1)S(1)}, bf16[256,4,256]{2,1,0:T(4,128)(2,1)}, u32[]{:S(2)}) copy-start(bf16[256,4,256]{2,1,0:T(4,128)(2,1)} %param.21) | copy-start | bytes 1572868
  9.2 0.9 copy-start.7
  9.2 1.0 copy-start.8
  10.2 1.1 %copy-start.4 = (bf16[256,4,256]{2,1,0:T(4,128)(2,1)S(1)}, bf16[256,4,256]{2,1,0:T(4,128)(2,1)}, u32[]{:S(2)}) copy-start(bf16[256,4,256]{2,1,0:T(4,128)(2,1)} %param.19) | copy-start | bytes 1572868
  12.2 1.1 %copy-start.5 = (bf16[256,4,256]{2,1,0:T(4,128)(2,1)S(1)}, bf16[256,4,256]{2,1,0:T(4,128)(2,1)}, u32[]{:S(2)}) copy-start(bf16[256,4,256]{2,1,0:T(4,128)(2,1)} %param.24) | copy-start | bytes 1572868
  14.3 20.4 %collective-permute-start.3 = (bf16[272,256]{1,0:T(8,128)(2,1)S(1)}, bf16[272,256]{1,0:T(8,128)(2,1)S(1)}, u32[]{:S(2)}, u32[]{:S(2)}) collective-permute-start(bf16[272,256]{1,0:T(8,128)(2,1)S(1)} %pad_maximum_fusion.9), channel_id=1, source_target_pairs={{0,4},{4,8},{8,12},{1,5},{5,9},{9,13},{2,6},{6,10},{10,14},{3,7},{... | collective-permute-start | bytes 417800 | tf_op jit(solution)/shard_map/ppermute | solution.py:20
  17.8 16.9 %collective-permute-start.2 = (bf16[272,256]{1,0:T(8,128)(2,1)S(1)}, bf16[272,256]{1,0:T(8,128)(2,1)S(1)}, u32[]{:S(2)}, u32[]{:S(2)}) collective-permute-start(bf16[272,256]{1,0:T(8,128)(2,1)S(1)} %pad_maximum_fusion.9), channel_id=1, source_target_pairs={{0,8},{4,12},{1,9},{5,13},{2,10},{6,14},{3,11},{7,15},{16,24},{20,... | collective-permute-start | bytes 417800 | tf_op jit(solution)/shard_map/ppermute | solution.py:20
  20.7 14.0 %collective-permute-start.1 = (bf16[272,256]{1,0:T(8,128)(2,1)S(1)}, bf16[272,256]{1,0:T(8,128)(2,1)S(1)}, u32[]{:S(2)}, u32[]{:S(2)}) collective-permute-start(bf16[272,256]{1,0:T(8,128)(2,1)S(1)} %pad_maximum_fusion.9), channel_id=1, source_target_pairs={{0,12},{1,13},{2,14},{3,15},{16,28},{17,29},{18,30},{19,31}} | collective-permute-start | bytes 417800 | tf_op jit(solution)/shard_map/ppermute | solution.py:20
  22.1 0.7 copy-start.17
  22.8 1.0 copy-start.9
  22.8 1.0 copy-start.10
  34.8 1.8 %collective-permute-start.5 = (bf16[816,256]{1,0:T(8,128)(2,1)S(1)}, bf16[816,256]{1,0:T(8,128)(2,1)S(1)}, u32[]{:S(2)}, u32[]{:S(2)}) collective-permute-start(bf16[816,256]{1,0:T(8,128)(2,1)S(1)} %pad_maximum_fusion.4), channel_id=1, source_target_pairs={{0,1},{1,0},{2,3},{3,2},{4,5},{5,4},{6,7},{7,6},{8,9},{9,8},{10,11... | collective-permute-start | bytes 1253384 | tf_op jit(solution)/shard_map/ppermute | solution.py:207
  63.0 10.5 %copy-start.14 = (f32[384,128]{1,0:T(8,128)S(1)}, f32[384,128]{1,0:T(8,128)}, u32[]{:S(2)}) copy-start(f32[384,128]{1,0:T(8,128)} %get-tuple-element.54) | copy-start | bytes 589828
  63.0 13.8 %collective-permute-start.6 = (f32[1024,256]{1,0:T(8,128)S(1)}, f32[1024,256]{1,0:T(8,128)S(1)}, u32[]{:S(2)}, u32[]{:S(2)}) collective-permute-start(f32[1024,256]{1,0:T(8,128)S(1)} %broadcast_select_fusion), channel_id=1, source_target_pairs={{0,1},{1,0},{2,3},{3,2},{4,5},{5,4},{6,7},{7,6},{8,9},{9,8},{10,11... | collective-permute-start | bytes 3145736 | tf_op jit(solution)/shard_map/ppermute | solution.py:227
  73.5 0.9 copy-start.16
  74.4 0.9 copy-start.13
  74.4 1.0 %copy-start.15 = (f32[384,128]{1,0:T(8,128)S(1)}, f32[384,128]{1,0:T(8,128)}, u32[]{:S(2)}) copy-start(f32[384,128]{1,0:T(8,128)} %get-tuple-element.57) | copy-start | bytes 589828
  74.4 2.4 %copy-start = (f32[1024,256]{1,0:T(8,128)S(1)}, f32[1024,256]{1,0:T(8,128)}, u32[]{:S(2)}) copy-start(f32[1024,256]{1,0:T(8,128)} %get-tuple-element.61) | copy-start | bytes 3145732
  74.5 2.4 %copy-start.1 = (f32[1024,256]{1,0:T(8,128)S(1)}, f32[1024,256]{1,0:T(8,128)}, u32[]{:S(2)}) copy-start(f32[1024,256]{1,0:T(8,128)} %get-tuple-element.62) | copy-start | bytes 3145732
  75.5 7.7 %collective-permute-start.4 = (bf16[128,512]{1,0:T(8,128)(2,1)S(1)}, bf16[128,512]{1,0:T(8,128)(2,1)S(1)}, u32[]{:S(2)}, u32[]{:S(2)}) collective-permute-start(bf16[128,512]{1,0:T(8,128)(2,1)S(1)} %pad_maximum_fusion.10), channel_id=1, source_target_pairs={{4,0},{8,4},{12,8},{5,1},{9,5},{13,9},{6,2},{10,6},{14,10},{7,3},{... | collective-permute-start | bytes 393224 | tf_op jit(solution)/shard_map/ppermute | solution.py:20
  77.1 10.0 %collective-permute-start.7 = (bf16[256,256]{1,0:T(8,128)(2,1)S(1)}, bf16[256,256]{1,0:T(8,128)(2,1)S(1)}, u32[]{:S(2)}, u32[]{:S(2)}) collective-permute-start(bf16[256,256]{1,0:T(8,128)(2,1)S(1)} %get-tuple-element.76), channel_id=1, source_target_pairs={{12,0},{13,1},{14,2},{15,3},{28,16},{29,17},{30,18},{31,19}} | collective-permute-start | bytes 393224 | tf_op jit(solution)/shard_map/ppermute | solution.py:20
  78.4 10.5 %collective-permute-start.9 = (bf16[256,256]{1,0:T(8,128)(2,1)S(1)}, bf16[256,256]{1,0:T(8,128)(2,1)S(1)}, u32[]{:S(2)}, u32[]{:S(2)}) collective-permute-start(bf16[256,256]{1,0:T(8,128)(2,1)S(1)} %get-tuple-element.77), channel_id=1, source_target_pairs={{4,0},{8,4},{12,8},{5,1},{9,5},{13,9},{6,2},{10,6},{14,10},{7,3},{... | collective-permute-start | bytes 393224 | tf_op jit(solution)/shard_map/ppermute | solution.py:20
  79.7 15.3 %collective-permute-start.8 = (bf16[256,256]{1,0:T(8,128)(2,1)S(1)}, bf16[256,256]{1,0:T(8,128)(2,1)S(1)}, u32[]{:S(2)}, u32[]{:S(2)}) collective-permute-start(bf16[256,256]{1,0:T(8,128)(2,1)S(1)} %get-tuple-element.78), channel_id=1, source_target_pairs={{8,0},{12,4},{9,1},{13,5},{10,2},{14,6},{11,3},{15,7},{24,16},{28,... | collective-permute-start | bytes 393224 | tf_op jit(solution)/shard_map/ppermute | solution.py:20
  95.0 1.0 copy-start.11
  95.0 1.0 %copy-start.12 = (bf16[256,512]{1,0:T(8,128)(2,1)S(1)}, bf16[256,512]{1,0:T(8,128)(2,1)}, u32[]{:S(2)}) copy-start(bf16[256,512]{1,0:T(8,128)(2,1)} %get-tuple-element.53) | copy-start | bytes 786436
  95.1 3.4 %collective-permute-start.10 = (f32[256,768]{1,0:T(8,128)S(1)}, f32[256,768]{1,0:T(8,128)S(1)}, u32[]{:S(2)}, u32[]{:S(2)}) collective-permute-start(f32[256,768]{1,0:T(8,128)S(1)} %pad_maximum_fusion), channel_id=1, source_target_pairs={{0,1},{1,0},{2,3},{3,2},{4,5},{5,4},{6,7},{7,6},{8,9},{9,8},{10,11... | collective-permute-start | bytes 2359304 | tf_op jit(solution)/shard_map/ppermute | solution.py:249
  96.1 1.2 %copy-start.6 = (bf16[256,1024]{1,0:T(8,128)(2,1)S(1)}, bf16[256,1024]{1,0:T(8,128)(2,1)}, u32[]{:S(2)}) copy-start(bf16[256,1024]{1,0:T(8,128)(2,1)} %get-tuple-element.63) | copy-start | bytes 1572868

commit v8 on v5

--- a/solution.py
+++ b/solution.py
@@ -24,7 +24,10 @@
     return jnp.where(half == 0, block[:, :HD], block[:, HD:])
 
 
-def attn_bwd_kernel(g0, gn, sink_ref, q_ref, do_ref, k_ref, v_ref, bias_ref, dq_ref, dk_ref, dv_ref):
+def attn_bwd_kernel(
+    g0, gn, window, sink_ref, q_ref, do_ref, k_ref, v_ref, qpos_ref, qseg_ref, kpos_ref, kseg_ref,
+    dq_ref, dk_ref, dv_ref,
+):
     g_rel = pl.program_id(0)
     g = g_rel + g0
     i = pl.program_id(1)
@@ -37,7 +40,12 @@
 
     k = pick_half(k_ref[...], g % 2)
     v = pick_half(v_ref[...], g % 2)
-    bias = bias_ref[...]
+    key_pos = kpos_ref[...]
+    distance = qpos_ref[...] - key_pos
+    visible = (distance >= 0) & (key_pos >= 0) & (qseg_ref[...] == kseg_ref[...])
+    if window is not None:
+        visible = visible & (distance < window)
+    bias = jnp.where(visible, 0.0, NEG).astype(jnp.float32)
     dk_acc = None
     dv_acc = None
     dq_parts = []
@@ -70,7 +78,8 @@
             dv_ref[:, gg * HD:(gg + 1) * HD] += dv_acc
 
 
-def attn_bwd(sinks, queries, grads, keys, values, bias, g0, gn):
+def attn_bwd(sinks, queries, grads, keys, values, mask_info, g0, gn):
+    query_pos, query_seg, key_pos, key_seg, window = mask_info
     n = queries.shape[0]
     m = keys.shape[0]
     heads = sinks.shape[1]
@@ -81,7 +90,7 @@
     width = heads * HD
 
     return pl.pallas_call(
-        functools.partial(attn_bwd_kernel, g0, gn),
+        functools.partial(attn_bwd_kernel, g0, gn, window),
         grid=grid,
         in_specs=[
             pl.BlockSpec(memory_space=pltpu.SMEM),
@@ -89,7 +98,10 @@
             pl.BlockSpec((rows, width), lambda g, i: (i, g + g0)),
             pl.BlockSpec((m, 2 * HD), lambda g, i: (0, (g + g0) // 2)),
             pl.BlockSpec((m, 2 * HD), lambda g, i: (0, (g + g0) // 2)),
-            pl.BlockSpec((rows, m), lambda g, i: (i, 0)),
+            pl.BlockSpec((rows, 1), lambda g, i: (i, 0)),
+            pl.BlockSpec((rows, 1), lambda g, i: (i, 0)),
+            pl.BlockSpec((1, m), lambda g, i: (0, 0)),
+            pl.BlockSpec((1, m), lambda g, i: (0, 0)),
         ],
         out_specs=[
             pl.BlockSpec((rows, width), lambda g, i: (i, g)),
@@ -108,9 +120,13 @@
         cost_estimate=pl.CostEstimate(
             flops=10 * gn * heads * n * m * HD,
             transcendentals=gn * heads * n * m,
-            bytes_accessed=4 * n * m + 4 * n * gn * heads * HD * 3 + 12 * m * gn * HD,
+            bytes_accessed=8 * (n + m) + 4 * n * gn * heads * HD * 3 + 12 * m * gn * HD,
         ),
-    )(sinks, queries, grads, keys, values, bias)
+    )(
+        sinks, queries, grads, keys, values,
+        query_pos.reshape(n, 1).astype(jnp.int32), query_seg.reshape(n, 1).astype(jnp.int32),
+        key_pos.reshape(1, m).astype(jnp.int32), key_seg.reshape(1, m).astype(jnp.int32),
+    )
 
 
 def make_bias(query_pos, query_seg, key_pos, key_seg, window):
@@ -176,7 +192,7 @@
     w_values = jnp.concatenate([halo[:WINDOW, cols:], window_values], axis=0)
     w_seg = jnp.concatenate([read_seg(halo[WINDOW:], WINDOW), segment_ids], axis=0)
     w_pos = seq_index * n - WINDOW + jnp.arange(n + WINDOW)
-    w_bias = make_bias(query_pos, segment_ids, w_pos, w_seg, WINDOW)
+    w_bias = (query_pos, segment_ids, w_pos, w_seg, WINDOW)
     w_q = (window_query.reshape(n, -1) * 0.125).astype(jnp.bfloat16)
     w_do = window_grad_out.reshape(n, -1)
     g_split = groups // 2 if groups > 1 else groups
@@ -197,7 +213,7 @@
     f_values = jnp.concatenate(value_parts + [full_values], axis=0)
     f_seg = jnp.concatenate(seg_parts + [segment_ids], axis=0)
     f_pos = (seq_index - (seq_count - 1)) * n + jnp.arange(seq_count * n)
-    f_bias = make_bias(query_pos, segment_ids, f_pos, f_seg, None)
+    f_bias = (query_pos, segment_ids, f_pos, f_seg, None)
     f_q = (full_query.reshape(n, -1) * 0.125).astype(jnp.bfloat16)
     f_do = full_grad_out.reshape(n, -1)
     f_dq, f_dk, f_dv = attn_bwd(full_sinks, f_q, f_do, f_keys, f_values, f_bias, 0, groups)

time: 95.9 us -> 98.3 us (1.025)
  Pallas kernels: 38.8 us -> 39.8 us
    select_n x2 -> x0, other arithmetic: 2.33 us -> none  [make_bias(): return jnp.where(visible, 0.0, NEG).astype(jnp.float32)]
    reshape x0 -> x2, local copies, waits for them, and re-layouts: none -> 1.39 us  [the longest x1 0.8 us: attn_bwd(): query_seg.reshape(n, 1).astype(jnp.int32)]
    pallas_call x3, Pallas kernels: 38.8 us -> 39.8 us  [attn_bwd(): pl.pallas_call(functools.partial(attn_bwd_kernel, g0, gn, window), grid=g...]
  transfers between devices with their start and end apart: 11 -> 11, of which waited for: 5 -> 5; matrix products, arithmetic and copies ran while one was open for 11% -> 12% of each run, Pallas kernels for 16% -> 16%
where the time goes in v8:
time: 98.3 us; the launch traced here: 97.6 us
  Pallas kernels  39.8 us (40%)
  starting transfers between devices  18.3 us (19%)
  waiting for transfers between devices  15.1 us (15%)
  local copies, waits for them, and re-layouts  14.5 us (15%)
  other arithmetic  8.81 us (9%)
  between operations  1.11 us (1%)
    pallas_call x3, Pallas kernels, attn_bwd(): pl.pallas_call(functools.partial(attn_bwd_kernel, g0, gn, window), grid=g...  39.8 us
    ppermute x8, starting transfers between devices, passed_along(): lax.ppermute(value, axis, [(source, source + steps) for source in range(f...  18 us
    ppermute x8, waiting for transfers between devices, passed_along(): lax.ppermute(value, axis, [(source, source + steps) for source in range(f...  14 us
    unnamed x44, local copies, waits for them, and re-layouts  9.02 us
  transfers between devices with their start and end apart: 11, of which 5 were waited for; matrix products, arithmetic and copies ran while one was open for 12% of the time, Pallas kernels for 16%

profile of v8, /device:TPU:0, one launch (start us, length us, event | category | flops | bytes accessed | tf_op | source)
XLA Modules:
  0.0 97.6 jit_solution(18008356552017258531)
XLA Ops:
  0.7 0.7 convert.16
  1.4 0.8 slice.139
  2.3 4.9 %collective-permute-start = (bf16[144,512]{1,0:T(8,128)(2,1)S(1)}, bf16[144,512]{1,0:T(8,128)(2,1)S(1)}, u32[]{:S(2)}, u32[]{:S(2)}) collective-permute-start(bf16[144,512]{1,0:T(8,128)(2,1)S(1)} %pad_maximum_fusion.8), channel_id=1, source_target_pairs={{0,4},{4,8},{8,12},{1,5},{5,9},{9,13},{2,6},{6,10},{10,14},{3,7},{... | collective-permute-start | bytes 442376 | tf_op jit(solution)/shard_map/ppermute | solution.py:20
  7.3 0.7 iota_add_fusion.qpos_ref
  7.9 0.6 iota_add_fusion.1.kpos_ref
  8.6 0.2 broadcast_multiply_fusion.1
  8.8 0.8 copy-done.3
  9.6 0.2 broadcast_multiply_fusion
  9.8 0.7 copy-done.7
  10.6 0.5 iota_add_fusion.2.kpos_ref
  11.1 0.7 copy-done.17
  11.8 0.8 copy.17.qseg_ref
  12.6 0.9 copy.20
  13.5 0.2 copy-done.4
  13.7 0.9 copy.21
  14.6 0.9 copy.23
  15.5 0.2 copy-done.5
  15.8 0.9 copy.24
  16.7 3.6 %collective-permute-start.3 = (bf16[272,256]{1,0:T(8,128)(2,1)S(1)}, bf16[272,256]{1,0:T(8,128)(2,1)S(1)}, u32[]{:S(2)}, u32[]{:S(2)}) collective-permute-start(bf16[272,256]{1,0:T(8,128)(2,1)S(1)} %pad_maximum_fusion.9), channel_id=1, source_target_pairs={{0,4},{4,8},{8,12},{1,5},{5,9},{9,13},{2,6},{6,10},{10,14},{3,7},{... | collective-permute-start | bytes 417800 | tf_op jit(solution)/shard_map/ppermute | solution.py:20
  20.3 2.9 %collective-permute-start.2 = (bf16[272,256]{1,0:T(8,128)(2,1)S(1)}, bf16[272,256]{1,0:T(8,128)(2,1)S(1)}, u32[]{:S(2)}, u32[]{:S(2)}) collective-permute-start(bf16[272,256]{1,0:T(8,128)(2,1)S(1)} %pad_maximum_fusion.9), channel_id=1, source_target_pairs={{0,8},{4,12},{1,9},{5,13},{2,10},{6,14},{3,11},{7,15},{16,24},{20,... | collective-permute-start | bytes 417800 | tf_op jit(solution)/shard_map/ppermute | solution.py:20
  23.3 1.3 %collective-permute-start.1 = (bf16[272,256]{1,0:T(8,128)(2,1)S(1)}, bf16[272,256]{1,0:T(8,128)(2,1)S(1)}, u32[]{:S(2)}, u32[]{:S(2)}) collective-permute-start(bf16[272,256]{1,0:T(8,128)(2,1)S(1)} %pad_maximum_fusion.9), channel_id=1, source_target_pairs={{0,12},{1,13},{2,14},{3,15},{16,28},{17,29},{18,30},{19,31}} | collective-permute-start | bytes 417800 | tf_op jit(solution)/shard_map/ppermute | solution.py:20
  24.6 0.6 reshape.136.kseg_ref
  25.2 0.8 pad_maximum_fusion.6
  26.0 7.9 %shard_map.154 = (bf16[256,512]{1,0:T(8,128)(2,1)}, f32[384,128]{1,0:T(8,128)}, f32[384,128]{1,0:T(8,128)}) custom-call(f32[4,4]{1,0:T(4,128)} %sink_ref.4, bf16[256,1024]{1,0:T(8,128)(2,1)} %bitcast.20, bf16[256,1024]{1,0:T(8,128)(2,1)} %bitcast.22, bf16[384,256]{1,0:T(8,128)(2,1)} %get-tuple-element.87.k_ref, bf16[384,256]{1,0:T(8,128)(2,1)} %get-tuple-element.88.v_ref, ...), custom_call_target="tpu_custom_call" | custom-call | flops 503316480 | bytes 2167808 | tf_op jit(solution)/shard_map/pallas_call | solution.py:92
  34.1 0.6 pad_add_fusion
  34.7 1.1 %collective-permute-done.5 = bf16[816,256]{1,0:T(8,128)(2,1)S(1)} collective-permute-done((bf16[816,256]{1,0:T(8,128)(2,1)S(1)}, bf16[816,256]{1,0:T(8,128)(2,1)S(1)}, u32[]{:S(2)}, u32[]{:S(2)}) %collective-permute-start.5) | collective-permute-done | bytes 417824 | tf_op jit(solution)/shard_map/ppermute | solution.py:203
  35.9 0.8 pad_maximum_fusion.3.v_ref
  36.7 0.8 pad_maximum_fusion.2.k_ref
  37.5 24.0 %shard_map.156 = (bf16[256,1024]{1,0:T(8,128)(2,1)}, f32[1024,256]{1,0:T(8,128)}, f32[1024,256]{1,0:T(8,128)}) custom-call(f32[4,4]{1,0:T(4,128)} %sink_ref.5, bf16[256,1024]{1,0:T(8,128)(2,1)} %bitcast.24, bf16[256,1024]{1,0:T(8,128)(2,1)} %bitcast.25, bf16[1024,256]{1,0:T(8,128)(2,1)} %pad_maximum_fusion.2.k_ref, ...), custom_call_target="tpu_custom_call" | custom-call | flops 2684354560 | bytes 6301696 | tf_op jit(solution)/shard_map/pallas_call | solution.py:92
  61.5 1.4 %broadcast_select_fusion = f32[1024,256]{1,0:T(8,128)S(1)} fusion(f32[1024,256]{1,0:T(8,128)} %get-tuple-element.62, f32[1024,256]{1,0:T(8,128)} %get-tuple-element.61, pred[]{:T(512)S(6)} %eq.3), kind=kLoop, calls=%fused_computation.9 | loop fusion | flops 262144 | bytes 3145729 | tf_op jit(solution)/shard_map/jit(_where)/select_n | solution.py:221
  62.9 0.2 collective-permute-start.6
  63.1 7.9 %shard_map.155 = (bf16[256,512]{1,0:T(8,128)(2,1)}, f32[384,128]{1,0:T(8,128)}, f32[384,128]{1,0:T(8,128)}) custom-call(f32[4,4]{1,0:T(4,128)} %sink_ref.4, bf16[256,1024]{1,0:T(8,128)(2,1)} %bitcast.21, bf16[256,1024]{1,0:T(8,128)(2,1)} %bitcast.23, bf16[384,256]{1,0:T(8,128)(2,1)} %get-tuple-element.87.k_ref, bf16[384,256]{1,0:T(8,128)(2,1)} %get-tuple-element.88.v_ref, ...), custom_call_target="tpu_custom_call" | custom-call | flops 503316480 | bytes 2167808 | tf_op jit(solution)/shard_map/pallas_call | solution.py:92
  71.0 0.9 copy-done.16
  72.0 0.8 copy-done.13
  73.0 1.3 %collective-permute-start.4 = (bf16[128,512]{1,0:T(8,128)(2,1)S(1)}, bf16[128,512]{1,0:T(8,128)(2,1)S(1)}, u32[]{:S(2)}, u32[]{:S(2)}) collective-permute-start(bf16[128,512]{1,0:T(8,128)(2,1)S(1)} %pad_maximum_fusion.10), channel_id=1, source_target_pairs={{4,0},{8,4},{12,8},{5,1},{9,5},{13,9},{6,2},{10,6},{14,10},{7,3},{... | collective-permute-start | bytes 393224 | tf_op jit(solution)/shard_map/ppermute | solution.py:20
  74.4 0.2 fusion.6
  74.6 1.3 %collective-permute-start.7 = (bf16[256,256]{1,0:T(8,128)(2,1)S(1)}, bf16[256,256]{1,0:T(8,128)(2,1)S(1)}, u32[]{:S(2)}, u32[]{:S(2)}) collective-permute-start(bf16[256,256]{1,0:T(8,128)(2,1)S(1)} %get-tuple-element.76), channel_id=1, source_target_pairs={{12,0},{13,1},{14,2},{15,3},{28,16},{29,17},{30,18},{31,19}} | collective-permute-start | bytes 393224 | tf_op jit(solution)/shard_map/ppermute | solution.py:20
  75.9 1.3 %collective-permute-start.9 = (bf16[256,256]{1,0:T(8,128)(2,1)S(1)}, bf16[256,256]{1,0:T(8,128)(2,1)S(1)}, u32[]{:S(2)}, u32[]{:S(2)}) collective-permute-start(bf16[256,256]{1,0:T(8,128)(2,1)S(1)} %get-tuple-element.77), channel_id=1, source_target_pairs={{4,0},{8,4},{12,8},{5,1},{9,5},{13,9},{6,2},{10,6},{14,10},{7,3},{... | collective-permute-start | bytes 393224 | tf_op jit(solution)/shard_map/ppermute | solution.py:20
  77.2 1.3 %collective-permute-start.8 = (bf16[256,256]{1,0:T(8,128)(2,1)S(1)}, bf16[256,256]{1,0:T(8,128)(2,1)S(1)}, u32[]{:S(2)}, u32[]{:S(2)}) collective-permute-start(bf16[256,256]{1,0:T(8,128)(2,1)S(1)} %get-tuple-element.78), channel_id=1, source_target_pairs={{8,0},{12,4},{9,1},{13,5},{10,2},{14,6},{11,3},{15,7},{24,16},{28,... | collective-permute-start | bytes 393224 | tf_op jit(solution)/shard_map/ppermute | solution.py:20
  78.5 2.2 %collective-permute-done.4 = bf16[128,512]{1,0:T(8,128)(2,1)S(1)} collective-permute-done((bf16[128,512]{1,0:T(8,128)(2,1)S(1)}, bf16[128,512]{1,0:T(8,128)(2,1)S(1)}, u32[]{:S(2)}, u32[]{:S(2)}) %collective-permute-start.4) | collective-permute-done | bytes 131104 | tf_op jit(solution)/shard_map/ppermute | solution.py:20
  80.8 3.9 %collective-permute-done.7 = bf16[256,256]{1,0:T(8,128)(2,1)S(1)} collective-permute-done((bf16[256,256]{1,0:T(8,128)(2,1)S(1)}, bf16[256,256]{1,0:T(8,128)(2,1)S(1)}, u32[]{:S(2)}, u32[]{:S(2)}) %collective-permute-start.7) | collective-permute-done | bytes 131104 | tf_op jit(solution)/shard_map/ppermute | solution.py:20
  84.7 1.7 %collective-permute-done.9 = bf16[256,256]{1,0:T(8,128)(2,1)S(1)} collective-permute-done((bf16[256,256]{1,0:T(8,128)(2,1)S(1)}, bf16[256,256]{1,0:T(8,128)(2,1)S(1)}, u32[]{:S(2)}, u32[]{:S(2)}) %collective-permute-start.9) | collective-permute-done | bytes 131104 | tf_op jit(solution)/shard_map/ppermute | solution.py:20
  86.4 6.1 %collective-permute-done.8 = bf16[256,256]{1,0:T(8,128)(2,1)S(1)} collective-permute-done((bf16[256,256]{1,0:T(8,128)(2,1)S(1)}, bf16[256,256]{1,0:T(8,128)(2,1)S(1)}, u32[]{:S(2)}, u32[]{:S(2)}) %collective-permute-start.8) | collective-permute-done | bytes 131104 | tf_op jit(solution)/shard_map/ppermute | solution.py:20
  92.8 0.8 copy-done.11
  93.7 1.2 %reshape.137 = bf16[256,4,256]{2,1,0:T(4,128)(2,1)} reshape(bf16[256,1024]{1,0:T(8,128)(2,1)S(1)} %pad_maximum_fusion.1) | data formatting | bytes 1048576 | tf_op jit(solution)/shard_map/reshape | solution.py:249
  94.9 1.2 %reshape.140 = bf16[256,4,256]{2,1,0:T(4,128)(2,1)} reshape(bf16[256,1024]{1,0:T(8,128)(2,1)S(1)} %copy-done.6) | data formatting | bytes 1048576 | tf_op jit(solution)/shard_map/reshape | solution.py:252
  96.1 0.7 fusion.8
  96.8 0.7 select_convert_fusion
  (70 shorter events, 1.1 us)
Async XLA Ops:
  0.6 1.7 %copy-start.10 = (bf16[256,256]{1,0:T(8,128)(2,1)S(1)}, bf16[256,256]{1,0:T(8,128)(2,1)}, u32[]{:S(2)}) copy-start(bf16[256,256]{1,0:T(8,128)(2,1)} %param.18) | copy-start | bytes 393220
  0.6 7.9 %copy-start.2 = (bf16[256,4,256]{2,1,0:T(4,128)(2,1)S(1)}, bf16[256,4,256]{2,1,0:T(4,128)(2,1)}, u32[]{:S(2)}) copy-start(bf16[256,4,256]{2,1,0:T(4,128)(2,1)} %param.16) | copy-start | bytes 1572868
  2.3 14.3 %collective-permute-start = (bf16[144,512]{1,0:T(8,128)(2,1)S(1)}, bf16[144,512]{1,0:T(8,128)(2,1)S(1)}, u32[]{:S(2)}, u32[]{:S(2)}) collective-permute-start(bf16[144,512]{1,0:T(8,128)(2,1)S(1)} %pad_maximum_fusion.8), channel_id=1, source_target_pairs={{0,4},{4,8},{8,12},{1,5},{5,9},{9,13},{2,6},{6,10},{10,14},{3,7},{... | collective-permute-start | bytes 442376 | tf_op jit(solution)/shard_map/ppermute | solution.py:20
  8.6 1.0 %copy-start.3 = (bf16[256,4,256]{2,1,0:T(4,128)(2,1)S(1)}, bf16[256,4,256]{2,1,0:T(4,128)(2,1)}, u32[]{:S(2)}) copy-start(bf16[256,4,256]{2,1,0:T(4,128)(2,1)} %param.21) | copy-start | bytes 1572868
  9.6 0.9 copy-start.7
  9.6 1.0 copy-start.8
  11.1 0.7 copy-start.17
  12.6 1.1 %copy-start.4 = (bf16[256,4,256]{2,1,0:T(4,128)(2,1)S(1)}, bf16[256,4,256]{2,1,0:T(4,128)(2,1)}, u32[]{:S(2)}) copy-start(bf16[256,4,256]{2,1,0:T(4,128)(2,1)} %param.19) | copy-start | bytes 1572868
  14.6 1.1 %copy-start.5 = (bf16[256,4,256]{2,1,0:T(4,128)(2,1)S(1)}, bf16[256,4,256]{2,1,0:T(4,128)(2,1)}, u32[]{:S(2)}) copy-start(bf16[256,4,256]{2,1,0:T(4,128)(2,1)} %param.24) | copy-start | bytes 1572868
  16.7 8.5 %copy-start.9 = (bf16[256,256]{1,0:T(8,128)(2,1)S(1)}, bf16[256,256]{1,0:T(8,128)(2,1)}, u32[]{:S(2)}) copy-start(bf16[256,256]{1,0:T(8,128)(2,1)} %param.17) | copy-start | bytes 393220
  16.7 17.2 %collective-permute-start.3 = (bf16[272,256]{1,0:T(8,128)(2,1)S(1)}, bf16[272,256]{1,0:T(8,128)(2,1)S(1)}, u32[]{:S(2)}, u32[]{:S(2)}) collective-permute-start(bf16[272,256]{1,0:T(8,128)(2,1)S(1)} %pad_maximum_fusion.9), channel_id=1, source_target_pairs={{0,4},{4,8},{8,12},{1,5},{5,9},{9,13},{2,6},{6,10},{10,14},{3,7},{... | collective-permute-start | bytes 417800 | tf_op jit(solution)/shard_map/ppermute | solution.py:20
  20.3 13.6 %collective-permute-start.2 = (bf16[272,256]{1,0:T(8,128)(2,1)S(1)}, bf16[272,256]{1,0:T(8,128)(2,1)S(1)}, u32[]{:S(2)}, u32[]{:S(2)}) collective-permute-start(bf16[272,256]{1,0:T(8,128)(2,1)S(1)} %pad_maximum_fusion.9), channel_id=1, source_target_pairs={{0,8},{4,12},{1,9},{5,13},{2,10},{6,14},{3,11},{7,15},{16,24},{20,... | collective-permute-start | bytes 417800 | tf_op jit(solution)/shard_map/ppermute | solution.py:20
  23.3 10.6 %collective-permute-start.1 = (bf16[272,256]{1,0:T(8,128)(2,1)S(1)}, bf16[272,256]{1,0:T(8,128)(2,1)S(1)}, u32[]{:S(2)}, u32[]{:S(2)}) collective-permute-start(bf16[272,256]{1,0:T(8,128)(2,1)S(1)} %pad_maximum_fusion.9), channel_id=1, source_target_pairs={{0,12},{1,13},{2,14},{3,15},{16,28},{17,29},{18,30},{19,31}} | collective-permute-start | bytes 417800 | tf_op jit(solution)/shard_map/ppermute | solution.py:20
  34.0 1.8 %collective-permute-start.5 = (bf16[816,256]{1,0:T(8,128)(2,1)S(1)}, bf16[816,256]{1,0:T(8,128)(2,1)S(1)}, u32[]{:S(2)}, u32[]{:S(2)}) collective-permute-start(bf16[816,256]{1,0:T(8,128)(2,1)S(1)} %pad_maximum_fusion.4), channel_id=1, source_target_pairs={{0,1},{1,0},{2,3},{3,2},{4,5},{5,4},{6,7},{7,6},{8,9},{9,8},{10,11... | collective-permute-start | bytes 1253384 | tf_op jit(solution)/shard_map/ppermute | solution.py:203
  62.9 8.1 %copy-start.14 = (f32[384,128]{1,0:T(8,128)S(1)}, f32[384,128]{1,0:T(8,128)}, u32[]{:S(2)}) copy-start(f32[384,128]{1,0:T(8,128)} %get-tuple-element.54) | copy-start | bytes 589828
  62.9 11.4 %collective-permute-start.6 = (f32[1024,256]{1,0:T(8,128)S(1)}, f32[1024,256]{1,0:T(8,128)S(1)}, u32[]{:S(2)}, u32[]{:S(2)}) collective-permute-start(f32[1024,256]{1,0:T(8,128)S(1)} %broadcast_select_fusion), channel_id=1, source_target_pairs={{0,1},{1,0},{2,3},{3,2},{4,5},{5,4},{6,7},{7,6},{8,9},{9,8},{10,11... | collective-permute-start | bytes 3145736 | tf_op jit(solution)/shard_map/ppermute | solution.py:223
  71.0 0.9 copy-start.16
  71.9 0.9 copy-start.13
  72.0 1.0 %copy-start.15 = (f32[384,128]{1,0:T(8,128)S(1)}, f32[384,128]{1,0:T(8,128)}, u32[]{:S(2)}) copy-start(f32[384,128]{1,0:T(8,128)} %get-tuple-element.57) | copy-start | bytes 589828
  72.0 2.4 %copy-start = (f32[1024,256]{1,0:T(8,128)S(1)}, f32[1024,256]{1,0:T(8,128)}, u32[]{:S(2)}) copy-start(f32[1024,256]{1,0:T(8,128)} %get-tuple-element.61) | copy-start | bytes 3145732
  72.0 2.4 %copy-start.1 = (f32[1024,256]{1,0:T(8,128)S(1)}, f32[1024,256]{1,0:T(8,128)}, u32[]{:S(2)}) copy-start(f32[1024,256]{1,0:T(8,128)} %get-tuple-element.62) | copy-start | bytes 3145732
  73.0 7.7 %collective-permute-start.4 = (bf16[128,512]{1,0:T(8,128)(2,1)S(1)}, bf16[128,512]{1,0:T(8,128)(2,1)S(1)}, u32[]{:S(2)}, u32[]{:S(2)}) collective-permute-start(bf16[128,512]{1,0:T(8,128)(2,1)S(1)} %pad_maximum_fusion.10), channel_id=1, source_target_pairs={{4,0},{8,4},{12,8},{5,1},{9,5},{13,9},{6,2},{10,6},{14,10},{7,3},{... | collective-permute-start | bytes 393224 | tf_op jit(solution)/shard_map/ppermute | solution.py:20
  74.6 10.1 %collective-permute-start.7 = (bf16[256,256]{1,0:T(8,128)(2,1)S(1)}, bf16[256,256]{1,0:T(8,128)(2,1)S(1)}, u32[]{:S(2)}, u32[]{:S(2)}) collective-permute-start(bf16[256,256]{1,0:T(8,128)(2,1)S(1)} %get-tuple-element.76), channel_id=1, source_target_pairs={{12,0},{13,1},{14,2},{15,3},{28,16},{29,17},{30,18},{31,19}} | collective-permute-start | bytes 393224 | tf_op jit(solution)/shard_map/ppermute | solution.py:20
  75.9 10.5 %collective-permute-start.9 = (bf16[256,256]{1,0:T(8,128)(2,1)S(1)}, bf16[256,256]{1,0:T(8,128)(2,1)S(1)}, u32[]{:S(2)}, u32[]{:S(2)}) collective-permute-start(bf16[256,256]{1,0:T(8,128)(2,1)S(1)} %get-tuple-element.77), channel_id=1, source_target_pairs={{4,0},{8,4},{12,8},{5,1},{9,5},{13,9},{6,2},{10,6},{14,10},{7,3},{... | collective-permute-start | bytes 393224 | tf_op jit(solution)/shard_map/ppermute | solution.py:20
  77.2 15.3 %collective-permute-start.8 = (bf16[256,256]{1,0:T(8,128)(2,1)S(1)}, bf16[256,256]{1,0:T(8,128)(2,1)S(1)}, u32[]{:S(2)}, u32[]{:S(2)}) collective-permute-start(bf16[256,256]{1,0:T(8,128)(2,1)S(1)} %get-tuple-element.78), channel_id=1, source_target_pairs={{8,0},{12,4},{9,1},{13,5},{10,2},{14,6},{11,3},{15,7},{24,16},{28,... | collective-permute-start | bytes 393224 | tf_op jit(solution)/shard_map/ppermute | solution.py:20
  92.6 1.0 copy-start.11
  92.6 1.0 %copy-start.12 = (bf16[256,512]{1,0:T(8,128)(2,1)S(1)}, bf16[256,512]{1,0:T(8,128)(2,1)}, u32[]{:S(2)}) copy-start(bf16[256,512]{1,0:T(8,128)(2,1)} %get-tuple-element.53) | copy-start | bytes 786436
  92.7 3.4 %collective-permute-start.10 = (f32[256,768]{1,0:T(8,128)S(1)}, f32[256,768]{1,0:T(8,128)S(1)}, u32[]{:S(2)}, u32[]{:S(2)}) collective-permute-start(f32[256,768]{1,0:T(8,128)S(1)} %pad_maximum_fusion), channel_id=1, source_target_pairs={{0,1},{1,0},{2,3},{3,2},{4,5},{5,4},{6,7},{7,6},{8,9},{9,8},{10,11... | collective-permute-start | bytes 2359304 | tf_op jit(solution)/shard_map/ppermute | solution.py:243
  93.7 1.2 %copy-start.6 = (bf16[256,1024]{1,0:T(8,128)(2,1)S(1)}, bf16[256,1024]{1,0:T(8,128)(2,1)}, u32[]{:S(2)}) copy-start(bf16[256,1024]{1,0:T(8,128)(2,1)} %get-tuple-element.63) | copy-start | bytes 1572868

commit v9 on v5

--- a/solution.py
+++ b/solution.py
@@ -205,11 +205,6 @@
     give = jnp.where(first, f_dv, f_dk)
     keep = jnp.where(first, f_dk, f_dv)
     summed = keep + lax.ppermute(give, "rep", swap)
-    f_final = summed[(seq_count - 1) * n:]
-    for jj, d in enumerate(order):
-        piece = summed[jj * n:(jj + 1) * n].astype(jnp.bfloat16)
-        f_final = f_final + passed_along(piece, "seq", -d).astype(jnp.float32)
-
     if g_split < groups:
         w_out2 = attn_bwd(window_sinks, w_q, w_do, w_keys, w_values, w_bias, g_split, groups - g_split)
         w_dq = jnp.concatenate([w_out1[0], w_out2[0]], axis=1)
@@ -217,9 +212,18 @@
         w_dv = jnp.concatenate([w_out1[2], w_out2[2]], axis=1)
     else:
         w_dq, w_dk, w_dv = w_out1
-    back_w = passed_along(
-        jnp.concatenate([w_dk[:WINDOW], w_dv[:WINDOW]], axis=1).astype(jnp.bfloat16), "seq", -1
-    ).astype(jnp.float32)
+
+    f_final = summed[(seq_count - 1) * n:]
+    back_w = jnp.zeros((WINDOW, 2 * cols), jnp.float32)
+    for jj, d in enumerate(order):
+        piece = summed[jj * n:(jj + 1) * n]
+        if d == 1:
+            piece = jnp.concatenate([piece, w_dk[:WINDOW], w_dv[:WINDOW]], axis=0)
+        got = passed_along(piece.astype(jnp.bfloat16), "seq", -d).astype(jnp.float32)
+        if d == 1:
+            back_w = jnp.concatenate([got[n:n + WINDOW], got[n + WINDOW:]], axis=1)
+            got = got[:n]
+        f_final = f_final + got
     w_kv = jnp.concatenate([w_dk[WINDOW:], w_dv[WINDOW:]], axis=1)
     w_kv = jnp.concatenate([w_kv[: n - WINDOW], w_kv[n - WINDOW:] + back_w], axis=0)
 

time: 95.9 us -> 94.4 us (0.984)
  starting transfers between devices: 18.2 us -> 16.9 us
    ppermute x8 -> x7, starting transfers between devices: 17.8 us -> 16.5 us  [passed_along(): lax.ppermute(value, axis, [(source, source + steps) for source in range(f...]
    concatenate x1, local copies, waits for them, and re-layouts: 0.01 us -> 1.02 us  [body(): w_dk = jnp.concatenate([w_out1[1], w_out2[1]], axis=1)]
    unnamed x44 -> x42, local copies, waits for them, and re-layouts: 8.98 us -> 8.07 us
    ppermute x8 -> x7, waiting for transfers between devices: 13.9 us -> 13.6 us  [passed_along(): lax.ppermute(value, axis, [(source, source + steps) for source in range(f...]
  transfers between devices with their start and end apart: 11 -> 10, of which waited for: 5 -> 3; matrix products, arithmetic and copies ran while one was open for 11% -> 12% of each run, Pallas kernels for 16% -> 17%
where the time goes in v9:
time: 94.4 us; the launch traced here: 93.7 us
  Pallas kernels  38.9 us (41%)
  starting transfers between devices  16.9 us (18%)
  local copies, waits for them, and re-layouts  14 us (15%)
  waiting for transfers between devices  13.9 us (15%)
  other arithmetic  8.87 us (9%)
  between operations  1.16 us (1%)
    pallas_call x3, Pallas kernels, attn_bwd(): pl.pallas_call(functools.partial(attn_bwd_kernel, g0, gn), grid=grid, in_...  38.9 us
    ppermute x7, starting transfers between devices, passed_along(): lax.ppermute(value, axis, [(source, source + steps) for source in range(f...  16.5 us
    ppermute x7, waiting for transfers between devices, passed_along(): lax.ppermute(value, axis, [(source, source + steps) for source in range(f...  13.6 us
    unnamed x42, local copies, waits for them, and re-layouts  8.07 us
    select_n x2, other arithmetic, make_bias(): return jnp.where(visible, 0.0, NEG).astype(jnp.float32)  2.34 us
  transfers between devices with their start and end apart: 10, of which 3 were waited for; matrix products, arithmetic and copies ran while one was open for 12% of the time, Pallas kernels for 17%

profile of v9, /device:TPU:0, one launch (start us, length us, event | category | flops | bytes accessed | tf_op | source)
XLA Modules:
  0.0 93.7 jit_solution(7942683118054283020)
XLA Ops:
  0.6 0.7 convert.17
  1.4 0.8 slice.148
  2.3 0.8 slice.149
  3.1 4.9 %collective-permute-start = (bf16[144,512]{1,0:T(8,128)(2,1)S(1)}, bf16[144,512]{1,0:T(8,128)(2,1)S(1)}, u32[]{:S(2)}, u32[]{:S(2)}) collective-permute-start(bf16[144,512]{1,0:T(8,128)(2,1)S(1)} %pad_maximum_fusion.9), channel_id=1, source_target_pairs={{0,4},{4,8},{8,12},{1,5},{5,9},{9,13},{2,6},{6,10},{10,14},{3,7},{... | collective-permute-start | bytes 442376 | tf_op jit(solution)/shard_map/ppermute | solution.py:20
  8.2 0.2 broadcast_multiply_fusion.1
  8.4 0.8 copy-done.3
  9.2 0.2 broadcast_multiply_fusion
  9.4 0.7 copy-done.7
  10.1 0.1 copy-done.8
  10.2 0.9 copy.17
  11.1 0.2 copy-done.4
  11.3 0.9 copy.18
  12.2 0.9 copy.20
  13.1 0.2 copy-done.5
  13.4 0.9 copy.21
  14.3 3.5 %collective-permute-start.3 = (bf16[272,256]{1,0:T(8,128)(2,1)S(1)}, bf16[272,256]{1,0:T(8,128)(2,1)S(1)}, u32[]{:S(2)}, u32[]{:S(2)}) collective-permute-start(bf16[272,256]{1,0:T(8,128)(2,1)S(1)} %pad_maximum_fusion.10), channel_id=1, source_target_pairs={{0,4},{4,8},{8,12},{1,5},{5,9},{9,13},{2,6},{6,10},{10,14},{3,7},{... | collective-permute-start | bytes 417800 | tf_op jit(solution)/shard_map/ppermute | solution.py:20
  17.8 2.9 %collective-permute-start.2 = (bf16[272,256]{1,0:T(8,128)(2,1)S(1)}, bf16[272,256]{1,0:T(8,128)(2,1)S(1)}, u32[]{:S(2)}, u32[]{:S(2)}) collective-permute-start(bf16[272,256]{1,0:T(8,128)(2,1)S(1)} %pad_maximum_fusion.10), channel_id=1, source_target_pairs={{0,8},{4,12},{1,9},{5,13},{2,10},{6,14},{3,11},{7,15},{16,24},{20,... | collective-permute-start | bytes 417800 | tf_op jit(solution)/shard_map/ppermute | solution.py:20
  20.7 1.3 %collective-permute-start.1 = (bf16[272,256]{1,0:T(8,128)(2,1)S(1)}, bf16[272,256]{1,0:T(8,128)(2,1)S(1)}, u32[]{:S(2)}, u32[]{:S(2)}) collective-permute-start(bf16[272,256]{1,0:T(8,128)(2,1)S(1)} %pad_maximum_fusion.10), channel_id=1, source_target_pairs={{0,12},{1,13},{2,14},{3,15},{16,28},{17,29},{18,30},{19,31}} | collective-permute-start | bytes 417800 | tf_op jit(solution)/shard_map/ppermute | solution.py:20
  22.1 0.7 copy-done.16
  22.8 1.0 %fusion.7.bias_ref = f32[256,384]{1,0:T(8,128)} fusion(s32[384]{0:T(512)S(1)} %get-tuple-element.91, s32[384]{0:T(512)S(1)} %get-tuple-element.92, s32[256]{0:T(256)S(1)} %iota_add_fusion.2, s32[256]{0:T(256)S(1)} %copy-done.16, pred[384]{0:T(512)(128)(4,1)S(1)} %broadcast_compare_fusion.1), kind=kLoop, calls=%fused_computation.20 | loop fusion | flops 786432 | bytes 398720 | tf_op jit(solution)/shard_map/jit(_where)/select_n | solution.py:121
  23.7 0.8 pad_maximum_fusion.7
  24.5 7.7 %shard_map.154 = (bf16[256,512]{1,0:T(8,128)(2,1)}, f32[384,128]{1,0:T(8,128)}, f32[384,128]{1,0:T(8,128)}) custom-call(f32[4,4]{1,0:T(4,128)} %sink_ref.4, bf16[256,1024]{1,0:T(8,128)(2,1)} %bitcast.18, bf16[256,1024]{1,0:T(8,128)(2,1)} %bitcast.20, bf16[384,256]{1,0:T(8,128)(2,1)} %get-tuple-element.89.k_ref, bf16[384,256]{1,0:T(8,128)(2,1)} %get-tuple-element.90.v_ref, ...), custom_call_target="tpu_custom_call" | custom-call | flops 503316480 | bytes 2555904 | tf_op jit(solution)/shard_map/pallas_call | solution.py:83
  32.4 0.1 collective-permute-start.4
  32.5 1.4 %fusion.2.bias_ref = f32[256,1024]{1,0:T(8,128)} fusion(s32[1024]{0:T(1024)S(1)} %pad_add_fusion, s32[1024]{0:T(1024)S(1)} %iota_add_fusion, s32[256]{0:T(256)S(1)} %iota_add_fusion.2, s32[256]{0:T(256)S(1)} %copy-done.16, pred[1024]{0:T(1024)(128)(4,1)S(1)} %broadcast_compare_fusion), kind=kLoop, calls=%fused_computation.4 | loop fusion | flops 1572864 | bytes 1059840 | tf_op jit(solution)/shard_map/jit(_where)/select_n | solution.py:121
  33.8 0.3 collective-permute-done.4
  34.2 0.8 pad_maximum_fusion.3.v_ref
  35.1 0.8 pad_maximum_fusion.2.k_ref
  35.9 23.3 %shard_map.156 = (bf16[256,1024]{1,0:T(8,128)(2,1)}, f32[1024,256]{1,0:T(8,128)}, f32[1024,256]{1,0:T(8,128)}) custom-call(f32[4,4]{1,0:T(4,128)} %sink_ref.5, bf16[256,1024]{1,0:T(8,128)(2,1)} %bitcast.22, bf16[256,1024]{1,0:T(8,128)(2,1)} %bitcast.23, bf16[1024,256]{1,0:T(8,128)(2,1)} %pad_maximum_fusion.2.k_ref, ...), custom_call_target="tpu_custom_call" | custom-call | flops 2684354560 | bytes 7340032 | tf_op jit(solution)/shard_map/pallas_call | solution.py:83
  59.2 1.4 %broadcast_select_fusion = f32[1024,256]{1,0:T(8,128)S(1)} fusion(f32[1024,256]{1,0:T(8,128)} %get-tuple-element.62, f32[1024,256]{1,0:T(8,128)} %get-tuple-element.61, pred[]{:T(512)S(6)} %eq.14), kind=kLoop, calls=%fused_computation.15 | loop fusion | flops 262144 | bytes 3145729 | tf_op jit(solution)/shard_map/jit(_where)/select_n | solution.py:205
  60.6 0.2 collective-permute-start.5
  60.8 7.8 %shard_map.155 = (bf16[256,512]{1,0:T(8,128)(2,1)}, f32[384,128]{1,0:T(8,128)}, f32[384,128]{1,0:T(8,128)}) custom-call(f32[4,4]{1,0:T(4,128)} %sink_ref.4, bf16[256,1024]{1,0:T(8,128)(2,1)} %bitcast.19, bf16[256,1024]{1,0:T(8,128)(2,1)} %bitcast.21, bf16[384,256]{1,0:T(8,128)(2,1)} %get-tuple-element.89.k_ref, bf16[384,256]{1,0:T(8,128)(2,1)} %get-tuple-element.90.v_ref, ...), custom_call_target="tpu_custom_call" | custom-call | flops 503316480 | bytes 2555904 | tf_op jit(solution)/shard_map/pallas_call | solution.py:83
  68.7 1.0 %constant_dynamic-update-slice_fusion = f32[384,256]{1,0:T(8,128)S(1)} fusion(f32[384,256]{1,0:T(8,128)S(1)} %constant_dynamic-update-slice_fusion.1, f32[384,128]{1,0:T(8,128)} %get-tuple-element.55), kind=kLoop, calls=%fused_computation.46 | loop fusion | bytes 393216 | tf_op jit(solution)/shard_map/concatenate | solution.py:211
  69.7 0.9 copy-done.15
  70.7 0.2 fusion.12
  71.0 1.3 %collective-permute-start.6 = (bf16[512,256]{1,0:T(8,128)(2,1)S(1)}, bf16[512,256]{1,0:T(8,128)(2,1)S(1)}, u32[]{:S(2)}, u32[]{:S(2)}) collective-permute-start(bf16[512,256]{1,0:T(8,128)(2,1)S(1)} %pad_maximum_fusion.6), channel_id=1, source_target_pairs={{4,0},{8,4},{12,8},{5,1},{9,5},{13,9},{6,2},{10,6},{14,10},{7,3},{... | collective-permute-start | bytes 786440 | tf_op jit(solution)/shard_map/ppermute | solution.py:20
  72.4 1.3 %collective-permute-start.7 = (bf16[256,256]{1,0:T(8,128)(2,1)S(1)}, bf16[256,256]{1,0:T(8,128)(2,1)S(1)}, u32[]{:S(2)}, u32[]{:S(2)}) collective-permute-start(bf16[256,256]{1,0:T(8,128)(2,1)S(1)} %get-tuple-element.76), channel_id=1, source_target_pairs={{12,0},{13,1},{14,2},{15,3},{28,16},{29,17},{30,18},{31,19}} | collective-permute-start | bytes 393224 | tf_op jit(solution)/shard_map/ppermute | solution.py:20
  73.7 1.3 %collective-permute-start.8 = (bf16[256,256]{1,0:T(8,128)(2,1)S(1)}, bf16[256,256]{1,0:T(8,128)(2,1)S(1)}, u32[]{:S(2)}, u32[]{:S(2)}) collective-permute-start(bf16[256,256]{1,0:T(8,128)(2,1)S(1)} %get-tuple-element.77), channel_id=1, source_target_pairs={{8,0},{12,4},{9,1},{13,5},{10,2},{14,6},{11,3},{15,7},{24,16},{28,... | collective-permute-start | bytes 393224 | tf_op jit(solution)/shard_map/ppermute | solution.py:20
  75.0 9.8 %collective-permute-done.6 = bf16[512,256]{1,0:T(8,128)(2,1)S(1)} collective-permute-done((bf16[512,256]{1,0:T(8,128)(2,1)S(1)}, bf16[512,256]{1,0:T(8,128)(2,1)S(1)}, u32[]{:S(2)}, u32[]{:S(2)}) %collective-permute-start.6) | collective-permute-done | bytes 262176 | tf_op jit(solution)/shard_map/ppermute | solution.py:20
  84.9 0.1 fusion.8
  84.9 3.7 %collective-permute-done.8 = bf16[256,256]{1,0:T(8,128)(2,1)S(1)} collective-permute-done((bf16[256,256]{1,0:T(8,128)(2,1)S(1)}, bf16[256,256]{1,0:T(8,128)(2,1)S(1)}, u32[]{:S(2)}, u32[]{:S(2)}) %collective-permute-start.8) | collective-permute-done | bytes 131104 | tf_op jit(solution)/shard_map/ppermute | solution.py:20
  88.8 0.1 collective-permute-start.9
  88.9 0.8 copy-done.11
  89.7 0.1 copy-done.12
  89.8 1.2 %reshape.119 = bf16[256,4,256]{2,1,0:T(4,128)(2,1)} reshape(bf16[256,1024]{1,0:T(8,128)(2,1)S(1)} %pad_maximum_fusion.1) | data formatting | bytes 1048576 | tf_op jit(solution)/shard_map/reshape | solution.py:237
  91.0 1.2 %reshape.121 = bf16[256,4,256]{2,1,0:T(4,128)(2,1)} reshape(bf16[256,1024]{1,0:T(8,128)(2,1)S(1)} %copy-done.6) | data formatting | bytes 1048576 | tf_op jit(solution)/shard_map/reshape | solution.py:240
  92.2 0.1 fusion.3
  92.2 0.7 fusion.14
  93.0 0.7 select_convert_fusion
  (69 shorter events, 0.7 us)
Async XLA Ops:
  0.6 7.5 %copy-start.2 = (bf16[256,4,256]{2,1,0:T(4,128)(2,1)S(1)}, bf16[256,4,256]{2,1,0:T(4,128)(2,1)}, u32[]{:S(2)}) copy-start(bf16[256,4,256]{2,1,0:T(4,128)(2,1)} %param.16) | copy-start | bytes 1572868
  3.1 11.1 %collective-permute-start = (bf16[144,512]{1,0:T(8,128)(2,1)S(1)}, bf16[144,512]{1,0:T(8,128)(2,1)S(1)}, u32[]{:S(2)}, u32[]{:S(2)}) collective-permute-start(bf16[144,512]{1,0:T(8,128)(2,1)S(1)} %pad_maximum_fusion.9), channel_id=1, source_target_pairs={{0,4},{4,8},{8,12},{1,5},{5,9},{9,13},{2,6},{6,10},{10,14},{3,7},{... | collective-permute-start | bytes 442376 | tf_op jit(solution)/shard_map/ppermute | solution.py:20
  8.1 1.0 %copy-start.3 = (bf16[256,4,256]{2,1,0:T(4,128)(2,1)S(1)}, bf16[256,4,256]{2,1,0:T(4,128)(2,1)}, u32[]{:S(2)}) copy-start(bf16[256,4,256]{2,1,0:T(4,128)(2,1)} %param.21) | copy-start | bytes 1572868
  9.2 0.9 copy-start.7
  9.2 1.0 %copy-start.8 = (bf16[256,256]{1,0:T(8,128)(2,1)S(1)}, bf16[256,256]{1,0:T(8,128)(2,1)}, u32[]{:S(2)}) copy-start(bf16[256,256]{1,0:T(8,128)(2,1)} %param.22) | copy-start | bytes 393220
  10.2 1.1 %copy-start.4 = (bf16[256,4,256]{2,1,0:T(4,128)(2,1)S(1)}, bf16[256,4,256]{2,1,0:T(4,128)(2,1)}, u32[]{:S(2)}) copy-start(bf16[256,4,256]{2,1,0:T(4,128)(2,1)} %param.19) | copy-start | bytes 1572868
  12.2 1.1 %copy-start.5 = (bf16[256,4,256]{2,1,0:T(4,128)(2,1)S(1)}, bf16[256,4,256]{2,1,0:T(4,128)(2,1)}, u32[]{:S(2)}) copy-start(bf16[256,4,256]{2,1,0:T(4,128)(2,1)} %param.24) | copy-start | bytes 1572868
  14.3 18.0 %collective-permute-start.3 = (bf16[272,256]{1,0:T(8,128)(2,1)S(1)}, bf16[272,256]{1,0:T(8,128)(2,1)S(1)}, u32[]{:S(2)}, u32[]{:S(2)}) collective-permute-start(bf16[272,256]{1,0:T(8,128)(2,1)S(1)} %pad_maximum_fusion.10), channel_id=1, source_target_pairs={{0,4},{4,8},{8,12},{1,5},{5,9},{9,13},{2,6},{6,10},{10,14},{3,7},{... | collective-permute-start | bytes 417800 | tf_op jit(solution)/shard_map/ppermute | solution.py:20
  17.8 14.5 %collective-permute-start.2 = (bf16[272,256]{1,0:T(8,128)(2,1)S(1)}, bf16[272,256]{1,0:T(8,128)(2,1)S(1)}, u32[]{:S(2)}, u32[]{:S(2)}) collective-permute-start(bf16[272,256]{1,0:T(8,128)(2,1)S(1)} %pad_maximum_fusion.10), channel_id=1, source_target_pairs={{0,8},{4,12},{1,9},{5,13},{2,10},{6,14},{3,11},{7,15},{16,24},{20,... | collective-permute-start | bytes 417800 | tf_op jit(solution)/shard_map/ppermute | solution.py:20
  20.7 11.6 %collective-permute-start.1 = (bf16[272,256]{1,0:T(8,128)(2,1)S(1)}, bf16[272,256]{1,0:T(8,128)(2,1)S(1)}, u32[]{:S(2)}, u32[]{:S(2)}) collective-permute-start(bf16[272,256]{1,0:T(8,128)(2,1)S(1)} %pad_maximum_fusion.10), channel_id=1, source_target_pairs={{0,12},{1,13},{2,14},{3,15},{16,28},{17,29},{18,30},{19,31}} | collective-permute-start | bytes 417800 | tf_op jit(solution)/shard_map/ppermute | solution.py:20
  22.1 0.7 copy-start.16
  22.8 1.0 %copy-start.9 = (bf16[256,256]{1,0:T(8,128)(2,1)S(1)}, bf16[256,256]{1,0:T(8,128)(2,1)}, u32[]{:S(2)}) copy-start(bf16[256,256]{1,0:T(8,128)(2,1)} %param.17) | copy-start | bytes 393220
  22.8 1.0 %copy-start.10 = (bf16[256,256]{1,0:T(8,128)(2,1)S(1)}, bf16[256,256]{1,0:T(8,128)(2,1)}, u32[]{:S(2)}) copy-start(bf16[256,256]{1,0:T(8,128)(2,1)} %param.18) | copy-start | bytes 393220
  32.4 1.8 %collective-permute-start.4 = (bf16[816,256]{1,0:T(8,128)(2,1)S(1)}, bf16[816,256]{1,0:T(8,128)(2,1)S(1)}, u32[]{:S(2)}, u32[]{:S(2)}) collective-permute-start(bf16[816,256]{1,0:T(8,128)(2,1)S(1)} %pad_maximum_fusion.4), channel_id=1, source_target_pairs={{0,1},{1,0},{2,3},{3,2},{4,5},{5,4},{6,7},{7,6},{8,9},{9,8},{10,11... | collective-permute-start | bytes 1253384 | tf_op jit(solution)/shard_map/ppermute | solution.py:187
  60.6 8.1 %copy-start.14 = (f32[384,128]{1,0:T(8,128)S(1)}, f32[384,128]{1,0:T(8,128)}, u32[]{:S(2)}) copy-start(f32[384,128]{1,0:T(8,128)} %get-tuple-element.54) | copy-start | bytes 589828
  60.6 10.1 %collective-permute-start.5 = (f32[1024,256]{1,0:T(8,128)S(1)}, f32[1024,256]{1,0:T(8,128)S(1)}, u32[]{:S(2)}, u32[]{:S(2)}) collective-permute-start(f32[1024,256]{1,0:T(8,128)S(1)} %broadcast_select_fusion), channel_id=1, source_target_pairs={{0,1},{1,0},{2,3},{3,2},{4,5},{5,4},{6,7},{7,6},{8,9},{9,8},{10,11... | collective-permute-start | bytes 3145736 | tf_op jit(solution)/shard_map/ppermute | solution.py:207
  60.8 8.9 %copy-start.13 = (f32[384,128]{1,0:T(8,128)S(1)}, f32[384,128]{1,0:T(8,128)}, u32[]{:S(2)}) copy-start(f32[384,128]{1,0:T(8,128)} %get-tuple-element.56) | copy-start | bytes 589828
  60.8 9.9 %copy-start.1 = (f32[1024,256]{1,0:T(8,128)S(1)}, f32[1024,256]{1,0:T(8,128)}, u32[]{:S(2)}) copy-start(f32[1024,256]{1,0:T(8,128)} %get-tuple-element.62) | copy-start | bytes 3145732
  68.6 2.1 %copy-start = (f32[1024,256]{1,0:T(8,128)S(1)}, f32[1024,256]{1,0:T(8,128)}, u32[]{:S(2)}) copy-start(f32[1024,256]{1,0:T(8,128)} %get-tuple-element.61) | copy-start | bytes 3145732
  69.7 0.9 copy-start.15
  71.0 13.8 %collective-permute-start.6 = (bf16[512,256]{1,0:T(8,128)(2,1)S(1)}, bf16[512,256]{1,0:T(8,128)(2,1)S(1)}, u32[]{:S(2)}, u32[]{:S(2)}) collective-permute-start(bf16[512,256]{1,0:T(8,128)(2,1)S(1)} %pad_maximum_fusion.6), channel_id=1, source_target_pairs={{4,0},{8,4},{12,8},{5,1},{9,5},{13,9},{6,2},{10,6},{14,10},{7,3},{... | collective-permute-start | bytes 786440 | tf_op jit(solution)/shard_map/ppermute | solution.py:20
  72.4 12.6 %collective-permute-start.7 = (bf16[256,256]{1,0:T(8,128)(2,1)S(1)}, bf16[256,256]{1,0:T(8,128)(2,1)S(1)}, u32[]{:S(2)}, u32[]{:S(2)}) collective-permute-start(bf16[256,256]{1,0:T(8,128)(2,1)S(1)} %get-tuple-element.76), channel_id=1, source_target_pairs={{12,0},{13,1},{14,2},{15,3},{28,16},{29,17},{30,18},{31,19}} | collective-permute-start | bytes 393224 | tf_op jit(solution)/shard_map/ppermute | solution.py:20
  73.7 15.0 %collective-permute-start.8 = (bf16[256,256]{1,0:T(8,128)(2,1)S(1)}, bf16[256,256]{1,0:T(8,128)(2,1)S(1)}, u32[]{:S(2)}, u32[]{:S(2)}) collective-permute-start(bf16[256,256]{1,0:T(8,128)(2,1)S(1)} %get-tuple-element.77), channel_id=1, source_target_pairs={{8,0},{12,4},{9,1},{13,5},{10,2},{14,6},{11,3},{15,7},{24,16},{28,... | collective-permute-start | bytes 393224 | tf_op jit(solution)/shard_map/ppermute | solution.py:20
  88.7 1.0 %copy-start.11 = (bf16[256,512]{1,0:T(8,128)(2,1)S(1)}, bf16[256,512]{1,0:T(8,128)(2,1)}, u32[]{:S(2)}) copy-start(bf16[256,512]{1,0:T(8,128)(2,1)} %get-tuple-element.52) | copy-start | bytes 786436
  88.7 1.0 %copy-start.12 = (bf16[256,512]{1,0:T(8,128)(2,1)S(1)}, bf16[256,512]{1,0:T(8,128)(2,1)}, u32[]{:S(2)}) copy-start(bf16[256,512]{1,0:T(8,128)(2,1)} %get-tuple-element.53) | copy-start | bytes 786436
  88.8 3.4 %collective-permute-start.9 = (f32[256,768]{1,0:T(8,128)S(1)}, f32[256,768]{1,0:T(8,128)S(1)}, u32[]{:S(2)}, u32[]{:S(2)}) collective-permute-start(f32[256,768]{1,0:T(8,128)S(1)} %pad_maximum_fusion), channel_id=1, source_target_pairs={{0,1},{1,0},{2,3},{3,2},{4,5},{5,4},{6,7},{7,6},{8,9},{9,8},{10,11... | collective-permute-start | bytes 2359304 | tf_op jit(solution)/shard_map/ppermute | solution.py:231
  89.8 1.2 %copy-start.6 = (bf16[256,1024]{1,0:T(8,128)(2,1)S(1)}, bf16[256,1024]{1,0:T(8,128)(2,1)}, u32[]{:S(2)}) copy-start(bf16[256,1024]{1,0:T(8,128)(2,1)} %get-tuple-element.63) | copy-start | bytes 1572868

commit v10 on v9

--- a/solution.py
+++ b/solution.py
@@ -24,80 +24,100 @@
     return jnp.where(half == 0, block[:, :HD], block[:, HD:])
 
 
-def attn_bwd_kernel(g0, gn, sink_ref, q_ref, do_ref, k_ref, v_ref, bias_ref, dq_ref, dk_ref, dv_ref):
-    g_rel = pl.program_id(0)
-    g = g_rel + g0
+def attn_bwd_kernel(g0, gn, pair, sink_ref, q_ref, do_ref, k_ref, v_ref, bias_ref, dq_ref, dk_ref, dv_ref):
+    t = pl.program_id(0)
     i = pl.program_id(1)
-    heads = q_ref.shape[1] // HD
-
-    @pl.when((g_rel == 0) & (i == 0))
+    heads = q_ref.shape[1] // (HD * pair)
+
+    @pl.when((t == 0) & (i == 0))
     def _():
         dk_ref[...] = jnp.zeros_like(dk_ref)
         dv_ref[...] = jnp.zeros_like(dv_ref)
 
-    k = pick_half(k_ref[...], g % 2)
-    v = pick_half(v_ref[...], g % 2)
     bias = bias_ref[...]
-    dk_acc = None
-    dv_acc = None
+    k_block = k_ref[...]
+    v_block = v_ref[...]
     dq_parts = []
-    for j in range(heads):
-        q = q_ref[:, j * HD:(j + 1) * HD]
-        do = do_ref[:, j * HD:(j + 1) * HD]
-        sink = sink_ref[g, j]
-        s = lax.dot_general(q, k, NT_DIMS, preferred_element_type=jnp.float32) + bias
-        row_max = jnp.maximum(jnp.max(s, axis=1, keepdims=True), sink)
-        e = jnp.exp(s - row_max)
-        total = jnp.sum(e, axis=1, keepdims=True) + jnp.exp(sink - row_max)
-        p = e * (1.0 / total)
-        p_low = p.astype(jnp.bfloat16)
-        dp = lax.dot_general(do, v, NT_DIMS, preferred_element_type=jnp.float32)
-        delta = jnp.sum(p_low.astype(jnp.float32) * dp, axis=1, keepdims=True)
-        ds_low = (p * (dp - delta)).astype(jnp.bfloat16)
-        dq_parts.append(
-            (jnp.dot(ds_low, k, preferred_element_type=jnp.float32) * 0.125).astype(dq_ref.dtype)
-        )
-        dk = jnp.dot(ds_low.T, q, preferred_element_type=jnp.float32)
-        dv = jnp.dot(p_low.T, do, preferred_element_type=jnp.float32)
-        dk_acc = dk if dk_acc is None else dk_acc + dk
-        dv_acc = dv if dv_acc is None else dv_acc + dv
+    dk_parts = []
+    dv_parts = []
+    for h in range(pair):
+        g = g0 + t * pair + h
+        if pair == 2:
+            k = k_block[:, h * HD:(h + 1) * HD]
+            v = v_block[:, h * HD:(h + 1) * HD]
+        else:
+            k = pick_half(k_block, g % 2)
+            v = pick_half(v_block, g % 2)
+        dk_acc = None
+        dv_acc = None
+        for j in range(heads):
+            col = (h * heads + j) * HD
+            q = q_ref[:, col:col + HD]
+            do = do_ref[:, col:col + HD]
+            sink = sink_ref[g, j]
+            s = lax.dot_general(q, k, NT_DIMS, preferred_element_type=jnp.float32) + bias
+            row_max = jnp.maximum(jnp.max(s, axis=1, keepdims=True), sink)
+            e = jnp.exp(s - row_max)
+            total = jnp.sum(e, axis=1, keepdims=True) + jnp.exp(sink - row_max)
+            p = e * (1.0 / total)
+            p_low = p.astype(jnp.bfloat16)
+            dp = lax.dot_general(do, v, NT_DIMS, preferred_element_type=jnp.float32)
+            delta = jnp.sum(p_low.astype(jnp.float32) * dp, axis=1, keepdims=True)
+            ds_low = (p * (dp - delta)).astype(jnp.bfloat16)
+            dq_parts.append(
+                (jnp.dot(ds_low, k, preferred_element_type=jnp.float32) * 0.125).astype(dq_ref.dtype)
+            )
+            dk = jnp.dot(ds_low.T, q, preferred_element_type=jnp.float32)
+            dv = jnp.dot(p_low.T, do, preferred_element_type=jnp.float32)
+            dk_acc = dk if dk_acc is None else dk_acc + dk
+            dv_acc = dv if dv_acc is None else dv_acc + dv
+        dk_parts.append(dk_acc)
+        dv_parts.append(dv_acc)
     dq_ref[...] = jnp.concatenate(dq_parts, axis=1)
-
-    for gg in range(gn):
-        @pl.when(g_rel == gg)
+    dk_step = jnp.concatenate(dk_parts, axis=1) if pair == 2 else dk_parts[0]
+    dv_step = jnp.concatenate(dv_parts, axis=1) if pair == 2 else dv_parts[0]
+    wide = pair * HD
+
+    for tt in range(gn // pair):
+        @pl.when(t == tt)
         def _():
-            dk_ref[:, gg * HD:(gg + 1) * HD] += dk_acc
-            dv_ref[:, gg * HD:(gg + 1) * HD] += dv_acc
+            dk_ref[:, tt * wide:(tt + 1) * wide] += dk_step
+            dv_ref[:, tt * wide:(tt + 1) * wide] += dv_step
 
 
 def attn_bwd(sinks, queries, grads, keys, values, bias, g0, gn):
     n = queries.shape[0]
     m = keys.shape[0]
     heads = sinks.shape[1]
+    pair = 2 if (g0 % 2 == 0 and gn % 2 == 0) else 1
     rows = n
     while rows > 8 and rows * m > (1 << 18):
         rows //= 2
-    grid = (gn, n // rows)
-    width = heads * HD
+    grid = (gn // pair, n // rows)
+    width = heads * HD * pair
+    if pair == 2:
+        key_map = lambda t, i: (0, g0 // 2 + t)
+    else:
+        key_map = lambda t, i: (0, (g0 + t) // 2)
 
     return pl.pallas_call(
-        functools.partial(attn_bwd_kernel, g0, gn),
+        functools.partial(attn_bwd_kernel, g0, gn, pair),
         grid=grid,
         in_specs=[
             pl.BlockSpec(memory_space=pltpu.SMEM),
-            pl.BlockSpec((rows, width), lambda g, i: (i, g + g0)),
-            pl.BlockSpec((rows, width), lambda g, i: (i, g + g0)),
-            pl.BlockSpec((m, 2 * HD), lambda g, i: (0, (g + g0) // 2)),
-            pl.BlockSpec((m, 2 * HD), lambda g, i: (0, (g + g0) // 2)),
-            pl.BlockSpec((rows, m), lambda g, i: (i, 0)),
+            pl.BlockSpec((rows, width), lambda t, i: (i, g0 // pair + t)),
+            pl.BlockSpec((rows, width), lambda t, i: (i, g0 // pair + t)),
+            pl.BlockSpec((m, 2 * HD), key_map),
+            pl.BlockSpec((m, 2 * HD), key_map),
+            pl.BlockSpec((rows, m), lambda t, i: (i, 0)),
         ],
         out_specs=[
-            pl.BlockSpec((rows, width), lambda g, i: (i, g)),
-            pl.BlockSpec((m, gn * HD), lambda g, i: (0, 0)),
-            pl.BlockSpec((m, gn * HD), lambda g, i: (0, 0)),
+            pl.BlockSpec((rows, width), lambda t, i: (i, t)),
+            pl.BlockSpec((m, gn * HD), lambda t, i: (0, 0)),
+            pl.BlockSpec((m, gn * HD), lambda t, i: (0, 0)),
         ],
         out_shape=[
-            jax.ShapeDtypeStruct((n, gn * width), jnp.bfloat16),
+            jax.ShapeDtypeStruct((n, gn * heads * HD), jnp.bfloat16),
             jax.ShapeDtypeStruct((m, gn * HD), jnp.float32),
             jax.ShapeDtypeStruct((m, gn * HD), jnp.float32),
         ],

time: 94.4 us -> 92.6 us (0.981)
  Pallas kernels: 38.9 us -> 37.1 us
    pallas_call x3, Pallas kernels: 38.9 us -> 37.1 us  [attn_bwd(): pl.pallas_call(functools.partial(attn_bwd_kernel, g0, gn, pair), grid=gri...]
  transfers between devices with their start and end apart: 10 -> 10, of which waited for: 3 -> 3; matrix products, arithmetic and copies ran while one was open for 12% -> 12% of each run, Pallas kernels for 17% -> 16%
where the time goes in v10:
time: 92.6 us; the launch traced here: 91.9 us
  Pallas kernels  37.1 us (40%)
  starting transfers between devices  16.9 us (18%)
  local copies, waits for them, and re-layouts  14 us (15%)
  waiting for transfers between devices  13.9 us (15%)
  other arithmetic  8.88 us (10%)
  between operations  1.14 us (1%)
    pallas_call x3, Pallas kernels, attn_bwd(): pl.pallas_call(functools.partial(attn_bwd_kernel, g0, gn, pair), grid=gri...  37.1 us
    ppermute x7, starting transfers between devices, passed_along(): lax.ppermute(value, axis, [(source, source + steps) for source in range(f...  16.5 us
    ppermute x7, waiting for transfers between devices, passed_along(): lax.ppermute(value, axis, [(source, source + steps) for source in range(f...  13.6 us
    unnamed x42, local copies, waits for them, and re-layouts  8.07 us
    select_n x2, other arithmetic, make_bias(): return jnp.where(visible, 0.0, NEG).astype(jnp.float32)  2.34 us
  transfers between devices with their start and end apart: 10, of which 3 were waited for; matrix products, arithmetic and copies ran while one was open for 12% of the time, Pallas kernels for 16%

profile of v10, /device:TPU:0, one launch (start us, length us, event | category | flops | bytes accessed | tf_op | source)
XLA Modules:
  0.0 91.9 jit_solution(7788109031300708283)
XLA Ops:
  0.6 0.7 convert.17
  1.4 0.8 slice.148
  2.3 0.8 slice.149
  3.1 4.9 %collective-permute-start = (bf16[144,512]{1,0:T(8,128)(2,1)S(1)}, bf16[144,512]{1,0:T(8,128)(2,1)S(1)}, u32[]{:S(2)}, u32[]{:S(2)}) collective-permute-start(bf16[144,512]{1,0:T(8,128)(2,1)S(1)} %pad_maximum_fusion.9), channel_id=1, source_target_pairs={{0,4},{4,8},{8,12},{1,5},{5,9},{9,13},{2,6},{6,10},{10,14},{3,7},{... | collective-permute-start | bytes 442376 | tf_op jit(solution)/shard_map/ppermute | solution.py:20
  8.2 0.2 broadcast_multiply_fusion.1
  8.4 0.8 copy-done.3
  9.2 0.2 broadcast_multiply_fusion
  9.4 0.7 copy-done.7
  10.1 0.1 copy-done.8
  10.2 0.9 copy.17
  11.1 0.2 copy-done.4
  11.3 0.9 copy.18
  12.2 0.9 copy.20
  13.1 0.2 copy-done.5
  13.4 0.9 copy.21
  14.3 3.5 %collective-permute-start.3 = (bf16[272,256]{1,0:T(8,128)(2,1)S(1)}, bf16[272,256]{1,0:T(8,128)(2,1)S(1)}, u32[]{:S(2)}, u32[]{:S(2)}) collective-permute-start(bf16[272,256]{1,0:T(8,128)(2,1)S(1)} %pad_maximum_fusion.10), channel_id=1, source_target_pairs={{0,4},{4,8},{8,12},{1,5},{5,9},{9,13},{2,6},{6,10},{10,14},{3,7},{... | collective-permute-start | bytes 417800 | tf_op jit(solution)/shard_map/ppermute | solution.py:20
  17.8 2.9 %collective-permute-start.2 = (bf16[272,256]{1,0:T(8,128)(2,1)S(1)}, bf16[272,256]{1,0:T(8,128)(2,1)S(1)}, u32[]{:S(2)}, u32[]{:S(2)}) collective-permute-start(bf16[272,256]{1,0:T(8,128)(2,1)S(1)} %pad_maximum_fusion.10), channel_id=1, source_target_pairs={{0,8},{4,12},{1,9},{5,13},{2,10},{6,14},{3,11},{7,15},{16,24},{20,... | collective-permute-start | bytes 417800 | tf_op jit(solution)/shard_map/ppermute | solution.py:20
  20.7 1.3 %collective-permute-start.1 = (bf16[272,256]{1,0:T(8,128)(2,1)S(1)}, bf16[272,256]{1,0:T(8,128)(2,1)S(1)}, u32[]{:S(2)}, u32[]{:S(2)}) collective-permute-start(bf16[272,256]{1,0:T(8,128)(2,1)S(1)} %pad_maximum_fusion.10), channel_id=1, source_target_pairs={{0,12},{1,13},{2,14},{3,15},{16,28},{17,29},{18,30},{19,31}} | collective-permute-start | bytes 417800 | tf_op jit(solution)/shard_map/ppermute | solution.py:20
  22.1 0.7 copy-done.16
  22.8 1.0 %fusion.7.bias_ref = f32[256,384]{1,0:T(8,128)} fusion(s32[384]{0:T(512)S(1)} %get-tuple-element.91, s32[384]{0:T(512)S(1)} %get-tuple-element.92, s32[256]{0:T(256)S(1)} %iota_add_fusion.2, s32[256]{0:T(256)S(1)} %copy-done.16, pred[384]{0:T(512)(128)(4,1)S(1)} %broadcast_compare_fusion.1), kind=kLoop, calls=%fused_computation.20 | loop fusion | flops 786432 | bytes 398720 | tf_op jit(solution)/shard_map/jit(_where)/select_n | solution.py:141
  23.7 0.8 pad_maximum_fusion.7
  24.5 7.3 %shard_map.154 = (bf16[256,512]{1,0:T(8,128)(2,1)}, f32[384,128]{1,0:T(8,128)}, f32[384,128]{1,0:T(8,128)}) custom-call(f32[4,4]{1,0:T(4,128)} %sink_ref.4, bf16[256,1024]{1,0:T(8,128)(2,1)} %bitcast.18, bf16[256,1024]{1,0:T(8,128)(2,1)} %bitcast.20, bf16[384,256]{1,0:T(8,128)(2,1)} %get-tuple-element.89.k_ref, bf16[384,256]{1,0:T(8,128)(2,1)} %get-tuple-element.90.v_ref, ...), custom_call_target="tpu_custom_call" | custom-call | flops 503316480 | bytes 2555904 | tf_op jit(solution)/shard_map/pallas_call | solution.py:103
  32.0 0.1 collective-permute-start.4
  32.1 1.4 %fusion.2.bias_ref = f32[256,1024]{1,0:T(8,128)} fusion(s32[1024]{0:T(1024)S(1)} %pad_add_fusion, s32[1024]{0:T(1024)S(1)} %iota_add_fusion, s32[256]{0:T(256)S(1)} %iota_add_fusion.2, s32[256]{0:T(256)S(1)} %copy-done.16, pred[1024]{0:T(1024)(128)(4,1)S(1)} %broadcast_compare_fusion), kind=kLoop, calls=%fused_computation.4 | loop fusion | flops 1572864 | bytes 1059840 | tf_op jit(solution)/shard_map/jit(_where)/select_n | solution.py:141
  33.4 0.3 collective-permute-done.4
  33.8 0.8 pad_maximum_fusion.3.v_ref
  34.7 0.8 pad_maximum_fusion.2.k_ref
  35.5 22.3 %shard_map.156 = (bf16[256,1024]{1,0:T(8,128)(2,1)}, f32[1024,256]{1,0:T(8,128)}, f32[1024,256]{1,0:T(8,128)}) custom-call(f32[4,4]{1,0:T(4,128)} %sink_ref.5, bf16[256,1024]{1,0:T(8,128)(2,1)} %bitcast.22, bf16[256,1024]{1,0:T(8,128)(2,1)} %bitcast.23, bf16[1024,256]{1,0:T(8,128)(2,1)} %pad_maximum_fusion.2.k_ref, ...), custom_call_target="tpu_custom_call" | custom-call | flops 2684354560 | bytes 7340032 | tf_op jit(solution)/shard_map/pallas_call | solution.py:103
  57.8 1.4 %broadcast_select_fusion = f32[1024,256]{1,0:T(8,128)S(1)} fusion(f32[1024,256]{1,0:T(8,128)} %get-tuple-element.62, f32[1024,256]{1,0:T(8,128)} %get-tuple-element.61, pred[]{:T(512)S(6)} %eq.14), kind=kLoop, calls=%fused_computation.15 | loop fusion | flops 262144 | bytes 3145729 | tf_op jit(solution)/shard_map/jit(_where)/select_n | solution.py:225
  59.2 0.2 collective-permute-start.5
  59.4 7.4 %shard_map.155 = (bf16[256,512]{1,0:T(8,128)(2,1)}, f32[384,128]{1,0:T(8,128)}, f32[384,128]{1,0:T(8,128)}) custom-call(f32[4,4]{1,0:T(4,128)} %sink_ref.4, bf16[256,1024]{1,0:T(8,128)(2,1)} %bitcast.19, bf16[256,1024]{1,0:T(8,128)(2,1)} %bitcast.21, bf16[384,256]{1,0:T(8,128)(2,1)} %get-tuple-element.89.k_ref, bf16[384,256]{1,0:T(8,128)(2,1)} %get-tuple-element.90.v_ref, ...), custom_call_target="tpu_custom_call" | custom-call | flops 503316480 | bytes 2555904 | tf_op jit(solution)/shard_map/pallas_call | solution.py:103
  66.9 1.0 %constant_dynamic-update-slice_fusion = f32[384,256]{1,0:T(8,128)S(1)} fusion(f32[384,256]{1,0:T(8,128)S(1)} %constant_dynamic-update-slice_fusion.1, f32[384,128]{1,0:T(8,128)} %get-tuple-element.55), kind=kLoop, calls=%fused_computation.46 | loop fusion | bytes 393216 | tf_op jit(solution)/shard_map/concatenate | solution.py:231
  67.9 0.9 copy-done.15
  68.9 0.2 fusion.12
  69.2 1.3 %collective-permute-start.6 = (bf16[512,256]{1,0:T(8,128)(2,1)S(1)}, bf16[512,256]{1,0:T(8,128)(2,1)S(1)}, u32[]{:S(2)}, u32[]{:S(2)}) collective-permute-start(bf16[512,256]{1,0:T(8,128)(2,1)S(1)} %pad_maximum_fusion.6), channel_id=1, source_target_pairs={{4,0},{8,4},{12,8},{5,1},{9,5},{13,9},{6,2},{10,6},{14,10},{7,3},{... | collective-permute-start | bytes 786440 | tf_op jit(solution)/shard_map/ppermute | solution.py:20
  70.6 1.3 %collective-permute-start.7 = (bf16[256,256]{1,0:T(8,128)(2,1)S(1)}, bf16[256,256]{1,0:T(8,128)(2,1)S(1)}, u32[]{:S(2)}, u32[]{:S(2)}) collective-permute-start(bf16[256,256]{1,0:T(8,128)(2,1)S(1)} %get-tuple-element.76), channel_id=1, source_target_pairs={{12,0},{13,1},{14,2},{15,3},{28,16},{29,17},{30,18},{31,19}} | collective-permute-start | bytes 393224 | tf_op jit(solution)/shard_map/ppermute | solution.py:20
  71.9 1.3 %collective-permute-start.8 = (bf16[256,256]{1,0:T(8,128)(2,1)S(1)}, bf16[256,256]{1,0:T(8,128)(2,1)S(1)}, u32[]{:S(2)}, u32[]{:S(2)}) collective-permute-start(bf16[256,256]{1,0:T(8,128)(2,1)S(1)} %get-tuple-element.77), channel_id=1, source_target_pairs={{8,0},{12,4},{9,1},{13,5},{10,2},{14,6},{11,3},{15,7},{24,16},{28,... | collective-permute-start | bytes 393224 | tf_op jit(solution)/shard_map/ppermute | solution.py:20
  73.2 10.2 %collective-permute-done.6 = bf16[512,256]{1,0:T(8,128)(2,1)S(1)} collective-permute-done((bf16[512,256]{1,0:T(8,128)(2,1)S(1)}, bf16[512,256]{1,0:T(8,128)(2,1)S(1)}, u32[]{:S(2)}, u32[]{:S(2)}) %collective-permute-start.6) | collective-permute-done | bytes 262176 | tf_op jit(solution)/shard_map/ppermute | solution.py:20
  83.4 0.1 fusion.8
  83.5 3.4 %collective-permute-done.8 = bf16[256,256]{1,0:T(8,128)(2,1)S(1)} collective-permute-done((bf16[256,256]{1,0:T(8,128)(2,1)S(1)}, bf16[256,256]{1,0:T(8,128)(2,1)S(1)}, u32[]{:S(2)}, u32[]{:S(2)}) %collective-permute-start.8) | collective-permute-done | bytes 131104 | tf_op jit(solution)/shard_map/ppermute | solution.py:20
  87.0 0.1 collective-permute-start.9
  87.1 0.8 copy-done.11
  87.9 0.1 copy-done.12
  88.0 1.2 %reshape.119 = bf16[256,4,256]{2,1,0:T(4,128)(2,1)} reshape(bf16[256,1024]{1,0:T(8,128)(2,1)S(1)} %pad_maximum_fusion.1) | data formatting | bytes 1048576 | tf_op jit(solution)/shard_map/reshape | solution.py:257
  89.2 1.2 %reshape.121 = bf16[256,4,256]{2,1,0:T(4,128)(2,1)} reshape(bf16[256,1024]{1,0:T(8,128)(2,1)S(1)} %copy-done.6) | data formatting | bytes 1048576 | tf_op jit(solution)/shard_map/reshape | solution.py:260
  90.4 0.1 fusion.3
  90.5 0.7 fusion.14
  91.2 0.7 select_convert_fusion
  (69 shorter events, 0.7 us)
Async XLA Ops:
  0.6 7.5 %copy-start.2 = (bf16[256,4,256]{2,1,0:T(4,128)(2,1)S(1)}, bf16[256,4,256]{2,1,0:T(4,128)(2,1)}, u32[]{:S(2)}) copy-start(bf16[256,4,256]{2,1,0:T(4,128)(2,1)} %param.16) | copy-start | bytes 1572868
  3.1 11.1 %collective-permute-start = (bf16[144,512]{1,0:T(8,128)(2,1)S(1)}, bf16[144,512]{1,0:T(8,128)(2,1)S(1)}, u32[]{:S(2)}, u32[]{:S(2)}) collective-permute-start(bf16[144,512]{1,0:T(8,128)(2,1)S(1)} %pad_maximum_fusion.9), channel_id=1, source_target_pairs={{0,4},{4,8},{8,12},{1,5},{5,9},{9,13},{2,6},{6,10},{10,14},{3,7},{... | collective-permute-start | bytes 442376 | tf_op jit(solution)/shard_map/ppermute | solution.py:20
  8.1 1.0 %copy-start.3 = (bf16[256,4,256]{2,1,0:T(4,128)(2,1)S(1)}, bf16[256,4,256]{2,1,0:T(4,128)(2,1)}, u32[]{:S(2)}) copy-start(bf16[256,4,256]{2,1,0:T(4,128)(2,1)} %param.21) | copy-start | bytes 1572868
  9.2 0.9 copy-start.7
  9.2 1.0 %copy-start.8 = (bf16[256,256]{1,0:T(8,128)(2,1)S(1)}, bf16[256,256]{1,0:T(8,128)(2,1)}, u32[]{:S(2)}) copy-start(bf16[256,256]{1,0:T(8,128)(2,1)} %param.22) | copy-start | bytes 393220
  10.2 1.1 %copy-start.4 = (bf16[256,4,256]{2,1,0:T(4,128)(2,1)S(1)}, bf16[256,4,256]{2,1,0:T(4,128)(2,1)}, u32[]{:S(2)}) copy-start(bf16[256,4,256]{2,1,0:T(4,128)(2,1)} %param.19) | copy-start | bytes 1572868
  12.2 1.1 %copy-start.5 = (bf16[256,4,256]{2,1,0:T(4,128)(2,1)S(1)}, bf16[256,4,256]{2,1,0:T(4,128)(2,1)}, u32[]{:S(2)}) copy-start(bf16[256,4,256]{2,1,0:T(4,128)(2,1)} %param.24) | copy-start | bytes 1572868
  14.3 17.6 %collective-permute-start.3 = (bf16[272,256]{1,0:T(8,128)(2,1)S(1)}, bf16[272,256]{1,0:T(8,128)(2,1)S(1)}, u32[]{:S(2)}, u32[]{:S(2)}) collective-permute-start(bf16[272,256]{1,0:T(8,128)(2,1)S(1)} %pad_maximum_fusion.10), channel_id=1, source_target_pairs={{0,4},{4,8},{8,12},{1,5},{5,9},{9,13},{2,6},{6,10},{10,14},{3,7},{... | collective-permute-start | bytes 417800 | tf_op jit(solution)/shard_map/ppermute | solution.py:20
  17.8 14.1 %collective-permute-start.2 = (bf16[272,256]{1,0:T(8,128)(2,1)S(1)}, bf16[272,256]{1,0:T(8,128)(2,1)S(1)}, u32[]{:S(2)}, u32[]{:S(2)}) collective-permute-start(bf16[272,256]{1,0:T(8,128)(2,1)S(1)} %pad_maximum_fusion.10), channel_id=1, source_target_pairs={{0,8},{4,12},{1,9},{5,13},{2,10},{6,14},{3,11},{7,15},{16,24},{20,... | collective-permute-start | bytes 417800 | tf_op jit(solution)/shard_map/ppermute | solution.py:20
  20.7 11.1 %collective-permute-start.1 = (bf16[272,256]{1,0:T(8,128)(2,1)S(1)}, bf16[272,256]{1,0:T(8,128)(2,1)S(1)}, u32[]{:S(2)}, u32[]{:S(2)}) collective-permute-start(bf16[272,256]{1,0:T(8,128)(2,1)S(1)} %pad_maximum_fusion.10), channel_id=1, source_target_pairs={{0,12},{1,13},{2,14},{3,15},{16,28},{17,29},{18,30},{19,31}} | collective-permute-start | bytes 417800 | tf_op jit(solution)/shard_map/ppermute | solution.py:20
  22.1 0.7 copy-start.16
  22.8 1.0 %copy-start.9 = (bf16[256,256]{1,0:T(8,128)(2,1)S(1)}, bf16[256,256]{1,0:T(8,128)(2,1)}, u32[]{:S(2)}) copy-start(bf16[256,256]{1,0:T(8,128)(2,1)} %param.17) | copy-start | bytes 393220
  22.8 1.0 %copy-start.10 = (bf16[256,256]{1,0:T(8,128)(2,1)S(1)}, bf16[256,256]{1,0:T(8,128)(2,1)}, u32[]{:S(2)}) copy-start(bf16[256,256]{1,0:T(8,128)(2,1)} %param.18) | copy-start | bytes 393220
  32.0 1.8 %collective-permute-start.4 = (bf16[816,256]{1,0:T(8,128)(2,1)S(1)}, bf16[816,256]{1,0:T(8,128)(2,1)S(1)}, u32[]{:S(2)}, u32[]{:S(2)}) collective-permute-start(bf16[816,256]{1,0:T(8,128)(2,1)S(1)} %pad_maximum_fusion.4), channel_id=1, source_target_pairs={{0,1},{1,0},{2,3},{3,2},{4,5},{5,4},{6,7},{7,6},{8,9},{9,8},{10,11... | collective-permute-start | bytes 1253384 | tf_op jit(solution)/shard_map/ppermute | solution.py:207
  59.2 7.7 %copy-start.14 = (f32[384,128]{1,0:T(8,128)S(1)}, f32[384,128]{1,0:T(8,128)}, u32[]{:S(2)}) copy-start(f32[384,128]{1,0:T(8,128)} %get-tuple-element.54) | copy-start | bytes 589828
  59.2 9.7 %collective-permute-start.5 = (f32[1024,256]{1,0:T(8,128)S(1)}, f32[1024,256]{1,0:T(8,128)S(1)}, u32[]{:S(2)}, u32[]{:S(2)}) collective-permute-start(f32[1024,256]{1,0:T(8,128)S(1)} %broadcast_select_fusion), channel_id=1, source_target_pairs={{0,1},{1,0},{2,3},{3,2},{4,5},{5,4},{6,7},{7,6},{8,9},{9,8},{10,11... | collective-permute-start | bytes 3145736 | tf_op jit(solution)/shard_map/ppermute | solution.py:227
  59.4 8.5 %copy-start.13 = (f32[384,128]{1,0:T(8,128)S(1)}, f32[384,128]{1,0:T(8,128)}, u32[]{:S(2)}) copy-start(f32[384,128]{1,0:T(8,128)} %get-tuple-element.56) | copy-start | bytes 589828
  59.4 9.5 %copy-start.1 = (f32[1024,256]{1,0:T(8,128)S(1)}, f32[1024,256]{1,0:T(8,128)}, u32[]{:S(2)}) copy-start(f32[1024,256]{1,0:T(8,128)} %get-tuple-element.62) | copy-start | bytes 3145732
  66.8 2.1 %copy-start = (f32[1024,256]{1,0:T(8,128)S(1)}, f32[1024,256]{1,0:T(8,128)}, u32[]{:S(2)}) copy-start(f32[1024,256]{1,0:T(8,128)} %get-tuple-element.61) | copy-start | bytes 3145732
  67.9 0.9 %copy-start.15 = (f32[384,128]{1,0:T(8,128)S(1)}, f32[384,128]{1,0:T(8,128)}, u32[]{:S(2)}) copy-start(f32[384,128]{1,0:T(8,128)} %get-tuple-element.57) | copy-start | bytes 589828
  69.2 14.1 %collective-permute-start.6 = (bf16[512,256]{1,0:T(8,128)(2,1)S(1)}, bf16[512,256]{1,0:T(8,128)(2,1)S(1)}, u32[]{:S(2)}, u32[]{:S(2)}) collective-permute-start(bf16[512,256]{1,0:T(8,128)(2,1)S(1)} %pad_maximum_fusion.6), channel_id=1, source_target_pairs={{4,0},{8,4},{12,8},{5,1},{9,5},{13,9},{6,2},{10,6},{14,10},{7,3},{... | collective-permute-start | bytes 786440 | tf_op jit(solution)/shard_map/ppermute | solution.py:20
  70.6 12.9 %collective-permute-start.7 = (bf16[256,256]{1,0:T(8,128)(2,1)S(1)}, bf16[256,256]{1,0:T(8,128)(2,1)S(1)}, u32[]{:S(2)}, u32[]{:S(2)}) collective-permute-start(bf16[256,256]{1,0:T(8,128)(2,1)S(1)} %get-tuple-element.76), channel_id=1, source_target_pairs={{12,0},{13,1},{14,2},{15,3},{28,16},{29,17},{30,18},{31,19}} | collective-permute-start | bytes 393224 | tf_op jit(solution)/shard_map/ppermute | solution.py:20
  71.9 15.0 %collective-permute-start.8 = (bf16[256,256]{1,0:T(8,128)(2,1)S(1)}, bf16[256,256]{1,0:T(8,128)(2,1)S(1)}, u32[]{:S(2)}, u32[]{:S(2)}) collective-permute-start(bf16[256,256]{1,0:T(8,128)(2,1)S(1)} %get-tuple-element.77), channel_id=1, source_target_pairs={{8,0},{12,4},{9,1},{13,5},{10,2},{14,6},{11,3},{15,7},{24,16},{28,... | collective-permute-start | bytes 393224 | tf_op jit(solution)/shard_map/ppermute | solution.py:20
  86.9 1.0 %copy-start.11 = (bf16[256,512]{1,0:T(8,128)(2,1)S(1)}, bf16[256,512]{1,0:T(8,128)(2,1)}, u32[]{:S(2)}) copy-start(bf16[256,512]{1,0:T(8,128)(2,1)} %get-tuple-element.52) | copy-start | bytes 786436
  86.9 1.0 %copy-start.12 = (bf16[256,512]{1,0:T(8,128)(2,1)S(1)}, bf16[256,512]{1,0:T(8,128)(2,1)}, u32[]{:S(2)}) copy-start(bf16[256,512]{1,0:T(8,128)(2,1)} %get-tuple-element.53) | copy-start | bytes 786436
  87.0 3.4 %collective-permute-start.9 = (f32[256,768]{1,0:T(8,128)S(1)}, f32[256,768]{1,0:T(8,128)S(1)}, u32[]{:S(2)}, u32[]{:S(2)}) collective-permute-start(f32[256,768]{1,0:T(8,128)S(1)} %pad_maximum_fusion), channel_id=1, source_target_pairs={{0,1},{1,0},{2,3},{3,2},{4,5},{5,4},{6,7},{7,6},{8,9},{9,8},{10,11... | collective-permute-start | bytes 2359304 | tf_op jit(solution)/shard_map/ppermute | solution.py:251
  88.0 1.2 %copy-start.6 = (bf16[256,1024]{1,0:T(8,128)(2,1)S(1)}, bf16[256,1024]{1,0:T(8,128)(2,1)}, u32[]{:S(2)}) copy-start(bf16[256,1024]{1,0:T(8,128)(2,1)} %get-tuple-element.63) | copy-start | bytes 1572868

commit v11 on v10

--- a/solution.py
+++ b/solution.py
@@ -42,7 +42,7 @@
     dv_parts = []
     for h in range(pair):
         g = g0 + t * pair + h
-        if pair == 2:
+        if pair >= 2:
             k = k_block[:, h * HD:(h + 1) * HD]
             v = v_block[:, h * HD:(h + 1) * HD]
         else:
@@ -74,8 +74,8 @@
         dk_parts.append(dk_acc)
         dv_parts.append(dv_acc)
     dq_ref[...] = jnp.concatenate(dq_parts, axis=1)
-    dk_step = jnp.concatenate(dk_parts, axis=1) if pair == 2 else dk_parts[0]
-    dv_step = jnp.concatenate(dv_parts, axis=1) if pair == 2 else dv_parts[0]
+    dk_step = jnp.concatenate(dk_parts, axis=1) if pair >= 2 else dk_parts[0]
+    dv_step = jnp.concatenate(dv_parts, axis=1) if pair >= 2 else dv_parts[0]
     wide = pair * HD
 
     for tt in range(gn // pair):
@@ -89,15 +89,22 @@
     n = queries.shape[0]
     m = keys.shape[0]
     heads = sinks.shape[1]
-    pair = 2 if (g0 % 2 == 0 and gn % 2 == 0) else 1
+    if gn % 2 == 0 and g0 % gn == 0:
+        pair = gn
+    elif gn % 2 == 0 and g0 % 2 == 0:
+        pair = 2
+    else:
+        pair = 1
     rows = n
     while rows > 8 and rows * m > (1 << 18):
         rows //= 2
     grid = (gn // pair, n // rows)
     width = heads * HD * pair
-    if pair == 2:
-        key_map = lambda t, i: (0, g0 // 2 + t)
+    if pair >= 2:
+        key_width = pair * HD
+        key_map = lambda t, i: (0, g0 // pair + t)
     else:
+        key_width = 2 * HD
         key_map = lambda t, i: (0, (g0 + t) // 2)
 
     return pl.pallas_call(
@@ -107,8 +114,8 @@
             pl.BlockSpec(memory_space=pltpu.SMEM),
             pl.BlockSpec((rows, width), lambda t, i: (i, g0 // pair + t)),
             pl.BlockSpec((rows, width), lambda t, i: (i, g0 // pair + t)),
-            pl.BlockSpec((m, 2 * HD), key_map),
-            pl.BlockSpec((m, 2 * HD), key_map),
+            pl.BlockSpec((m, key_width), key_map),
+            pl.BlockSpec((m, key_width), key_map),
             pl.BlockSpec((rows, m), lambda t, i: (i, 0)),
         ],
         out_specs=[

time: 92.6 us -> 92.3 us (level)
  no operation moved by 1% of the time
where the time goes in v11:
time: 92.3 us; the launch traced here: 91.6 us
  Pallas kernels  36.8 us (40%)
  starting transfers between devices  16.9 us (18%)
  local copies, waits for them, and re-layouts  14 us (15%)
  waiting for transfers between devices  13.9 us (15%)
  other arithmetic  8.87 us (10%)
  between operations  1.14 us (1%)
    pallas_call x3, Pallas kernels, attn_bwd(): pl.pallas_call(functools.partial(attn_bwd_kernel, g0, gn, pair), grid=gri...  36.8 us
    ppermute x7, starting transfers between devices, passed_along(): lax.ppermute(value, axis, [(source, source + steps) for source in range(f...  16.5 us
    ppermute x7, waiting for transfers between devices, passed_along(): lax.ppermute(value, axis, [(source, source + steps) for source in range(f...  13.6 us
    unnamed x42, local copies, waits for them, and re-layouts  8.07 us
    select_n x2, other arithmetic, make_bias(): return jnp.where(visible, 0.0, NEG).astype(jnp.float32)  2.34 us
  transfers between devices with their start and end apart: 10, of which 3 were waited for; matrix products, arithmetic and copies ran while one was open for 12% of the time, Pallas kernels for 16%

profile of v11, /device:TPU:0, one launch (start us, length us, event | category | flops | bytes accessed | tf_op | source)
XLA Modules:
  0.0 91.6 jit_solution(10516439239840921534)
XLA Ops:
  0.6 0.7 convert.17
  1.4 0.8 slice.148
  2.3 0.8 slice.149
  3.1 4.9 %collective-permute-start = (bf16[144,512]{1,0:T(8,128)(2,1)S(1)}, bf16[144,512]{1,0:T(8,128)(2,1)S(1)}, u32[]{:S(2)}, u32[]{:S(2)}) collective-permute-start(bf16[144,512]{1,0:T(8,128)(2,1)S(1)} %pad_maximum_fusion.9), channel_id=1, source_target_pairs={{0,4},{4,8},{8,12},{1,5},{5,9},{9,13},{2,6},{6,10},{10,14},{3,7},{... | collective-permute-start | bytes 442376 | tf_op jit(solution)/shard_map/ppermute | solution.py:20
  8.2 0.2 broadcast_multiply_fusion.1
  8.4 0.8 copy-done.3
  9.2 0.2 broadcast_multiply_fusion
  9.4 0.7 copy-done.7
  10.1 0.1 copy-done.8
  10.2 0.9 copy.17
  11.1 0.2 copy-done.4
  11.3 0.9 copy.18
  12.2 0.9 copy.20
  13.1 0.2 copy-done.5
  13.4 0.9 copy.21
  14.3 3.5 %collective-permute-start.3 = (bf16[272,256]{1,0:T(8,128)(2,1)S(1)}, bf16[272,256]{1,0:T(8,128)(2,1)S(1)}, u32[]{:S(2)}, u32[]{:S(2)}) collective-permute-start(bf16[272,256]{1,0:T(8,128)(2,1)S(1)} %pad_maximum_fusion.10), channel_id=1, source_target_pairs={{0,4},{4,8},{8,12},{1,5},{5,9},{9,13},{2,6},{6,10},{10,14},{3,7},{... | collective-permute-start | bytes 417800 | tf_op jit(solution)/shard_map/ppermute | solution.py:20
  17.8 2.9 %collective-permute-start.2 = (bf16[272,256]{1,0:T(8,128)(2,1)S(1)}, bf16[272,256]{1,0:T(8,128)(2,1)S(1)}, u32[]{:S(2)}, u32[]{:S(2)}) collective-permute-start(bf16[272,256]{1,0:T(8,128)(2,1)S(1)} %pad_maximum_fusion.10), channel_id=1, source_target_pairs={{0,8},{4,12},{1,9},{5,13},{2,10},{6,14},{3,11},{7,15},{16,24},{20,... | collective-permute-start | bytes 417800 | tf_op jit(solution)/shard_map/ppermute | solution.py:20
  20.7 1.3 %collective-permute-start.1 = (bf16[272,256]{1,0:T(8,128)(2,1)S(1)}, bf16[272,256]{1,0:T(8,128)(2,1)S(1)}, u32[]{:S(2)}, u32[]{:S(2)}) collective-permute-start(bf16[272,256]{1,0:T(8,128)(2,1)S(1)} %pad_maximum_fusion.10), channel_id=1, source_target_pairs={{0,12},{1,13},{2,14},{3,15},{16,28},{17,29},{18,30},{19,31}} | collective-permute-start | bytes 417800 | tf_op jit(solution)/shard_map/ppermute | solution.py:20
  22.1 0.7 copy-done.16
  22.8 1.0 %fusion.7.bias_ref = f32[256,384]{1,0:T(8,128)} fusion(s32[384]{0:T(512)S(1)} %get-tuple-element.91, s32[384]{0:T(512)S(1)} %get-tuple-element.92, s32[256]{0:T(256)S(1)} %iota_add_fusion.2, s32[256]{0:T(256)S(1)} %copy-done.16, pred[384]{0:T(512)(128)(4,1)S(1)} %broadcast_compare_fusion.1), kind=kLoop, calls=%fused_computation.20 | loop fusion | flops 786432 | bytes 398720 | tf_op jit(solution)/shard_map/jit(_where)/select_n | solution.py:148
  23.7 0.8 pad_maximum_fusion.7
  24.5 7.3 %shard_map.154 = (bf16[256,512]{1,0:T(8,128)(2,1)}, f32[384,128]{1,0:T(8,128)}, f32[384,128]{1,0:T(8,128)}) custom-call(f32[4,4]{1,0:T(4,128)} %sink_ref.4, bf16[256,1024]{1,0:T(8,128)(2,1)} %bitcast.18, bf16[256,1024]{1,0:T(8,128)(2,1)} %bitcast.20, bf16[384,256]{1,0:T(8,128)(2,1)} %get-tuple-element.89.k_ref, bf16[384,256]{1,0:T(8,128)(2,1)} %get-tuple-element.90.v_ref, ...), custom_call_target="tpu_custom_call" | custom-call | flops 503316480 | bytes 2555904 | tf_op jit(solution)/shard_map/pallas_call | solution.py:110
  32.0 0.1 collective-permute-start.4
  32.1 1.4 %fusion.2.bias_ref = f32[256,1024]{1,0:T(8,128)} fusion(s32[1024]{0:T(1024)S(1)} %pad_add_fusion, s32[1024]{0:T(1024)S(1)} %iota_add_fusion, s32[256]{0:T(256)S(1)} %iota_add_fusion.2, s32[256]{0:T(256)S(1)} %copy-done.16, pred[1024]{0:T(1024)(128)(4,1)S(1)} %broadcast_compare_fusion), kind=kLoop, calls=%fused_computation.4 | loop fusion | flops 1572864 | bytes 1059840 | tf_op jit(solution)/shard_map/jit(_where)/select_n | solution.py:148
  33.4 0.3 collective-permute-done.4
  33.8 0.8 pad_maximum_fusion.3.v_ref
  34.7 0.8 pad_maximum_fusion.2.k_ref
  35.5 21.7 %shard_map.156 = (bf16[256,1024]{1,0:T(8,128)(2,1)}, f32[1024,256]{1,0:T(8,128)}, f32[1024,256]{1,0:T(8,128)}) custom-call(f32[4,4]{1,0:T(4,128)} %sink_ref.5, bf16[256,1024]{1,0:T(8,128)(2,1)} %bitcast.22, bf16[256,1024]{1,0:T(8,128)(2,1)} %bitcast.23, bf16[1024,256]{1,0:T(8,128)(2,1)} %pad_maximum_fusion.2.k_ref, ...), custom_call_target="tpu_custom_call" | custom-call | flops 2684354560 | bytes 7340032 | tf_op jit(solution)/shard_map/pallas_call | solution.py:110
  57.2 1.4 %broadcast_select_fusion = f32[1024,256]{1,0:T(8,128)S(1)} fusion(f32[1024,256]{1,0:T(8,128)} %get-tuple-element.62, f32[1024,256]{1,0:T(8,128)} %get-tuple-element.61, pred[]{:T(512)S(6)} %eq.14), kind=kLoop, calls=%fused_computation.15 | loop fusion | flops 262144 | bytes 3145729 | tf_op jit(solution)/shard_map/jit(_where)/select_n | solution.py:232
  58.6 0.2 collective-permute-start.5
  58.8 7.7 %shard_map.155 = (bf16[256,512]{1,0:T(8,128)(2,1)}, f32[384,128]{1,0:T(8,128)}, f32[384,128]{1,0:T(8,128)}) custom-call(f32[4,4]{1,0:T(4,128)} %sink_ref.4, bf16[256,1024]{1,0:T(8,128)(2,1)} %bitcast.19, bf16[256,1024]{1,0:T(8,128)(2,1)} %bitcast.21, bf16[384,256]{1,0:T(8,128)(2,1)} %get-tuple-element.89.k_ref, bf16[384,256]{1,0:T(8,128)(2,1)} %get-tuple-element.90.v_ref, ...), custom_call_target="tpu_custom_call" | custom-call | flops 503316480 | bytes 2555904 | tf_op jit(solution)/shard_map/pallas_call | solution.py:110
  66.5 1.0 %constant_dynamic-update-slice_fusion = f32[384,256]{1,0:T(8,128)S(1)} fusion(f32[384,256]{1,0:T(8,128)S(1)} %constant_dynamic-update-slice_fusion.1, f32[384,128]{1,0:T(8,128)} %get-tuple-element.55), kind=kLoop, calls=%fused_computation.46 | loop fusion | bytes 393216 | tf_op jit(solution)/shard_map/concatenate | solution.py:238
  67.6 0.9 copy-done.15
  68.6 0.2 fusion.12
  68.9 1.3 %collective-permute-start.6 = (bf16[512,256]{1,0:T(8,128)(2,1)S(1)}, bf16[512,256]{1,0:T(8,128)(2,1)S(1)}, u32[]{:S(2)}, u32[]{:S(2)}) collective-permute-start(bf16[512,256]{1,0:T(8,128)(2,1)S(1)} %pad_maximum_fusion.6), channel_id=1, source_target_pairs={{4,0},{8,4},{12,8},{5,1},{9,5},{13,9},{6,2},{10,6},{14,10},{7,3},{... | collective-permute-start | bytes 786440 | tf_op jit(solution)/shard_map/ppermute | solution.py:20
  70.2 1.3 %collective-permute-start.7 = (bf16[256,256]{1,0:T(8,128)(2,1)S(1)}, bf16[256,256]{1,0:T(8,128)(2,1)S(1)}, u32[]{:S(2)}, u32[]{:S(2)}) collective-permute-start(bf16[256,256]{1,0:T(8,128)(2,1)S(1)} %get-tuple-element.76), channel_id=1, source_target_pairs={{12,0},{13,1},{14,2},{15,3},{28,16},{29,17},{30,18},{31,19}} | collective-permute-start | bytes 393224 | tf_op jit(solution)/shard_map/ppermute | solution.py:20
  71.5 1.3 %collective-permute-start.8 = (bf16[256,256]{1,0:T(8,128)(2,1)S(1)}, bf16[256,256]{1,0:T(8,128)(2,1)S(1)}, u32[]{:S(2)}, u32[]{:S(2)}) collective-permute-start(bf16[256,256]{1,0:T(8,128)(2,1)S(1)} %get-tuple-element.77), channel_id=1, source_target_pairs={{8,0},{12,4},{9,1},{13,5},{10,2},{14,6},{11,3},{15,7},{24,16},{28,... | collective-permute-start | bytes 393224 | tf_op jit(solution)/shard_map/ppermute | solution.py:20
  72.8 10.2 %collective-permute-done.6 = bf16[512,256]{1,0:T(8,128)(2,1)S(1)} collective-permute-done((bf16[512,256]{1,0:T(8,128)(2,1)S(1)}, bf16[512,256]{1,0:T(8,128)(2,1)S(1)}, u32[]{:S(2)}, u32[]{:S(2)}) %collective-permute-start.6) | collective-permute-done | bytes 262176 | tf_op jit(solution)/shard_map/ppermute | solution.py:20
  83.1 0.1 fusion.8
  83.2 3.4 %collective-permute-done.8 = bf16[256,256]{1,0:T(8,128)(2,1)S(1)} collective-permute-done((bf16[256,256]{1,0:T(8,128)(2,1)S(1)}, bf16[256,256]{1,0:T(8,128)(2,1)S(1)}, u32[]{:S(2)}, u32[]{:S(2)}) %collective-permute-start.8) | collective-permute-done | bytes 131104 | tf_op jit(solution)/shard_map/ppermute | solution.py:20
  86.7 0.1 collective-permute-start.9
  86.8 0.8 copy-done.11
  87.6 0.1 copy-done.12
  87.7 1.2 %reshape.119 = bf16[256,4,256]{2,1,0:T(4,128)(2,1)} reshape(bf16[256,1024]{1,0:T(8,128)(2,1)S(1)} %pad_maximum_fusion.1) | data formatting | bytes 1048576 | tf_op jit(solution)/shard_map/reshape | solution.py:264
  88.9 1.2 %reshape.121 = bf16[256,4,256]{2,1,0:T(4,128)(2,1)} reshape(bf16[256,1024]{1,0:T(8,128)(2,1)S(1)} %copy-done.6) | data formatting | bytes 1048576 | tf_op jit(solution)/shard_map/reshape | solution.py:267
  90.1 0.1 fusion.3
  90.1 0.7 fusion.14
  90.8 0.7 select_convert_fusion
  (69 shorter events, 0.7 us)
Async XLA Ops:
  0.6 7.5 %copy-start.2 = (bf16[256,4,256]{2,1,0:T(4,128)(2,1)S(1)}, bf16[256,4,256]{2,1,0:T(4,128)(2,1)}, u32[]{:S(2)}) copy-start(bf16[256,4,256]{2,1,0:T(4,128)(2,1)} %param.16) | copy-start | bytes 1572868
  3.1 11.1 %collective-permute-start = (bf16[144,512]{1,0:T(8,128)(2,1)S(1)}, bf16[144,512]{1,0:T(8,128)(2,1)S(1)}, u32[]{:S(2)}, u32[]{:S(2)}) collective-permute-start(bf16[144,512]{1,0:T(8,128)(2,1)S(1)} %pad_maximum_fusion.9), channel_id=1, source_target_pairs={{0,4},{4,8},{8,12},{1,5},{5,9},{9,13},{2,6},{6,10},{10,14},{3,7},{... | collective-permute-start | bytes 442376 | tf_op jit(solution)/shard_map/ppermute | solution.py:20
  8.1 1.0 %copy-start.3 = (bf16[256,4,256]{2,1,0:T(4,128)(2,1)S(1)}, bf16[256,4,256]{2,1,0:T(4,128)(2,1)}, u32[]{:S(2)}) copy-start(bf16[256,4,256]{2,1,0:T(4,128)(2,1)} %param.21) | copy-start | bytes 1572868
  9.2 0.9 copy-start.7
  9.2 1.0 %copy-start.8 = (bf16[256,256]{1,0:T(8,128)(2,1)S(1)}, bf16[256,256]{1,0:T(8,128)(2,1)}, u32[]{:S(2)}) copy-start(bf16[256,256]{1,0:T(8,128)(2,1)} %param.22) | copy-start | bytes 393220
  10.2 1.1 %copy-start.4 = (bf16[256,4,256]{2,1,0:T(4,128)(2,1)S(1)}, bf16[256,4,256]{2,1,0:T(4,128)(2,1)}, u32[]{:S(2)}) copy-start(bf16[256,4,256]{2,1,0:T(4,128)(2,1)} %param.19) | copy-start | bytes 1572868
  12.2 1.1 %copy-start.5 = (bf16[256,4,256]{2,1,0:T(4,128)(2,1)S(1)}, bf16[256,4,256]{2,1,0:T(4,128)(2,1)}, u32[]{:S(2)}) copy-start(bf16[256,4,256]{2,1,0:T(4,128)(2,1)} %param.24) | copy-start | bytes 1572868
  14.3 17.6 %collective-permute-start.3 = (bf16[272,256]{1,0:T(8,128)(2,1)S(1)}, bf16[272,256]{1,0:T(8,128)(2,1)S(1)}, u32[]{:S(2)}, u32[]{:S(2)}) collective-permute-start(bf16[272,256]{1,0:T(8,128)(2,1)S(1)} %pad_maximum_fusion.10), channel_id=1, source_target_pairs={{0,4},{4,8},{8,12},{1,5},{5,9},{9,13},{2,6},{6,10},{10,14},{3,7},{... | collective-permute-start | bytes 417800 | tf_op jit(solution)/shard_map/ppermute | solution.py:20
  17.8 14.1 %collective-permute-start.2 = (bf16[272,256]{1,0:T(8,128)(2,1)S(1)}, bf16[272,256]{1,0:T(8,128)(2,1)S(1)}, u32[]{:S(2)}, u32[]{:S(2)}) collective-permute-start(bf16[272,256]{1,0:T(8,128)(2,1)S(1)} %pad_maximum_fusion.10), channel_id=1, source_target_pairs={{0,8},{4,12},{1,9},{5,13},{2,10},{6,14},{3,11},{7,15},{16,24},{20,... | collective-permute-start | bytes 417800 | tf_op jit(solution)/shard_map/ppermute | solution.py:20
  20.7 11.1 %collective-permute-start.1 = (bf16[272,256]{1,0:T(8,128)(2,1)S(1)}, bf16[272,256]{1,0:T(8,128)(2,1)S(1)}, u32[]{:S(2)}, u32[]{:S(2)}) collective-permute-start(bf16[272,256]{1,0:T(8,128)(2,1)S(1)} %pad_maximum_fusion.10), channel_id=1, source_target_pairs={{0,12},{1,13},{2,14},{3,15},{16,28},{17,29},{18,30},{19,31}} | collective-permute-start | bytes 417800 | tf_op jit(solution)/shard_map/ppermute | solution.py:20
  22.1 0.7 copy-start.16
  22.8 1.0 %copy-start.9 = (bf16[256,256]{1,0:T(8,128)(2,1)S(1)}, bf16[256,256]{1,0:T(8,128)(2,1)}, u32[]{:S(2)}) copy-start(bf16[256,256]{1,0:T(8,128)(2,1)} %param.17) | copy-start | bytes 393220
  22.8 1.0 %copy-start.10 = (bf16[256,256]{1,0:T(8,128)(2,1)S(1)}, bf16[256,256]{1,0:T(8,128)(2,1)}, u32[]{:S(2)}) copy-start(bf16[256,256]{1,0:T(8,128)(2,1)} %param.18) | copy-start | bytes 393220
  32.0 1.8 %collective-permute-start.4 = (bf16[816,256]{1,0:T(8,128)(2,1)S(1)}, bf16[816,256]{1,0:T(8,128)(2,1)S(1)}, u32[]{:S(2)}, u32[]{:S(2)}) collective-permute-start(bf16[816,256]{1,0:T(8,128)(2,1)S(1)} %pad_maximum_fusion.4), channel_id=1, source_target_pairs={{0,1},{1,0},{2,3},{3,2},{4,5},{5,4},{6,7},{7,6},{8,9},{9,8},{10,11... | collective-permute-start | bytes 1253384 | tf_op jit(solution)/shard_map/ppermute | solution.py:214
  58.6 7.9 %copy-start.14 = (f32[384,128]{1,0:T(8,128)S(1)}, f32[384,128]{1,0:T(8,128)}, u32[]{:S(2)}) copy-start(f32[384,128]{1,0:T(8,128)} %get-tuple-element.54) | copy-start | bytes 589828
  58.6 9.9 %collective-permute-start.5 = (f32[1024,256]{1,0:T(8,128)S(1)}, f32[1024,256]{1,0:T(8,128)S(1)}, u32[]{:S(2)}, u32[]{:S(2)}) collective-permute-start(f32[1024,256]{1,0:T(8,128)S(1)} %broadcast_select_fusion), channel_id=1, source_target_pairs={{0,1},{1,0},{2,3},{3,2},{4,5},{5,4},{6,7},{7,6},{8,9},{9,8},{10,11... | collective-permute-start | bytes 3145736 | tf_op jit(solution)/shard_map/ppermute | solution.py:234
  58.8 8.8 %copy-start.13 = (f32[384,128]{1,0:T(8,128)S(1)}, f32[384,128]{1,0:T(8,128)}, u32[]{:S(2)}) copy-start(f32[384,128]{1,0:T(8,128)} %get-tuple-element.56) | copy-start | bytes 589828
  58.8 9.8 %copy-start.1 = (f32[1024,256]{1,0:T(8,128)S(1)}, f32[1024,256]{1,0:T(8,128)}, u32[]{:S(2)}) copy-start(f32[1024,256]{1,0:T(8,128)} %get-tuple-element.62) | copy-start | bytes 3145732
  66.5 2.1 %copy-start = (f32[1024,256]{1,0:T(8,128)S(1)}, f32[1024,256]{1,0:T(8,128)}, u32[]{:S(2)}) copy-start(f32[1024,256]{1,0:T(8,128)} %get-tuple-element.61) | copy-start | bytes 3145732
  67.6 0.9 %copy-start.15 = (f32[384,128]{1,0:T(8,128)S(1)}, f32[384,128]{1,0:T(8,128)}, u32[]{:S(2)}) copy-start(f32[384,128]{1,0:T(8,128)} %get-tuple-element.57) | copy-start | bytes 589828
  68.9 14.1 %collective-permute-start.6 = (bf16[512,256]{1,0:T(8,128)(2,1)S(1)}, bf16[512,256]{1,0:T(8,128)(2,1)S(1)}, u32[]{:S(2)}, u32[]{:S(2)}) collective-permute-start(bf16[512,256]{1,0:T(8,128)(2,1)S(1)} %pad_maximum_fusion.6), channel_id=1, source_target_pairs={{4,0},{8,4},{12,8},{5,1},{9,5},{13,9},{6,2},{10,6},{14,10},{7,3},{... | collective-permute-start | bytes 786440 | tf_op jit(solution)/shard_map/ppermute | solution.py:20
  70.2 12.9 %collective-permute-start.7 = (bf16[256,256]{1,0:T(8,128)(2,1)S(1)}, bf16[256,256]{1,0:T(8,128)(2,1)S(1)}, u32[]{:S(2)}, u32[]{:S(2)}) collective-permute-start(bf16[256,256]{1,0:T(8,128)(2,1)S(1)} %get-tuple-element.76), channel_id=1, source_target_pairs={{12,0},{13,1},{14,2},{15,3},{28,16},{29,17},{30,18},{31,19}} | collective-permute-start | bytes 393224 | tf_op jit(solution)/shard_map/ppermute | solution.py:20
  71.5 15.0 %collective-permute-start.8 = (bf16[256,256]{1,0:T(8,128)(2,1)S(1)}, bf16[256,256]{1,0:T(8,128)(2,1)S(1)}, u32[]{:S(2)}, u32[]{:S(2)}) collective-permute-start(bf16[256,256]{1,0:T(8,128)(2,1)S(1)} %get-tuple-element.77), channel_id=1, source_target_pairs={{8,0},{12,4},{9,1},{13,5},{10,2},{14,6},{11,3},{15,7},{24,16},{28,... | collective-permute-start | bytes 393224 | tf_op jit(solution)/shard_map/ppermute | solution.py:20
  86.6 1.0 %copy-start.11 = (bf16[256,512]{1,0:T(8,128)(2,1)S(1)}, bf16[256,512]{1,0:T(8,128)(2,1)}, u32[]{:S(2)}) copy-start(bf16[256,512]{1,0:T(8,128)(2,1)} %get-tuple-element.52) | copy-start | bytes 786436
  86.6 1.0 %copy-start.12 = (bf16[256,512]{1,0:T(8,128)(2,1)S(1)}, bf16[256,512]{1,0:T(8,128)(2,1)}, u32[]{:S(2)}) copy-start(bf16[256,512]{1,0:T(8,128)(2,1)} %get-tuple-element.53) | copy-start | bytes 786436
  86.7 3.4 %collective-permute-start.9 = (f32[256,768]{1,0:T(8,128)S(1)}, f32[256,768]{1,0:T(8,128)S(1)}, u32[]{:S(2)}, u32[]{:S(2)}) collective-permute-start(f32[256,768]{1,0:T(8,128)S(1)} %pad_maximum_fusion), channel_id=1, source_target_pairs={{0,1},{1,0},{2,3},{3,2},{4,5},{5,4},{6,7},{7,6},{8,9},{9,8},{10,11... | collective-permute-start | bytes 2359304 | tf_op jit(solution)/shard_map/ppermute | solution.py:258
  87.7 1.2 %copy-start.6 = (bf16[256,1024]{1,0:T(8,128)(2,1)S(1)}, bf16[256,1024]{1,0:T(8,128)(2,1)}, u32[]{:S(2)}) copy-start(bf16[256,1024]{1,0:T(8,128)(2,1)} %get-tuple-element.63) | copy-start | bytes 1572868

commit v12 on v11

--- a/solution.py
+++ b/solution.py
@@ -24,7 +24,10 @@
     return jnp.where(half == 0, block[:, :HD], block[:, HD:])
 
 
-def attn_bwd_kernel(g0, gn, pair, sink_ref, q_ref, do_ref, k_ref, v_ref, bias_ref, dq_ref, dk_ref, dv_ref):
+def attn_bwd_kernel(
+    g0, gn, pair, window, sink_ref, q_ref, do_ref, k_ref, v_ref, qpos_ref, qseg_ref, kpos_ref, kseg_ref,
+    dq_ref, dk_ref, dv_ref,
+):
     t = pl.program_id(0)
     i = pl.program_id(1)
     heads = q_ref.shape[1] // (HD * pair)
@@ -34,7 +37,12 @@
         dk_ref[...] = jnp.zeros_like(dk_ref)
         dv_ref[...] = jnp.zeros_like(dv_ref)
 
-    bias = bias_ref[...]
+    key_pos = kpos_ref[...]
+    distance = qpos_ref[...] - key_pos
+    visible = (distance >= 0) & (key_pos >= 0) & (qseg_ref[...] == kseg_ref[...])
+    if window is not None:
+        visible = visible & (distance < window)
+    bias = jnp.where(visible, 0.0, NEG).astype(jnp.float32)
     k_block = k_ref[...]
     v_block = v_ref[...]
     dq_parts = []
@@ -85,7 +93,8 @@
             dv_ref[:, tt * wide:(tt + 1) * wide] += dv_step
 
 
-def attn_bwd(sinks, queries, grads, keys, values, bias, g0, gn):
+def attn_bwd(sinks, queries, grads, keys, values, mask_info, g0, gn):
+    query_pos, query_seg, key_pos, key_seg, window = mask_info
     n = queries.shape[0]
     m = keys.shape[0]
     heads = sinks.shape[1]
@@ -108,7 +117,7 @@
         key_map = lambda t, i: (0, (g0 + t) // 2)
 
     return pl.pallas_call(
-        functools.partial(attn_bwd_kernel, g0, gn, pair),
+        functools.partial(attn_bwd_kernel, g0, gn, pair, window),
         grid=grid,
         in_specs=[
             pl.BlockSpec(memory_space=pltpu.SMEM),
@@ -116,7 +125,10 @@
             pl.BlockSpec((rows, width), lambda t, i: (i, g0 // pair + t)),
             pl.BlockSpec((m, key_width), key_map),
             pl.BlockSpec((m, key_width), key_map),
-            pl.BlockSpec((rows, m), lambda t, i: (i, 0)),
+            pl.BlockSpec((rows, 1), lambda t, i: (i, 0)),
+            pl.BlockSpec((rows, 1), lambda t, i: (i, 0)),
+            pl.BlockSpec((1, m), lambda t, i: (0, 0)),
+            pl.BlockSpec((1, m), lambda t, i: (0, 0)),
         ],
         out_specs=[
             pl.BlockSpec((rows, width), lambda t, i: (i, t)),
@@ -135,9 +147,13 @@
         cost_estimate=pl.CostEstimate(
             flops=10 * gn * heads * n * m * HD,
             transcendentals=gn * heads * n * m,
-            bytes_accessed=4 * n * m + 4 * n * gn * heads * HD * 3 + 12 * m * gn * HD,
+            bytes_accessed=8 * (n + m) + 4 * n * gn * heads * HD * 3 + 12 * m * gn * HD,
         ),
-    )(sinks, queries, grads, keys, values, bias)
+    )(
+        sinks, queries, grads, keys, values,
+        query_pos.reshape(n, 1).astype(jnp.int32), query_seg.reshape(n, 1).astype(jnp.int32),
+        key_pos.reshape(1, m).astype(jnp.int32), key_seg.reshape(1, m).astype(jnp.int32),
+    )
 
 
 def make_bias(query_pos, query_seg, key_pos, key_seg, window):
@@ -203,7 +219,7 @@
     w_values = jnp.concatenate([halo[:WINDOW, cols:], window_values], axis=0)
     w_seg = jnp.concatenate([read_seg(halo[WINDOW:], WINDOW), segment_ids], axis=0)
     w_pos = seq_index * n - WINDOW + jnp.arange(n + WINDOW)
-    w_bias = make_bias(query_pos, segment_ids, w_pos, w_seg, WINDOW)
+    w_bias = (query_pos, segment_ids, w_pos, w_seg, WINDOW)
     w_q = (window_query.reshape(n, -1) * 0.125).astype(jnp.bfloat16)
     w_do = window_grad_out.reshape(n, -1)
     g_split = groups // 2 if groups > 1 else groups
@@ -224,7 +240,7 @@
     f_values = jnp.concatenate(value_parts + [full_values], axis=0)
     f_seg = jnp.concatenate(seg_parts + [segment_ids], axis=0)
     f_pos = (seq_index - (seq_count - 1)) * n + jnp.arange(seq_count * n)
-    f_bias = make_bias(query_pos, segment_ids, f_pos, f_seg, None)
+    f_bias = (query_pos, segment_ids, f_pos, f_seg, None)
     f_q = (full_query.reshape(n, -1) * 0.125).astype(jnp.bfloat16)
     f_do = full_grad_out.reshape(n, -1)
     f_dq, f_dk, f_dv = attn_bwd(full_sinks, f_q, f_do, f_keys, f_values, f_bias, 0, groups)

time: 92.3 us -> 94.5 us (1.024)
  waiting for transfers between devices: 13.9 us -> 15.7 us
    select_n x2 -> x0, other arithmetic: 2.34 us -> none  [make_bias(): return jnp.where(visible, 0.0, NEG).astype(jnp.float32)]
    reshape x0 -> x2, local copies, waits for them, and re-layouts: none -> 1.32 us  [the longest x1 0.8 us: attn_bwd(): query_seg.reshape(n, 1).astype(jnp.int32)]
    ppermute x7, waiting for transfers between devices: 13.6 us -> 14.6 us  [passed_along(): lax.ppermute(value, axis, [(source, source + steps) for source in range(f...]
  transfers between devices with their start and end apart: 10 -> 10, of which waited for: 3 -> 3; matrix products, arithmetic and copies ran while one was open for 12% -> 13% of each run, Pallas kernels for 16% -> 16%
where the time goes in v12:
time: 94.5 us; the launch traced here: 93.8 us
  Pallas kernels  36.5 us (39%)
  starting transfers between devices  17 us (18%)
  waiting for transfers between devices  15.7 us (17%)
  local copies, waits for them, and re-layouts  14.6 us (15%)
  other arithmetic  8.92 us (9%)
  between operations  1.08 us (1%)
    pallas_call x3, Pallas kernels, attn_bwd(): pl.pallas_call(functools.partial(attn_bwd_kernel, g0, gn, pair, window),...  36.5 us
    ppermute x7, starting transfers between devices, passed_along(): lax.ppermute(value, axis, [(source, source + steps) for source in range(f...  16.7 us
    ppermute x7, waiting for transfers between devices, passed_along(): lax.ppermute(value, axis, [(source, source + steps) for source in range(f...  14.6 us
    unnamed x42, local copies, waits for them, and re-layouts  8.12 us
  transfers between devices with their start and end apart: 10, of which 3 were waited for; matrix products, arithmetic and copies ran while one was open for 13% of the time, Pallas kernels for 16%

profile of v12, /device:TPU:0, one launch (start us, length us, event | category | flops | bytes accessed | tf_op | source)
XLA Modules:
  0.0 93.8 jit_solution(5147394728711698485)
XLA Ops:
  0.7 0.7 convert.17
  1.4 0.8 slice.148
  2.3 4.9 %collective-permute-start = (bf16[144,512]{1,0:T(8,128)(2,1)S(1)}, bf16[144,512]{1,0:T(8,128)(2,1)S(1)}, u32[]{:S(2)}, u32[]{:S(2)}) collective-permute-start(bf16[144,512]{1,0:T(8,128)(2,1)S(1)} %pad_maximum_fusion.9), channel_id=1, source_target_pairs={{0,4},{4,8},{8,12},{1,5},{5,9},{9,13},{2,6},{6,10},{10,14},{3,7},{... | collective-permute-start | bytes 442376 | tf_op jit(solution)/shard_map/ppermute | solution.py:20
  7.3 0.7 iota_add_fusion.qpos_ref
  7.9 0.6 iota_add_fusion.1.kpos_ref
  8.6 0.2 broadcast_multiply_fusion.1
  8.8 0.8 copy-done.3
  9.6 0.2 broadcast_multiply_fusion
  9.8 0.7 copy-done.7
  10.6 0.5 iota_add_fusion.2.kpos_ref
  11.2 0.7 copy-done.16
  11.8 0.8 copy.17.qseg_ref
  12.6 0.9 copy.20
  13.5 0.2 copy-done.4
  13.8 0.9 copy.21
  14.7 0.9 copy.23
  15.5 0.2 copy-done.5
  15.8 0.9 copy.24
  16.8 3.6 %collective-permute-start.3 = (bf16[272,256]{1,0:T(8,128)(2,1)S(1)}, bf16[272,256]{1,0:T(8,128)(2,1)S(1)}, u32[]{:S(2)}, u32[]{:S(2)}) collective-permute-start(bf16[272,256]{1,0:T(8,128)(2,1)S(1)} %pad_maximum_fusion.10), channel_id=1, source_target_pairs={{0,4},{4,8},{8,12},{1,5},{5,9},{9,13},{2,6},{6,10},{10,14},{3,7},{... | collective-permute-start | bytes 417800 | tf_op jit(solution)/shard_map/ppermute | solution.py:20
  20.4 2.9 %collective-permute-start.2 = (bf16[272,256]{1,0:T(8,128)(2,1)S(1)}, bf16[272,256]{1,0:T(8,128)(2,1)S(1)}, u32[]{:S(2)}, u32[]{:S(2)}) collective-permute-start(bf16[272,256]{1,0:T(8,128)(2,1)S(1)} %pad_maximum_fusion.10), channel_id=1, source_target_pairs={{0,8},{4,12},{1,9},{5,13},{2,10},{6,14},{3,11},{7,15},{16,24},{20,... | collective-permute-start | bytes 417800 | tf_op jit(solution)/shard_map/ppermute | solution.py:20
  23.3 1.3 %collective-permute-start.1 = (bf16[272,256]{1,0:T(8,128)(2,1)S(1)}, bf16[272,256]{1,0:T(8,128)(2,1)S(1)}, u32[]{:S(2)}, u32[]{:S(2)}) collective-permute-start(bf16[272,256]{1,0:T(8,128)(2,1)S(1)} %pad_maximum_fusion.10), channel_id=1, source_target_pairs={{0,12},{1,13},{2,14},{3,15},{16,28},{17,29},{18,30},{19,31}} | collective-permute-start | bytes 417800 | tf_op jit(solution)/shard_map/ppermute | solution.py:20
  24.7 0.5 reshape.136.kseg_ref
  25.2 0.8 pad_maximum_fusion.7
  26.0 7.3 %shard_map.154 = (bf16[256,512]{1,0:T(8,128)(2,1)}, f32[384,128]{1,0:T(8,128)}, f32[384,128]{1,0:T(8,128)}) custom-call(f32[4,4]{1,0:T(4,128)} %sink_ref.4, bf16[256,1024]{1,0:T(8,128)(2,1)} %bitcast.20, bf16[256,1024]{1,0:T(8,128)(2,1)} %bitcast.22, bf16[384,256]{1,0:T(8,128)(2,1)} %get-tuple-element.89.k_ref, bf16[384,256]{1,0:T(8,128)(2,1)} %get-tuple-element.90.v_ref, ...), custom_call_target="tpu_custom_call" | custom-call | flops 503316480 | bytes 2167808 | tf_op jit(solution)/shard_map/pallas_call | solution.py:119
  33.3 0.1 collective-permute-start.4
  33.4 0.6 pad_add_fusion
  34.0 1.1 %collective-permute-done.4 = bf16[816,256]{1,0:T(8,128)(2,1)S(1)} collective-permute-done((bf16[816,256]{1,0:T(8,128)(2,1)S(1)}, bf16[816,256]{1,0:T(8,128)(2,1)S(1)}, u32[]{:S(2)}, u32[]{:S(2)}) %collective-permute-start.4) | collective-permute-done | bytes 417824 | tf_op jit(solution)/shard_map/ppermute | solution.py:230
  35.2 0.8 pad_maximum_fusion.3.v_ref
  36.0 0.8 pad_maximum_fusion.2.k_ref
  36.9 21.7 %shard_map.156 = (bf16[256,1024]{1,0:T(8,128)(2,1)}, f32[1024,256]{1,0:T(8,128)}, f32[1024,256]{1,0:T(8,128)}) custom-call(f32[4,4]{1,0:T(4,128)} %sink_ref.5, bf16[256,1024]{1,0:T(8,128)(2,1)} %bitcast.24, bf16[256,1024]{1,0:T(8,128)(2,1)} %bitcast.25, bf16[1024,256]{1,0:T(8,128)(2,1)} %pad_maximum_fusion.2.k_ref, ...), custom_call_target="tpu_custom_call" | custom-call | flops 2684354560 | bytes 6301696 | tf_op jit(solution)/shard_map/pallas_call | solution.py:119
  58.5 1.4 %broadcast_select_fusion = f32[1024,256]{1,0:T(8,128)S(1)} fusion(f32[1024,256]{1,0:T(8,128)} %get-tuple-element.62, f32[1024,256]{1,0:T(8,128)} %get-tuple-element.61, pred[]{:T(512)S(6)} %eq.3), kind=kLoop, calls=%fused_computation.9 | loop fusion | flops 262144 | bytes 3145729 | tf_op jit(solution)/shard_map/jit(_where)/select_n | solution.py:248
  59.9 0.2 collective-permute-start.5
  60.1 7.6 %shard_map.155 = (bf16[256,512]{1,0:T(8,128)(2,1)}, f32[384,128]{1,0:T(8,128)}, f32[384,128]{1,0:T(8,128)}) custom-call(f32[4,4]{1,0:T(4,128)} %sink_ref.4, bf16[256,1024]{1,0:T(8,128)(2,1)} %bitcast.21, bf16[256,1024]{1,0:T(8,128)(2,1)} %bitcast.23, bf16[384,256]{1,0:T(8,128)(2,1)} %get-tuple-element.89.k_ref, bf16[384,256]{1,0:T(8,128)(2,1)} %get-tuple-element.90.v_ref, ...), custom_call_target="tpu_custom_call" | custom-call | flops 503316480 | bytes 2167808 | tf_op jit(solution)/shard_map/pallas_call | solution.py:119
  67.7 1.0 %constant_dynamic-update-slice_fusion = f32[384,256]{1,0:T(8,128)S(1)} fusion(f32[384,256]{1,0:T(8,128)S(1)} %constant_dynamic-update-slice_fusion.1, f32[384,128]{1,0:T(8,128)} %get-tuple-element.55), kind=kLoop, calls=%fused_computation.37 | loop fusion | bytes 393216 | tf_op jit(solution)/shard_map/concatenate | solution.py:254
  68.8 0.9 copy-done.15
  69.8 0.2 fusion.5
  70.1 1.3 %collective-permute-start.6 = (bf16[512,256]{1,0:T(8,128)(2,1)S(1)}, bf16[512,256]{1,0:T(8,128)(2,1)S(1)}, u32[]{:S(2)}, u32[]{:S(2)}) collective-permute-start(bf16[512,256]{1,0:T(8,128)(2,1)S(1)} %pad_maximum_fusion.6), channel_id=1, source_target_pairs={{4,0},{8,4},{12,8},{5,1},{9,5},{13,9},{6,2},{10,6},{14,10},{7,3},{... | collective-permute-start | bytes 786440 | tf_op jit(solution)/shard_map/ppermute | solution.py:20
  71.4 1.3 %collective-permute-start.7 = (bf16[256,256]{1,0:T(8,128)(2,1)S(1)}, bf16[256,256]{1,0:T(8,128)(2,1)S(1)}, u32[]{:S(2)}, u32[]{:S(2)}) collective-permute-start(bf16[256,256]{1,0:T(8,128)(2,1)S(1)} %get-tuple-element.76), channel_id=1, source_target_pairs={{12,0},{13,1},{14,2},{15,3},{28,16},{29,17},{30,18},{31,19}} | collective-permute-start | bytes 393224 | tf_op jit(solution)/shard_map/ppermute | solution.py:20
  72.7 1.3 %collective-permute-start.8 = (bf16[256,256]{1,0:T(8,128)(2,1)S(1)}, bf16[256,256]{1,0:T(8,128)(2,1)S(1)}, u32[]{:S(2)}, u32[]{:S(2)}) collective-permute-start(bf16[256,256]{1,0:T(8,128)(2,1)S(1)} %get-tuple-element.77), channel_id=1, source_target_pairs={{8,0},{12,4},{9,1},{13,5},{10,2},{14,6},{11,3},{15,7},{24,16},{28,... | collective-permute-start | bytes 393224 | tf_op jit(solution)/shard_map/ppermute | solution.py:20
  74.0 10.4 %collective-permute-done.6 = bf16[512,256]{1,0:T(8,128)(2,1)S(1)} collective-permute-done((bf16[512,256]{1,0:T(8,128)(2,1)S(1)}, bf16[512,256]{1,0:T(8,128)(2,1)S(1)}, u32[]{:S(2)}, u32[]{:S(2)}) %collective-permute-start.6) | collective-permute-done | bytes 262176 | tf_op jit(solution)/shard_map/ppermute | solution.py:20
  84.6 4.2 %collective-permute-done.8 = bf16[256,256]{1,0:T(8,128)(2,1)S(1)} collective-permute-done((bf16[256,256]{1,0:T(8,128)(2,1)S(1)}, bf16[256,256]{1,0:T(8,128)(2,1)S(1)}, u32[]{:S(2)}, u32[]{:S(2)}) %collective-permute-start.8) | collective-permute-done | bytes 131104 | tf_op jit(solution)/shard_map/ppermute | solution.py:20
  88.9 0.1 collective-permute-start.9
  89.0 0.8 copy-done.11
  89.8 0.1 copy-done.12
  89.9 1.2 %reshape.137 = bf16[256,4,256]{2,1,0:T(4,128)(2,1)} reshape(bf16[256,1024]{1,0:T(8,128)(2,1)S(1)} %pad_maximum_fusion.1) | data formatting | bytes 1048576 | tf_op jit(solution)/shard_map/reshape | solution.py:280
  91.1 1.2 %reshape.140 = bf16[256,4,256]{2,1,0:T(4,128)(2,1)} reshape(bf16[256,1024]{1,0:T(8,128)(2,1)S(1)} %copy-done.6) | data formatting | bytes 1048576 | tf_op jit(solution)/shard_map/reshape | solution.py:283
  92.3 0.7 fusion.7
  93.0 0.7 select_convert_fusion
  (68 shorter events, 0.9 us)
Async XLA Ops:
  0.6 1.7 %copy-start.10 = (bf16[256,256]{1,0:T(8,128)(2,1)S(1)}, bf16[256,256]{1,0:T(8,128)(2,1)}, u32[]{:S(2)}) copy-start(bf16[256,256]{1,0:T(8,128)(2,1)} %param.18) | copy-start | bytes 393220
  0.6 7.9 %copy-start.2 = (bf16[256,4,256]{2,1,0:T(4,128)(2,1)S(1)}, bf16[256,4,256]{2,1,0:T(4,128)(2,1)}, u32[]{:S(2)}) copy-start(bf16[256,4,256]{2,1,0:T(4,128)(2,1)} %param.16) | copy-start | bytes 1572868
  2.3 14.4 %collective-permute-start = (bf16[144,512]{1,0:T(8,128)(2,1)S(1)}, bf16[144,512]{1,0:T(8,128)(2,1)S(1)}, u32[]{:S(2)}, u32[]{:S(2)}) collective-permute-start(bf16[144,512]{1,0:T(8,128)(2,1)S(1)} %pad_maximum_fusion.9), channel_id=1, source_target_pairs={{0,4},{4,8},{8,12},{1,5},{5,9},{9,13},{2,6},{6,10},{10,14},{3,7},{... | collective-permute-start | bytes 442376 | tf_op jit(solution)/shard_map/ppermute | solution.py:20
  8.6 1.0 %copy-start.3 = (bf16[256,4,256]{2,1,0:T(4,128)(2,1)S(1)}, bf16[256,4,256]{2,1,0:T(4,128)(2,1)}, u32[]{:S(2)}) copy-start(bf16[256,4,256]{2,1,0:T(4,128)(2,1)} %param.21) | copy-start | bytes 1572868
  9.6 0.9 copy-start.7
  9.6 1.0 %copy-start.8 = (bf16[256,256]{1,0:T(8,128)(2,1)S(1)}, bf16[256,256]{1,0:T(8,128)(2,1)}, u32[]{:S(2)}) copy-start(bf16[256,256]{1,0:T(8,128)(2,1)} %param.22) | copy-start | bytes 393220
  11.1 0.7 copy-start.16
  12.6 1.1 %copy-start.4 = (bf16[256,4,256]{2,1,0:T(4,128)(2,1)S(1)}, bf16[256,4,256]{2,1,0:T(4,128)(2,1)}, u32[]{:S(2)}) copy-start(bf16[256,4,256]{2,1,0:T(4,128)(2,1)} %param.19) | copy-start | bytes 1572868
  14.7 1.1 %copy-start.5 = (bf16[256,4,256]{2,1,0:T(4,128)(2,1)S(1)}, bf16[256,4,256]{2,1,0:T(4,128)(2,1)}, u32[]{:S(2)}) copy-start(bf16[256,4,256]{2,1,0:T(4,128)(2,1)} %param.24) | copy-start | bytes 1572868
  16.7 8.5 %copy-start.9 = (bf16[256,256]{1,0:T(8,128)(2,1)S(1)}, bf16[256,256]{1,0:T(8,128)(2,1)}, u32[]{:S(2)}) copy-start(bf16[256,256]{1,0:T(8,128)(2,1)} %param.17) | copy-start | bytes 393220
  16.8 16.5 %collective-permute-start.3 = (bf16[272,256]{1,0:T(8,128)(2,1)S(1)}, bf16[272,256]{1,0:T(8,128)(2,1)S(1)}, u32[]{:S(2)}, u32[]{:S(2)}) collective-permute-start(bf16[272,256]{1,0:T(8,128)(2,1)S(1)} %pad_maximum_fusion.10), channel_id=1, source_target_pairs={{0,4},{4,8},{8,12},{1,5},{5,9},{9,13},{2,6},{6,10},{10,14},{3,7},{... | collective-permute-start | bytes 417800 | tf_op jit(solution)/shard_map/ppermute | solution.py:20
  20.4 12.9 %collective-permute-start.2 = (bf16[272,256]{1,0:T(8,128)(2,1)S(1)}, bf16[272,256]{1,0:T(8,128)(2,1)S(1)}, u32[]{:S(2)}, u32[]{:S(2)}) collective-permute-start(bf16[272,256]{1,0:T(8,128)(2,1)S(1)} %pad_maximum_fusion.10), channel_id=1, source_target_pairs={{0,8},{4,12},{1,9},{5,13},{2,10},{6,14},{3,11},{7,15},{16,24},{20,... | collective-permute-start | bytes 417800 | tf_op jit(solution)/shard_map/ppermute | solution.py:20
  23.3 9.9 %collective-permute-start.1 = (bf16[272,256]{1,0:T(8,128)(2,1)S(1)}, bf16[272,256]{1,0:T(8,128)(2,1)S(1)}, u32[]{:S(2)}, u32[]{:S(2)}) collective-permute-start(bf16[272,256]{1,0:T(8,128)(2,1)S(1)} %pad_maximum_fusion.10), channel_id=1, source_target_pairs={{0,12},{1,13},{2,14},{3,15},{16,28},{17,29},{18,30},{19,31}} | collective-permute-start | bytes 417800 | tf_op jit(solution)/shard_map/ppermute | solution.py:20
  33.3 1.8 %collective-permute-start.4 = (bf16[816,256]{1,0:T(8,128)(2,1)S(1)}, bf16[816,256]{1,0:T(8,128)(2,1)S(1)}, u32[]{:S(2)}, u32[]{:S(2)}) collective-permute-start(bf16[816,256]{1,0:T(8,128)(2,1)S(1)} %pad_maximum_fusion.4), channel_id=1, source_target_pairs={{0,1},{1,0},{2,3},{3,2},{4,5},{5,4},{6,7},{7,6},{8,9},{9,8},{10,11... | collective-permute-start | bytes 1253384 | tf_op jit(solution)/shard_map/ppermute | solution.py:230
  59.9 7.8 %copy-start.14 = (f32[384,128]{1,0:T(8,128)S(1)}, f32[384,128]{1,0:T(8,128)}, u32[]{:S(2)}) copy-start(f32[384,128]{1,0:T(8,128)} %get-tuple-element.54) | copy-start | bytes 589828
  59.9 9.8 %collective-permute-start.5 = (f32[1024,256]{1,0:T(8,128)S(1)}, f32[1024,256]{1,0:T(8,128)S(1)}, u32[]{:S(2)}, u32[]{:S(2)}) collective-permute-start(f32[1024,256]{1,0:T(8,128)S(1)} %broadcast_select_fusion), channel_id=1, source_target_pairs={{0,1},{1,0},{2,3},{3,2},{4,5},{5,4},{6,7},{7,6},{8,9},{9,8},{10,11... | collective-permute-start | bytes 3145736 | tf_op jit(solution)/shard_map/ppermute | solution.py:250
  60.1 8.7 %copy-start.13 = (f32[384,128]{1,0:T(8,128)S(1)}, f32[384,128]{1,0:T(8,128)}, u32[]{:S(2)}) copy-start(f32[384,128]{1,0:T(8,128)} %get-tuple-element.56) | copy-start | bytes 589828
  60.1 9.6 %copy-start.1 = (f32[1024,256]{1,0:T(8,128)S(1)}, f32[1024,256]{1,0:T(8,128)}, u32[]{:S(2)}) copy-start(f32[1024,256]{1,0:T(8,128)} %get-tuple-element.62) | copy-start | bytes 3145732
  67.7 2.1 %copy-start = (f32[1024,256]{1,0:T(8,128)S(1)}, f32[1024,256]{1,0:T(8,128)}, u32[]{:S(2)}) copy-start(f32[1024,256]{1,0:T(8,128)} %get-tuple-element.61) | copy-start | bytes 3145732
  68.8 0.9 copy-start.15
  70.1 14.3 %collective-permute-start.6 = (bf16[512,256]{1,0:T(8,128)(2,1)S(1)}, bf16[512,256]{1,0:T(8,128)(2,1)S(1)}, u32[]{:S(2)}, u32[]{:S(2)}) collective-permute-start(bf16[512,256]{1,0:T(8,128)(2,1)S(1)} %pad_maximum_fusion.6), channel_id=1, source_target_pairs={{4,0},{8,4},{12,8},{5,1},{9,5},{13,9},{6,2},{10,6},{14,10},{7,3},{... | collective-permute-start | bytes 786440 | tf_op jit(solution)/shard_map/ppermute | solution.py:20
  71.4 13.1 %collective-permute-start.7 = (bf16[256,256]{1,0:T(8,128)(2,1)S(1)}, bf16[256,256]{1,0:T(8,128)(2,1)S(1)}, u32[]{:S(2)}, u32[]{:S(2)}) collective-permute-start(bf16[256,256]{1,0:T(8,128)(2,1)S(1)} %get-tuple-element.76), channel_id=1, source_target_pairs={{12,0},{13,1},{14,2},{15,3},{28,16},{29,17},{30,18},{31,19}} | collective-permute-start | bytes 393224 | tf_op jit(solution)/shard_map/ppermute | solution.py:20
  72.7 16.0 %collective-permute-start.8 = (bf16[256,256]{1,0:T(8,128)(2,1)S(1)}, bf16[256,256]{1,0:T(8,128)(2,1)S(1)}, u32[]{:S(2)}, u32[]{:S(2)}) collective-permute-start(bf16[256,256]{1,0:T(8,128)(2,1)S(1)} %get-tuple-element.77), channel_id=1, source_target_pairs={{8,0},{12,4},{9,1},{13,5},{10,2},{14,6},{11,3},{15,7},{24,16},{28,... | collective-permute-start | bytes 393224 | tf_op jit(solution)/shard_map/ppermute | solution.py:20
  88.8 1.0 %copy-start.11 = (bf16[256,512]{1,0:T(8,128)(2,1)S(1)}, bf16[256,512]{1,0:T(8,128)(2,1)}, u32[]{:S(2)}) copy-start(bf16[256,512]{1,0:T(8,128)(2,1)} %get-tuple-element.52) | copy-start | bytes 786436
  88.8 1.0 %copy-start.12 = (bf16[256,512]{1,0:T(8,128)(2,1)S(1)}, bf16[256,512]{1,0:T(8,128)(2,1)}, u32[]{:S(2)}) copy-start(bf16[256,512]{1,0:T(8,128)(2,1)} %get-tuple-element.53) | copy-start | bytes 786436
  88.9 3.4 %collective-permute-start.9 = (f32[256,768]{1,0:T(8,128)S(1)}, f32[256,768]{1,0:T(8,128)S(1)}, u32[]{:S(2)}, u32[]{:S(2)}) collective-permute-start(f32[256,768]{1,0:T(8,128)S(1)} %pad_maximum_fusion), channel_id=1, source_target_pairs={{0,1},{1,0},{2,3},{3,2},{4,5},{5,4},{6,7},{7,6},{8,9},{9,8},{10,11... | collective-permute-start | bytes 2359304 | tf_op jit(solution)/shard_map/ppermute | solution.py:274
  89.9 1.2 %copy-start.6 = (bf16[256,1024]{1,0:T(8,128)(2,1)S(1)}, bf16[256,1024]{1,0:T(8,128)(2,1)}, u32[]{:S(2)}) copy-start(bf16[256,1024]{1,0:T(8,128)(2,1)} %get-tuple-element.63) | copy-start | bytes 1572868

commit v13 on v11

--- a/solution.py
+++ b/solution.py
@@ -229,9 +229,9 @@
     f_do = full_grad_out.reshape(n, -1)
     f_dq, f_dk, f_dv = attn_bwd(full_sinks, f_q, f_do, f_keys, f_values, f_bias, 0, groups)
 
-    give = jnp.where(first, f_dv, f_dk)
-    keep = jnp.where(first, f_dk, f_dv)
-    summed = keep + lax.ppermute(give, "rep", swap)
+    to_second = lax.ppermute(f_dv, "rep", [(0, 1)])
+    to_first = lax.ppermute(f_dk, "rep", [(1, 0)])
+    summed = jnp.where(first, f_dk + to_first, f_dv + to_second)
     if g_split < groups:
         w_out2 = attn_bwd(window_sinks, w_q, w_do, w_keys, w_values, w_bias, g_split, groups - g_split)
         w_dq = jnp.concatenate([w_out1[0], w_out2[0]], axis=1)

time: 92.3 us -> 94.4 us (1.023)
  starting transfers between devices: 16.9 us -> 21.5 us
  other arithmetic: 8.87 us -> 7.62 us
  waiting for transfers between devices: 13.9 us -> 12.9 us
    ppermute x1 -> x2, starting transfers between devices: 0.2 us -> 4.79 us  [the longest x1 3.51 us: body(): to_second = lax.ppermute(f_dv, 'rep', [(0, 1)])]
    select_n x1 -> x0, other arithmetic: 1.36 us -> none  [body(): give = jnp.where(first, f_dv, f_dk)]
    ppermute x7, waiting for transfers between devices: 13.6 us -> 12.5 us  [passed_along(): lax.ppermute(value, axis, [(source, source + steps) for source in range(f...]
  transfers between devices with their start and end apart: 10 -> 11, of which waited for: 3 -> 4; matrix products, arithmetic and copies ran while one was open for 12% -> 12% of each run, Pallas kernels for 16% -> 16%
where the time goes in v13:
time: 94.4 us; the launch traced here: 93.7 us
  Pallas kernels  36.5 us (39%)
  starting transfers between devices  21.5 us (23%)
  local copies, waits for them, and re-layouts  14 us (15%)
  waiting for transfers between devices  12.9 us (14%)
  other arithmetic  7.62 us (8%)
  between operations  1.16 us (1%)
    pallas_call x3, Pallas kernels, attn_bwd(): pl.pallas_call(functools.partial(attn_bwd_kernel, g0, gn, pair), grid=gri...  36.5 us
    ppermute x7, starting transfers between devices, passed_along(): lax.ppermute(value, axis, [(source, source + steps) for source in range(f...  16.5 us
    ppermute x7, waiting for transfers between devices, passed_along(): lax.ppermute(value, axis, [(source, source + steps) for source in range(f...  12.5 us
    unnamed x42, local copies, waits for them, and re-layouts  8.07 us
    ppermute x1, starting transfers between devices, body(): to_second = lax.ppermute(f_dv, 'rep', [(0, 1)])  3.51 us
    select_n x2, other arithmetic, make_bias(): return jnp.where(visible, 0.0, NEG).astype(jnp.float32)  2.33 us
  transfers between devices with their start and end apart: 11, of which 4 were waited for; matrix products, arithmetic and copies ran while one was open for 12% of the time, Pallas kernels for 16%

profile of v13, /device:TPU:0, one launch (start us, length us, event | category | flops | bytes accessed | tf_op | source)
XLA Modules:
  0.0 93.7 jit_solution(8931050788757940786)
XLA Ops:
  0.6 0.7 convert.17
  1.4 0.8 slice.148
  2.3 0.8 slice.149
  3.1 4.9 %collective-permute-start = (bf16[144,512]{1,0:T(8,128)(2,1)S(1)}, bf16[144,512]{1,0:T(8,128)(2,1)S(1)}, u32[]{:S(2)}, u32[]{:S(2)}) collective-permute-start(bf16[144,512]{1,0:T(8,128)(2,1)S(1)} %pad_maximum_fusion.9), channel_id=1, source_target_pairs={{0,4},{4,8},{8,12},{1,5},{5,9},{9,13},{2,6},{6,10},{10,14},{3,7},{... | collective-permute-start | bytes 442376 | tf_op jit(solution)/shard_map/ppermute | solution.py:20
  8.2 0.2 broadcast_multiply_fusion.1
  8.4 0.8 copy-done.3
  9.2 0.2 broadcast_multiply_fusion
  9.4 0.7 copy-done.7
  10.2 0.9 copy.17
  11.1 0.2 copy-done.4
  11.3 0.9 copy.18
  12.2 0.9 copy.20
  13.1 0.2 copy-done.5
  13.4 0.9 copy.21
  14.3 3.5 %collective-permute-start.3 = (bf16[272,256]{1,0:T(8,128)(2,1)S(1)}, bf16[272,256]{1,0:T(8,128)(2,1)S(1)}, u32[]{:S(2)}, u32[]{:S(2)}) collective-permute-start(bf16[272,256]{1,0:T(8,128)(2,1)S(1)} %pad_maximum_fusion.10), channel_id=1, source_target_pairs={{0,4},{4,8},{8,12},{1,5},{5,9},{9,13},{2,6},{6,10},{10,14},{3,7},{... | collective-permute-start | bytes 417800 | tf_op jit(solution)/shard_map/ppermute | solution.py:20
  17.8 2.9 %collective-permute-start.2 = (bf16[272,256]{1,0:T(8,128)(2,1)S(1)}, bf16[272,256]{1,0:T(8,128)(2,1)S(1)}, u32[]{:S(2)}, u32[]{:S(2)}) collective-permute-start(bf16[272,256]{1,0:T(8,128)(2,1)S(1)} %pad_maximum_fusion.10), channel_id=1, source_target_pairs={{0,8},{4,12},{1,9},{5,13},{2,10},{6,14},{3,11},{7,15},{16,24},{20,... | collective-permute-start | bytes 417800 | tf_op jit(solution)/shard_map/ppermute | solution.py:20
  20.7 1.3 %collective-permute-start.1 = (bf16[272,256]{1,0:T(8,128)(2,1)S(1)}, bf16[272,256]{1,0:T(8,128)(2,1)S(1)}, u32[]{:S(2)}, u32[]{:S(2)}) collective-permute-start(bf16[272,256]{1,0:T(8,128)(2,1)S(1)} %pad_maximum_fusion.10), channel_id=1, source_target_pairs={{0,12},{1,13},{2,14},{3,15},{16,28},{17,29},{18,30},{19,31}} | collective-permute-start | bytes 417800 | tf_op jit(solution)/shard_map/ppermute | solution.py:20
  22.1 0.7 copy-done.16
  22.8 1.0 %fusion.7.bias_ref = f32[256,384]{1,0:T(8,128)} fusion(s32[384]{0:T(512)S(1)} %get-tuple-element.91, s32[384]{0:T(512)S(1)} %get-tuple-element.92, s32[256]{0:T(256)S(1)} %iota_add_fusion.2, s32[256]{0:T(256)S(1)} %copy-done.16, pred[384]{0:T(512)(128)(4,1)S(1)} %broadcast_compare_fusion.1), kind=kLoop, calls=%fused_computation.19 | loop fusion | flops 786432 | bytes 398720 | tf_op jit(solution)/shard_map/jit(_where)/select_n | solution.py:148
  23.7 0.8 pad_maximum_fusion.7
  24.5 7.4 %shard_map.154 = (bf16[256,512]{1,0:T(8,128)(2,1)}, f32[384,128]{1,0:T(8,128)}, f32[384,128]{1,0:T(8,128)}) custom-call(f32[4,4]{1,0:T(4,128)} %sink_ref.4, bf16[256,1024]{1,0:T(8,128)(2,1)} %bitcast.18, bf16[256,1024]{1,0:T(8,128)(2,1)} %bitcast.20, bf16[384,256]{1,0:T(8,128)(2,1)} %get-tuple-element.89.k_ref, bf16[384,256]{1,0:T(8,128)(2,1)} %get-tuple-element.90.v_ref, ...), custom_call_target="tpu_custom_call" | custom-call | flops 503316480 | bytes 2555904 | tf_op jit(solution)/shard_map/pallas_call | solution.py:110
  32.0 0.1 collective-permute-start.4
  32.1 1.4 %fusion.2.bias_ref = f32[256,1024]{1,0:T(8,128)} fusion(s32[1024]{0:T(1024)S(1)} %pad_add_fusion, s32[1024]{0:T(1024)S(1)} %iota_add_fusion, s32[256]{0:T(256)S(1)} %iota_add_fusion.2, s32[256]{0:T(256)S(1)} %copy-done.16, pred[1024]{0:T(1024)(128)(4,1)S(1)} %broadcast_compare_fusion), kind=kLoop, calls=%fused_computation.4 | loop fusion | flops 1572864 | bytes 1059840 | tf_op jit(solution)/shard_map/jit(_where)/select_n | solution.py:148
  33.4 0.4 collective-permute-done.4
  33.9 0.8 pad_maximum_fusion.3.v_ref
  34.7 0.9 pad_maximum_fusion.2.k_ref
  35.5 21.7 %shard_map.156 = (bf16[256,1024]{1,0:T(8,128)(2,1)}, f32[1024,256]{1,0:T(8,128)}, f32[1024,256]{1,0:T(8,128)}) custom-call(f32[4,4]{1,0:T(4,128)} %sink_ref.5, bf16[256,1024]{1,0:T(8,128)(2,1)} %bitcast.22, bf16[256,1024]{1,0:T(8,128)(2,1)} %bitcast.23, bf16[1024,256]{1,0:T(8,128)(2,1)} %pad_maximum_fusion.2.k_ref, ...), custom_call_target="tpu_custom_call" | custom-call | flops 2684354560 | bytes 7340032 | tf_op jit(solution)/shard_map/pallas_call | solution.py:110
  57.2 1.3 %collective-permute-start.5 = (f32[1024,256]{1,0:T(8,128)}, f32[1024,256]{1,0:T(8,128)S(1)}, u32[]{:S(2)}, u32[]{:S(2)}) collective-permute-start(f32[1024,256]{1,0:T(8,128)} %get-tuple-element.61), channel_id=1, source_target_pairs={{1,0},{3,2},{5,4},{7,6},{9,8},{11,10},{13,12},{15,14},{17,16},{19,... | collective-permute-start | bytes 3145736 | tf_op jit(solution)/shard_map/ppermute | solution.py:233
  58.5 3.5 %collective-permute-start.6 = (f32[1024,256]{1,0:T(8,128)}, f32[1024,256]{1,0:T(8,128)S(1)}, u32[]{:S(2)}, u32[]{:S(2)}) collective-permute-start(f32[1024,256]{1,0:T(8,128)} %get-tuple-element.62), channel_id=1, source_target_pairs={{0,1},{2,3},{4,5},{6,7},{8,9},{10,11},{12,13},{14,15},{16,17},{18,... | collective-permute-start | bytes 3145736 | tf_op jit(solution)/shard_map/ppermute | solution.py:232
  62.1 7.5 %shard_map.155 = (bf16[256,512]{1,0:T(8,128)(2,1)}, f32[384,128]{1,0:T(8,128)}, f32[384,128]{1,0:T(8,128)}) custom-call(f32[4,4]{1,0:T(4,128)} %sink_ref.4, bf16[256,1024]{1,0:T(8,128)(2,1)} %bitcast.19, bf16[256,1024]{1,0:T(8,128)(2,1)} %bitcast.21, bf16[384,256]{1,0:T(8,128)(2,1)} %get-tuple-element.89.k_ref, bf16[384,256]{1,0:T(8,128)(2,1)} %get-tuple-element.90.v_ref, ...), custom_call_target="tpu_custom_call" | custom-call | flops 503316480 | bytes 2555904 | tf_op jit(solution)/shard_map/pallas_call | solution.py:110
  69.6 1.0 %constant_dynamic-update-slice_fusion = f32[384,256]{1,0:T(8,128)S(1)} fusion(f32[384,256]{1,0:T(8,128)S(1)} %constant_dynamic-update-slice_fusion.1, f32[384,128]{1,0:T(8,128)} %get-tuple-element.55), kind=kLoop, calls=%fused_computation.45 | loop fusion | bytes 393216 | tf_op jit(solution)/shard_map/concatenate | solution.py:238
  70.7 0.9 copy-done.15
  71.6 0.3 fusion.12
  72.0 1.3 %collective-permute-start.7 = (bf16[512,256]{1,0:T(8,128)(2,1)S(1)}, bf16[512,256]{1,0:T(8,128)(2,1)S(1)}, u32[]{:S(2)}, u32[]{:S(2)}) collective-permute-start(bf16[512,256]{1,0:T(8,128)(2,1)S(1)} %pad_maximum_fusion.6), channel_id=1, source_target_pairs={{4,0},{8,4},{12,8},{5,1},{9,5},{13,9},{6,2},{10,6},{14,10},{7,3},{... | collective-permute-start | bytes 786440 | tf_op jit(solution)/shard_map/ppermute | solution.py:20
  73.4 1.3 %collective-permute-start.8 = (bf16[256,256]{1,0:T(8,128)(2,1)S(1)}, bf16[256,256]{1,0:T(8,128)(2,1)S(1)}, u32[]{:S(2)}, u32[]{:S(2)}) collective-permute-start(bf16[256,256]{1,0:T(8,128)(2,1)S(1)} %get-tuple-element.76), channel_id=1, source_target_pairs={{12,0},{13,1},{14,2},{15,3},{28,16},{29,17},{30,18},{31,19}} | collective-permute-start | bytes 393224 | tf_op jit(solution)/shard_map/ppermute | solution.py:20
  74.7 1.3 %collective-permute-start.9 = (bf16[256,256]{1,0:T(8,128)(2,1)S(1)}, bf16[256,256]{1,0:T(8,128)(2,1)S(1)}, u32[]{:S(2)}, u32[]{:S(2)}) collective-permute-start(bf16[256,256]{1,0:T(8,128)(2,1)S(1)} %get-tuple-element.77), channel_id=1, source_target_pairs={{8,0},{12,4},{9,1},{13,5},{10,2},{14,6},{11,3},{15,7},{24,16},{28,... | collective-permute-start | bytes 393224 | tf_op jit(solution)/shard_map/ppermute | solution.py:20
  76.0 9.0 %collective-permute-done.7 = bf16[512,256]{1,0:T(8,128)(2,1)S(1)} collective-permute-done((bf16[512,256]{1,0:T(8,128)(2,1)S(1)}, bf16[512,256]{1,0:T(8,128)(2,1)S(1)}, u32[]{:S(2)}, u32[]{:S(2)}) %collective-permute-start.7) | collective-permute-done | bytes 262176 | tf_op jit(solution)/shard_map/ppermute | solution.py:20
  85.1 0.2 collective-permute-done.8
  85.3 3.4 %collective-permute-done.9 = bf16[256,256]{1,0:T(8,128)(2,1)S(1)} collective-permute-done((bf16[256,256]{1,0:T(8,128)(2,1)S(1)}, bf16[256,256]{1,0:T(8,128)(2,1)S(1)}, u32[]{:S(2)}, u32[]{:S(2)}) %collective-permute-start.9) | collective-permute-done | bytes 131104 | tf_op jit(solution)/shard_map/ppermute | solution.py:20
  88.6 0.1 slice_add_fusion.1
  88.8 0.1 collective-permute-start.10
  88.9 0.8 copy-done.11
  89.7 0.1 copy-done.12
  89.8 1.2 %reshape.119 = bf16[256,4,256]{2,1,0:T(4,128)(2,1)} reshape(bf16[256,1024]{1,0:T(8,128)(2,1)S(1)} %pad_maximum_fusion.1) | data formatting | bytes 1048576 | tf_op jit(solution)/shard_map/reshape | solution.py:264
  91.0 1.2 %reshape.121 = bf16[256,4,256]{2,1,0:T(4,128)(2,1)} reshape(bf16[256,1024]{1,0:T(8,128)(2,1)S(1)} %copy-done.6) | data formatting | bytes 1048576 | tf_op jit(solution)/shard_map/reshape | solution.py:267
  92.2 0.1 fusion.3
  92.2 0.7 fusion.14
  92.9 0.7 select_convert_fusion
  (70 shorter events, 0.8 us)
Async XLA Ops:
  0.6 7.5 %copy-start.2 = (bf16[256,4,256]{2,1,0:T(4,128)(2,1)S(1)}, bf16[256,4,256]{2,1,0:T(4,128)(2,1)}, u32[]{:S(2)}) copy-start(bf16[256,4,256]{2,1,0:T(4,128)(2,1)} %param.16) | copy-start | bytes 1572868
  3.1 11.1 %collective-permute-start = (bf16[144,512]{1,0:T(8,128)(2,1)S(1)}, bf16[144,512]{1,0:T(8,128)(2,1)S(1)}, u32[]{:S(2)}, u32[]{:S(2)}) collective-permute-start(bf16[144,512]{1,0:T(8,128)(2,1)S(1)} %pad_maximum_fusion.9), channel_id=1, source_target_pairs={{0,4},{4,8},{8,12},{1,5},{5,9},{9,13},{2,6},{6,10},{10,14},{3,7},{... | collective-permute-start | bytes 442376 | tf_op jit(solution)/shard_map/ppermute | solution.py:20
  8.1 1.0 %copy-start.3 = (bf16[256,4,256]{2,1,0:T(4,128)(2,1)S(1)}, bf16[256,4,256]{2,1,0:T(4,128)(2,1)}, u32[]{:S(2)}) copy-start(bf16[256,4,256]{2,1,0:T(4,128)(2,1)} %param.21) | copy-start | bytes 1572868
  9.2 0.9 copy-start.7
  9.2 1.0 %copy-start.8 = (bf16[256,256]{1,0:T(8,128)(2,1)S(1)}, bf16[256,256]{1,0:T(8,128)(2,1)}, u32[]{:S(2)}) copy-start(bf16[256,256]{1,0:T(8,128)(2,1)} %param.22) | copy-start | bytes 393220
  10.2 1.1 %copy-start.4 = (bf16[256,4,256]{2,1,0:T(4,128)(2,1)S(1)}, bf16[256,4,256]{2,1,0:T(4,128)(2,1)}, u32[]{:S(2)}) copy-start(bf16[256,4,256]{2,1,0:T(4,128)(2,1)} %param.19) | copy-start | bytes 1572868
  12.2 1.1 %copy-start.5 = (bf16[256,4,256]{2,1,0:T(4,128)(2,1)S(1)}, bf16[256,4,256]{2,1,0:T(4,128)(2,1)}, u32[]{:S(2)}) copy-start(bf16[256,4,256]{2,1,0:T(4,128)(2,1)} %param.24) | copy-start | bytes 1572868
  14.3 17.6 %collective-permute-start.3 = (bf16[272,256]{1,0:T(8,128)(2,1)S(1)}, bf16[272,256]{1,0:T(8,128)(2,1)S(1)}, u32[]{:S(2)}, u32[]{:S(2)}) collective-permute-start(bf16[272,256]{1,0:T(8,128)(2,1)S(1)} %pad_maximum_fusion.10), channel_id=1, source_target_pairs={{0,4},{4,8},{8,12},{1,5},{5,9},{9,13},{2,6},{6,10},{10,14},{3,7},{... | collective-permute-start | bytes 417800 | tf_op jit(solution)/shard_map/ppermute | solution.py:20
  17.8 14.1 %collective-permute-start.2 = (bf16[272,256]{1,0:T(8,128)(2,1)S(1)}, bf16[272,256]{1,0:T(8,128)(2,1)S(1)}, u32[]{:S(2)}, u32[]{:S(2)}) collective-permute-start(bf16[272,256]{1,0:T(8,128)(2,1)S(1)} %pad_maximum_fusion.10), channel_id=1, source_target_pairs={{0,8},{4,12},{1,9},{5,13},{2,10},{6,14},{3,11},{7,15},{16,24},{20,... | collective-permute-start | bytes 417800 | tf_op jit(solution)/shard_map/ppermute | solution.py:20
  20.7 11.2 %collective-permute-start.1 = (bf16[272,256]{1,0:T(8,128)(2,1)S(1)}, bf16[272,256]{1,0:T(8,128)(2,1)S(1)}, u32[]{:S(2)}, u32[]{:S(2)}) collective-permute-start(bf16[272,256]{1,0:T(8,128)(2,1)S(1)} %pad_maximum_fusion.10), channel_id=1, source_target_pairs={{0,12},{1,13},{2,14},{3,15},{16,28},{17,29},{18,30},{19,31}} | collective-permute-start | bytes 417800 | tf_op jit(solution)/shard_map/ppermute | solution.py:20
  22.1 0.7 copy-start.16
  22.8 1.0 %copy-start.9 = (bf16[256,256]{1,0:T(8,128)(2,1)S(1)}, bf16[256,256]{1,0:T(8,128)(2,1)}, u32[]{:S(2)}) copy-start(bf16[256,256]{1,0:T(8,128)(2,1)} %param.17) | copy-start | bytes 393220
  22.8 1.0 %copy-start.10 = (bf16[256,256]{1,0:T(8,128)(2,1)S(1)}, bf16[256,256]{1,0:T(8,128)(2,1)}, u32[]{:S(2)}) copy-start(bf16[256,256]{1,0:T(8,128)(2,1)} %param.18) | copy-start | bytes 393220
  32.0 1.8 %collective-permute-start.4 = (bf16[816,256]{1,0:T(8,128)(2,1)S(1)}, bf16[816,256]{1,0:T(8,128)(2,1)S(1)}, u32[]{:S(2)}, u32[]{:S(2)}) collective-permute-start(bf16[816,256]{1,0:T(8,128)(2,1)S(1)} %pad_maximum_fusion.4), channel_id=1, source_target_pairs={{0,1},{1,0},{2,3},{3,2},{4,5},{5,4},{6,7},{7,6},{8,9},{9,8},{10,11... | collective-permute-start | bytes 1253384 | tf_op jit(solution)/shard_map/ppermute | solution.py:214
  57.2 14.3 %collective-permute-start.5 = (f32[1024,256]{1,0:T(8,128)}, f32[1024,256]{1,0:T(8,128)S(1)}, u32[]{:S(2)}, u32[]{:S(2)}) collective-permute-start(f32[1024,256]{1,0:T(8,128)} %get-tuple-element.61), channel_id=1, source_target_pairs={{1,0},{3,2},{5,4},{7,6},{9,8},{11,10},{13,12},{15,14},{17,16},{19,... | collective-permute-start | bytes 3145736 | tf_op jit(solution)/shard_map/ppermute | solution.py:233
  58.5 11.0 %copy-start.14 = (f32[384,128]{1,0:T(8,128)S(1)}, f32[384,128]{1,0:T(8,128)}, u32[]{:S(2)}) copy-start(f32[384,128]{1,0:T(8,128)} %get-tuple-element.54) | copy-start | bytes 589828
  58.5 13.1 %collective-permute-start.6 = (f32[1024,256]{1,0:T(8,128)}, f32[1024,256]{1,0:T(8,128)S(1)}, u32[]{:S(2)}, u32[]{:S(2)}) collective-permute-start(f32[1024,256]{1,0:T(8,128)} %get-tuple-element.62), channel_id=1, source_target_pairs={{0,1},{2,3},{4,5},{6,7},{8,9},{10,11},{12,13},{14,15},{16,17},{18,... | collective-permute-start | bytes 3145736 | tf_op jit(solution)/shard_map/ppermute | solution.py:232
  62.1 8.6 %copy-start.13 = (f32[384,128]{1,0:T(8,128)S(1)}, f32[384,128]{1,0:T(8,128)}, u32[]{:S(2)}) copy-start(f32[384,128]{1,0:T(8,128)} %get-tuple-element.56) | copy-start | bytes 589828
  62.1 9.5 %copy-start.1 = (f32[1024,256]{1,0:T(8,128)S(1)}, f32[1024,256]{1,0:T(8,128)}, u32[]{:S(2)}) copy-start(f32[1024,256]{1,0:T(8,128)} %get-tuple-element.62) | copy-start | bytes 3145732
  69.5 2.1 %copy-start = (f32[1024,256]{1,0:T(8,128)S(1)}, f32[1024,256]{1,0:T(8,128)}, u32[]{:S(2)}) copy-start(f32[1024,256]{1,0:T(8,128)} %get-tuple-element.61) | copy-start | bytes 3145732
  70.6 0.9 copy-start.15
  72.0 12.9 %collective-permute-start.7 = (bf16[512,256]{1,0:T(8,128)(2,1)S(1)}, bf16[512,256]{1,0:T(8,128)(2,1)S(1)}, u32[]{:S(2)}, u32[]{:S(2)}) collective-permute-start(bf16[512,256]{1,0:T(8,128)(2,1)S(1)} %pad_maximum_fusion.6), channel_id=1, source_target_pairs={{4,0},{8,4},{12,8},{5,1},{9,5},{13,9},{6,2},{10,6},{14,10},{7,3},{... | collective-permute-start | bytes 786440 | tf_op jit(solution)/shard_map/ppermute | solution.py:20
  73.4 11.9 %collective-permute-start.8 = (bf16[256,256]{1,0:T(8,128)(2,1)S(1)}, bf16[256,256]{1,0:T(8,128)(2,1)S(1)}, u32[]{:S(2)}, u32[]{:S(2)}) collective-permute-start(bf16[256,256]{1,0:T(8,128)(2,1)S(1)} %get-tuple-element.76), channel_id=1, source_target_pairs={{12,0},{13,1},{14,2},{15,3},{28,16},{29,17},{30,18},{31,19}} | collective-permute-start | bytes 393224 | tf_op jit(solution)/shard_map/ppermute | solution.py:20
  74.7 13.9 %collective-permute-start.9 = (bf16[256,256]{1,0:T(8,128)(2,1)S(1)}, bf16[256,256]{1,0:T(8,128)(2,1)S(1)}, u32[]{:S(2)}, u32[]{:S(2)}) collective-permute-start(bf16[256,256]{1,0:T(8,128)(2,1)S(1)} %get-tuple-element.77), channel_id=1, source_target_pairs={{8,0},{12,4},{9,1},{13,5},{10,2},{14,6},{11,3},{15,7},{24,16},{28,... | collective-permute-start | bytes 393224 | tf_op jit(solution)/shard_map/ppermute | solution.py:20
  88.7 1.0 %copy-start.11 = (bf16[256,512]{1,0:T(8,128)(2,1)S(1)}, bf16[256,512]{1,0:T(8,128)(2,1)}, u32[]{:S(2)}) copy-start(bf16[256,512]{1,0:T(8,128)(2,1)} %get-tuple-element.52) | copy-start | bytes 786436
  88.7 1.0 %copy-start.12 = (bf16[256,512]{1,0:T(8,128)(2,1)S(1)}, bf16[256,512]{1,0:T(8,128)(2,1)}, u32[]{:S(2)}) copy-start(bf16[256,512]{1,0:T(8,128)(2,1)} %get-tuple-element.53) | copy-start | bytes 786436
  88.8 3.4 %collective-permute-start.10 = (f32[256,768]{1,0:T(8,128)S(1)}, f32[256,768]{1,0:T(8,128)S(1)}, u32[]{:S(2)}, u32[]{:S(2)}) collective-permute-start(f32[256,768]{1,0:T(8,128)S(1)} %pad_maximum_fusion), channel_id=1, source_target_pairs={{0,1},{1,0},{2,3},{3,2},{4,5},{5,4},{6,7},{7,6},{8,9},{9,8},{10,11... | collective-permute-start | bytes 2359304 | tf_op jit(solution)/shard_map/ppermute | solution.py:258
  89.8 1.2 %copy-start.6 = (bf16[256,1024]{1,0:T(8,128)(2,1)S(1)}, bf16[256,1024]{1,0:T(8,128)(2,1)}, u32[]{:S(2)}) copy-start(bf16[256,1024]{1,0:T(8,128)(2,1)} %get-tuple-element.63) | copy-start | bytes 1572868

commit v14 on v11

--- a/solution.py
+++ b/solution.py
@@ -34,7 +34,7 @@
         dk_ref[...] = jnp.zeros_like(dk_ref)
         dv_ref[...] = jnp.zeros_like(dv_ref)
 
-    bias = bias_ref[...]
+    bias = bias_ref[...].astype(jnp.float32)
     k_block = k_ref[...]
     v_block = v_ref[...]
     dq_parts = []
@@ -135,7 +135,7 @@
         cost_estimate=pl.CostEstimate(
             flops=10 * gn * heads * n * m * HD,
             transcendentals=gn * heads * n * m,
-            bytes_accessed=4 * n * m + 4 * n * gn * heads * HD * 3 + 12 * m * gn * HD,
+            bytes_accessed=2 * n * m + 4 * n * gn * heads * HD * 3 + 12 * m * gn * HD,
         ),
     )(sinks, queries, grads, keys, values, bias)
 
@@ -145,7 +145,7 @@
     visible = (distance >= 0) & (key_pos[None, :] >= 0) & (query_seg[:, None] == key_seg[None, :])
     if window is not None:
         visible = visible & (distance < window)
-    return jnp.where(visible, 0.0, NEG).astype(jnp.float32)
+    return jnp.where(visible, 0.0, NEG).astype(jnp.bfloat16)
 
 
 def seg_rows(ids, width):

time: 92.3 us -> 92 us (level)
    select_n x2 -> x0, other arithmetic: 2.34 us -> none  [make_bias(): return jnp.where(visible, 0.0, NEG).astype(jnp.float32)]
    convert_element_type x0 -> x2, other arithmetic: none -> 2.11 us  [make_bias(): return jnp.where(visible, 0.0, NEG).astype(jnp.bfloat16)]
where the time goes in v14:
time: 92 us; the launch traced here: 91.3 us
  Pallas kernels  36.4 us (40%)
  starting transfers between devices  17 us (18%)
  waiting for transfers between devices  14.7 us (16%)
  local copies, waits for them, and re-layouts  13.4 us (15%)
  other arithmetic  8.63 us (9%)
  between operations  1.15 us (1%)
    pallas_call x3, Pallas kernels, attn_bwd(): pl.pallas_call(functools.partial(attn_bwd_kernel, g0, gn, pair), grid=gri...  36.4 us
    ppermute x7, starting transfers between devices, passed_along(): lax.ppermute(value, axis, [(source, source + steps) for source in range(f...  16.7 us
    ppermute x7, waiting for transfers between devices, passed_along(): lax.ppermute(value, axis, [(source, source + steps) for source in range(f...  14.2 us
    unnamed x42, local copies, waits for them, and re-layouts  7.4 us
    convert_element_type x2, other arithmetic, make_bias(): return jnp.where(visible, 0.0, NEG).astype(jnp.bfloat16)  2.11 us
  transfers between devices with their start and end apart: 10, of which 3 were waited for; matrix products, arithmetic and copies ran while one was open for 12% of the time, Pallas kernels for 16%

profile of v14, /device:TPU:0, one launch (start us, length us, event | category | flops | bytes accessed | tf_op | source)
XLA Modules:
  0.0 91.3 jit_solution(4665324253903281499)
XLA Ops:
  0.6 0.7 convert.17
  1.4 0.8 slice.148
  2.3 0.8 slice.149
  3.1 4.9 %collective-permute-start = (bf16[144,512]{1,0:T(8,128)(2,1)S(1)}, bf16[144,512]{1,0:T(8,128)(2,1)S(1)}, u32[]{:S(2)}, u32[]{:S(2)}) collective-permute-start(bf16[144,512]{1,0:T(8,128)(2,1)S(1)} %pad_maximum_fusion.9), channel_id=1, source_target_pairs={{0,4},{4,8},{8,12},{1,5},{5,9},{9,13},{2,6},{6,10},{10,14},{3,7},{... | collective-permute-start | bytes 442376 | tf_op jit(solution)/shard_map/ppermute | solution.py:20
  8.2 0.2 broadcast_multiply_fusion.1
  8.4 0.8 copy-done.3
  9.2 0.2 broadcast_multiply_fusion
  9.4 0.7 copy-done.7
  10.1 0.1 copy-done.8
  10.2 0.9 copy.17
  11.1 0.2 copy-done.4
  11.3 0.9 copy.18
  12.2 0.9 copy.20
  13.1 0.2 copy-done.5
  13.4 0.9 copy.21
  14.3 3.6 %collective-permute-start.3 = (bf16[272,256]{1,0:T(8,128)(2,1)S(1)}, bf16[272,256]{1,0:T(8,128)(2,1)S(1)}, u32[]{:S(2)}, u32[]{:S(2)}) collective-permute-start(bf16[272,256]{1,0:T(8,128)(2,1)S(1)} %pad_maximum_fusion.10), channel_id=1, source_target_pairs={{0,4},{4,8},{8,12},{1,5},{5,9},{9,13},{2,6},{6,10},{10,14},{3,7},{... | collective-permute-start | bytes 417800 | tf_op jit(solution)/shard_map/ppermute | solution.py:20
  18.0 2.9 %collective-permute-start.2 = (bf16[272,256]{1,0:T(8,128)(2,1)S(1)}, bf16[272,256]{1,0:T(8,128)(2,1)S(1)}, u32[]{:S(2)}, u32[]{:S(2)}) collective-permute-start(bf16[272,256]{1,0:T(8,128)(2,1)S(1)} %pad_maximum_fusion.10), channel_id=1, source_target_pairs={{0,8},{4,12},{1,9},{5,13},{2,10},{6,14},{3,11},{7,15},{16,24},{20,... | collective-permute-start | bytes 417800 | tf_op jit(solution)/shard_map/ppermute | solution.py:20
  20.9 1.3 %collective-permute-start.1 = (bf16[272,256]{1,0:T(8,128)(2,1)S(1)}, bf16[272,256]{1,0:T(8,128)(2,1)S(1)}, u32[]{:S(2)}, u32[]{:S(2)}) collective-permute-start(bf16[272,256]{1,0:T(8,128)(2,1)S(1)} %pad_maximum_fusion.10), channel_id=1, source_target_pairs={{0,12},{1,13},{2,14},{3,15},{16,28},{17,29},{18,30},{19,31}} | collective-permute-start | bytes 417800 | tf_op jit(solution)/shard_map/ppermute | solution.py:20
  22.3 0.9 select_convert_fusion.1.bias_ref
  23.2 0.8 pad_maximum_fusion.7
  23.9 7.3 %shard_map.154 = (bf16[256,512]{1,0:T(8,128)(2,1)}, f32[384,128]{1,0:T(8,128)}, f32[384,128]{1,0:T(8,128)}) custom-call(f32[4,4]{1,0:T(4,128)} %sink_ref.4, bf16[256,1024]{1,0:T(8,128)(2,1)} %bitcast.18, bf16[256,1024]{1,0:T(8,128)(2,1)} %bitcast.20, bf16[384,256]{1,0:T(8,128)(2,1)} %get-tuple-element.89.k_ref, bf16[384,256]{1,0:T(8,128)(2,1)} %get-tuple-element.90.v_ref, ...), custom_call_target="tpu_custom_call" | custom-call | flops 503316480 | bytes 2359296 | tf_op jit(solution)/shard_map/pallas_call | solution.py:110
  31.3 0.1 collective-permute-start.4
  31.4 1.2 %select_convert_fusion.bias_ref = bf16[256,1024]{1,0:T(8,128)(2,1)} fusion(s32[1024]{0:T(1024)S(1)} %pad_add_fusion, s32[1024]{0:T(1024)S(1)} %iota_add_fusion, s32[256]{0:T(256)S(1)} %iota_add_fusion.2, s32[256]{0:T(256)S(1)} %copy-done.16, pred[1024]{0:T(1024)(128)(4,1)S(1)} %broadcast_compare_fusion), kind=kLoop, calls=%fused_computation.1 | loop fusion | flops 1835008 | bytes 535552 | tf_op jit(solution)/shard_map/convert_element_type | solution.py:148
  32.6 0.5 collective-permute-done.4
  33.2 0.8 pad_maximum_fusion.3.v_ref
  34.0 0.8 pad_maximum_fusion.2.k_ref
  34.8 21.6 %shard_map.156 = (bf16[256,1024]{1,0:T(8,128)(2,1)}, f32[1024,256]{1,0:T(8,128)}, f32[1024,256]{1,0:T(8,128)}) custom-call(f32[4,4]{1,0:T(4,128)} %sink_ref.5, bf16[256,1024]{1,0:T(8,128)(2,1)} %bitcast.22, bf16[256,1024]{1,0:T(8,128)(2,1)} %bitcast.23, bf16[1024,256]{1,0:T(8,128)(2,1)} %pad_maximum_fusion.2.k_ref, ...), custom_call_target="tpu_custom_call" | custom-call | flops 2684354560 | bytes 6815744 | tf_op jit(solution)/shard_map/pallas_call | solution.py:110
  56.4 1.4 %broadcast_select_fusion = f32[1024,256]{1,0:T(8,128)S(1)} fusion(f32[1024,256]{1,0:T(8,128)} %get-tuple-element.62, f32[1024,256]{1,0:T(8,128)} %get-tuple-element.61, pred[]{:T(512)S(6)} %eq.14), kind=kLoop, calls=%fused_computation.15 | loop fusion | flops 262144 | bytes 3145729 | tf_op jit(solution)/shard_map/jit(_where)/select_n | solution.py:232
  57.8 0.2 collective-permute-start.5
  58.0 7.6 %shard_map.155 = (bf16[256,512]{1,0:T(8,128)(2,1)}, f32[384,128]{1,0:T(8,128)}, f32[384,128]{1,0:T(8,128)}) custom-call(f32[4,4]{1,0:T(4,128)} %sink_ref.4, bf16[256,1024]{1,0:T(8,128)(2,1)} %bitcast.19, bf16[256,1024]{1,0:T(8,128)(2,1)} %bitcast.21, bf16[384,256]{1,0:T(8,128)(2,1)} %get-tuple-element.89.k_ref, bf16[384,256]{1,0:T(8,128)(2,1)} %get-tuple-element.90.v_ref, ...), custom_call_target="tpu_custom_call" | custom-call | flops 503316480 | bytes 2359296 | tf_op jit(solution)/shard_map/pallas_call | solution.py:110
  65.6 1.0 %constant_dynamic-update-slice_fusion = f32[384,256]{1,0:T(8,128)S(1)} fusion(f32[384,256]{1,0:T(8,128)S(1)} %constant_dynamic-update-slice_fusion.1, f32[384,128]{1,0:T(8,128)} %get-tuple-element.55), kind=kLoop, calls=%fused_computation.46 | loop fusion | bytes 393216 | tf_op jit(solution)/shard_map/concatenate | solution.py:238
  66.7 0.9 copy-done.15
  67.6 0.2 fusion.10
  67.9 1.3 %collective-permute-start.6 = (bf16[512,256]{1,0:T(8,128)(2,1)S(1)}, bf16[512,256]{1,0:T(8,128)(2,1)S(1)}, u32[]{:S(2)}, u32[]{:S(2)}) collective-permute-start(bf16[512,256]{1,0:T(8,128)(2,1)S(1)} %pad_maximum_fusion.6), channel_id=1, source_target_pairs={{4,0},{8,4},{12,8},{5,1},{9,5},{13,9},{6,2},{10,6},{14,10},{7,3},{... | collective-permute-start | bytes 786440 | tf_op jit(solution)/shard_map/ppermute | solution.py:20
  69.3 1.3 %collective-permute-start.7 = (bf16[256,256]{1,0:T(8,128)(2,1)S(1)}, bf16[256,256]{1,0:T(8,128)(2,1)S(1)}, u32[]{:S(2)}, u32[]{:S(2)}) collective-permute-start(bf16[256,256]{1,0:T(8,128)(2,1)S(1)} %get-tuple-element.76), channel_id=1, source_target_pairs={{12,0},{13,1},{14,2},{15,3},{28,16},{29,17},{30,18},{31,19}} | collective-permute-start | bytes 393224 | tf_op jit(solution)/shard_map/ppermute | solution.py:20
  70.6 1.3 %collective-permute-start.8 = (bf16[256,256]{1,0:T(8,128)(2,1)S(1)}, bf16[256,256]{1,0:T(8,128)(2,1)S(1)}, u32[]{:S(2)}, u32[]{:S(2)}) collective-permute-start(bf16[256,256]{1,0:T(8,128)(2,1)S(1)} %get-tuple-element.77), channel_id=1, source_target_pairs={{8,0},{12,4},{9,1},{13,5},{10,2},{14,6},{11,3},{15,7},{24,16},{28,... | collective-permute-start | bytes 393224 | tf_op jit(solution)/shard_map/ppermute | solution.py:20
  71.9 10.5 %collective-permute-done.6 = bf16[512,256]{1,0:T(8,128)(2,1)S(1)} collective-permute-done((bf16[512,256]{1,0:T(8,128)(2,1)S(1)}, bf16[512,256]{1,0:T(8,128)(2,1)S(1)}, u32[]{:S(2)}, u32[]{:S(2)}) %collective-permute-start.6) | collective-permute-done | bytes 262176 | tf_op jit(solution)/shard_map/ppermute | solution.py:20
  82.4 0.1 fusion.6
  82.5 3.7 %collective-permute-done.8 = bf16[256,256]{1,0:T(8,128)(2,1)S(1)} collective-permute-done((bf16[256,256]{1,0:T(8,128)(2,1)S(1)}, bf16[256,256]{1,0:T(8,128)(2,1)S(1)}, u32[]{:S(2)}, u32[]{:S(2)}) %collective-permute-start.8) | collective-permute-done | bytes 131104 | tf_op jit(solution)/shard_map/ppermute | solution.py:20
  86.2 0.1 slice_add_fusion.1
  86.4 0.1 collective-permute-start.9
  86.4 0.8 copy-done.11
  87.2 0.1 copy-done.12
  87.4 1.2 %reshape.119 = bf16[256,4,256]{2,1,0:T(4,128)(2,1)} reshape(bf16[256,1024]{1,0:T(8,128)(2,1)S(1)} %pad_maximum_fusion.1) | data formatting | bytes 1048576 | tf_op jit(solution)/shard_map/reshape | solution.py:264
  88.6 1.2 %reshape.121 = bf16[256,4,256]{2,1,0:T(4,128)(2,1)} reshape(bf16[256,1024]{1,0:T(8,128)(2,1)S(1)} %copy-done.6) | data formatting | bytes 1048576 | tf_op jit(solution)/shard_map/reshape | solution.py:267
  89.7 0.1 fusion.2
  89.8 0.7 fusion.12
  90.5 0.7 select_convert_fusion.2
  (69 shorter events, 0.7 us)
Async XLA Ops:
  0.6 7.5 %copy-start.2 = (bf16[256,4,256]{2,1,0:T(4,128)(2,1)S(1)}, bf16[256,4,256]{2,1,0:T(4,128)(2,1)}, u32[]{:S(2)}) copy-start(bf16[256,4,256]{2,1,0:T(4,128)(2,1)} %param.16) | copy-start | bytes 1572868
  3.1 11.1 %collective-permute-start = (bf16[144,512]{1,0:T(8,128)(2,1)S(1)}, bf16[144,512]{1,0:T(8,128)(2,1)S(1)}, u32[]{:S(2)}, u32[]{:S(2)}) collective-permute-start(bf16[144,512]{1,0:T(8,128)(2,1)S(1)} %pad_maximum_fusion.9), channel_id=1, source_target_pairs={{0,4},{4,8},{8,12},{1,5},{5,9},{9,13},{2,6},{6,10},{10,14},{3,7},{... | collective-permute-start | bytes 442376 | tf_op jit(solution)/shard_map/ppermute | solution.py:20
  8.1 1.0 %copy-start.3 = (bf16[256,4,256]{2,1,0:T(4,128)(2,1)S(1)}, bf16[256,4,256]{2,1,0:T(4,128)(2,1)}, u32[]{:S(2)}) copy-start(bf16[256,4,256]{2,1,0:T(4,128)(2,1)} %param.21) | copy-start | bytes 1572868
  9.2 0.9 copy-start.7
  9.2 1.0 %copy-start.8 = (bf16[256,256]{1,0:T(8,128)(2,1)S(1)}, bf16[256,256]{1,0:T(8,128)(2,1)}, u32[]{:S(2)}) copy-start(bf16[256,256]{1,0:T(8,128)(2,1)} %param.22) | copy-start | bytes 393220
  10.2 1.1 %copy-start.4 = (bf16[256,4,256]{2,1,0:T(4,128)(2,1)S(1)}, bf16[256,4,256]{2,1,0:T(4,128)(2,1)}, u32[]{:S(2)}) copy-start(bf16[256,4,256]{2,1,0:T(4,128)(2,1)} %param.19) | copy-start | bytes 1572868
  12.2 1.1 %copy-start.5 = (bf16[256,4,256]{2,1,0:T(4,128)(2,1)S(1)}, bf16[256,4,256]{2,1,0:T(4,128)(2,1)}, u32[]{:S(2)}) copy-start(bf16[256,4,256]{2,1,0:T(4,128)(2,1)} %param.24) | copy-start | bytes 1572868
  14.3 8.0 %copy-start.16 = (s32[256]{0:T(256)S(1)}, s32[256]{0:T(256)}, u32[]{:S(2)}) copy-start(s32[256]{0:T(256)} %param.15) | copy-start | bytes 3076
  14.3 8.9 %copy-start.10 = (bf16[256,256]{1,0:T(8,128)(2,1)S(1)}, bf16[256,256]{1,0:T(8,128)(2,1)}, u32[]{:S(2)}) copy-start(bf16[256,256]{1,0:T(8,128)(2,1)} %param.18) | copy-start | bytes 393220
  14.3 8.8 %copy-start.9 = (bf16[256,256]{1,0:T(8,128)(2,1)S(1)}, bf16[256,256]{1,0:T(8,128)(2,1)}, u32[]{:S(2)}) copy-start(bf16[256,256]{1,0:T(8,128)(2,1)} %param.17) | copy-start | bytes 393220
  14.3 16.9 %collective-permute-start.3 = (bf16[272,256]{1,0:T(8,128)(2,1)S(1)}, bf16[272,256]{1,0:T(8,128)(2,1)S(1)}, u32[]{:S(2)}, u32[]{:S(2)}) collective-permute-start(bf16[272,256]{1,0:T(8,128)(2,1)S(1)} %pad_maximum_fusion.10), channel_id=1, source_target_pairs={{0,4},{4,8},{8,12},{1,5},{5,9},{9,13},{2,6},{6,10},{10,14},{3,7},{... | collective-permute-start | bytes 417800 | tf_op jit(solution)/shard_map/ppermute | solution.py:20
  18.0 13.2 %collective-permute-start.2 = (bf16[272,256]{1,0:T(8,128)(2,1)S(1)}, bf16[272,256]{1,0:T(8,128)(2,1)S(1)}, u32[]{:S(2)}, u32[]{:S(2)}) collective-permute-start(bf16[272,256]{1,0:T(8,128)(2,1)S(1)} %pad_maximum_fusion.10), channel_id=1, source_target_pairs={{0,8},{4,12},{1,9},{5,13},{2,10},{6,14},{3,11},{7,15},{16,24},{20,... | collective-permute-start | bytes 417800 | tf_op jit(solution)/shard_map/ppermute | solution.py:20
  20.9 10.3 %collective-permute-start.1 = (bf16[272,256]{1,0:T(8,128)(2,1)S(1)}, bf16[272,256]{1,0:T(8,128)(2,1)S(1)}, u32[]{:S(2)}, u32[]{:S(2)}) collective-permute-start(bf16[272,256]{1,0:T(8,128)(2,1)S(1)} %pad_maximum_fusion.10), channel_id=1, source_target_pairs={{0,12},{1,13},{2,14},{3,15},{16,28},{17,29},{18,30},{19,31}} | collective-permute-start | bytes 417800 | tf_op jit(solution)/shard_map/ppermute | solution.py:20
  31.3 1.8 %collective-permute-start.4 = (bf16[816,256]{1,0:T(8,128)(2,1)S(1)}, bf16[816,256]{1,0:T(8,128)(2,1)S(1)}, u32[]{:S(2)}, u32[]{:S(2)}) collective-permute-start(bf16[816,256]{1,0:T(8,128)(2,1)S(1)} %pad_maximum_fusion.4), channel_id=1, source_target_pairs={{0,1},{1,0},{2,3},{3,2},{4,5},{5,4},{6,7},{7,6},{8,9},{9,8},{10,11... | collective-permute-start | bytes 1253384 | tf_op jit(solution)/shard_map/ppermute | solution.py:214
  57.8 7.8 %copy-start.14 = (f32[384,128]{1,0:T(8,128)S(1)}, f32[384,128]{1,0:T(8,128)}, u32[]{:S(2)}) copy-start(f32[384,128]{1,0:T(8,128)} %get-tuple-element.54) | copy-start | bytes 589828
  57.8 9.8 %collective-permute-start.5 = (f32[1024,256]{1,0:T(8,128)S(1)}, f32[1024,256]{1,0:T(8,128)S(1)}, u32[]{:S(2)}, u32[]{:S(2)}) collective-permute-start(f32[1024,256]{1,0:T(8,128)S(1)} %broadcast_select_fusion), channel_id=1, source_target_pairs={{0,1},{1,0},{2,3},{3,2},{4,5},{5,4},{6,7},{7,6},{8,9},{9,8},{10,11... | collective-permute-start | bytes 3145736 | tf_op jit(solution)/shard_map/ppermute | solution.py:234
  58.0 8.7 %copy-start.13 = (f32[384,128]{1,0:T(8,128)S(1)}, f32[384,128]{1,0:T(8,128)}, u32[]{:S(2)}) copy-start(f32[384,128]{1,0:T(8,128)} %get-tuple-element.56) | copy-start | bytes 589828
  58.0 9.6 %copy-start.1 = (f32[1024,256]{1,0:T(8,128)S(1)}, f32[1024,256]{1,0:T(8,128)}, u32[]{:S(2)}) copy-start(f32[1024,256]{1,0:T(8,128)} %get-tuple-element.62) | copy-start | bytes 3145732
  65.6 2.1 %copy-start = (f32[1024,256]{1,0:T(8,128)S(1)}, f32[1024,256]{1,0:T(8,128)}, u32[]{:S(2)}) copy-start(f32[1024,256]{1,0:T(8,128)} %get-tuple-element.61) | copy-start | bytes 3145732
  66.6 0.9 %copy-start.15 = (f32[384,128]{1,0:T(8,128)S(1)}, f32[384,128]{1,0:T(8,128)}, u32[]{:S(2)}) copy-start(f32[384,128]{1,0:T(8,128)} %get-tuple-element.57) | copy-start | bytes 589828
  67.9 14.4 %collective-permute-start.6 = (bf16[512,256]{1,0:T(8,128)(2,1)S(1)}, bf16[512,256]{1,0:T(8,128)(2,1)S(1)}, u32[]{:S(2)}, u32[]{:S(2)}) collective-permute-start(bf16[512,256]{1,0:T(8,128)(2,1)S(1)} %pad_maximum_fusion.6), channel_id=1, source_target_pairs={{4,0},{8,4},{12,8},{5,1},{9,5},{13,9},{6,2},{10,6},{14,10},{7,3},{... | collective-permute-start | bytes 786440 | tf_op jit(solution)/shard_map/ppermute | solution.py:20
  69.3 13.2 %collective-permute-start.7 = (bf16[256,256]{1,0:T(8,128)(2,1)S(1)}, bf16[256,256]{1,0:T(8,128)(2,1)S(1)}, u32[]{:S(2)}, u32[]{:S(2)}) collective-permute-start(bf16[256,256]{1,0:T(8,128)(2,1)S(1)} %get-tuple-element.76), channel_id=1, source_target_pairs={{12,0},{13,1},{14,2},{15,3},{28,16},{29,17},{30,18},{31,19}} | collective-permute-start | bytes 393224 | tf_op jit(solution)/shard_map/ppermute | solution.py:20
  70.6 15.6 %collective-permute-start.8 = (bf16[256,256]{1,0:T(8,128)(2,1)S(1)}, bf16[256,256]{1,0:T(8,128)(2,1)S(1)}, u32[]{:S(2)}, u32[]{:S(2)}) collective-permute-start(bf16[256,256]{1,0:T(8,128)(2,1)S(1)} %get-tuple-element.77), channel_id=1, source_target_pairs={{8,0},{12,4},{9,1},{13,5},{10,2},{14,6},{11,3},{15,7},{24,16},{28,... | collective-permute-start | bytes 393224 | tf_op jit(solution)/shard_map/ppermute | solution.py:20
  86.3 1.0 %copy-start.11 = (bf16[256,512]{1,0:T(8,128)(2,1)S(1)}, bf16[256,512]{1,0:T(8,128)(2,1)}, u32[]{:S(2)}) copy-start(bf16[256,512]{1,0:T(8,128)(2,1)} %get-tuple-element.52) | copy-start | bytes 786436
  86.3 1.0 %copy-start.12 = (bf16[256,512]{1,0:T(8,128)(2,1)S(1)}, bf16[256,512]{1,0:T(8,128)(2,1)}, u32[]{:S(2)}) copy-start(bf16[256,512]{1,0:T(8,128)(2,1)} %get-tuple-element.53) | copy-start | bytes 786436
  86.4 3.4 %collective-permute-start.9 = (f32[256,768]{1,0:T(8,128)S(1)}, f32[256,768]{1,0:T(8,128)S(1)}, u32[]{:S(2)}, u32[]{:S(2)}) collective-permute-start(f32[256,768]{1,0:T(8,128)S(1)} %pad_maximum_fusion), channel_id=1, source_target_pairs={{0,1},{1,0},{2,3},{3,2},{4,5},{5,4},{6,7},{7,6},{8,9},{9,8},{10,11... | collective-permute-start | bytes 2359304 | tf_op jit(solution)/shard_map/ppermute | solution.py:258
  87.4 1.2 %copy-start.6 = (bf16[256,1024]{1,0:T(8,128)(2,1)S(1)}, bf16[256,1024]{1,0:T(8,128)(2,1)}, u32[]{:S(2)}) copy-start(bf16[256,1024]{1,0:T(8,128)(2,1)} %get-tuple-element.63) | copy-start | bytes 1572868

commit v15 on v14

--- a/solution.py
+++ b/solution.py
@@ -24,15 +24,16 @@
     return jnp.where(half == 0, block[:, :HD], block[:, HD:])
 
 
-def attn_bwd_kernel(g0, gn, pair, sink_ref, q_ref, do_ref, k_ref, v_ref, bias_ref, dq_ref, dk_ref, dv_ref):
+def attn_bwd_kernel(g0, gn, pair, single, sink_ref, q_ref, do_ref, k_ref, v_ref, bias_ref, dq_ref, dk_ref, dv_ref):
     t = pl.program_id(0)
     i = pl.program_id(1)
     heads = q_ref.shape[1] // (HD * pair)
 
-    @pl.when((t == 0) & (i == 0))
-    def _():
-        dk_ref[...] = jnp.zeros_like(dk_ref)
-        dv_ref[...] = jnp.zeros_like(dv_ref)
+    if not single:
+        @pl.when((t == 0) & (i == 0))
+        def _():
+            dk_ref[...] = jnp.zeros_like(dk_ref)
+            dv_ref[...] = jnp.zeros_like(dv_ref)
 
     bias = bias_ref[...].astype(jnp.float32)
     k_block = k_ref[...]
@@ -78,6 +79,10 @@
     dv_step = jnp.concatenate(dv_parts, axis=1) if pair >= 2 else dv_parts[0]
     wide = pair * HD
 
+    if single:
+        dk_ref[...] = dk_step
+        dv_ref[...] = dv_step
+        return
     for tt in range(gn // pair):
         @pl.when(t == tt)
         def _():
@@ -108,7 +113,7 @@
         key_map = lambda t, i: (0, (g0 + t) // 2)
 
     return pl.pallas_call(
-        functools.partial(attn_bwd_kernel, g0, gn, pair),
+        functools.partial(attn_bwd_kernel, g0, gn, pair, gn == pair and rows == n),
         grid=grid,
         in_specs=[
             pl.BlockSpec(memory_space=pltpu.SMEM),

time: 92 us -> 92 us (level)
  no operation moved by 1% of the time
where the time goes in v15:
time: 92 us; the launch traced here: 91.3 us
  Pallas kernels  36.4 us (40%)
  starting transfers between devices  17 us (18%)
  waiting for transfers between devices  14.7 us (16%)
  local copies, waits for them, and re-layouts  13.4 us (15%)
  other arithmetic  8.63 us (9%)
  between operations  1.15 us (1%)
    pallas_call x3, Pallas kernels, attn_bwd(): pl.pallas_call(functools.partial(attn_bwd_kernel, g0, gn, pair, gn == pai...  36.4 us
    ppermute x7, starting transfers between devices, passed_along(): lax.ppermute(value, axis, [(source, source + steps) for source in range(f...  16.7 us
    ppermute x7, waiting for transfers between devices, passed_along(): lax.ppermute(value, axis, [(source, source + steps) for source in range(f...  14.2 us
    unnamed x42, local copies, waits for them, and re-layouts  7.4 us
    convert_element_type x2, other arithmetic, make_bias(): return jnp.where(visible, 0.0, NEG).astype(jnp.bfloat16)  2.11 us
  transfers between devices with their start and end apart: 10, of which 3 were waited for; matrix products, arithmetic and copies ran while one was open for 12% of the time, Pallas kernels for 16%

profile of v15, /device:TPU:0, one launch (start us, length us, event | category | flops | bytes accessed | tf_op | source)
XLA Modules:
  0.0 91.3 jit_solution(7926837292385127787)
XLA Ops:
  0.6 0.7 convert.17
  1.4 0.8 slice.148
  2.3 0.8 slice.149
  3.1 4.9 %collective-permute-start = (bf16[144,512]{1,0:T(8,128)(2,1)S(1)}, bf16[144,512]{1,0:T(8,128)(2,1)S(1)}, u32[]{:S(2)}, u32[]{:S(2)}) collective-permute-start(bf16[144,512]{1,0:T(8,128)(2,1)S(1)} %pad_maximum_fusion.9), channel_id=1, source_target_pairs={{0,4},{4,8},{8,12},{1,5},{5,9},{9,13},{2,6},{6,10},{10,14},{3,7},{... | collective-permute-start | bytes 442376 | tf_op jit(solution)/shard_map/ppermute | solution.py:20
  8.2 0.2 broadcast_multiply_fusion.1
  8.4 0.8 copy-done.3
  9.2 0.2 broadcast_multiply_fusion
  9.4 0.7 copy-done.7
  10.1 0.1 copy-done.8
  10.2 0.9 copy.17
  11.1 0.2 copy-done.4
  11.3 0.9 copy.18
  12.2 0.9 copy.20
  13.1 0.2 copy-done.5
  13.4 0.9 copy.21
  14.3 3.6 %collective-permute-start.3 = (bf16[272,256]{1,0:T(8,128)(2,1)S(1)}, bf16[272,256]{1,0:T(8,128)(2,1)S(1)}, u32[]{:S(2)}, u32[]{:S(2)}) collective-permute-start(bf16[272,256]{1,0:T(8,128)(2,1)S(1)} %pad_maximum_fusion.10), channel_id=1, source_target_pairs={{0,4},{4,8},{8,12},{1,5},{5,9},{9,13},{2,6},{6,10},{10,14},{3,7},{... | collective-permute-start | bytes 417800 | tf_op jit(solution)/shard_map/ppermute | solution.py:20
  18.0 2.9 %collective-permute-start.2 = (bf16[272,256]{1,0:T(8,128)(2,1)S(1)}, bf16[272,256]{1,0:T(8,128)(2,1)S(1)}, u32[]{:S(2)}, u32[]{:S(2)}) collective-permute-start(bf16[272,256]{1,0:T(8,128)(2,1)S(1)} %pad_maximum_fusion.10), channel_id=1, source_target_pairs={{0,8},{4,12},{1,9},{5,13},{2,10},{6,14},{3,11},{7,15},{16,24},{20,... | collective-permute-start | bytes 417800 | tf_op jit(solution)/shard_map/ppermute | solution.py:20
  20.9 1.3 %collective-permute-start.1 = (bf16[272,256]{1,0:T(8,128)(2,1)S(1)}, bf16[272,256]{1,0:T(8,128)(2,1)S(1)}, u32[]{:S(2)}, u32[]{:S(2)}) collective-permute-start(bf16[272,256]{1,0:T(8,128)(2,1)S(1)} %pad_maximum_fusion.10), channel_id=1, source_target_pairs={{0,12},{1,13},{2,14},{3,15},{16,28},{17,29},{18,30},{19,31}} | collective-permute-start | bytes 417800 | tf_op jit(solution)/shard_map/ppermute | solution.py:20
  22.3 0.9 select_convert_fusion.1.bias_ref
  23.2 0.8 pad_maximum_fusion.7
  23.9 7.3 %shard_map.154 = (bf16[256,512]{1,0:T(8,128)(2,1)}, f32[384,128]{1,0:T(8,128)}, f32[384,128]{1,0:T(8,128)}) custom-call(f32[4,4]{1,0:T(4,128)} %sink_ref.4, bf16[256,1024]{1,0:T(8,128)(2,1)} %bitcast.18, bf16[256,1024]{1,0:T(8,128)(2,1)} %bitcast.20, bf16[384,256]{1,0:T(8,128)(2,1)} %get-tuple-element.89.k_ref, bf16[384,256]{1,0:T(8,128)(2,1)} %get-tuple-element.90.v_ref, ...), custom_call_target="tpu_custom_call" | custom-call | flops 503316480 | bytes 2359296 | tf_op jit(solution)/shard_map/pallas_call | solution.py:115
  31.3 0.1 collective-permute-start.4
  31.4 1.2 %select_convert_fusion.bias_ref = bf16[256,1024]{1,0:T(8,128)(2,1)} fusion(s32[1024]{0:T(1024)S(1)} %pad_add_fusion, s32[1024]{0:T(1024)S(1)} %iota_add_fusion, s32[256]{0:T(256)S(1)} %iota_add_fusion.2, s32[256]{0:T(256)S(1)} %copy-done.16, pred[1024]{0:T(1024)(128)(4,1)S(1)} %broadcast_compare_fusion), kind=kLoop, calls=%fused_computation.1 | loop fusion | flops 1835008 | bytes 535552 | tf_op jit(solution)/shard_map/convert_element_type | solution.py:153
  32.6 0.5 collective-permute-done.4
  33.2 0.8 pad_maximum_fusion.3.v_ref
  34.0 0.8 pad_maximum_fusion.2.k_ref
  34.8 21.6 %shard_map.156 = (bf16[256,1024]{1,0:T(8,128)(2,1)}, f32[1024,256]{1,0:T(8,128)}, f32[1024,256]{1,0:T(8,128)}) custom-call(f32[4,4]{1,0:T(4,128)} %sink_ref.5, bf16[256,1024]{1,0:T(8,128)(2,1)} %bitcast.22, bf16[256,1024]{1,0:T(8,128)(2,1)} %bitcast.23, bf16[1024,256]{1,0:T(8,128)(2,1)} %pad_maximum_fusion.2.k_ref, ...), custom_call_target="tpu_custom_call" | custom-call | flops 2684354560 | bytes 6815744 | tf_op jit(solution)/shard_map/pallas_call | solution.py:115
  56.4 1.4 %broadcast_select_fusion = f32[1024,256]{1,0:T(8,128)S(1)} fusion(f32[1024,256]{1,0:T(8,128)} %get-tuple-element.62, f32[1024,256]{1,0:T(8,128)} %get-tuple-element.61, pred[]{:T(512)S(6)} %eq.14), kind=kLoop, calls=%fused_computation.15 | loop fusion | flops 262144 | bytes 3145729 | tf_op jit(solution)/shard_map/jit(_where)/select_n | solution.py:237
  57.8 0.2 collective-permute-start.5
  58.0 7.6 %shard_map.155 = (bf16[256,512]{1,0:T(8,128)(2,1)}, f32[384,128]{1,0:T(8,128)}, f32[384,128]{1,0:T(8,128)}) custom-call(f32[4,4]{1,0:T(4,128)} %sink_ref.4, bf16[256,1024]{1,0:T(8,128)(2,1)} %bitcast.19, bf16[256,1024]{1,0:T(8,128)(2,1)} %bitcast.21, bf16[384,256]{1,0:T(8,128)(2,1)} %get-tuple-element.89.k_ref, bf16[384,256]{1,0:T(8,128)(2,1)} %get-tuple-element.90.v_ref, ...), custom_call_target="tpu_custom_call" | custom-call | flops 503316480 | bytes 2359296 | tf_op jit(solution)/shard_map/pallas_call | solution.py:115
  65.6 1.0 %constant_dynamic-update-slice_fusion = f32[384,256]{1,0:T(8,128)S(1)} fusion(f32[384,256]{1,0:T(8,128)S(1)} %constant_dynamic-update-slice_fusion.1, f32[384,128]{1,0:T(8,128)} %get-tuple-element.55), kind=kLoop, calls=%fused_computation.46 | loop fusion | bytes 393216 | tf_op jit(solution)/shard_map/concatenate | solution.py:243
  66.7 0.9 copy-done.15
  67.6 0.2 fusion.10
  67.9 1.3 %collective-permute-start.6 = (bf16[512,256]{1,0:T(8,128)(2,1)S(1)}, bf16[512,256]{1,0:T(8,128)(2,1)S(1)}, u32[]{:S(2)}, u32[]{:S(2)}) collective-permute-start(bf16[512,256]{1,0:T(8,128)(2,1)S(1)} %pad_maximum_fusion.6), channel_id=1, source_target_pairs={{4,0},{8,4},{12,8},{5,1},{9,5},{13,9},{6,2},{10,6},{14,10},{7,3},{... | collective-permute-start | bytes 786440 | tf_op jit(solution)/shard_map/ppermute | solution.py:20
  69.3 1.3 %collective-permute-start.7 = (bf16[256,256]{1,0:T(8,128)(2,1)S(1)}, bf16[256,256]{1,0:T(8,128)(2,1)S(1)}, u32[]{:S(2)}, u32[]{:S(2)}) collective-permute-start(bf16[256,256]{1,0:T(8,128)(2,1)S(1)} %get-tuple-element.76), channel_id=1, source_target_pairs={{12,0},{13,1},{14,2},{15,3},{28,16},{29,17},{30,18},{31,19}} | collective-permute-start | bytes 393224 | tf_op jit(solution)/shard_map/ppermute | solution.py:20
  70.6 1.3 %collective-permute-start.8 = (bf16[256,256]{1,0:T(8,128)(2,1)S(1)}, bf16[256,256]{1,0:T(8,128)(2,1)S(1)}, u32[]{:S(2)}, u32[]{:S(2)}) collective-permute-start(bf16[256,256]{1,0:T(8,128)(2,1)S(1)} %get-tuple-element.77), channel_id=1, source_target_pairs={{8,0},{12,4},{9,1},{13,5},{10,2},{14,6},{11,3},{15,7},{24,16},{28,... | collective-permute-start | bytes 393224 | tf_op jit(solution)/shard_map/ppermute | solution.py:20
  71.9 10.5 %collective-permute-done.6 = bf16[512,256]{1,0:T(8,128)(2,1)S(1)} collective-permute-done((bf16[512,256]{1,0:T(8,128)(2,1)S(1)}, bf16[512,256]{1,0:T(8,128)(2,1)S(1)}, u32[]{:S(2)}, u32[]{:S(2)}) %collective-permute-start.6) | collective-permute-done | bytes 262176 | tf_op jit(solution)/shard_map/ppermute | solution.py:20
  82.4 0.1 fusion.6
  82.5 3.7 %collective-permute-done.8 = bf16[256,256]{1,0:T(8,128)(2,1)S(1)} collective-permute-done((bf16[256,256]{1,0:T(8,128)(2,1)S(1)}, bf16[256,256]{1,0:T(8,128)(2,1)S(1)}, u32[]{:S(2)}, u32[]{:S(2)}) %collective-permute-start.8) | collective-permute-done | bytes 131104 | tf_op jit(solution)/shard_map/ppermute | solution.py:20
  86.2 0.1 slice_add_fusion.1
  86.4 0.1 collective-permute-start.9
  86.4 0.8 copy-done.11
  87.2 0.1 copy-done.12
  87.4 1.2 %reshape.119 = bf16[256,4,256]{2,1,0:T(4,128)(2,1)} reshape(bf16[256,1024]{1,0:T(8,128)(2,1)S(1)} %pad_maximum_fusion.1) | data formatting | bytes 1048576 | tf_op jit(solution)/shard_map/reshape | solution.py:269
  88.6 1.2 %reshape.121 = bf16[256,4,256]{2,1,0:T(4,128)(2,1)} reshape(bf16[256,1024]{1,0:T(8,128)(2,1)S(1)} %copy-done.6) | data formatting | bytes 1048576 | tf_op jit(solution)/shard_map/reshape | solution.py:272
  89.7 0.1 fusion.2
  89.8 0.7 fusion.12
  90.5 0.7 select_convert_fusion.2
  (69 shorter events, 0.7 us)
Async XLA Ops:
  0.6 7.5 %copy-start.2 = (bf16[256,4,256]{2,1,0:T(4,128)(2,1)S(1)}, bf16[256,4,256]{2,1,0:T(4,128)(2,1)}, u32[]{:S(2)}) copy-start(bf16[256,4,256]{2,1,0:T(4,128)(2,1)} %param.16) | copy-start | bytes 1572868
  3.1 11.1 %collective-permute-start = (bf16[144,512]{1,0:T(8,128)(2,1)S(1)}, bf16[144,512]{1,0:T(8,128)(2,1)S(1)}, u32[]{:S(2)}, u32[]{:S(2)}) collective-permute-start(bf16[144,512]{1,0:T(8,128)(2,1)S(1)} %pad_maximum_fusion.9), channel_id=1, source_target_pairs={{0,4},{4,8},{8,12},{1,5},{5,9},{9,13},{2,6},{6,10},{10,14},{3,7},{... | collective-permute-start | bytes 442376 | tf_op jit(solution)/shard_map/ppermute | solution.py:20
  8.1 1.0 %copy-start.3 = (bf16[256,4,256]{2,1,0:T(4,128)(2,1)S(1)}, bf16[256,4,256]{2,1,0:T(4,128)(2,1)}, u32[]{:S(2)}) copy-start(bf16[256,4,256]{2,1,0:T(4,128)(2,1)} %param.21) | copy-start | bytes 1572868
  9.2 0.9 copy-start.7
  9.2 1.0 %copy-start.8 = (bf16[256,256]{1,0:T(8,128)(2,1)S(1)}, bf16[256,256]{1,0:T(8,128)(2,1)}, u32[]{:S(2)}) copy-start(bf16[256,256]{1,0:T(8,128)(2,1)} %param.22) | copy-start | bytes 393220
  10.2 1.1 %copy-start.4 = (bf16[256,4,256]{2,1,0:T(4,128)(2,1)S(1)}, bf16[256,4,256]{2,1,0:T(4,128)(2,1)}, u32[]{:S(2)}) copy-start(bf16[256,4,256]{2,1,0:T(4,128)(2,1)} %param.19) | copy-start | bytes 1572868
  12.2 1.1 %copy-start.5 = (bf16[256,4,256]{2,1,0:T(4,128)(2,1)S(1)}, bf16[256,4,256]{2,1,0:T(4,128)(2,1)}, u32[]{:S(2)}) copy-start(bf16[256,4,256]{2,1,0:T(4,128)(2,1)} %param.24) | copy-start | bytes 1572868
  14.3 8.0 %copy-start.16 = (s32[256]{0:T(256)S(1)}, s32[256]{0:T(256)}, u32[]{:S(2)}) copy-start(s32[256]{0:T(256)} %param.15) | copy-start | bytes 3076
  14.3 8.9 %copy-start.10 = (bf16[256,256]{1,0:T(8,128)(2,1)S(1)}, bf16[256,256]{1,0:T(8,128)(2,1)}, u32[]{:S(2)}) copy-start(bf16[256,256]{1,0:T(8,128)(2,1)} %param.18) | copy-start | bytes 393220
  14.3 8.8 %copy-start.9 = (bf16[256,256]{1,0:T(8,128)(2,1)S(1)}, bf16[256,256]{1,0:T(8,128)(2,1)}, u32[]{:S(2)}) copy-start(bf16[256,256]{1,0:T(8,128)(2,1)} %param.17) | copy-start | bytes 393220
  14.3 16.9 %collective-permute-start.3 = (bf16[272,256]{1,0:T(8,128)(2,1)S(1)}, bf16[272,256]{1,0:T(8,128)(2,1)S(1)}, u32[]{:S(2)}, u32[]{:S(2)}) collective-permute-start(bf16[272,256]{1,0:T(8,128)(2,1)S(1)} %pad_maximum_fusion.10), channel_id=1, source_target_pairs={{0,4},{4,8},{8,12},{1,5},{5,9},{9,13},{2,6},{6,10},{10,14},{3,7},{... | collective-permute-start | bytes 417800 | tf_op jit(solution)/shard_map/ppermute | solution.py:20
  18.0 13.2 %collective-permute-start.2 = (bf16[272,256]{1,0:T(8,128)(2,1)S(1)}, bf16[272,256]{1,0:T(8,128)(2,1)S(1)}, u32[]{:S(2)}, u32[]{:S(2)}) collective-permute-start(bf16[272,256]{1,0:T(8,128)(2,1)S(1)} %pad_maximum_fusion.10), channel_id=1, source_target_pairs={{0,8},{4,12},{1,9},{5,13},{2,10},{6,14},{3,11},{7,15},{16,24},{20,... | collective-permute-start | bytes 417800 | tf_op jit(solution)/shard_map/ppermute | solution.py:20
  20.9 10.3 %collective-permute-start.1 = (bf16[272,256]{1,0:T(8,128)(2,1)S(1)}, bf16[272,256]{1,0:T(8,128)(2,1)S(1)}, u32[]{:S(2)}, u32[]{:S(2)}) collective-permute-start(bf16[272,256]{1,0:T(8,128)(2,1)S(1)} %pad_maximum_fusion.10), channel_id=1, source_target_pairs={{0,12},{1,13},{2,14},{3,15},{16,28},{17,29},{18,30},{19,31}} | collective-permute-start | bytes 417800 | tf_op jit(solution)/shard_map/ppermute | solution.py:20
  31.3 1.8 %collective-permute-start.4 = (bf16[816,256]{1,0:T(8,128)(2,1)S(1)}, bf16[816,256]{1,0:T(8,128)(2,1)S(1)}, u32[]{:S(2)}, u32[]{:S(2)}) collective-permute-start(bf16[816,256]{1,0:T(8,128)(2,1)S(1)} %pad_maximum_fusion.4), channel_id=1, source_target_pairs={{0,1},{1,0},{2,3},{3,2},{4,5},{5,4},{6,7},{7,6},{8,9},{9,8},{10,11... | collective-permute-start | bytes 1253384 | tf_op jit(solution)/shard_map/ppermute | solution.py:219
  57.8 7.8 %copy-start.14 = (f32[384,128]{1,0:T(8,128)S(1)}, f32[384,128]{1,0:T(8,128)}, u32[]{:S(2)}) copy-start(f32[384,128]{1,0:T(8,128)} %get-tuple-element.54) | copy-start | bytes 589828
  57.8 9.8 %collective-permute-start.5 = (f32[1024,256]{1,0:T(8,128)S(1)}, f32[1024,256]{1,0:T(8,128)S(1)}, u32[]{:S(2)}, u32[]{:S(2)}) collective-permute-start(f32[1024,256]{1,0:T(8,128)S(1)} %broadcast_select_fusion), channel_id=1, source_target_pairs={{0,1},{1,0},{2,3},{3,2},{4,5},{5,4},{6,7},{7,6},{8,9},{9,8},{10,11... | collective-permute-start | bytes 3145736 | tf_op jit(solution)/shard_map/ppermute | solution.py:239
  58.0 8.7 %copy-start.13 = (f32[384,128]{1,0:T(8,128)S(1)}, f32[384,128]{1,0:T(8,128)}, u32[]{:S(2)}) copy-start(f32[384,128]{1,0:T(8,128)} %get-tuple-element.56) | copy-start | bytes 589828
  58.0 9.6 %copy-start.1 = (f32[1024,256]{1,0:T(8,128)S(1)}, f32[1024,256]{1,0:T(8,128)}, u32[]{:S(2)}) copy-start(f32[1024,256]{1,0:T(8,128)} %get-tuple-element.62) | copy-start | bytes 3145732
  65.6 2.1 %copy-start = (f32[1024,256]{1,0:T(8,128)S(1)}, f32[1024,256]{1,0:T(8,128)}, u32[]{:S(2)}) copy-start(f32[1024,256]{1,0:T(8,128)} %get-tuple-element.61) | copy-start | bytes 3145732
  66.6 0.9 %copy-start.15 = (f32[384,128]{1,0:T(8,128)S(1)}, f32[384,128]{1,0:T(8,128)}, u32[]{:S(2)}) copy-start(f32[384,128]{1,0:T(8,128)} %get-tuple-element.57) | copy-start | bytes 589828
  67.9 14.4 %collective-permute-start.6 = (bf16[512,256]{1,0:T(8,128)(2,1)S(1)}, bf16[512,256]{1,0:T(8,128)(2,1)S(1)}, u32[]{:S(2)}, u32[]{:S(2)}) collective-permute-start(bf16[512,256]{1,0:T(8,128)(2,1)S(1)} %pad_maximum_fusion.6), channel_id=1, source_target_pairs={{4,0},{8,4},{12,8},{5,1},{9,5},{13,9},{6,2},{10,6},{14,10},{7,3},{... | collective-permute-start | bytes 786440 | tf_op jit(solution)/shard_map/ppermute | solution.py:20
  69.3 13.2 %collective-permute-start.7 = (bf16[256,256]{1,0:T(8,128)(2,1)S(1)}, bf16[256,256]{1,0:T(8,128)(2,1)S(1)}, u32[]{:S(2)}, u32[]{:S(2)}) collective-permute-start(bf16[256,256]{1,0:T(8,128)(2,1)S(1)} %get-tuple-element.76), channel_id=1, source_target_pairs={{12,0},{13,1},{14,2},{15,3},{28,16},{29,17},{30,18},{31,19}} | collective-permute-start | bytes 393224 | tf_op jit(solution)/shard_map/ppermute | solution.py:20
  70.6 15.6 %collective-permute-start.8 = (bf16[256,256]{1,0:T(8,128)(2,1)S(1)}, bf16[256,256]{1,0:T(8,128)(2,1)S(1)}, u32[]{:S(2)}, u32[]{:S(2)}) collective-permute-start(bf16[256,256]{1,0:T(8,128)(2,1)S(1)} %get-tuple-element.77), channel_id=1, source_target_pairs={{8,0},{12,4},{9,1},{13,5},{10,2},{14,6},{11,3},{15,7},{24,16},{28,... | collective-permute-start | bytes 393224 | tf_op jit(solution)/shard_map/ppermute | solution.py:20
  86.3 1.0 %copy-start.11 = (bf16[256,512]{1,0:T(8,128)(2,1)S(1)}, bf16[256,512]{1,0:T(8,128)(2,1)}, u32[]{:S(2)}) copy-start(bf16[256,512]{1,0:T(8,128)(2,1)} %get-tuple-element.52) | copy-start | bytes 786436
  86.3 1.0 %copy-start.12 = (bf16[256,512]{1,0:T(8,128)(2,1)S(1)}, bf16[256,512]{1,0:T(8,128)(2,1)}, u32[]{:S(2)}) copy-start(bf16[256,512]{1,0:T(8,128)(2,1)} %get-tuple-element.53) | copy-start | bytes 786436
  86.4 3.4 %collective-permute-start.9 = (f32[256,768]{1,0:T(8,128)S(1)}, f32[256,768]{1,0:T(8,128)S(1)}, u32[]{:S(2)}, u32[]{:S(2)}) collective-permute-start(f32[256,768]{1,0:T(8,128)S(1)} %pad_maximum_fusion), channel_id=1, source_target_pairs={{0,1},{1,0},{2,3},{3,2},{4,5},{5,4},{6,7},{7,6},{8,9},{9,8},{10,11... | collective-permute-start | bytes 2359304 | tf_op jit(solution)/shard_map/ppermute | solution.py:263
  87.4 1.2 %copy-start.6 = (bf16[256,1024]{1,0:T(8,128)(2,1)S(1)}, bf16[256,1024]{1,0:T(8,128)(2,1)}, u32[]{:S(2)}) copy-start(bf16[256,1024]{1,0:T(8,128)(2,1)} %get-tuple-element.63) | copy-start | bytes 1572868
